TPU v7x, 32 devices: a whole 2x2x4 slice. The times are simulated.
32 devices in a mesh: ctx: 16 (over z, y, core), head: 2 (over x).
Axes of the slice: x: 2, y: 2, z: 4, core: 2. Of those that a mesh axis runs over, the one named last changes fastest.
Arguments:
- queries: bfloat16 [8192, 32, 128], P('ctx', 'head'), may hold values from -6 to 6
- keys: bfloat16 [8192, 32, 128], P('ctx', 'head'), may hold values from -6 to 6
- values: bfloat16 [8192, 32, 128], P('ctx', 'head'), may hold values from -6 to 6
- far_blocks: int32 [128, 5], replicated, may hold values from 0 to 127, as said below
- out_weight: bfloat16 [4096, 4096], P('head'), may hold values from -0.125 to 0.125
Outputs:
- mixed: bfloat16 [8192, 4096], P('ctx', 'head')
Inputs may be any that keep to these rules, and one draw needn't show every extreme that they name: `far_blocks`: entry j (from 0) of query block q either equals q, or names a block of the group of 8 consecutive blocks that lies 2**j groups before the group of q (groups begin at multiples of 8); it names such a block only when q % 8 is a multiple of 2**j.
All inputs are finite; a program needn't handle non-finite values.
Results may differ from a plain program's by a relative error of at most 0.006.
Values may be sent and summed in bfloat16 or wider, within the bound.
No kernel may reach another device: no remote copies, remote signals or barrier semaphores. Data moves between devices by JAX's collectives and lax.ppermute only.
A program may use at most 192 MiB of HBM per device.

v0:
```python
import math

import jax
import jax.numpy as jnp
from jax import lax
from jax.sharding import PartitionSpec as P

BLOCK = 64
WINDOW = 512
NOFF = 5


def from_behind(value, axis, steps):
    count = lax.axis_size(axis)
    initial, last = (max(0, -steps), min(count, count - steps))
    return lax.ppermute(value, axis, [(source, source + steps) for source in range(initial, last)])


def per_device(queries, keys, values, far_blocks, out_weight):
    rows, heads, width = queries.shape
    per_dev = rows // BLOCK
    device = lax.axis_index("ctx")
    cycle_size = lax.axis_size("ctx")
    scale = 1.0 / math.sqrt(width)
    prev_k, prev_v = from_behind((keys, values), "ctx", 1)
    own = lax.dynamic_slice_in_dim(far_blocks, device * per_dev, per_dev, 0)
    key_blocks = keys.reshape(per_dev, BLOCK, heads, width)
    value_blocks = values.reshape(per_dev, BLOCK, heads, width)
    first = jnp.clip(own[:, 0] - (device - 1) * per_dev, 0, per_dev - 1)
    far_keys = [prev_k.reshape(per_dev, BLOCK, heads, width)[first]]
    far_values = [prev_v.reshape(per_dev, BLOCK, heads, width)[first]]
    for level in range(1, NOFF):
        offset = 2**level
        if offset >= cycle_size:
            far_keys.append(jnp.zeros_like(key_blocks))
            far_values.append(jnp.zeros_like(value_blocks))
            continue
        target = lax.dynamic_slice_in_dim(far_blocks, (device + offset) * per_dev, per_dev, 0)[
            ::offset, level
        ]
        local = jnp.clip(target - device * per_dev, 0, per_dev - 1)
        sent_k, sent_v = from_behind((key_blocks[local], value_blocks[local]), "ctx", offset)
        far_keys.append(jnp.repeat(sent_k, offset, axis=0)[:per_dev])
        far_values.append(jnp.repeat(sent_v, offset, axis=0)[:per_dev])
    far_k = jnp.stack(far_keys, axis=1).reshape(per_dev, NOFF * BLOCK, heads, width)
    far_v = jnp.stack(far_values, axis=1).reshape(per_dev, NOFF * BLOCK, heads, width)
    query_index = device * per_dev + jnp.arange(per_dev, dtype=jnp.int32)
    used = own <= (query_index - WINDOW // BLOCK - 1)[:, None]
    far_mask = jnp.repeat(used, BLOCK, axis=1)
    ext_k = jnp.concatenate([prev_k, keys], axis=0)
    ext_v = jnp.concatenate([prev_v, values], axis=0)
    tile = math.gcd(rows, 256)
    blocks_tile = tile // BLOCK
    span = WINDOW + tile
    results = []
    for index in range(rows // tile):
        start = index * tile
        q_tile = queries[start : start + tile]
        k_win = ext_k[rows + start - WINDOW : rows + start + tile]
        v_win = ext_v[rows + start - WINDOW : rows + start + tile]
        pos_q = device * rows + start + jnp.arange(tile, dtype=jnp.int32)
        pos_k = device * rows + start - WINDOW + jnp.arange(span, dtype=jnp.int32)
        win_ok = (
            (pos_k[None, :] <= pos_q[:, None])
            & (pos_k[None, :] > pos_q[:, None] - WINDOW)
            & (pos_k[None, :] >= 0)
        )
        s_win = (
            jnp.einsum("thd,shd->hts", q_tile, k_win, preferred_element_type=jnp.float32) * scale
        )
        s_win = jnp.where(win_ok[None], s_win, -jnp.inf)
        q_blocks = q_tile.reshape(blocks_tile, BLOCK, heads, width)
        k_far = far_k[index * blocks_tile : (index + 1) * blocks_tile]
        v_far = far_v[index * blocks_tile : (index + 1) * blocks_tile]
        mask_far = far_mask[index * blocks_tile : (index + 1) * blocks_tile]
        s_far = (
            jnp.einsum("bthd,bshd->hbts", q_blocks, k_far, preferred_element_type=jnp.float32)
            * scale
        )
        s_far = jnp.where(mask_far[None, :, None, :], s_far, -jnp.inf)
        top = jnp.maximum(jnp.max(s_win, axis=-1), jnp.max(s_far, axis=-1).reshape(heads, tile))
        p_win = jnp.exp(s_win - top[..., None])
        p_far = jnp.exp(s_far - top.reshape(heads, blocks_tile, BLOCK)[..., None])
        total = jnp.sum(p_win, axis=-1) + jnp.sum(p_far, axis=-1).reshape(heads, tile)
        summed = jnp.einsum(
            "hts,shd->thd", p_win.astype(jnp.bfloat16), v_win, preferred_element_type=jnp.float32
        )
        summed = summed + jnp.einsum(
            "hbts,bshd->bthd", p_far.astype(jnp.bfloat16), v_far, preferred_element_type=jnp.float32
        ).reshape(tile, heads, width)
        results.append((summed / jnp.transpose(total)[:, :, None]).astype(jnp.bfloat16))
    attended = jnp.concatenate(results, axis=0).reshape(rows, heads * width)
    partial_value = jnp.dot(attended, out_weight, preferred_element_type=jnp.float32)
    return lax.psum_scatter(
        partial_value.astype(jnp.bfloat16), "head", scatter_dimension=1, tiled=True
    )


def solution(mesh):
    placed = (
        P("ctx", "head", None),
        P("ctx", "head", None),
        P("ctx", "head", None),
        P(),
        P("head", None),
    )
    return jax.shard_map(
        per_device, mesh=mesh, in_specs=placed, out_specs=P("ctx", "head"), check_vma=False
    )
```

profile of v0, /device:TPU:0, one launch (start us, length us, event | category | flops | bytes accessed | tf_op | source)
XLA Modules:
  0.0 339.0 jit_solution(16597704453311775977)
XLA Ops:
  6.5 4.4 %copy.51 = bf16[512,16,128]{0,2,1:T(8,128)(2,1)} copy(bf16[512,16,128]{2,1,0:T(8,128)(2,1)} %param.7) | data formatting | bytes 4194304 | tf_op args[2]
  19.0 4.1 %collective-permute-start.5 = (bf16[4,64,16,128]{3,2,1,0:T(8,128)(2,1)}, bf16[4,64,16,128]{3,2,1,0:T(8,128)(2,1)}, u32[]{:S(2)}, u32[]{:S(2)}) collective-permute-start(bf16[4,64,16,128]{3,2,1,0:T(8,128)(2,1)} %gather_fusion.4), channel_id=1, source_target_pairs={{0,4},{2,6},{4,8},{6,10},{8,12},{10,14},{12,16},{14,18},{16,20},{1... | collective-permute-start | bytes 3145736 | tf_op jit(solution)/shard_map/ppermute | solution.py:16
  32.3 4.4 %collective-permute-start.7 = (bf16[1,64,16,128]{3,2,1,0:T(8,128)(2,1)}, bf16[1,64,16,128]{3,2,1,0:T(8,128)(2,1)}, u32[]{:S(2)}, u32[]{:S(2)}) collective-permute-start(bf16[1,64,16,128]{3,2,1,0:T(8,128)(2,1)} %constant_dynamic-slice_fusion), channel_id=1, source_target_pairs={{0,16},{2,18},{4,20},{6,22},{8,24},{10,26},{12,28},{14,30},{1,17},... | collective-permute-start | bytes 786440 | tf_op jit(solution)/shard_map/ppermute | solution.py:16
  57.9 4.5 %copy.60 = bf16[512,16,128]{2,1,0:T(8,128)(2,1)} copy(bf16[512,16,128]{0,2,1:T(8,128)(2,1)} %collective-permute-done) | data formatting | bytes 4194304 | tf_op jit(solution)/shard_map/ppermute | solution.py:16
  69.5 5.2 %collective-permute-start.3 = (bf16[2,64,16,128]{3,2,1,0:T(8,128)(2,1)}, bf16[2,64,16,128]{3,2,1,0:T(8,128)(2,1)}, u32[]{:S(2)}, u32[]{:S(2)}) collective-permute-start(bf16[2,64,16,128]{3,2,1,0:T(8,128)(2,1)} %gather_fusion.2), channel_id=1, source_target_pairs={{0,8},{2,10},{4,12},{6,14},{8,16},{10,18},{12,20},{14,22},{16,24},... | collective-permute-start | bytes 1572872 | tf_op jit(solution)/shard_map/ppermute | solution.py:16
  77.9 4.5 %collective-permute-start.4 = (bf16[1,64,16,128]{3,2,1,0:T(8,128)(2,1)}, bf16[1,64,16,128]{3,2,1,0:T(8,128)(2,1)}, u32[]{:S(2)}, u32[]{:S(2)}) collective-permute-start(bf16[1,64,16,128]{3,2,1,0:T(8,128)(2,1)} %constant_dynamic-slice_fusion.1), channel_id=1, source_target_pairs={{0,16},{2,18},{4,20},{6,22},{8,24},{10,26},{12,28},{14,30},{1,17},... | collective-permute-start | bytes 786440 | tf_op jit(solution)/shard_map/ppermute | solution.py:16
  89.7 10.9 %fusion.63 = (bf16[4,5,64,16,128]{4,3,2,0,1:T(8,128)(2,1)}, bf16[4,5,64,16,128]{4,3,2,0,1:T(8,128)(2,1)}) fusion(bf16[8,5,64,16,128]{4,3,2,0,1:T(8,128)(2,1)} %broadcast_dynamic-update-slice_fusion.1), kind=kLoop, calls=%fused_computation.111 | loop fusion | bytes 20971520 | tf_op jit(solution)/shard_map/slice | solution.py:74
  100.6 6.2 %copy.69 = bf16[4,5,64,16,128]{4,2,1,3,0:T(8,128)(2,1)} copy(bf16[4,5,64,16,128]{4,3,2,0,1:T(8,128)(2,1)} %get-tuple-element.32) | data formatting | bytes 10485760 | tf_op jit(solution)/shard_map/slice | solution.py:74
  106.8 4.4 %copy.57 = bf16[8,64,16,128]{3,2,1,0:T(8,128)(2,1)} copy(bf16[8,64,16,128]{3,1,0,2:T(8,128)(2,1)} %bitcast.1) | data formatting | bytes 4194304 | tf_op jit(solution)/shard_map/reshape | solution.py:30
  128.7 11.0 %fusion.62 = (bf16[4,5,64,16,128]{4,3,2,0,1:T(8,128)(2,1)}, bf16[4,5,64,16,128]{4,3,2,0,1:T(8,128)(2,1)}) fusion(bf16[8,5,64,16,128]{4,3,2,0,1:T(8,128)(2,1)} %broadcast_dynamic-update-slice_fusion.2), kind=kLoop, calls=%fused_computation.110 | loop fusion | bytes 20971520 | tf_op jit(solution)/shard_map/slice | solution.py:73
  139.7 6.6 %copy.67 = bf16[4,5,64,16,128]{4,2,1,0,3:T(8,128)(2,1)} copy(bf16[4,5,64,16,128]{4,3,2,0,1:T(8,128)(2,1)} %get-tuple-element.30) | data formatting | bytes 10485760 | tf_op jit(solution)/shard_map/slice | solution.py:73
  148.9 5.7 %fusion.5 = (f32[16,256]{1,0:T(8,128)S(1)}, f32[16,768,256]{2,1,0:T(8,128)}) fusion(pred[256,768]{0,1:T(8,128)(4,1)S(1)} %and_and_fusion, bf16[256,16,128]{2,1,0:T(8,128)(2,1)S(1)} %copy-done.3, bf16[1024,16,128]{2,0,1:T(8,128)(2,1)S(1)} %constant_dynamic-update-slice_fusion), kind=kOutput, calls=%fused_computation.15 | convolution fusion | flops 814739456 | bytes 16990208 | tf_op jit(solution)/shard_map/thd,shd->hts/dot_general | solution.py:69
  154.7 7.0 %bitcast_reduce_fusion = (f32[16,4,64]{2,1,0:T(4,128)S(1)}, f32[16,4,320,64]{2,3,1,0:T(8,128)}) fusion(pred[4,320]{1,0:T(4,128)(4,1)S(1)} %copy-done.14, bf16[4,320,16,128]{3,1,0,2:T(8,128)(2,1)} %bitcast.108, bf16[4,64,16,128]{3,1,0,2:T(8,128)(2,1)S(1)} %bitcast.126), kind=kOutput, calls=%fused_computation.19 | convolution fusion | flops 339472384 | bytes 11552000 | tf_op jit(solution)/shard_map/bthd,bshd->hbts/dot_general | solution.py:77
  162.4 4.7 %fusion.22 = (f32[16,4,64]{2,1,0:T(4,128)}, bf16[16,4,64,320]{3,2,1,0:T(8,128)(2,1)S(1)}) fusion(f32[16,4,320,64]{2,3,1,0:T(8,128)} %get-tuple-element.47, f32[16,4,64]{2,1,0:T(4,128)S(1)} %max.57, pred[4,320]{1,0:T(4,128)(4,1)S(1)} %copy-done.14), kind=kLoop, calls=%fused_computation.37 | loop fusion | flops 6549504 | bytes 7898368 | tf_op jit(solution)/shard_map/reduce_sum | solution.py:84
  173.1 6.3 %copy.61 = bf16[4,5,64,16,128]{4,2,1,3,0:T(8,128)(2,1)} copy(bf16[4,5,64,16,128]{4,3,2,0,1:T(8,128)(2,1)} %get-tuple-element.31) | data formatting | bytes 10485760 | tf_op jit(solution)/shard_map/slice | solution.py:74
  183.2 5.9 %fusion.4 = (f32[16,256]{1,0:T(8,128)S(1)}, f32[16,768,256]{2,1,0:T(8,128)}) fusion(pred[256,768]{0,1:T(8,128)(4,1)S(1)} %and_and_fusion.1, bf16[256,16,128]{2,1,0:T(8,128)(2,1)S(1)} %copy-done.2, bf16[1024,16,128]{2,0,1:T(8,128)(2,1)S(1)} %copy-done.7), kind=kOutput, calls=%fused_computation.14 | convolution fusion | flops 814739456 | bytes 16990208 | tf_op jit(solution)/shard_map/thd,shd->hts/dot_general | solution.py:69
  189.2 7.0 %bitcast_reduce_fusion.1 = (f32[16,4,64]{2,1,0:T(4,128)S(1)}, f32[16,4,320,64]{2,3,1,0:T(8,128)}) fusion(pred[4,320]{1,0:T(4,128)(4,1)S(1)} %copy-done.13, bf16[4,320,16,128]{3,1,0,2:T(8,128)(2,1)} %bitcast.109, bf16[4,64,16,128]{3,1,0,2:T(8,128)(2,1)S(1)} %bitcast.125), kind=kOutput, calls=%fused_computation.22 | convolution fusion | flops 339472384 | bytes 11552000 | tf_op jit(solution)/shard_map/bthd,bshd->hbts/dot_general | solution.py:77
  196.3 4.1 %fusion.20 = (f32[16,4,64]{2,1,0:T(4,128)S(1)}, bf16[16,4,64,320]{3,2,1,0:T(8,128)(2,1)S(1)}) fusion(f32[16,4,320,64]{2,3,1,0:T(8,128)} %get-tuple-element.51, f32[16,4,64]{2,1,0:T(4,128)S(1)} %max.55, pred[4,320]{1,0:T(4,128)(4,1)S(1)} %copy-done.13), kind=kLoop, calls=%fused_computation.35 | loop fusion | flops 6549504 | bytes 7898368 | tf_op jit(solution)/shard_map/reduce_sum | solution.py:84
  205.0 7.2 %fusion.2 = f32[16,256]{1,0:T(8,128)S(1)} fusion(f32[16,768,256]{2,1,0:T(8,128)} %get-tuple-element.45, f32[16,256]{1,0:T(8,128)S(1)} %max.56, pred[256,768]{0,1:T(8,128)(4,1)S(1)} %and_and_fusion), kind=kLoop, calls=%fused_computation.12 | loop fusion | flops 12578816 | bytes 12812288 | tf_op jit(solution)/shard_map/reduce_sum | solution.py:84
  212.9 7.2 %fusion = f32[16,256]{1,0:T(8,128)S(1)} fusion(f32[16,768,256]{2,1,0:T(8,128)} %get-tuple-element.49, f32[16,256]{1,0:T(8,128)S(1)} %max.54, pred[256,768]{0,1:T(8,128)(4,1)S(1)} %and_and_fusion.1), kind=kLoop, calls=%fused_computation.10 | loop fusion | flops 12578816 | bytes 12812288 | tf_op jit(solution)/shard_map/reduce_sum | solution.py:84
  220.8 4.7 %fusion.36 = bf16[256,16,128]{0,2,1:T(8,128)(2,1)S(1)} fusion(f32[256,16,128]{0,2,1:T(8,128)S(1)} %copy-done.5, f32[16,768,256]{2,1,0:T(8,128)S(1)} %bitcast.114, f32[16,256]{1,0:T(8,128)} %copy-done.10, pred[256,768]{0,1:T(8,128)(4,1)} %copy-done.8, bf16[512,16,128]{0,2,1:T(8,128)(2,1)S(1)} %copy-done.4, bf16[512,16,128]{0,2,1:T(8,128)(2,1)} %collective-permute-done, ...), kind=kOutput, calls=%fused_computation.55 | convolution fusion | flops 825753600 | bytes 20152320 | tf_op jit(solution)/shard_map/hts,shd->thd/dot_general | solution.py:85
  225.5 9.1 %fusion.38 = bf16[256,16,128]{0,2,1:T(8,128)(2,1)S(1)} fusion(f32[256,16,128]{0,2,1:T(8,128)} %copy.64, f32[16,768,256]{2,1,0:T(8,128)} %get-tuple-element.49, f32[16,256]{1,0:T(8,128)} %copy-done.11, pred[256,768]{0,1:T(8,128)(4,1)} %copy-done.9, bf16[512,16,128]{0,2,1:T(8,128)(2,1)} %collective-permute-done, bf16[512,16,128]{0,2,1:T(8,128)(2,1)S(1)} %copy-done.4, ...), kind=kOutput, calls=%fused_computation.59 | convolution fusion | flops 825753600 | bytes 20152320 | tf_op jit(solution)/shard_map/hts,shd->thd/dot_general | solution.py:85
  234.7 14.1 %convolution_convert_fusion = bf16[512,4096]{1,0:T(8,128)(2,1)} fusion(bf16[512,2048]{0,1:T(8,128)(2,1)S(1)} %bitcast.127, bf16[2048,4096]{1,0:T(8,128)(2,1)} %param.9), kind=kOutput, calls=%fused_computation.34 | convolution fusion | flops 8592031744 | bytes 23068672 | tf_op jit(solution)/shard_map/dot_general | solution.py:93
  248.9 83.0 %reduce-scatter.2.cloned.1.call-done = bf16[512,2048]{1,0:T(8,128)(2,1)} async-done(((bf16[512,4096]{1,0:T(8,128)(2,1)}), bf16[512,2048]{1,0:T(8,128)(2,1)}) %reduce-scatter.2.cloned.1.call-update) | async-done | bytes 2097168 | tf_op jit(solution)/shard_map/reduce_scatter | solution.py:94
  (141 shorter events, 92.2 us)
Async XLA Ops:
  6.5 30.1 %copy-start = (bf16[512,16,128]{2,1,0:T(8,128)(2,1)S(1)}, bf16[512,16,128]{2,1,0:T(8,128)(2,1)}, u32[]{:S(2)}) copy-start(bf16[512,16,128]{2,1,0:T(8,128)(2,1)} %param.6) | copy-start | bytes 6291460
  6.5 325.4 %reduce-scatter.2.cloned.1.call-start = ((), (), s32[]{:S(2)}) async-start(), calls=%async_computation.1 | async-start | bytes 6291456 | tf_op jit(solution)/shard_map/reduce_scatter | solution.py:94
  11.0 31.2 %copy-start.12 = (s32[128,5]{0,1:T(8,128)S(1)}, s32[128,5]{0,1:T(8,128)}, u32[]{:S(2)}) copy-start(s32[128,5]{0,1:T(8,128)} %param.8) | copy-start | bytes 7684
  11.0 43.9 %collective-permute-start = (bf16[512,16,128]{0,2,1:T(8,128)(2,1)}, bf16[512,16,128]{0,2,1:T(8,128)(2,1)}, u32[]{:S(2)}, u32[]{:S(2)}) collective-permute-start(bf16[512,16,128]{0,2,1:T(8,128)(2,1)} %copy.51), channel_id=1, source_target_pairs={{0,2},{2,4},{4,6},{6,8},{8,10},{10,12},{12,14},{14,16},{16,18},{18... | collective-permute-start | bytes 6291464 | tf_op jit(solution)/shard_map/ppermute | solution.py:16
  19.0 50.5 %collective-permute-start.5 = (bf16[4,64,16,128]{3,2,1,0:T(8,128)(2,1)}, bf16[4,64,16,128]{3,2,1,0:T(8,128)(2,1)}, u32[]{:S(2)}, u32[]{:S(2)}) collective-permute-start(bf16[4,64,16,128]{3,2,1,0:T(8,128)(2,1)} %gather_fusion.4), channel_id=1, source_target_pairs={{0,4},{2,6},{4,8},{6,10},{8,12},{10,14},{12,16},{14,18},{16,20},{1... | collective-permute-start | bytes 3145736 | tf_op jit(solution)/shard_map/ppermute | solution.py:16
  26.2 51.7 %collective-permute-start.6 = (bf16[2,64,16,128]{3,2,1,0:T(8,128)(2,1)}, bf16[2,64,16,128]{3,2,1,0:T(8,128)(2,1)}, u32[]{:S(2)}, u32[]{:S(2)}) collective-permute-start(bf16[2,64,16,128]{3,2,1,0:T(8,128)(2,1)} %gather_fusion.5), channel_id=1, source_target_pairs={{0,8},{2,10},{4,12},{6,14},{8,16},{10,18},{12,20},{14,22},{16,24},... | collective-permute-start | bytes 1572872 | tf_op jit(solution)/shard_map/ppermute | solution.py:16
  32.3 53.3 %collective-permute-start.7 = (bf16[1,64,16,128]{3,2,1,0:T(8,128)(2,1)}, bf16[1,64,16,128]{3,2,1,0:T(8,128)(2,1)}, u32[]{:S(2)}, u32[]{:S(2)}) collective-permute-start(bf16[1,64,16,128]{3,2,1,0:T(8,128)(2,1)} %constant_dynamic-slice_fusion), channel_id=1, source_target_pairs={{0,16},{2,18},{4,20},{6,22},{8,24},{10,26},{12,28},{14,30},{1,17},... | collective-permute-start | bytes 786440 | tf_op jit(solution)/shard_map/ppermute | solution.py:16
  38.5 68.3 %collective-permute-start.1 = (bf16[512,16,128]{2,0,1:T(8,128)(2,1)}, bf16[512,16,128]{2,0,1:T(8,128)(2,1)}, u32[]{:S(2)}, u32[]{:S(2)}) collective-permute-start(bf16[512,16,128]{2,0,1:T(8,128)(2,1)} %copy.53), channel_id=1, source_target_pairs={{0,2},{2,4},{4,6},{6,8},{8,10},{10,12},{12,14},{14,16},{16,18},{18... | collective-permute-start | bytes 6291464 | tf_op jit(solution)/shard_map/ppermute | solution.py:16
  45.8 159.2 %copy-start.8 = (pred[256,768]{0,1:T(8,128)(4,1)}, pred[256,768]{0,1:T(8,128)(4,1)S(1)}, u32[]{:S(2)}) copy-start(pred[256,768]{0,1:T(8,128)(4,1)S(1)} %and_and_fusion) | copy-start | bytes 589828
  46.1 166.8 %copy-start.9 = (pred[256,768]{0,1:T(8,128)(4,1)}, pred[256,768]{0,1:T(8,128)(4,1)S(1)}, u32[]{:S(2)}) copy-start(pred[256,768]{0,1:T(8,128)(4,1)S(1)} %and_and_fusion.1) | copy-start | bytes 589828
  54.9 63.4 %collective-permute-start.2 = (bf16[4,64,16,128]{3,2,1,0:T(8,128)(2,1)}, bf16[4,64,16,128]{3,2,1,0:T(8,128)(2,1)}, u32[]{:S(2)}, u32[]{:S(2)}) collective-permute-start(bf16[4,64,16,128]{3,2,1,0:T(8,128)(2,1)} %gather_fusion.1), channel_id=1, source_target_pairs={{0,4},{2,6},{4,8},{6,10},{8,12},{10,14},{12,16},{14,18},{16,20},{1... | collective-permute-start | bytes 3145736 | tf_op jit(solution)/shard_map/ppermute | solution.py:16
  69.5 52.0 %collective-permute-start.3 = (bf16[2,64,16,128]{3,2,1,0:T(8,128)(2,1)}, bf16[2,64,16,128]{3,2,1,0:T(8,128)(2,1)}, u32[]{:S(2)}, u32[]{:S(2)}) collective-permute-start(bf16[2,64,16,128]{3,2,1,0:T(8,128)(2,1)} %gather_fusion.2), channel_id=1, source_target_pairs={{0,8},{2,10},{4,12},{6,14},{8,16},{10,18},{12,20},{14,22},{16,24},... | collective-permute-start | bytes 1572872 | tf_op jit(solution)/shard_map/ppermute | solution.py:16
  77.9 46.7 %collective-permute-start.4 = (bf16[1,64,16,128]{3,2,1,0:T(8,128)(2,1)}, bf16[1,64,16,128]{3,2,1,0:T(8,128)(2,1)}, u32[]{:S(2)}, u32[]{:S(2)}) collective-permute-start(bf16[1,64,16,128]{3,2,1,0:T(8,128)(2,1)} %constant_dynamic-slice_fusion.1), channel_id=1, source_target_pairs={{0,16},{2,18},{4,20},{6,22},{8,24},{10,26},{12,28},{14,30},{1,17},... | collective-permute-start | bytes 786440 | tf_op jit(solution)/shard_map/ppermute | solution.py:16
  169.7 9.8 %slice-start.4 = ((s8[5242880]{0:T(1024)(128)(4,1)}), s8[1048576]{0:T(1024)(128)(4,1)S(1)}, s32[]{:S(2)}) async-start(s8[5242880]{0:T(1024)(128)(4,1)} %bitcast.106), calls=%async_computation.6 | async-start | bytes 2097152
  172.2 32.8 %copy-start.10 = (f32[16,256]{1,0:T(8,128)}, f32[16,256]{1,0:T(8,128)S(1)}, u32[]{:S(2)}) copy-start(f32[16,256]{1,0:T(8,128)S(1)} %max.56) | copy-start | bytes 49156
  173.1 6.3 %slice-start.5 = ((s8[5242880]{0:T(1024)(128)(4,1)}), s8[4194304]{0:T(1024)(128)(4,1)S(1)}, s32[]{:S(2)}) async-start(s8[5242880]{0:T(1024)(128)(4,1)} %bitcast.106), calls=%async_computation.7 | async-start | bytes 8388608
  183.2 6.0 %copy-start.1 = (bf16[256,16,128]{2,0,1:T(8,128)(2,1)S(1)}, bf16[256,16,128]{2,0,1:T(8,128)(2,1)}, u32[]{:S(2)}) copy-start(bf16[256,16,128]{2,0,1:T(8,128)(2,1)} %copy.75) | copy-start | bytes 3145732
  183.2 6.0 %copy-start.13 = (pred[4,320]{1,0:T(4,128)(4,1)S(1)}, pred[4,320]{1,0:T(4,128)(4,1)}, u32[]{:S(2)}) copy-start(pred[4,320]{1,0:T(4,128)(4,1)} %broadcast_in_dim.91) | copy-start | bytes 3844
  204.9 8.0 %copy-start.11 = (f32[16,256]{1,0:T(8,128)}, f32[16,256]{1,0:T(8,128)S(1)}, u32[]{:S(2)}) copy-start(f32[16,256]{1,0:T(8,128)S(1)} %max.54) | copy-start | bytes 49156
  205.0 15.7 %slice-start.6 = ((s8[12582912]{0:T(1024)(128)(4,1)}), s8[4194304]{0:T(1024)(128)(4,1)S(1)}, s32[]{:S(2)}) async-start(s8[12582912]{0:T(1024)(128)(4,1)} %bitcast.113), calls=%async_computation.8 | async-start | bytes 8388608
  205.0 15.7 %slice-start.7 = ((s8[12582912]{0:T(1024)(128)(4,1)}), s8[4194304]{0:T(1024)(128)(4,1)S(1)}, s32[]{:S(2)}) async-start(s8[12582912]{0:T(1024)(128)(4,1)} %bitcast.113), calls=%async_computation.9 | async-start | bytes 8388608
  212.9 7.9 %slice-start.8 = ((s8[12582912]{0:T(1024)(128)(4,1)}), s8[4194304]{0:T(1024)(128)(4,1)S(1)}, s32[]{:S(2)}) async-start(s8[12582912]{0:T(1024)(128)(4,1)} %bitcast.113), calls=%async_computation.10 | async-start | bytes 8388608
  212.9 7.9 %copy-start.4 = (bf16[512,16,128]{0,2,1:T(8,128)(2,1)S(1)}, bf16[512,16,128]{0,2,1:T(8,128)(2,1)}, u32[]{:S(2)}) copy-start(bf16[512,16,128]{0,2,1:T(8,128)(2,1)} %copy.51) | copy-start | bytes 6291460
  212.9 7.9 %copy-start.5 = (f32[256,16,128]{0,2,1:T(8,128)S(1)}, f32[256,16,128]{0,2,1:T(8,128)}, u32[]{:S(2)}) copy-start(f32[256,16,128]{0,2,1:T(8,128)} %copy.72) | copy-start | bytes 6291460
  (9 other events, 40.3 us)
Sparse Core Ops, SparseCore 0:
  249.0 82.8 reduce-scatter.1
where the time goes:
time: 345 us; the launch traced here: 339 us
  local copies, waits for them, and re-layouts  128 us (37%)
  waiting for transfers between devices  83.1 us (24%)
  matrix products  56 us (16%)
  starting transfers between devices  31.2 us (9%)
  other arithmetic  26.2 us (8%)
  between operations  14.6 us (4%)
    reduce_scatter x1, waiting for transfers between devices, per_device(): lax.psum_scatter(partial_value.astype(jnp.bfloat16), 'head', scatter_dime...  83 us
    ppermute x8, starting transfers between devices, from_behind(): lax.ppermute(value, axis, [(source, source + steps) for source in range(i...  31.2 us
    unnamed x61, local copies, waits for them, and re-layouts  31.1 us
    slice x3, local copies, waits for them, and re-layouts, per_device(): v_far = far_v[index * blocks_tile:(index + 1) * blocks_tile]  23.4 us
    slice x3, local copies, waits for them, and re-layouts, per_device(): k_far = far_k[index * blocks_tile:(index + 1) * blocks_tile]  21.3 us
    reduce_sum x2, other arithmetic, per_device(): jnp.sum(p_win, axis=-1) + jnp.sum(p_far, axis=-1).reshape(heads, tile)  14.5 us
    dot_general x1, matrix products, per_device(): jnp.dot(attended, out_weight, preferred_element_type=jnp.float32)  14.1 us
    dot_general x2, matrix products, per_device(): jnp.einsum('bthd,bshd->hbts', q_blocks, k_far, preferred_element_type=jnp...  14 us
  transfers between devices with their start and end apart: 9, of which 1 were waited for; matrix products, arithmetic and copies ran while one was open for 24% of the time, Pallas kernels for 0%

commit v1 on v0

v1 whole, which is shorter than its diff:
```python
import functools
import math

import jax
import jax.numpy as jnp
from jax import lax
from jax.experimental import pallas as pl
from jax.experimental.pallas import tpu as pltpu
from jax.sharding import PartitionSpec as P

BLOCK = 64
WINDOW = 512
NOFF = 5
HEADS_PER_STEP = 2


def from_behind(value, axis, steps):
    count = lax.axis_size(axis)
    initial, last = (max(0, -steps), min(count, count - steps))
    return lax.ppermute(value, axis, [(source, source + steps) for source in range(initial, last)])


def attention_kernel(levels, per_dev, width, scale, meta_ref, used_ref, q_ref, kp_ref, vp_ref,
                     ko_ref, vo_ref, *rest):
    far_refs = rest[:-1]
    o_ref = rest[-1]
    prev_ok = meta_ref[0] > 0
    neg = jnp.float32(-jnp.inf)
    for hh in range(HEADS_PER_STEP):
        cols = pl.ds(hh * width, width)
        for i in range(per_dev):
            lo = i * BLOCK
            q = q_ref[lo:lo + BLOCK, cols]
            pieces = []

            def score(keys):
                return lax.dot_general(
                    q, keys, (((1,), (1,)), ((), ())), preferred_element_type=jnp.float32
                ) * scale

            n_prev = per_dev * BLOCK - lo
            s_p = score(kp_ref[lo:, cols])
            r_ids = lax.broadcasted_iota(jnp.int32, (BLOCK, n_prev), 0)
            c_ids = lax.broadcasted_iota(jnp.int32, (BLOCK, n_prev), 1)
            s_p = jnp.where((c_ids > r_ids) & prev_ok, s_p, neg)
            pieces.append((s_p, vp_ref[lo:, cols]))
            n_own = lo + BLOCK
            s_o = score(ko_ref[:n_own, cols])
            r_ids = lax.broadcasted_iota(jnp.int32, (BLOCK, n_own), 0)
            c_ids = lax.broadcasted_iota(jnp.int32, (BLOCK, n_own), 1)
            s_o = jnp.where(c_ids <= r_ids + lo, s_o, neg)
            pieces.append((s_o, vo_ref[:n_own, cols]))
            start = pl.multiple_of(meta_ref[1 + i] * BLOCK, BLOCK)
            s_f = score(kp_ref[pl.ds(start, BLOCK), cols])
            s_f = jnp.where(used_ref[i * NOFF] > 0, s_f, neg)
            pieces.append((s_f, vp_ref[pl.ds(start, BLOCK), cols]))
            for level, (k_ref, v_ref) in zip(levels, zip(far_refs[0::2], far_refs[1::2])):
                offset = 2**level
                if i % offset:
                    continue
                flo = (i // offset) * BLOCK
                s_f = score(k_ref[flo:flo + BLOCK, cols])
                s_f = jnp.where(used_ref[i * NOFF + level] > 0, s_f, neg)
                pieces.append((s_f, v_ref[flo:flo + BLOCK, cols]))
            top = pieces[0][0].max(axis=1, keepdims=True)
            for s, _ in pieces[1:]:
                top = jnp.maximum(top, s.max(axis=1, keepdims=True))
            total = None
            summed = None
            for s, v in pieces:
                p = jnp.exp(s - top)
                part_total = p.sum(axis=1, keepdims=True)
                part = jnp.dot(p.astype(jnp.bfloat16), v, preferred_element_type=jnp.float32)
                total = part_total if total is None else total + part_total
                summed = part if summed is None else summed + part
            o_ref[lo:lo + BLOCK, cols] = (summed / total).astype(o_ref.dtype)


def per_device(queries, keys, values, far_blocks, out_weight):
    rows, heads, width = queries.shape
    per_dev = rows // BLOCK
    device = lax.axis_index("ctx")
    cycle_size = lax.axis_size("ctx")
    scale = 1.0 / math.sqrt(width)
    prev_k, prev_v = from_behind((keys, values), "ctx", 1)
    key_blocks = keys.reshape(per_dev, BLOCK, heads, width)
    value_blocks = values.reshape(per_dev, BLOCK, heads, width)
    levels = []
    far_arrays = []
    for level in range(1, NOFF):
        offset = 2**level
        if offset >= cycle_size:
            continue
        target = lax.dynamic_slice_in_dim(far_blocks, (device + offset) * per_dev, per_dev, 0)[
            ::offset, level
        ]
        local = jnp.clip(target - device * per_dev, 0, per_dev - 1)
        sent_k, sent_v = from_behind((key_blocks[local], value_blocks[local]), "ctx", offset)
        levels.append(level)
        far_arrays.append(sent_k.reshape(-1, heads * width))
        far_arrays.append(sent_v.reshape(-1, heads * width))

    own = lax.dynamic_slice_in_dim(far_blocks, device * per_dev, per_dev, 0)
    query_index = device * per_dev + jnp.arange(per_dev, dtype=jnp.int32)
    used = (own <= (query_index - WINDOW // BLOCK - 1)[:, None]).astype(jnp.int32).reshape(-1)
    pick = jnp.clip(own[:, 0] - (device - 1) * per_dev, 0, per_dev - 1)
    meta = jnp.concatenate([(device > 0).astype(jnp.int32)[None], pick.astype(jnp.int32)])

    flat = lambda a: a.reshape(rows, heads * width)
    cw = HEADS_PER_STEP * width
    row_spec = pl.BlockSpec((rows, cw), lambda h, *_: (0, h))
    far_specs = [pl.BlockSpec((a.shape[0], cw), lambda h, *_: (0, h)) for a in far_arrays]
    n_keys = WINDOW + BLOCK + NOFF * BLOCK
    cost = pl.CostEstimate(
        flops=4 * rows * heads * width * n_keys,
        transcendentals=rows * heads * n_keys,
        bytes_accessed=2 * heads * width * (6 * rows + sum(a.shape[0] for a in far_arrays)),
    )
    attended = pl.pallas_call(
        functools.partial(attention_kernel, levels, per_dev, width, scale),
        out_shape=jax.ShapeDtypeStruct((rows, heads * width), queries.dtype),
        grid_spec=pltpu.PrefetchScalarGridSpec(
            num_scalar_prefetch=2,
            grid=(heads // HEADS_PER_STEP,),
            in_specs=[row_spec] * 5 + far_specs,
            out_specs=row_spec,
        ),
        compiler_params=pltpu.CompilerParams(dimension_semantics=("arbitrary",)),
        cost_estimate=cost,
    )(meta, used, flat(queries), flat(prev_k), flat(prev_v), flat(keys), flat(values), *far_arrays)

    n_head = lax.axis_size("head")
    if n_head != 2:
        partial_value = jnp.dot(attended, out_weight, preferred_element_type=jnp.float32)
        return lax.psum_scatter(
            partial_value.astype(jnp.bfloat16), "head", scatter_dimension=1, tiled=True
        )
    hidx = lax.axis_index("head")
    split_w = out_weight.reshape(out_weight.shape[0], 2, -1)
    w_other = lax.dynamic_index_in_dim(split_w, 1 - hidx, axis=1, keepdims=False)
    w_own = lax.dynamic_index_in_dim(split_w, hidx, axis=1, keepdims=False)
    p_other = jnp.dot(attended, w_other, preferred_element_type=jnp.float32).astype(jnp.bfloat16)
    received = lax.ppermute(p_other, "head", [(0, 1), (1, 0)])
    p_own = jnp.dot(attended, w_own, preferred_element_type=jnp.float32).astype(jnp.bfloat16)
    return (p_own.astype(jnp.float32) + received.astype(jnp.float32)).astype(jnp.bfloat16)


def solution(mesh):
    placed = (
        P("ctx", "head", None),
        P("ctx", "head", None),
        P("ctx", "head", None),
        P(),
        P("head", None),
    )
    return jax.shard_map(
        per_device, mesh=mesh, in_specs=placed, out_specs=P("ctx", "head"), check_vma=False
    )
```

time: 345 us -> 259 us (0.75)
  the two profiles are of different devices: /device:TPU:0 before, /device:TPU:1 now
where the time goes in v1:
time: 259 us; the launch traced here: 258 us
  starting transfers between devices  102 us (39%)
  local copies, waits for them, and re-layouts  65 us (25%)
  Pallas kernels  45.5 us (18%)
  waiting for transfers between devices  24 us (9%)
  matrix products  19.5 us (8%)
    ppermute x8, starting transfers between devices, from_behind(): lax.ppermute(value, axis, [(source, source + steps) for source in range(i...  101 us
    pallas_call x1, Pallas kernels, per_device(): pl.pallas_call(functools.partial(attention_kernel, levels, per_dev, width...  45.5 us
    unnamed x16, local copies, waits for them, and re-layouts  44.4 us
    ppermute x1, waiting for transfers between devices, per_device(): received = lax.ppermute(p_other, 'head', [(0, 1), (1, 0)])  24 us
    dot_general x1, matrix products, per_device(): jnp.dot(attended, w_other, preferred_element_type=jnp.float32)  10 us
    dot_general x1, matrix products, per_device(): jnp.dot(attended, w_own, preferred_element_type=jnp.float32)  9.44 us
    gather x3, local copies, waits for them, and re-layouts, per_device(): value_blocks[local]  7.02 us
    gather x3, local copies, waits for them, and re-layouts, per_device(): key_blocks[local]  5.77 us
  transfers between devices with their start and end apart: 9, of which 1 were waited for; matrix products, arithmetic and copies ran while one was open for 24% of the time, Pallas kernels for 0%

profile of v1, /device:TPU:1, one launch (start us, length us, event | category | flops | bytes accessed | tf_op | source)
XLA Modules:
  0.0 257.5 jit_solution(10053656447616150416)
XLA Ops:
  0.0 4.5 %collective-permute-start = (bf16[512,16,128]{2,1,0:T(8,128)(2,1)}, bf16[512,16,128]{2,1,0:T(8,128)(2,1)}, u32[]{:S(2)}, u32[]{:S(2)}) collective-permute-start(bf16[512,16,128]{2,1,0:T(8,128)(2,1)} %param.6), channel_id=1, source_target_pairs={{0,2},{2,4},{4,6},{6,8},{8,10},{10,12},{12,14},{14,16},{16,18},{18... | collective-permute-start | bytes 6291464 | tf_op jit(solution)/shard_map/ppermute | solution.py:20
  7.7 4.9 %collective-permute-start.6 = (bf16[1,64,16,128]{3,2,1,0:T(8,128)(2,1)S(1)}, bf16[1,64,16,128]{3,2,1,0:T(8,128)(2,1)}, u32[]{:S(2)}, u32[]{:S(2)}) collective-permute-start(bf16[1,64,16,128]{3,2,1,0:T(8,128)(2,1)S(1)} %constant_dynamic-slice_fusion.1), channel_id=1, source_target_pairs={{0,16},{2,18},{4,20},{6,22},{8,24},{10,26},{12,28},{14,30},{1,17},... | collective-permute-start | bytes 786440 | tf_op jit(solution)/shard_map/ppermute | solution.py:20
  12.7 2.2 collective-permute-start.1
  16.5 2.0 collective-permute-start.7
  18.7 3.0 %gather_fusion.2 = bf16[2,64,16,128]{3,2,1,0:T(8,128)(2,1)} fusion(bf16[8,64,16,128]{3,2,1,0:T(8,128)(2,1)} %bitcast.83, s32[1024]{0:T(1024)S(1)} %pad_clamp_fusion), kind=kCustom, calls=%fused_computation.2 | custom fusion | bytes 1048584 | tf_op jit(solution)/shard_map/gather | solution.py:98
  21.7 4.0 %collective-permute-start.4 = (bf16[2,64,16,128]{3,2,1,0:T(8,128)(2,1)}, bf16[2,64,16,128]{3,2,1,0:T(8,128)(2,1)}, u32[]{:S(2)}, u32[]{:S(2)}) collective-permute-start(bf16[2,64,16,128]{3,2,1,0:T(8,128)(2,1)} %gather_fusion.2), channel_id=1, source_target_pairs={{0,8},{2,10},{4,12},{6,14},{8,16},{10,18},{12,20},{14,22},{16,24},... | collective-permute-start | bytes 1572872 | tf_op jit(solution)/shard_map/ppermute | solution.py:20
  25.8 2.3 gather_fusion.1
  29.8 21.7 %collective-permute-start.2 = (bf16[4,64,16,128]{3,2,1,0:T(8,128)(2,1)}, bf16[4,64,16,128]{3,2,1,0:T(8,128)(2,1)}, u32[]{:S(2)}, u32[]{:S(2)}) collective-permute-start(bf16[4,64,16,128]{3,2,1,0:T(8,128)(2,1)} %gather_fusion), channel_id=1, source_target_pairs={{0,4},{2,6},{4,8},{6,10},{8,12},{10,14},{12,16},{14,18},{16,20},{1... | collective-permute-start | bytes 3145736 | tf_op jit(solution)/shard_map/ppermute | solution.py:20
  51.5 48.0 %collective-permute-start.3 = (bf16[4,64,16,128]{3,2,1,0:T(8,128)(2,1)S(1)}, bf16[4,64,16,128]{3,2,1,0:T(8,128)(2,1)}, u32[]{:S(2)}, u32[]{:S(2)}) collective-permute-start(bf16[4,64,16,128]{3,2,1,0:T(8,128)(2,1)S(1)} %gather_fusion.1), channel_id=1, source_target_pairs={{0,4},{2,6},{4,8},{6,10},{8,12},{10,14},{12,16},{14,18},{16,20},{1... | collective-permute-start | bytes 3145736 | tf_op jit(solution)/shard_map/ppermute | solution.py:20
  99.5 3.0 %gather_fusion.3 = bf16[2,64,16,128]{3,2,1,0:T(8,128)(2,1)} fusion(bf16[8,64,16,128]{3,2,1,0:T(8,128)(2,1)} %bitcast.88, s32[1024]{0:T(1024)S(1)} %pad_clamp_fusion), kind=kCustom, calls=%fused_computation.3 | custom fusion | bytes 1048584 | tf_op jit(solution)/shard_map/gather | solution.py:98
  103.2 3.5 %copy.36 = bf16[64,8,16,128]{3,1,2,0:T(8,128)(2,1)} copy(bf16[64,8,16,128]{3,2,1,0:T(8,128)(2,1)} %bitcast.94) | data formatting | bytes 4194304
  106.7 22.5 %copy.9 = bf16[2048,4096]{0,1:T(8,128)(2,1)} copy(bf16[2048,4096]{1,0:T(8,128)(2,1)} %param.9) | data formatting | bytes 33554432 | tf_op args[4]
  129.9 13.4 %collective-permute-start.5 = (bf16[2,64,16,128]{3,2,1,0:T(8,128)(2,1)}, bf16[2,64,16,128]{3,2,1,0:T(8,128)(2,1)S(1)}, u32[]{:S(2)}, u32[]{:S(2)}) collective-permute-start(bf16[2,64,16,128]{3,2,1,0:T(8,128)(2,1)} %gather_fusion.3), channel_id=1, source_target_pairs={{0,8},{2,10},{4,12},{6,14},{8,16},{10,18},{12,20},{14,22},{16,24},... | collective-permute-start | bytes 1572872 | tf_op jit(solution)/shard_map/ppermute | solution.py:20
  143.3 5.7 %copy_bitcast_fusion = (bf16[512,2048]{1,0:T(8,128)(2,1)}, bf16[512,2048]{1,0:T(8,128)(2,1)}) fusion(bf16[64,8,16,128]{3,2,1,0:T(8,128)(2,1)} %bitcast.89, bf16[64,8,16,128]{3,2,1,0:T(8,128)(2,1)S(1)} %bitcast.85), kind=kLoop, calls=%fused_computation.13 | loop fusion | bytes 8388608 | tf_op jit(solution)/shard_map/reshape | solution.py:109
  150.7 1.7 copy.41
  152.4 2.0 copy.40
  155.3 2.5 copy.38
  157.9 2.5 copy.37
  160.3 3.5 %copy.35 = bf16[64,8,16,128]{3,1,2,0:T(8,128)(2,1)} copy(bf16[64,8,16,128]{3,2,1,0:T(8,128)(2,1)} %bitcast.16) | data formatting | bytes 4194304
  163.8 3.5 %copy.34 = bf16[64,8,16,128]{3,1,2,0:T(8,128)(2,1)} copy(bf16[64,8,16,128]{3,2,1,0:T(8,128)(2,1)} %bitcast.18) | data formatting | bytes 4194304
  167.3 45.5 %shard_map.55 = bf16[512,2048]{1,0:T(8,128)(2,1)} custom-call(s32[9]{0:T(128)} %pad_add_fusion.meta_ref, s32[40]{0:T(128)} %reshape.121.used_ref, bf16[512,2048]{1,0:T(8,128)(2,1)} %bitcast.79, bf16[512,2048]{1,0:T(8,128)(2,1)} %bitcast.80, bf16[512,2048]{1,0:T(8,128)(2,1)} %bitcast.81, bf16[512,2048]{1,0:T(8,128)(2,1)} %get-tuple-element.33.ko_ref, ...), custom_call_target="tpu_custom_call" | custom-call | flops 3758096384 | bytes 16252928 | tf_op jit(solution)/shard_map/pallas_call | solution.py:119
  212.8 10.0 %fusion.9 = bf16[512,2048]{1,0:T(8,128)(2,1)} fusion(bf16[512,2048]{1,0:T(8,128)(2,1)} %shard_map.55, bf16[2048,2,2048]{0,2,1:T(8,128)(2,1)} %bitcast.77, s32[]{:T(128)S(6)} %select_n.38), kind=kOutput, calls=%fused_computation.12 | convolution fusion | flops 4296015872 | bytes 12582916 | tf_op jit(solution)/shard_map/dot_general | solution.py:142
  224.1 24.0 %collective-permute-done.8 = bf16[512,2048]{1,0:T(8,128)(2,1)} collective-permute-done((bf16[512,2048]{1,0:T(8,128)(2,1)}, bf16[512,2048]{1,0:T(8,128)(2,1)}, u32[]{:S(2)}, u32[]{:S(2)}) %collective-permute-start.8) | collective-permute-done | bytes 2097184 | tf_op jit(solution)/shard_map/ppermute | solution.py:143
  248.1 9.4 %add_convert_fusion = bf16[512,2048]{1,0:T(8,128)(2,1)} fusion(bf16[512,2048]{1,0:T(8,128)(2,1)} %collective-permute-done.8, bf16[512,2048]{1,0:T(8,128)(2,1)S(1)} %copy-done.1, bf16[2048,2,2048]{0,2,1:T(8,128)(2,1)} %bitcast.78, s32[]{:T(128)S(6)} %select_n.37), kind=kOutput, calls=%fused_computation.10 | convolution fusion | flops 4300210176 | bytes 14680068 | tf_op jit(solution)/shard_map/dot_general | solution.py:144
  (34 shorter events, 11.4 us)
Async XLA Ops:
  0.0 160.3 %collective-permute-start = (bf16[512,16,128]{2,1,0:T(8,128)(2,1)}, bf16[512,16,128]{2,1,0:T(8,128)(2,1)}, u32[]{:S(2)}, u32[]{:S(2)}) collective-permute-start(bf16[512,16,128]{2,1,0:T(8,128)(2,1)} %param.6), channel_id=1, source_target_pairs={{0,2},{2,4},{4,6},{6,8},{8,10},{10,12},{12,14},{14,16},{16,18},{18... | collective-permute-start | bytes 6291464 | tf_op jit(solution)/shard_map/ppermute | solution.py:20
  6.6 21.5 %copy-start = (bf16[512,16,128]{2,1,0:T(8,128)(2,1)S(1)}, bf16[512,16,128]{2,1,0:T(8,128)(2,1)}, u32[]{:S(2)}) copy-start(bf16[512,16,128]{2,1,0:T(8,128)(2,1)} %param.6) | copy-start | bytes 6291460
  7.7 22.1 %collective-permute-start.6 = (bf16[1,64,16,128]{3,2,1,0:T(8,128)(2,1)S(1)}, bf16[1,64,16,128]{3,2,1,0:T(8,128)(2,1)}, u32[]{:S(2)}, u32[]{:S(2)}) collective-permute-start(bf16[1,64,16,128]{3,2,1,0:T(8,128)(2,1)S(1)} %constant_dynamic-slice_fusion.1), channel_id=1, source_target_pairs={{0,16},{2,18},{4,20},{6,22},{8,24},{10,26},{12,28},{14,30},{1,17},... | collective-permute-start | bytes 786440 | tf_op jit(solution)/shard_map/ppermute | solution.py:20
  12.7 151.2 %collective-permute-start.1 = (bf16[512,16,128]{2,1,0:T(8,128)(2,1)}, bf16[512,16,128]{2,1,0:T(8,128)(2,1)}, u32[]{:S(2)}, u32[]{:S(2)}) collective-permute-start(bf16[512,16,128]{2,1,0:T(8,128)(2,1)} %param.7), channel_id=1, source_target_pairs={{0,2},{2,4},{4,6},{6,8},{8,10},{10,12},{12,14},{14,16},{16,18},{18... | collective-permute-start | bytes 6291464 | tf_op jit(solution)/shard_map/ppermute | solution.py:20
  16.5 34.9 %collective-permute-start.7 = (bf16[1,64,16,128]{3,2,1,0:T(8,128)(2,1)}, bf16[1,64,16,128]{3,2,1,0:T(8,128)(2,1)}, u32[]{:S(2)}, u32[]{:S(2)}) collective-permute-start(bf16[1,64,16,128]{3,2,1,0:T(8,128)(2,1)} %constant_dynamic-slice_fusion), channel_id=1, source_target_pairs={{0,16},{2,18},{4,20},{6,22},{8,24},{10,26},{12,28},{14,30},{1,17},... | collective-permute-start | bytes 786440 | tf_op jit(solution)/shard_map/ppermute | solution.py:20
  21.7 108.2 %collective-permute-start.4 = (bf16[2,64,16,128]{3,2,1,0:T(8,128)(2,1)}, bf16[2,64,16,128]{3,2,1,0:T(8,128)(2,1)}, u32[]{:S(2)}, u32[]{:S(2)}) collective-permute-start(bf16[2,64,16,128]{3,2,1,0:T(8,128)(2,1)} %gather_fusion.2), channel_id=1, source_target_pairs={{0,8},{2,10},{4,12},{6,14},{8,16},{10,18},{12,20},{14,22},{16,24},... | collective-permute-start | bytes 1572872 | tf_op jit(solution)/shard_map/ppermute | solution.py:20
  25.8 73.7 %copy-start.2 = (s32[128,5]{0,1:T(8,128)S(1)}, s32[128,5]{0,1:T(8,128)}, u32[]{:S(2)}) copy-start(s32[128,5]{0,1:T(8,128)} %param.8) | copy-start | bytes 7684
  29.8 125.6 %collective-permute-start.2 = (bf16[4,64,16,128]{3,2,1,0:T(8,128)(2,1)}, bf16[4,64,16,128]{3,2,1,0:T(8,128)(2,1)}, u32[]{:S(2)}, u32[]{:S(2)}) collective-permute-start(bf16[4,64,16,128]{3,2,1,0:T(8,128)(2,1)} %gather_fusion), channel_id=1, source_target_pairs={{0,4},{2,6},{4,8},{6,10},{8,12},{10,14},{12,16},{14,18},{16,20},{1... | collective-permute-start | bytes 3145736 | tf_op jit(solution)/shard_map/ppermute | solution.py:20
  51.5 106.4 %collective-permute-start.3 = (bf16[4,64,16,128]{3,2,1,0:T(8,128)(2,1)S(1)}, bf16[4,64,16,128]{3,2,1,0:T(8,128)(2,1)}, u32[]{:S(2)}, u32[]{:S(2)}) collective-permute-start(bf16[4,64,16,128]{3,2,1,0:T(8,128)(2,1)S(1)} %gather_fusion.1), channel_id=1, source_target_pairs={{0,4},{2,6},{4,8},{6,10},{8,12},{10,14},{12,16},{14,18},{16,20},{1... | collective-permute-start | bytes 3145736 | tf_op jit(solution)/shard_map/ppermute | solution.py:20
  129.9 24.5 %collective-permute-start.5 = (bf16[2,64,16,128]{3,2,1,0:T(8,128)(2,1)}, bf16[2,64,16,128]{3,2,1,0:T(8,128)(2,1)S(1)}, u32[]{:S(2)}, u32[]{:S(2)}) collective-permute-start(bf16[2,64,16,128]{3,2,1,0:T(8,128)(2,1)} %gather_fusion.3), channel_id=1, source_target_pairs={{0,8},{2,10},{4,12},{6,14},{8,16},{10,18},{12,20},{14,22},{16,24},... | collective-permute-start | bytes 1572872 | tf_op jit(solution)/shard_map/ppermute | solution.py:20
  212.8 35.2 %copy-start.1 = (bf16[512,2048]{1,0:T(8,128)(2,1)S(1)}, bf16[512,2048]{1,0:T(8,128)(2,1)}, u32[]{:S(2)}) copy-start(bf16[512,2048]{1,0:T(8,128)(2,1)} %shard_map.55) | copy-start | bytes 6291460
  222.9 25.2 %collective-permute-start.8 = (bf16[512,2048]{1,0:T(8,128)(2,1)}, bf16[512,2048]{1,0:T(8,128)(2,1)}, u32[]{:S(2)}, u32[]{:S(2)}) collective-permute-start(bf16[512,2048]{1,0:T(8,128)(2,1)} %fusion.9), channel_id=1, source_target_pairs={{0,1},{1,0},{2,3},{3,2},{4,5},{5,4},{6,7},{7,6},{8,9},{9,8},{10,11... | collective-permute-start | bytes 6291464 | tf_op jit(solution)/shard_map/ppermute | solution.py:143

commit v2 on v1

--- a/solution.py
+++ b/solution.py
@@ -11,7 +11,7 @@
 BLOCK = 64
 WINDOW = 512
 NOFF = 5
-HEADS_PER_STEP = 2
+HEADS_PER_STEP = 1
 
 
 def from_behind(value, axis, steps):
@@ -26,8 +26,8 @@
     o_ref = rest[-1]
     prev_ok = meta_ref[0] > 0
     neg = jnp.float32(-jnp.inf)
-    for hh in range(HEADS_PER_STEP):
-        cols = pl.ds(hh * width, width)
+    if True:
+        cols = slice(None)
         for i in range(per_dev):
             lo = i * BLOCK
             q = q_ref[lo:lo + BLOCK, cols]
@@ -76,15 +76,45 @@
             o_ref[lo:lo + BLOCK, cols] = (summed / total).astype(o_ref.dtype)
 
 
+def matmul_kernel(sel_ref, a_ref, w_ref, o_ref):
+    o_ref[...] = jnp.dot(a_ref[...], w_ref[...], preferred_element_type=jnp.float32).astype(
+        o_ref.dtype
+    )
+
+
+def project_half(attended, weight, half, tn=512):
+    rows, depth = attended.shape
+    cw = weight.shape[1] // 2
+    steps = cw // tn
+    return pl.pallas_call(
+        matmul_kernel,
+        out_shape=jax.ShapeDtypeStruct((rows, cw), jnp.bfloat16),
+        grid_spec=pltpu.PrefetchScalarGridSpec(
+            num_scalar_prefetch=1,
+            grid=(steps,),
+            in_specs=[
+                pl.BlockSpec((rows, depth), lambda j, sel: (0, 0)),
+                pl.BlockSpec((depth, tn), lambda j, sel: (0, sel[0] * steps + j)),
+            ],
+            out_specs=pl.BlockSpec((rows, tn), lambda j, sel: (0, j)),
+        ),
+        compiler_params=pltpu.CompilerParams(dimension_semantics=("arbitrary",)),
+        cost_estimate=pl.CostEstimate(
+            flops=2 * rows * depth * cw,
+            transcendentals=0,
+            bytes_accessed=2 * (rows * depth + depth * cw + rows * cw),
+        ),
+    )(jnp.reshape(half, (1,)).astype(jnp.int32), attended, weight)
+
+
 def per_device(queries, keys, values, far_blocks, out_weight):
     rows, heads, width = queries.shape
     per_dev = rows // BLOCK
     device = lax.axis_index("ctx")
     cycle_size = lax.axis_size("ctx")
     scale = 1.0 / math.sqrt(width)
-    prev_k, prev_v = from_behind((keys, values), "ctx", 1)
-    key_blocks = keys.reshape(per_dev, BLOCK, heads, width)
-    value_blocks = values.reshape(per_dev, BLOCK, heads, width)
+    q_t, k_t, v_t = (jnp.transpose(a, (1, 0, 2)) for a in (queries, keys, values))
+    prev_k, prev_v = from_behind((k_t, v_t), "ctx", 1)
     levels = []
     far_arrays = []
     for level in range(1, NOFF):
@@ -95,10 +125,17 @@
             ::offset, level
         ]
         local = jnp.clip(target - device * per_dev, 0, per_dev - 1)
-        sent_k, sent_v = from_behind((key_blocks[local], value_blocks[local]), "ctx", offset)
+        picked = [
+            jnp.concatenate(
+                [lax.dynamic_slice_in_dim(a, local[b] * BLOCK, BLOCK, axis=1) for b in range(local.shape[0])],
+                axis=1,
+            )
+            for a in (k_t, v_t)
+        ]
+        sent_k, sent_v = from_behind(tuple(picked), "ctx", offset)
         levels.append(level)
-        far_arrays.append(sent_k.reshape(-1, heads * width))
-        far_arrays.append(sent_v.reshape(-1, heads * width))
+        far_arrays.append(sent_k)
+        far_arrays.append(sent_v)
 
     own = lax.dynamic_slice_in_dim(far_blocks, device * per_dev, per_dev, 0)
     query_index = device * per_dev + jnp.arange(per_dev, dtype=jnp.int32)
@@ -106,15 +143,14 @@
     pick = jnp.clip(own[:, 0] - (device - 1) * per_dev, 0, per_dev - 1)
     meta = jnp.concatenate([(device > 0).astype(jnp.int32)[None], pick.astype(jnp.int32)])
 
-    flat = lambda a: a.reshape(rows, heads * width)
-    cw = HEADS_PER_STEP * width
-    row_spec = pl.BlockSpec((rows, cw), lambda h, *_: (0, h))
-    far_specs = [pl.BlockSpec((a.shape[0], cw), lambda h, *_: (0, h)) for a in far_arrays]
+    row_spec = pl.BlockSpec((None, rows, width), lambda h, *_: (h, 0, 0))
+    out_spec = pl.BlockSpec((rows, width), lambda h, *_: (0, h))
+    far_specs = [pl.BlockSpec((None, a.shape[1], width), lambda h, *_: (h, 0, 0)) for a in far_arrays]
     n_keys = WINDOW + BLOCK + NOFF * BLOCK
     cost = pl.CostEstimate(
         flops=4 * rows * heads * width * n_keys,
         transcendentals=rows * heads * n_keys,
-        bytes_accessed=2 * heads * width * (6 * rows + sum(a.shape[0] for a in far_arrays)),
+        bytes_accessed=2 * heads * width * (6 * rows + sum(a.shape[1] for a in far_arrays)),
     )
     attended = pl.pallas_call(
         functools.partial(attention_kernel, levels, per_dev, width, scale),
@@ -123,11 +159,11 @@
             num_scalar_prefetch=2,
             grid=(heads // HEADS_PER_STEP,),
             in_specs=[row_spec] * 5 + far_specs,
-            out_specs=row_spec,
+            out_specs=out_spec,
         ),
         compiler_params=pltpu.CompilerParams(dimension_semantics=("arbitrary",)),
         cost_estimate=cost,
-    )(meta, used, flat(queries), flat(prev_k), flat(prev_v), flat(keys), flat(values), *far_arrays)
+    )(meta, used, q_t, prev_k, prev_v, k_t, v_t, *far_arrays)
 
     n_head = lax.axis_size("head")
     if n_head != 2:
@@ -136,12 +172,9 @@
             partial_value.astype(jnp.bfloat16), "head", scatter_dimension=1, tiled=True
         )
     hidx = lax.axis_index("head")
-    split_w = out_weight.reshape(out_weight.shape[0], 2, -1)
-    w_other = lax.dynamic_index_in_dim(split_w, 1 - hidx, axis=1, keepdims=False)
-    w_own = lax.dynamic_index_in_dim(split_w, hidx, axis=1, keepdims=False)
-    p_other = jnp.dot(attended, w_other, preferred_element_type=jnp.float32).astype(jnp.bfloat16)
+    p_other = project_half(attended, out_weight, 1 - hidx)
     received = lax.ppermute(p_other, "head", [(0, 1), (1, 0)])
-    p_own = jnp.dot(attended, w_own, preferred_element_type=jnp.float32).astype(jnp.bfloat16)
+    p_own = project_half(attended, out_weight, hidx)
     return (p_own.astype(jnp.float32) + received.astype(jnp.float32)).astype(jnp.bfloat16)
 
 

time: 259 us -> 228 us (0.88)
  the two profiles are of different devices: /device:TPU:1 before, /device:TPU:21 now
where the time goes in v2:
time: 228 us
  waiting for transfers between devices  97.2 us (43%)
  Pallas kernels  64.3 us (28%)
  starting transfers between devices  38.3 us (17%)
  local copies, waits for them, and re-layouts  13.9 us (6%)
  other arithmetic  9.37 us (4%)
  between operations  4.61 us (2%)
    ppermute x8, waiting for transfers between devices, from_behind(): lax.ppermute(value, axis, [(source, source + steps) for source in range(i...  82.1 us
    pallas_call x1, Pallas kernels, per_device(): pl.pallas_call(functools.partial(attention_kernel, levels, per_dev, width...  46.8 us
    ppermute x8, starting transfers between devices, from_behind(): lax.ppermute(value, axis, [(source, source + steps) for source in range(i...  37.1 us
    pallas_call x2, Pallas kernels, project_half(): pl.pallas_call(matmul_kernel, out_shape=jax.ShapeDtypeStruct((rows, cw),...  17.5 us
    ppermute x1, waiting for transfers between devices, per_device(): received = lax.ppermute(p_other, 'head', [(0, 1), (1, 0)])  15.1 us
    unnamed x11, local copies, waits for them, and re-layouts  8.58 us
    concatenate x4, other arithmetic, per_device(): jnp.concatenate([lax.dynamic_slice_in_dim(a, local[b] * BLOCK, BLOCK, axi...  4.8 us
  transfers between devices with their start and end apart: 9, of which 4 were waited for; matrix products, arithmetic and copies ran while one was open for 7% of the time, Pallas kernels for 4%

profile of v2, /device:TPU:21, one launch (start us, length us, event | category | flops | bytes accessed | tf_op | source)
XLA Modules:
  0.0 227.6 jit_solution(16689111570139338538)
XLA Ops:
  0.0 2.3 %copy.31 = bf16[512,16,128]{2,0,1:T(8,128)(2,1)S(1)} copy(bf16[512,16,128]{2,1,0:T(8,128)(2,1)} %param.6) | data formatting | bytes 4194304 | tf_op args[1]
  2.3 3.8 %collective-permute-start = (bf16[16,512,128]{2,1,0:T(8,128)(2,1)S(1)}, bf16[16,512,128]{2,1,0:T(8,128)(2,1)}, u32[]{:S(2)}, u32[]{:S(2)}) collective-permute-start(bf16[16,512,128]{2,1,0:T(8,128)(2,1)S(1)} %bitcast.49), channel_id=1, source_target_pairs={{0,2},{2,4},{4,6},{6,8},{8,10},{10,12},{12,14},{14,16},{16,18},{18... | collective-permute-start | bytes 6291464 | tf_op jit(solution)/shard_map/ppermute | solution.py:20
  6.2 1.9 copy.30
  8.0 1.9 collective-permute-start.1
  17.5 1.9 collective-permute-start.4
  19.4 1.3 collective-permute-start.6
  20.7 2.3 %dynamic-slice_bitcast_fusion = (bf16[16,64,128]{2,1,0:T(8,128)(2,1)S(1)}, bf16[16,64,128]{2,1,0:T(8,128)(2,1)S(1)}, bf16[16,64,128]{2,1,0:T(8,128)(2,1)}, bf16[...) fusion(bf16[512,16,128]{2,0,1:T(8,128)(2,1)} %copy.30, ...), kind=kLoop, calls=%fused_computation.6 | loop fusion | bytes 3670044 | tf_op jit(solution)/shard_map/dynamic_slice | solution.py:130
  23.0 1.3 collective-permute-start.7
  24.3 1.1 pad_maximum_fusion.1
  25.4 1.1 pad_maximum_fusion
  26.5 61.5 %collective-permute-done.6.rest_4_ = bf16[16,64,128]{2,1,0:T(8,128)(2,1)} collective-permute-done((bf16[16,64,128]{2,1,0:T(8,128)(2,1)S(1)}, bf16[16,64,128]{2,1,0:T(8,128)(2,1)}, u32[]{:S(2)}, u32[]{:S(2)}) %collective-permute-start.6) | collective-permute-done | bytes 262176 | tf_op jit(solution)/shard_map/ppermute | solution.py:20
  88.0 1.9 collective-permute-start.3
  89.9 3.7 %collective-permute-done.7.rest_5_ = bf16[16,64,128]{2,1,0:T(8,128)(2,1)} collective-permute-done((bf16[16,64,128]{2,1,0:T(8,128)(2,1)S(1)}, bf16[16,64,128]{2,1,0:T(8,128)(2,1)}, u32[]{:S(2)}, u32[]{:S(2)}) %collective-permute-start.7) | collective-permute-done | bytes 262176 | tf_op jit(solution)/shard_map/ppermute | solution.py:20
  93.6 22.2 %collective-permute-start.2 = (bf16[16,256,128]{2,1,0:T(8,128)(2,1)}, bf16[16,256,128]{2,1,0:T(8,128)(2,1)}, u32[]{:S(2)}, u32[]{:S(2)}) collective-permute-start(bf16[16,256,128]{2,1,0:T(8,128)(2,1)} %pad_maximum_fusion), channel_id=1, source_target_pairs={{0,4},{2,6},{4,8},{6,10},{8,12},{10,14},{12,16},{14,18},{16,20},{1... | collective-permute-start | bytes 3145736 | tf_op jit(solution)/shard_map/ppermute | solution.py:20
  115.9 1.8 pad_maximum_fusion.3
  117.7 2.7 %collective-permute-start.5 = (bf16[16,128,128]{2,1,0:T(8,128)(2,1)}, bf16[16,128,128]{2,1,0:T(8,128)(2,1)}, u32[]{:S(2)}, u32[]{:S(2)}) collective-permute-start(bf16[16,128,128]{2,1,0:T(8,128)(2,1)} %pad_maximum_fusion.3), channel_id=1, source_target_pairs={{0,8},{2,10},{4,12},{6,14},{8,16},{10,18},{12,20},{14,22},{16,24},... | collective-permute-start | bytes 1572872 | tf_op jit(solution)/shard_map/ppermute | solution.py:20
  121.2 3.5 %copy.29 = bf16[512,16,128]{2,0,1:T(8,128)(2,1)} copy(bf16[512,16,128]{2,1,0:T(8,128)(2,1)} %param.5) | data formatting | bytes 4194304 | tf_op args[0]
  125.3 16.9 %collective-permute-done.5.rest_3_ = bf16[16,128,128]{2,1,0:T(8,128)(2,1)} collective-permute-done((bf16[16,128,128]{2,1,0:T(8,128)(2,1)}, bf16[16,128,128]{2,1,0:T(8,128)(2,1)}, u32[]{:S(2)}, u32[]{:S(2)}) %collective-permute-start.5) | collective-permute-done | bytes 524320 | tf_op jit(solution)/shard_map/ppermute | solution.py:20
  143.2 46.8 %shard_map.55.a_ref = bf16[512,2048]{1,0:T(8,128)(2,1)} custom-call(s32[9]{0:T(128)} %pad_add_fusion.meta_ref, s32[40]{0:T(128)} %reshape.75.used_ref, bf16[16,512,128]{2,1,0:T(8,128)(2,1)} %bitcast.51, bf16[16,512,128]{2,1,0:T(8,128)(2,1)} %collective-permute-done.kp_ref, bf16[16,512,128]{2,1,0:T(8,128)(2,1)} %collective-permute-done.1.vp_ref, ...), custom_call_target="tpu_custom_call" | custom-call | flops 3758096384 | bytes 16252928 | tf_op jit(solution)/shard_map/pallas_call | solution.py:155
  190.0 8.7 %shard_map.57 = bf16[512,2048]{1,0:T(8,128)(2,1)} custom-call(s32[1]{0:T(128)} %bitcast.29.sel_ref, bf16[512,2048]{1,0:T(8,128)(2,1)} %shard_map.55.a_ref, bf16[2048,4096]{1,0:T(8,128)(2,1)} %w_ref.3), custom_call_target="tpu_custom_call" | custom-call | flops 4294967296 | bytes 12582912 | tf_op jit(solution)/shard_map/pallas_call | solution.py:89
  198.7 1.2 collective-permute-start.8
  199.9 8.8 %shard_map.56 = bf16[512,2048]{1,0:T(8,128)(2,1)} custom-call(s32[1]{0:T(128)} %bitcast.sel_ref, bf16[512,2048]{1,0:T(8,128)(2,1)} %shard_map.55.a_ref, bf16[2048,4096]{1,0:T(8,128)(2,1)} %w_ref.3), custom_call_target="tpu_custom_call" | custom-call | flops 4294967296 | bytes 12582912 | tf_op jit(solution)/shard_map/pallas_call | solution.py:89
  208.7 15.1 %collective-permute-done.8 = bf16[512,2048]{1,0:T(8,128)(2,1)S(1)} collective-permute-done((bf16[512,2048]{1,0:T(8,128)(2,1)}, bf16[512,2048]{1,0:T(8,128)(2,1)S(1)}, u32[]{:S(2)}, u32[]{:S(2)}) %collective-permute-start.8) | collective-permute-done | bytes 2097184 | tf_op jit(solution)/shard_map/ppermute | solution.py:176
  223.8 3.8 %add_convert_fusion = bf16[512,2048]{1,0:T(8,128)(2,1)} fusion(bf16[512,2048]{1,0:T(8,128)(2,1)S(1)} %collective-permute-done.8, bf16[512,2048]{1,0:T(8,128)(2,1)} %shard_map.56), kind=kLoop, calls=%fused_computation | loop fusion | flops 4194304 | bytes 6291456 | tf_op jit(solution)/shard_map/convert_element_type | solution.py:178
  (29 shorter events, 5.5 us)
Async XLA Ops:
  0.0 6.2 %copy-start.1 = (bf16[512,16,128]{2,1,0:T(8,128)(2,1)S(1)}, bf16[512,16,128]{2,1,0:T(8,128)(2,1)}, u32[]{:S(2)}) copy-start(bf16[512,16,128]{2,1,0:T(8,128)(2,1)} %param.7) | copy-start | bytes 6291460
  2.3 14.1 %copy-start = (bf16[512,16,128]{2,0,1:T(8,128)(2,1)}, bf16[512,16,128]{2,0,1:T(8,128)(2,1)S(1)}, u32[]{:S(2)}) copy-start(bf16[512,16,128]{2,0,1:T(8,128)(2,1)S(1)} %copy.31) | copy-start | bytes 6291460
  2.3 7.7 %copy-start.3 = (s32[128,5]{0,1:T(8,128)S(1)}, s32[128,5]{0,1:T(8,128)}, u32[]{:S(2)}) copy-start(s32[128,5]{0,1:T(8,128)} %param.8) | copy-start | bytes 7684
  2.3 139.9 %collective-permute-start = (bf16[16,512,128]{2,1,0:T(8,128)(2,1)S(1)}, bf16[16,512,128]{2,1,0:T(8,128)(2,1)}, u32[]{:S(2)}, u32[]{:S(2)}) collective-permute-start(bf16[16,512,128]{2,1,0:T(8,128)(2,1)S(1)} %bitcast.49), channel_id=1, source_target_pairs={{0,2},{2,4},{4,6},{6,8},{8,10},{10,12},{12,14},{14,16},{16,18},{18... | collective-permute-start | bytes 6291464 | tf_op jit(solution)/shard_map/ppermute | solution.py:20
  8.0 134.2 %collective-permute-start.1 = (bf16[16,512,128]{2,1,0:T(8,128)(2,1)}, bf16[16,512,128]{2,1,0:T(8,128)(2,1)}, u32[]{:S(2)}, u32[]{:S(2)}) collective-permute-start(bf16[16,512,128]{2,1,0:T(8,128)(2,1)} %bitcast.46.clone.2.vo_ref), channel_id=1, source_target_pairs={{0,2},{2,4},{4,6},{6,8},{8,10},{10,12},{12,14},{14,16},{16,18},{18... | collective-permute-start | bytes 6291464 | tf_op jit(solution)/shard_map/ppermute | solution.py:20
  17.5 100.2 %collective-permute-start.4 = (bf16[16,128,128]{2,1,0:T(8,128)(2,1)}, bf16[16,128,128]{2,1,0:T(8,128)(2,1)}, u32[]{:S(2)}, u32[]{:S(2)}) collective-permute-start(bf16[16,128,128]{2,1,0:T(8,128)(2,1)} %pad_maximum_fusion.2), channel_id=1, source_target_pairs={{0,8},{2,10},{4,12},{6,14},{8,16},{10,18},{12,20},{14,22},{16,24},... | collective-permute-start | bytes 1572872 | tf_op jit(solution)/shard_map/ppermute | solution.py:20
  19.4 68.6 %collective-permute-start.6 = (bf16[16,64,128]{2,1,0:T(8,128)(2,1)S(1)}, bf16[16,64,128]{2,1,0:T(8,128)(2,1)}, u32[]{:S(2)}, u32[]{:S(2)}) collective-permute-start(bf16[16,64,128]{2,1,0:T(8,128)(2,1)S(1)} %get-tuple-element.14), channel_id=1, source_target_pairs={{0,16},{2,18},{4,20},{6,22},{8,24},{10,26},{12,28},{14,30},{1,17},... | collective-permute-start | bytes 786440 | tf_op jit(solution)/shard_map/ppermute | solution.py:20
  23.0 70.6 %collective-permute-start.7 = (bf16[16,64,128]{2,1,0:T(8,128)(2,1)S(1)}, bf16[16,64,128]{2,1,0:T(8,128)(2,1)}, u32[]{:S(2)}, u32[]{:S(2)}) collective-permute-start(bf16[16,64,128]{2,1,0:T(8,128)(2,1)S(1)} %get-tuple-element.7), channel_id=1, source_target_pairs={{0,16},{2,18},{4,20},{6,22},{8,24},{10,26},{12,28},{14,30},{1,17},... | collective-permute-start | bytes 786440 | tf_op jit(solution)/shard_map/ppermute | solution.py:20
  88.0 54.2 %collective-permute-start.3 = (bf16[16,256,128]{2,1,0:T(8,128)(2,1)}, bf16[16,256,128]{2,1,0:T(8,128)(2,1)S(1)}, u32[]{:S(2)}, u32[]{:S(2)}) collective-permute-start(bf16[16,256,128]{2,1,0:T(8,128)(2,1)} %pad_maximum_fusion.1), channel_id=1, source_target_pairs={{0,4},{2,6},{4,8},{6,10},{8,12},{10,14},{12,16},{14,18},{16,20},{1... | collective-permute-start | bytes 3145736 | tf_op jit(solution)/shard_map/ppermute | solution.py:20
  93.6 48.6 %collective-permute-start.2 = (bf16[16,256,128]{2,1,0:T(8,128)(2,1)}, bf16[16,256,128]{2,1,0:T(8,128)(2,1)}, u32[]{:S(2)}, u32[]{:S(2)}) collective-permute-start(bf16[16,256,128]{2,1,0:T(8,128)(2,1)} %pad_maximum_fusion), channel_id=1, source_target_pairs={{0,4},{2,6},{4,8},{6,10},{8,12},{10,14},{12,16},{14,18},{16,20},{1... | collective-permute-start | bytes 3145736 | tf_op jit(solution)/shard_map/ppermute | solution.py:20
  117.7 24.6 %collective-permute-start.5 = (bf16[16,128,128]{2,1,0:T(8,128)(2,1)}, bf16[16,128,128]{2,1,0:T(8,128)(2,1)}, u32[]{:S(2)}, u32[]{:S(2)}) collective-permute-start(bf16[16,128,128]{2,1,0:T(8,128)(2,1)} %pad_maximum_fusion.3), channel_id=1, source_target_pairs={{0,8},{2,10},{4,12},{6,14},{8,16},{10,18},{12,20},{14,22},{16,24},... | collective-permute-start | bytes 1572872 | tf_op jit(solution)/shard_map/ppermute | solution.py:20
  142.2 1.0 copy-start.2
  198.7 25.1 %collective-permute-start.8 = (bf16[512,2048]{1,0:T(8,128)(2,1)}, bf16[512,2048]{1,0:T(8,128)(2,1)S(1)}, u32[]{:S(2)}, u32[]{:S(2)}) collective-permute-start(bf16[512,2048]{1,0:T(8,128)(2,1)} %shard_map.57), channel_id=1, source_target_pairs={{0,1},{1,0},{2,3},{3,2},{4,5},{5,4},{6,7},{7,6},{8,9},{9,8},{10,11... | collective-permute-start | bytes 6291464 | tf_op jit(solution)/shard_map/ppermute | solution.py:176

commit v3 on v2

--- a/solution.py
+++ b/solution.py
@@ -54,14 +54,24 @@
             s_f = score(kp_ref[pl.ds(start, BLOCK), cols])
             s_f = jnp.where(used_ref[i * NOFF] > 0, s_f, neg)
             pieces.append((s_f, vp_ref[pl.ds(start, BLOCK), cols]))
-            for level, (k_ref, v_ref) in zip(levels, zip(far_refs[0::2], far_refs[1::2])):
+            pos = 0
+            for level in levels:
                 offset = 2**level
+                n_src = 2 if level == 1 else 1
+                refs = far_refs[pos:pos + 2 * n_src]
+                pos += 2 * n_src
                 if i % offset:
                     continue
                 flo = (i // offset) * BLOCK
-                s_f = score(k_ref[flo:flo + BLOCK, cols])
+                k_blk = refs[0][flo:flo + BLOCK, cols]
+                v_blk = refs[1][flo:flo + BLOCK, cols]
+                if n_src == 2:
+                    odd = meta_ref[1 + per_dev] > 0
+                    k_blk = jnp.where(odd, refs[2][flo:flo + BLOCK, cols], k_blk)
+                    v_blk = jnp.where(odd, refs[3][flo:flo + BLOCK, cols], v_blk)
+                s_f = score(k_blk)
                 s_f = jnp.where(used_ref[i * NOFF + level] > 0, s_f, neg)
-                pieces.append((s_f, v_ref[flo:flo + BLOCK, cols]))
+                pieces.append((s_f, v_blk))
             top = pieces[0][0].max(axis=1, keepdims=True)
             for s, _ in pieces[1:]:
                 top = jnp.maximum(top, s.max(axis=1, keepdims=True))
@@ -107,14 +117,22 @@
     )(jnp.reshape(half, (1,)).astype(jnp.int32), attended, weight)
 
 
+def pick_blocks(kv, local):
+    return jnp.concatenate(
+        [lax.dynamic_slice_in_dim(kv, local[b] * BLOCK, BLOCK, axis=2) for b in range(local.shape[0])],
+        axis=2,
+    )
+
+
 def per_device(queries, keys, values, far_blocks, out_weight):
     rows, heads, width = queries.shape
     per_dev = rows // BLOCK
     device = lax.axis_index("ctx")
     cycle_size = lax.axis_size("ctx")
     scale = 1.0 / math.sqrt(width)
-    q_t, k_t, v_t = (jnp.transpose(a, (1, 0, 2)) for a in (queries, keys, values))
-    prev_k, prev_v = from_behind((k_t, v_t), "ctx", 1)
+    q_t = jnp.transpose(queries, (1, 0, 2))
+    kv_t = jnp.stack([jnp.transpose(keys, (1, 0, 2)), jnp.transpose(values, (1, 0, 2))])
+    prev_kv = from_behind(kv_t, "ctx", 1)
     levels = []
     far_arrays = []
     for level in range(1, NOFF):
@@ -125,32 +143,44 @@
             ::offset, level
         ]
         local = jnp.clip(target - device * per_dev, 0, per_dev - 1)
-        picked = [
-            jnp.concatenate(
-                [lax.dynamic_slice_in_dim(a, local[b] * BLOCK, BLOCK, axis=1) for b in range(local.shape[0])],
-                axis=1,
+        if level == 1:
+            direct = lax.ppermute(
+                pick_blocks(kv_t, local), "ctx",
+                [(s, s + 2) for s in range(0, cycle_size - 2, 2)],
             )
-            for a in (k_t, v_t)
-        ]
-        sent_k, sent_v = from_behind(tuple(picked), "ctx", offset)
+            nxt = lax.dynamic_slice_in_dim(far_blocks, (device + 1) * per_dev, per_dev, 0)[::2, 1]
+            fwd_local = jnp.clip(nxt - (device - 1) * per_dev, 0, per_dev - 1)
+            forwarded = lax.ppermute(
+                pick_blocks(prev_kv, fwd_local), "ctx",
+                [(s, s + 1) for s in range(0, cycle_size - 1, 2)],
+            )
+            far_arrays.append((direct, forwarded))
+        else:
+            far_arrays.append((from_behind(pick_blocks(kv_t, local), "ctx", offset),))
         levels.append(level)
-        far_arrays.append(sent_k)
-        far_arrays.append(sent_v)
 
     own = lax.dynamic_slice_in_dim(far_blocks, device * per_dev, per_dev, 0)
     query_index = device * per_dev + jnp.arange(per_dev, dtype=jnp.int32)
     used = (own <= (query_index - WINDOW // BLOCK - 1)[:, None]).astype(jnp.int32).reshape(-1)
     pick = jnp.clip(own[:, 0] - (device - 1) * per_dev, 0, per_dev - 1)
-    meta = jnp.concatenate([(device > 0).astype(jnp.int32)[None], pick.astype(jnp.int32)])
+    meta = jnp.concatenate(
+        [(device > 0).astype(jnp.int32)[None], pick.astype(jnp.int32), (device % 2)[None]]
+    )
 
     row_spec = pl.BlockSpec((None, rows, width), lambda h, *_: (h, 0, 0))
     out_spec = pl.BlockSpec((rows, width), lambda h, *_: (0, h))
-    far_specs = [pl.BlockSpec((None, a.shape[1], width), lambda h, *_: (h, 0, 0)) for a in far_arrays]
+    k_spec = lambda n: pl.BlockSpec((None, None, n, width), lambda h, *_: (0, h, 0, 0))
+    v_spec = lambda n: pl.BlockSpec((None, None, n, width), lambda h, *_: (1, h, 0, 0))
+    far_specs, far_operands = [], []
+    for group in far_arrays:
+        for a in group:
+            far_specs += [k_spec(a.shape[2]), v_spec(a.shape[2])]
+            far_operands += [a, a]
     n_keys = WINDOW + BLOCK + NOFF * BLOCK
     cost = pl.CostEstimate(
         flops=4 * rows * heads * width * n_keys,
         transcendentals=rows * heads * n_keys,
-        bytes_accessed=2 * heads * width * (6 * rows + sum(a.shape[1] for a in far_arrays)),
+        bytes_accessed=2 * heads * width * (6 * rows + sum(a.shape[2] for a in far_operands)),
     )
     attended = pl.pallas_call(
         functools.partial(attention_kernel, levels, per_dev, width, scale),
@@ -158,12 +188,12 @@
         grid_spec=pltpu.PrefetchScalarGridSpec(
             num_scalar_prefetch=2,
             grid=(heads // HEADS_PER_STEP,),
-            in_specs=[row_spec] * 5 + far_specs,
+            in_specs=[row_spec, k_spec(rows), v_spec(rows), k_spec(rows), v_spec(rows)] + far_specs,
             out_specs=out_spec,
         ),
         compiler_params=pltpu.CompilerParams(dimension_semantics=("arbitrary",)),
         cost_estimate=cost,
-    )(meta, used, q_t, prev_k, prev_v, k_t, v_t, *far_arrays)
+    )(meta, used, q_t, prev_kv, prev_kv, kv_t, kv_t, *far_operands)
 
     n_head = lax.axis_size("head")
     if n_head != 2:

time: 228 us -> 240 us (1.053)
  the two profiles are of different devices: /device:TPU:21 before, /device:TPU:28 now
where the time goes in v3:
time: 240 us
  waiting for transfers between devices  130 us (54%)
  Pallas kernels  64.4 us (27%)
  other arithmetic  14.8 us (6%)
  local copies, waits for them, and re-layouts  13.2 us (6%)
  starting transfers between devices  9.89 us (4%)
  between operations  7.04 us (3%)
    ppermute x3, waiting for transfers between devices, from_behind(): lax.ppermute(value, axis, [(source, source + steps) for source in range(i...  95.9 us
    pallas_call x1, Pallas kernels, per_device(): pl.pallas_call(functools.partial(attention_kernel, levels, per_dev, width...  46.9 us
    ppermute x1, waiting for transfers between devices, per_device(): received = lax.ppermute(p_other, 'head', [(0, 1), (1, 0)])  34.4 us
    pallas_call x2, Pallas kernels, project_half(): pl.pallas_call(matmul_kernel, out_shape=jax.ShapeDtypeStruct((rows, cw),...  17.5 us
    another operation x3, other arithmetic, per_device(): jnp.stack([jnp.transpose(keys, (1, 0, 2)), jnp.transpose(values, (1, 0, 2...  6.2 us
  transfers between devices with their start and end apart: 6, of which 3 were waited for; matrix products, arithmetic and copies ran while one was open for 7% of the time, Pallas kernels for 4%

profile of v3, /device:TPU:28, one launch (start us, length us, event | category | flops | bytes accessed | tf_op | source)
XLA Modules:
  0.0 239.6 jit_solution(766632796790834188)
XLA Ops:
  0.0 3.3 %copy_bitcast_fusion = (bf16[1,16,512,128]{3,2,1,0:T(8,128)(2,1)S(1)}, bf16[1,16,512,128]{3,2,1,0:T(8,128)(2,1)S(1)}) fusion(bf16[512,16,128]{2,1,0:T(8,128)(2,1)} %param.7, bf16[512,16,128]{2,1,0:T(8,128)(2,1)} %param.6), kind=kLoop, calls=%fused_computation.18 | loop fusion | bytes 8388608 | tf_op jit(solution)/shard_map/stack | solution.py:134
  3.3 2.5 %pad_maximum_fusion.ko_ref.vo_ref = bf16[2,16,512,128]{3,2,1,0:T(8,128)(2,1)} fusion(bf16[1,16,512,128]{3,2,1,0:T(8,128)(2,1)S(1)} %get-tuple-element.33, bf16[1,16,512,128]{3,2,1,0:T(8,128)(2,1)S(1)} %get-tuple-element.34), kind=kLoop, calls=%fused_computation.7 | loop fusion | flops 2097152 | bytes 8388608 | tf_op jit(solution)/shard_map/stack | solution.py:134
  6.0 1.9 collective-permute-start
  13.9 2.7 %fusion.6 = (bf16[2,16,64,128]{3,2,1,0:T(8,128)(2,1)S(1)}, bf16[2,16,64,128]{3,2,1,0:T(8,128)(2,1)S(1)}, bf16[2,16,64,128]{3,2,1,0:T(8,128)(2,1)S(1)}, bf16[2,16...) fusion(s32[]{:T(128)S(6)} %select_n.71, ...), kind=kLoop, calls=%fused_computation.28 | loop fusion | flops 6291456 | bytes 7340056 | tf_op jit(solution)/shard_map/stack | solution.py:134
  16.6 1.5 pad_maximum_fusion.1
  18.1 1.3 collective-permute-start.1
  22.5 56.1 %collective-permute-done.kp_ref.vp_ref = bf16[2,16,512,128]{3,2,1,0:T(8,128)(2,1)} collective-permute-done((bf16[2,16,512,128]{3,2,1,0:T(8,128)(2,1)}, bf16[2,16,512,128]{3,2,1,0:T(8,128)(2,1)}, u32[]{:S(2)}, u32[]{:S(2)}) %collective-permute-start) | collective-permute-done | bytes 4194336 | tf_op jit(solution)/shard_map/ppermute | solution.py:20
  78.6 1.7 constant_dynamic-slice_fusion.5
  80.3 1.5 pad_maximum_fusion.2
  81.8 2.6 %collective-permute-start.2 = (bf16[2,16,256,128]{3,2,1,0:T(8,128)(2,1)}, bf16[2,16,256,128]{3,2,1,0:T(8,128)(2,1)}, u32[]{:S(2)}, u32[]{:S(2)}) collective-permute-start(bf16[2,16,256,128]{3,2,1,0:T(8,128)(2,1)} %pad_maximum_fusion.2), channel_id=1, source_target_pairs={{0,2},{4,6},{8,10},{12,14},{16,18},{20,22},{24,26},{28,30},{1,3},{... | collective-permute-start | bytes 6291464 | tf_op jit(solution)/shard_map/ppermute | solution.py:153
  85.0 1.0 fusion.5
  86.0 1.1 pad_maximum_fusion.3
  87.0 1.3 collective-permute-start.3
  88.3 1.3 collective-permute-start.4
  89.8 0.7 reshape.104.used_ref
  90.5 3.5 %copy.13 = bf16[512,16,128]{2,0,1:T(8,128)(2,1)} copy(bf16[512,16,128]{2,1,0:T(8,128)(2,1)} %param.5) | data formatting | bytes 4194304 | tf_op args[0]
  94.6 39.8 %collective-permute-done.4.rest_6_.rest_7_ = bf16[2,16,64,128]{3,2,1,0:T(8,128)(2,1)S(1)} collective-permute-done((bf16[2,16,64,128]{3,2,1,0:T(8,128)(2,1)S(1)}, bf16[2,16,64,128]{3,2,1,0:T(8,128)(2,1)S(1)}, u32[]{:S(2)}, u32[]{:S(2)}) %collective-permute-start.4) | collective-permute-done | bytes 524320 | tf_op jit(solution)/shard_map/ppermute | solution.py:20
  134.4 0.8 copy-done.2
  135.5 46.9 %shard_map.55.a_ref = bf16[512,2048]{1,0:T(8,128)(2,1)} custom-call(s32[10]{0:T(128)} %pad_add_fusion.meta_ref, s32[40]{0:T(128)} %reshape.104.used_ref, bf16[16,512,128]{2,1,0:T(8,128)(2,1)} %bitcast.30, bf16[2,16,512,128]{3,2,1,0:T(8,128)(2,1)} %collective-permute-done.kp_ref.vp_ref, bf16[2,16,512,128]{3,2,1,0:T(8,128)(2,1)} %collective-permute-done.kp_ref.vp_ref, ...), custom_call_target="tpu_custom_call" | custom-call | flops 3758096384 | bytes 18350080 | tf_op jit(solution)/shard_map/pallas_call | solution.py:185
  182.4 8.7 %shard_map.57 = bf16[512,2048]{1,0:T(8,128)(2,1)} custom-call(s32[1]{0:T(128)} %bitcast.22.sel_ref, bf16[512,2048]{1,0:T(8,128)(2,1)} %shard_map.55.a_ref, bf16[2048,4096]{1,0:T(8,128)(2,1)} %w_ref.3), custom_call_target="tpu_custom_call" | custom-call | flops 4294967296 | bytes 12582912 | tf_op jit(solution)/shard_map/pallas_call | solution.py:99
  191.1 1.5 collective-permute-start.5
  192.6 8.8 %shard_map.56 = bf16[512,2048]{1,0:T(8,128)(2,1)} custom-call(s32[1]{0:T(128)} %bitcast.sel_ref, bf16[512,2048]{1,0:T(8,128)(2,1)} %shard_map.55.a_ref, bf16[2048,4096]{1,0:T(8,128)(2,1)} %w_ref.3), custom_call_target="tpu_custom_call" | custom-call | flops 4294967296 | bytes 12582912 | tf_op jit(solution)/shard_map/pallas_call | solution.py:99
  201.4 34.4 %collective-permute-done.5 = bf16[512,2048]{1,0:T(8,128)(2,1)S(1)} collective-permute-done((bf16[512,2048]{1,0:T(8,128)(2,1)}, bf16[512,2048]{1,0:T(8,128)(2,1)S(1)}, u32[]{:S(2)}, u32[]{:S(2)}) %collective-permute-start.5) | collective-permute-done | bytes 2097184 | tf_op jit(solution)/shard_map/ppermute | solution.py:206
  235.7 3.8 %add_convert_fusion = bf16[512,2048]{1,0:T(8,128)(2,1)} fusion(bf16[512,2048]{1,0:T(8,128)(2,1)S(1)} %collective-permute-done.5, bf16[512,2048]{1,0:T(8,128)(2,1)} %shard_map.56), kind=kLoop, calls=%fused_computation.15 | loop fusion | flops 4194304 | bytes 6291456 | tf_op jit(solution)/shard_map/convert_element_type | solution.py:208
  (25 shorter events, 4.1 us)
Async XLA Ops:
  3.3 2.7 %copy-start = (bf16[1,16,512,128]{3,2,1,0:T(8,128)(2,1)}, bf16[1,16,512,128]{3,2,1,0:T(8,128)(2,1)S(1)}, u32[]{:S(2)}) copy-start(bf16[1,16,512,128]{3,2,1,0:T(8,128)(2,1)S(1)} %get-tuple-element.34) | copy-start | bytes 6291460
  3.3 4.6 %copy-start.3 = (s32[128,5]{0,1:T(8,128)S(1)}, s32[128,5]{0,1:T(8,128)}, u32[]{:S(2)}) copy-start(s32[128,5]{0,1:T(8,128)} %param.8) | copy-start | bytes 7684
  6.0 72.6 %collective-permute-start = (bf16[2,16,512,128]{3,2,1,0:T(8,128)(2,1)}, bf16[2,16,512,128]{3,2,1,0:T(8,128)(2,1)}, u32[]{:S(2)}, u32[]{:S(2)}) collective-permute-start(bf16[2,16,512,128]{3,2,1,0:T(8,128)(2,1)} %pad_maximum_fusion.ko_ref.vo_ref), channel_id=1, source_target_pairs={{0,2},{2,4},{4,6},{6,8},{8,10},{10,12},{12,14},{14,16},{16,18},{18... | collective-permute-start | bytes 12582920 | tf_op jit(solution)/shard_map/ppermute | solution.py:20
  18.1 116.2 %collective-permute-start.1 = (bf16[2,16,256,128]{3,2,1,0:T(8,128)(2,1)}, bf16[2,16,256,128]{3,2,1,0:T(8,128)(2,1)}, u32[]{:S(2)}, u32[]{:S(2)}) collective-permute-start(bf16[2,16,256,128]{3,2,1,0:T(8,128)(2,1)} %pad_maximum_fusion.1), channel_id=1, source_target_pairs={{0,4},{4,8},{8,12},{12,16},{16,20},{20,24},{24,28},{1,5},{5,9},{9,... | collective-permute-start | bytes 6291464 | tf_op jit(solution)/shard_map/ppermute | solution.py:147
  81.8 52.6 %collective-permute-start.2 = (bf16[2,16,256,128]{3,2,1,0:T(8,128)(2,1)}, bf16[2,16,256,128]{3,2,1,0:T(8,128)(2,1)}, u32[]{:S(2)}, u32[]{:S(2)}) collective-permute-start(bf16[2,16,256,128]{3,2,1,0:T(8,128)(2,1)} %pad_maximum_fusion.2), channel_id=1, source_target_pairs={{0,2},{4,6},{8,10},{12,14},{16,18},{20,22},{24,26},{28,30},{1,3},{... | collective-permute-start | bytes 6291464 | tf_op jit(solution)/shard_map/ppermute | solution.py:153
  87.0 47.3 %collective-permute-start.3 = (bf16[2,16,128,128]{3,2,1,0:T(8,128)(2,1)}, bf16[2,16,128,128]{3,2,1,0:T(8,128)(2,1)S(1)}, u32[]{:S(2)}, u32[]{:S(2)}) collective-permute-start(bf16[2,16,128,128]{3,2,1,0:T(8,128)(2,1)} %pad_maximum_fusion.3), channel_id=1, source_target_pairs={{0,8},{2,10},{4,12},{6,14},{8,16},{10,18},{12,20},{14,22},{16,24},... | collective-permute-start | bytes 3145736 | tf_op jit(solution)/shard_map/ppermute | solution.py:20
  88.3 46.0 %collective-permute-start.4 = (bf16[2,16,64,128]{3,2,1,0:T(8,128)(2,1)S(1)}, bf16[2,16,64,128]{3,2,1,0:T(8,128)(2,1)S(1)}, u32[]{:S(2)}, u32[]{:S(2)}) collective-permute-start(bf16[2,16,64,128]{3,2,1,0:T(8,128)(2,1)S(1)} %get-tuple-element.7), channel_id=1, source_target_pairs={{0,16},{2,18},{4,20},{6,22},{8,24},{10,26},{12,28},{14,30},{1,17},... | collective-permute-start | bytes 1572872 | tf_op jit(solution)/shard_map/ppermute | solution.py:20
  134.4 0.8 copy-start.2
  134.4 1.2 copy-start.1
  191.1 44.6 %collective-permute-start.5 = (bf16[512,2048]{1,0:T(8,128)(2,1)}, bf16[512,2048]{1,0:T(8,128)(2,1)S(1)}, u32[]{:S(2)}, u32[]{:S(2)}) collective-permute-start(bf16[512,2048]{1,0:T(8,128)(2,1)} %shard_map.57), channel_id=1, source_target_pairs={{0,1},{1,0},{2,3},{3,2},{4,5},{5,4},{6,7},{7,6},{8,9},{9,8},{10,11... | collective-permute-start | bytes 6291464 | tf_op jit(solution)/shard_map/ppermute | solution.py:206

commit v4 on v3

v4 whole, which is shorter than its diff:
```python
import functools
import math

import jax
import jax.numpy as jnp
from jax import lax
from jax.experimental import pallas as pl
from jax.experimental.pallas import tpu as pltpu
from jax.sharding import PartitionSpec as P

BLOCK = 64
WINDOW = 512
NOFF = 5
HEADS_PER_STEP = 1


def from_behind(value, axis, steps):
    count = lax.axis_size(axis)
    initial, last = (max(0, -steps), min(count, count - steps))
    return lax.ppermute(value, axis, [(source, source + steps) for source in range(initial, last)])


def block_scores(q, keys, scale):
    return lax.dot_general(
        q, keys, (((1,), (1,)), ((), ())), preferred_element_type=jnp.float32
    ) * scale


def merge(pieces, m_old, l_old, acc_old):
    top = m_old
    for s, _ in pieces:
        row_max = s.max(axis=1, keepdims=True)
        top = row_max if top is None else jnp.maximum(top, row_max)
    total = None
    summed = None
    for s, v in pieces:
        p = jnp.exp(s - top)
        part_total = p.sum(axis=1, keepdims=True)
        part = jnp.dot(p.astype(jnp.bfloat16), v, preferred_element_type=jnp.float32)
        total = part_total if total is None else total + part_total
        summed = part if summed is None else summed + part
    if m_old is not None:
        alpha = jnp.exp(m_old - top)
        total = total + l_old * alpha
        summed = summed + acc_old * alpha
    return top, total, summed


def pack_stats(m, l, width):
    lane = lax.broadcasted_iota(jnp.int32, (m.shape[0], width), 1)
    return jnp.where(lane == 0, m, jnp.where(lane == 1, l, 0.0))


def own_kernel(per_dev, width, scale, q_ref, k_ref, v_ref, acc_ref, st_ref):
    neg = jnp.float32(-jnp.inf)
    for i in range(per_dev):
        lo = i * BLOCK
        q = q_ref[lo:lo + BLOCK, :]
        n_own = lo + BLOCK
        s_o = block_scores(q, k_ref[:n_own, :], scale)
        r_ids = lax.broadcasted_iota(jnp.int32, (BLOCK, n_own), 0)
        c_ids = lax.broadcasted_iota(jnp.int32, (BLOCK, n_own), 1)
        s_o = jnp.where(c_ids <= r_ids + lo, s_o, neg)
        m, l, acc = merge([(s_o, v_ref[:n_own, :])], None, None, None)
        acc_ref[lo:lo + BLOCK, :] = acc
        st_ref[lo:lo + BLOCK, :] = pack_stats(m, l, width)


def prev_kernel(per_dev, width, scale, meta_ref, used_ref, q_ref, kp_ref, vp_ref, acc_ref, st_ref,
                odd_ref, acc_out, st_out):
    prev_ok = meta_ref[0] > 0
    neg = jnp.float32(-jnp.inf)
    for i in range(per_dev):
        lo = i * BLOCK
        q = q_ref[lo:lo + BLOCK, :]
        n_prev = per_dev * BLOCK - lo
        s_p = block_scores(q, kp_ref[lo:, :], scale)
        r_ids = lax.broadcasted_iota(jnp.int32, (BLOCK, n_prev), 0)
        c_ids = lax.broadcasted_iota(jnp.int32, (BLOCK, n_prev), 1)
        s_p = jnp.where((c_ids > r_ids) & prev_ok, s_p, neg)
        start = pl.multiple_of(meta_ref[1 + i] * BLOCK, BLOCK)
        s_f = block_scores(q, kp_ref[pl.ds(start, BLOCK), :], scale)
        s_f = jnp.where(used_ref[i * NOFF] > 0, s_f, neg)
        st = st_ref[lo:lo + BLOCK, :]
        m, l, acc = merge(
            [(s_p, vp_ref[lo:, :]), (s_f, vp_ref[pl.ds(start, BLOCK), :])],
            st[:, 0:1], st[:, 1:2], acc_ref[lo:lo + BLOCK, :],
        )
        half = (i // 2) * BLOCK
        if i % 2:
            odd_ref[half:half + BLOCK, :] = (acc / l).astype(odd_ref.dtype)
        else:
            acc_out[half:half + BLOCK, :] = acc
            st_out[half:half + BLOCK, :] = pack_stats(m, l, width)


def far_kernel(levels, per_dev, width, scale, meta_ref, used_ref, q_ref, acc_ref, st_ref, *rest):
    far_refs = rest[:-1]
    even_ref = rest[-1]
    neg = jnp.float32(-jnp.inf)
    for i in range(0, per_dev, 2):
        lo = i * BLOCK
        half = (i // 2) * BLOCK
        q = q_ref[lo:lo + BLOCK, :]
        pieces = []
        pos = 0
        for level in levels:
            offset = 2**level
            n_src = 2 if level == 1 else 1
            refs = far_refs[pos:pos + 2 * n_src]
            pos += 2 * n_src
            if i % offset:
                continue
            flo = (i // offset) * BLOCK
            k_blk = refs[0][flo:flo + BLOCK, :]
            v_blk = refs[1][flo:flo + BLOCK, :]
            if n_src == 2:
                odd = meta_ref[1 + per_dev] > 0
                k_blk = jnp.where(odd, refs[2][flo:flo + BLOCK, :], k_blk)
                v_blk = jnp.where(odd, refs[3][flo:flo + BLOCK, :], v_blk)
            s_f = block_scores(q, k_blk, scale)
            s_f = jnp.where(used_ref[i * NOFF + level] > 0, s_f, neg)
            pieces.append((s_f, v_blk))
        st = st_ref[half:half + BLOCK, :]
        m, l, acc = merge(pieces, st[:, 0:1], st[:, 1:2], acc_ref[half:half + BLOCK, :])
        even_ref[half:half + BLOCK, :] = (acc / l).astype(even_ref.dtype)


def matmul_kernel(sel_ref, a_ref, w_ref, o_ref):
    o_ref[...] = jnp.dot(a_ref[...], w_ref[...], preferred_element_type=jnp.float32).astype(
        o_ref.dtype
    )


def project_half(attended, weight, half, tn=512):
    rows, depth = attended.shape
    cw = weight.shape[1] // 2
    steps = cw // tn
    return pl.pallas_call(
        matmul_kernel,
        out_shape=jax.ShapeDtypeStruct((rows, cw), jnp.bfloat16),
        grid_spec=pltpu.PrefetchScalarGridSpec(
            num_scalar_prefetch=1,
            grid=(steps,),
            in_specs=[
                pl.BlockSpec((rows, depth), lambda j, sel: (0, 0)),
                pl.BlockSpec((depth, tn), lambda j, sel: (0, sel[0] * steps + j)),
            ],
            out_specs=pl.BlockSpec((rows, tn), lambda j, sel: (0, j)),
        ),
        compiler_params=pltpu.CompilerParams(dimension_semantics=("arbitrary",)),
        cost_estimate=pl.CostEstimate(
            flops=2 * rows * depth * cw,
            transcendentals=0,
            bytes_accessed=2 * (rows * depth + depth * cw + rows * cw),
        ),
    )(jnp.reshape(half, (1,)).astype(jnp.int32), attended, weight)


def pick_blocks(kv, local):
    return jnp.concatenate(
        [lax.dynamic_slice_in_dim(kv, local[b] * BLOCK, BLOCK, axis=2) for b in range(local.shape[0])],
        axis=2,
    )


def per_device(queries, keys, values, far_blocks, out_weight):
    rows, heads, width = queries.shape
    per_dev = rows // BLOCK
    device = lax.axis_index("ctx")
    cycle_size = lax.axis_size("ctx")
    scale = 1.0 / math.sqrt(width)
    q_t = jnp.transpose(queries, (1, 0, 2))
    kv_t = jnp.stack([jnp.transpose(keys, (1, 0, 2)), jnp.transpose(values, (1, 0, 2))])
    prev_kv = from_behind(kv_t, "ctx", 1)
    levels = []
    far_arrays = []
    for level in range(1, NOFF):
        offset = 2**level
        if offset >= cycle_size:
            continue
        target = lax.dynamic_slice_in_dim(far_blocks, (device + offset) * per_dev, per_dev, 0)[
            ::offset, level
        ]
        local = jnp.clip(target - device * per_dev, 0, per_dev - 1)
        if level == 1:
            direct = lax.ppermute(
                pick_blocks(kv_t, local), "ctx",
                [(s, s + 2) for s in range(0, cycle_size - 2, 2)],
            )
            nxt = lax.dynamic_slice_in_dim(far_blocks, (device + 1) * per_dev, per_dev, 0)[::2, 1]
            fwd_local = jnp.clip(nxt - (device - 1) * per_dev, 0, per_dev - 1)
            far_arrays.append((direct, None))
        else:
            far_arrays.append((from_behind(pick_blocks(kv_t, local), "ctx", offset),))
        levels.append(level)

    own = lax.dynamic_slice_in_dim(far_blocks, device * per_dev, per_dev, 0)
    query_index = device * per_dev + jnp.arange(per_dev, dtype=jnp.int32)
    used = (own <= (query_index - WINDOW // BLOCK - 1)[:, None]).astype(jnp.int32).reshape(-1)
    pick = jnp.clip(own[:, 0] - (device - 1) * per_dev, 0, per_dev - 1)
    meta = jnp.concatenate(
        [(device > 0).astype(jnp.int32)[None], pick.astype(jnp.int32), (device % 2)[None]]
    )

    row_spec = lambda n: pl.BlockSpec((None, n, width), lambda h, *_: (h, 0, 0))
    out_spec = lambda n: pl.BlockSpec((n, width), lambda h, *_: (0, h))
    k_spec = lambda n: pl.BlockSpec((None, None, n, width), lambda h, *_: (0, h, 0, 0))
    v_spec = lambda n: pl.BlockSpec((None, None, n, width), lambda h, *_: (1, h, 0, 0))
    half_rows = rows // 2
    f32 = jnp.float32
    params = pltpu.CompilerParams(dimension_semantics=("arbitrary",))
    state = lambda n: jax.ShapeDtypeStruct((heads, n, width), f32)

    def cost(keys_per_row, n_rows, extra_bytes):
        return pl.CostEstimate(
            flops=4 * n_rows * heads * width * keys_per_row,
            transcendentals=n_rows * heads * keys_per_row,
            bytes_accessed=extra_bytes,
        )

    acc0, st0 = pl.pallas_call(
        functools.partial(own_kernel, per_dev, width, scale),
        out_shape=(state(rows), state(rows)),
        grid=(heads,),
        in_specs=[row_spec(rows), k_spec(rows), v_spec(rows)],
        out_specs=(row_spec(rows), row_spec(rows)),
        compiler_params=params,
        cost_estimate=cost(WINDOW // 2, rows, 2 * heads * rows * width * (3 * 2 + 2 * 4)),
    )(q_t, kv_t, kv_t)

    prev_kv, acc0, st0 = lax.optimization_barrier((prev_kv, acc0, st0))
    if far_arrays and far_arrays[0][1] is None:
        forwarded = lax.ppermute(
            pick_blocks(prev_kv, fwd_local), "ctx",
            [(s, s + 1) for s in range(0, cycle_size - 1, 2)],
        )
        far_arrays[0] = (far_arrays[0][0], forwarded)
    far_specs, far_operands = [], []
    for group in far_arrays:
        for a in group:
            far_specs += [k_spec(a.shape[2]), v_spec(a.shape[2])]
            far_operands += [a, a]
    att_odd, acc1, st1 = pl.pallas_call(
        functools.partial(prev_kernel, per_dev, width, scale),
        out_shape=(
            jax.ShapeDtypeStruct((half_rows, heads * width), queries.dtype),
            state(half_rows),
            state(half_rows),
        ),
        grid_spec=pltpu.PrefetchScalarGridSpec(
            num_scalar_prefetch=2,
            grid=(heads,),
            in_specs=[row_spec(rows), k_spec(rows), v_spec(rows), row_spec(rows), row_spec(rows)],
            out_specs=(out_spec(half_rows), row_spec(half_rows), row_spec(half_rows)),
        ),
        compiler_params=params,
        cost_estimate=cost(WINDOW // 2 + BLOCK, rows, heads * rows * width * (3 * 2 + 2 * 4 + 8)),
    )(meta, used, q_t, prev_kv, prev_kv, acc0, st0)

    att_even = pl.pallas_call(
        functools.partial(far_kernel, levels, per_dev, width, scale),
        out_shape=jax.ShapeDtypeStruct((half_rows, heads * width), queries.dtype),
        grid_spec=pltpu.PrefetchScalarGridSpec(
            num_scalar_prefetch=2,
            grid=(heads,),
            in_specs=[row_spec(rows), row_spec(half_rows), row_spec(half_rows)] + far_specs,
            out_specs=out_spec(half_rows),
        ),
        compiler_params=params,
        cost_estimate=cost(2 * BLOCK, half_rows, heads * width * (2 * rows + 8 * half_rows + 2 * sum(a.shape[2] for a in far_operands))),
    )(meta, used, q_t, acc1, st1, *far_operands)

    n_head = lax.axis_size("head")
    if n_head != 2:
        parts = []
        for att in (att_even, att_odd):
            partial_value = jnp.dot(att, out_weight, preferred_element_type=jnp.float32)
            parts.append(lax.psum_scatter(
                partial_value.astype(jnp.bfloat16), "head", scatter_dimension=1, tiled=True
            ))
    else:
        hidx = lax.axis_index("head")
        parts = []
        for att in (att_odd, att_even):
            p_other = project_half(att, out_weight, 1 - hidx)
            received = lax.ppermute(p_other, "head", [(0, 1), (1, 0)])
            p_own = project_half(att, out_weight, hidx)
            parts.append(
                (p_own.astype(jnp.float32) + received.astype(jnp.float32)).astype(jnp.bfloat16)
            )
        parts = parts[::-1]
    even, odd = (p.reshape(per_dev // 2, BLOCK, -1) for p in parts)
    return jnp.stack([even, odd], axis=1).reshape(rows, -1)


def solution(mesh):
    placed = (
        P("ctx", "head", None),
        P("ctx", "head", None),
        P("ctx", "head", None),
        P(),
        P("head", None),
    )
    return jax.shard_map(
        per_device, mesh=mesh, in_specs=placed, out_specs=P("ctx", "head"), check_vma=False
    )
```

time: 240 us -> 207 us (0.86)
  the two profiles are of different devices: /device:TPU:28 before, /device:TPU:0 now
where the time goes in v4:
time: 207 us; the launch traced here: 206 us
  Pallas kernels  129 us (62%)
  starting transfers between devices  33.9 us (16%)
  other arithmetic  15 us (7%)
  local copies, waits for them, and re-layouts  14.9 us (7%)
  between operations  7.25 us (4%)
  waiting for transfers between devices  6.03 us (3%)
    pallas_call x1, Pallas kernels, per_device(): pl.pallas_call(functools.partial(prev_kernel, per_dev, width, scale), out...  47.4 us
    pallas_call x1, Pallas kernels, per_device(): pl.pallas_call(functools.partial(own_kernel, per_dev, width, scale), out_...  36 us
    pallas_call x4, Pallas kernels, project_half(): pl.pallas_call(matmul_kernel, out_shape=jax.ShapeDtypeStruct((rows, cw),...  26.4 us
    pallas_call x1, Pallas kernels, per_device(): pl.pallas_call(functools.partial(far_kernel, levels, per_dev, width, scal...  19.2 us
    ppermute x1, starting transfers between devices, per_device(): lax.ppermute(pick_blocks(prev_kv, fwd_local), 'ctx', [(s, s + 1) for s in...  14.5 us
    ppermute x3, starting transfers between devices, from_behind(): lax.ppermute(value, axis, [(source, source + steps) for source in range(i...  13.5 us
    another operation x3, other arithmetic, per_device(): jnp.stack([jnp.transpose(keys, (1, 0, 2)), jnp.transpose(values, (1, 0, 2...  6.66 us
    ppermute x2, waiting for transfers between devices, per_device(): received = lax.ppermute(p_other, 'head', [(0, 1), (1, 0)])  6.02 us
  transfers between devices with their start and end apart: 7, of which 1 were waited for; matrix products, arithmetic and copies ran while one was open for 10% of the time, Pallas kernels for 63%

profile of v4, /device:TPU:0, one launch (start us, length us, event | category | flops | bytes accessed | tf_op | source)
XLA Modules:
  0.0 206.1 jit_solution(13995916855330376917)
XLA Ops:
  0.0 3.3 %copy_bitcast_fusion = (bf16[1,16,512,128]{3,2,1,0:T(8,128)(2,1)S(1)}, bf16[1,16,512,128]{3,2,1,0:T(8,128)(2,1)S(1)}) fusion(bf16[512,16,128]{2,1,0:T(8,128)(2,1)} %param.7, bf16[512,16,128]{2,1,0:T(8,128)(2,1)} %param.6), kind=kLoop, calls=%fused_computation.18 | loop fusion | bytes 8388608 | tf_op jit(solution)/shard_map/stack | solution.py:174
  3.3 2.6 %pad_maximum_fusion.k_ref.v_ref = bf16[2,16,512,128]{3,2,1,0:T(8,128)(2,1)} fusion(bf16[1,16,512,128]{3,2,1,0:T(8,128)(2,1)S(1)} %get-tuple-element.49, bf16[1,16,512,128]{3,2,1,0:T(8,128)(2,1)S(1)} %get-tuple-element.50), kind=kLoop, calls=%fused_computation.7 | loop fusion | flops 2097152 | bytes 8388608 | tf_op jit(solution)/shard_map/stack | solution.py:174
  5.9 4.3 %collective-permute-start = (bf16[2,16,512,128]{3,2,1,0:T(8,128)(2,1)}, bf16[2,16,512,128]{3,2,1,0:T(8,128)(2,1)}, u32[]{:S(2)}, u32[]{:S(2)}) collective-permute-start(bf16[2,16,512,128]{3,2,1,0:T(8,128)(2,1)} %pad_maximum_fusion.k_ref.v_ref), channel_id=1, source_target_pairs={{0,2},{2,4},{4,6},{6,8},{8,10},{10,12},{12,14},{14,16},{16,18},{18... | collective-permute-start | bytes 12582920 | tf_op jit(solution)/shard_map/ppermute | solution.py:20
  16.3 3.1 %fusion.6 = (bf16[2,16,64,128]{3,2,1,0:T(8,128)(2,1)}, bf16[2,16,64,128]{3,2,1,0:T(8,128)(2,1)S(1)}, bf16[2,16,64,128]{3,2,1,0:T(8,128)(2,1)S(1)}, bf16[2,16,64,...) fusion(s32[]{:T(128)S(6)} %select_n.71, ...), kind=kLoop, calls=%fused_computation.30 | loop fusion | flops 6291456 | bytes 7340056 | tf_op jit(solution)/shard_map/stack | solution.py:174
  19.3 1.5 pad_maximum_fusion.1
  20.9 3.8 %collective-permute-start.1 = (bf16[2,16,256,128]{3,2,1,0:T(8,128)(2,1)}, bf16[2,16,256,128]{3,2,1,0:T(8,128)(2,1)}, u32[]{:S(2)}, u32[]{:S(2)}) collective-permute-start(bf16[2,16,256,128]{3,2,1,0:T(8,128)(2,1)} %pad_maximum_fusion.1), channel_id=1, source_target_pairs={{0,4},{4,8},{8,12},{12,16},{16,20},{20,24},{24,28},{1,5},{5,9},{9,... | collective-permute-start | bytes 6291464 | tf_op jit(solution)/shard_map/ppermute | solution.py:187
  28.0 3.5 %copy.14 = bf16[512,16,128]{2,0,1:T(8,128)(2,1)} copy(bf16[512,16,128]{2,1,0:T(8,128)(2,1)} %param.5) | data formatting | bytes 4194304 | tf_op args[0]
  31.4 36.0 %shard_map.55 = (f32[16,512,128]{2,1,0:T(8,128)}, f32[16,512,128]{2,1,0:T(8,128)}) custom-call(bf16[16,512,128]{2,1,0:T(8,128)(2,1)} %bitcast.33, bf16[2,16,512,128]{3,2,1,0:T(8,128)(2,1)} %pad_maximum_fusion.k_ref.v_ref, bf16[2,16,512,128]{3,2,1,0:T(8,128)(2,1)} %pad_maximum_fusion.k_ref.v_ref), custom_call_target="tpu_custom_call" | custom-call | flops 1073741824 | bytes 29360128 | tf_op jit(solution)/shard_map/pallas_call | solution.py:222
  67.4 2.1 %constant_dynamic-slice_fusion.5 = (bf16[2,16,64,128]{3,2,1,0:T(8,128)(2,1)S(1)}, bf16[2,16,64,128]{3,2,1,0:T(8,128)(2,1)S(1)}, bf16[2,16,64,128]{3,2,1,0:T(8,128)(2,1)S(1)}, bf16[2,16,64,128]{3,2,1,0:T(8,128)(2,1)S(1)}) fusion(bf16[2,16,512,128]{3,2,1,0:T(8,128)(2,1)} %collective-permute-done.kp_ref.vp_ref, s32[]{:T(128)S(6)} %select_n.63, ...), kind=kLoop, calls=%fused_computation.36 | loop fusion | bytes 4194320 | tf_op jit(solution)/shard_map/dynamic_slice | solution.py:162
  69.6 1.5 pad_maximum_fusion.2
  71.1 14.5 %collective-permute-start.2 = (bf16[2,16,256,128]{3,2,1,0:T(8,128)(2,1)}, bf16[2,16,256,128]{3,2,1,0:T(8,128)(2,1)}, u32[]{:S(2)}, u32[]{:S(2)}) collective-permute-start(bf16[2,16,256,128]{3,2,1,0:T(8,128)(2,1)} %pad_maximum_fusion.2), channel_id=1, source_target_pairs={{0,2},{4,6},{8,10},{12,14},{16,18},{20,22},{24,26},{28,30},{1,3},{... | collective-permute-start | bytes 6291464 | tf_op jit(solution)/shard_map/ppermute | solution.py:234
  85.6 5.6 %collective-permute-start.4 = (bf16[2,16,64,128]{3,2,1,0:T(8,128)(2,1)}, bf16[2,16,64,128]{3,2,1,0:T(8,128)(2,1)S(1)}, u32[]{:S(2)}, u32[]{:S(2)}) collective-permute-start(bf16[2,16,64,128]{3,2,1,0:T(8,128)(2,1)} %get-tuple-element.23), channel_id=1, source_target_pairs={{0,16},{2,18},{4,20},{6,22},{8,24},{10,26},{12,28},{14,30},{1,17},... | collective-permute-start | bytes 1572872 | tf_op jit(solution)/shard_map/ppermute | solution.py:20
  93.9 3.5 %collective-permute-start.3 = (bf16[2,16,128,128]{3,2,1,0:T(8,128)(2,1)}, bf16[2,16,128,128]{3,2,1,0:T(8,128)(2,1)S(1)}, u32[]{:S(2)}, u32[]{:S(2)}) collective-permute-start(bf16[2,16,128,128]{3,2,1,0:T(8,128)(2,1)} %pad_maximum_fusion.4), channel_id=1, source_target_pairs={{0,8},{2,10},{4,12},{6,14},{8,16},{10,18},{12,20},{14,22},{16,24},... | collective-permute-start | bytes 3145736 | tf_op jit(solution)/shard_map/ppermute | solution.py:20
  99.0 47.4 %shard_map.56 = (bf16[256,2048]{1,0:T(8,128)(2,1)}, f32[16,256,128]{2,1,0:T(8,128)}, f32[16,256,128]{2,1,0:T(8,128)}) custom-call(s32[10]{0:T(128)} %pad_add_fusion.meta_ref, s32[40]{0:T(128)} %reshape.110.used_ref, bf16[16,512,128]{2,1,0:T(8,128)(2,1)} %bitcast.34, bf16[2,16,512,128]{3,2,1,0:T(8,128)(2,1)} %collective-permute-done.kp_ref.vp_ref, ...), custom_call_target="tpu_custom_call" | custom-call | flops 1342177280 | bytes 23068672 | tf_op jit(solution)/shard_map/pallas_call | solution.py:244
  146.4 6.6 %shard_map.61 = bf16[256,2048]{1,0:T(8,128)(2,1)} custom-call(s32[1]{0:T(128)} %bitcast.22.sel_ref, bf16[256,2048]{1,0:T(8,128)(2,1)} %get-tuple-element.20.a_ref, bf16[2048,4096]{1,0:T(8,128)(2,1)} %w_ref.7), custom_call_target="tpu_custom_call" | custom-call | flops 2147483648 | bytes 10485760 | tf_op jit(solution)/shard_map/pallas_call | solution.py:139
  152.9 1.5 collective-permute-start.6
  155.6 19.2 %shard_map.57.a_ref = bf16[256,2048]{1,0:T(8,128)(2,1)} custom-call(s32[10]{0:T(128)} %pad_add_fusion.meta_ref, s32[40]{0:T(128)} %reshape.110.used_ref, bf16[16,512,128]{2,1,0:T(8,128)(2,1)} %bitcast.35, f32[16,256,128]{2,1,0:T(8,128)} %get-tuple-element.18.acc_ref, f32[16,256,128]{2,1,0:T(8,128)} %get-tuple-element.19.st_ref, ...), custom_call_target="tpu_custom_call" | custom-call | flops 268435456 | bytes 12058624 | tf_op jit(solution)/shard_map/pallas_call | solution.py:261
  174.8 6.6 %shard_map.59 = bf16[256,2048]{1,0:T(8,128)(2,1)} custom-call(s32[1]{0:T(128)} %bitcast.22.sel_ref, bf16[256,2048]{1,0:T(8,128)(2,1)} %shard_map.57.a_ref, bf16[2048,4096]{1,0:T(8,128)(2,1)} %w_ref.7), custom_call_target="tpu_custom_call" | custom-call | flops 2147483648 | bytes 10485760 | tf_op jit(solution)/shard_map/pallas_call | solution.py:139
  182.0 6.6 %shard_map.60 = bf16[256,2048]{1,0:T(8,128)(2,1)} custom-call(s32[1]{0:T(128)} %bitcast.sel_ref, bf16[256,2048]{1,0:T(8,128)(2,1)} %get-tuple-element.20.a_ref, bf16[2048,4096]{1,0:T(8,128)(2,1)} %w_ref.7), custom_call_target="tpu_custom_call" | custom-call | flops 2147483648 | bytes 10485760 | tf_op jit(solution)/shard_map/pallas_call | solution.py:139
  188.6 1.6 add_convert_fusion
  190.2 6.6 %shard_map.58 = bf16[256,2048]{1,0:T(8,128)(2,1)} custom-call(s32[1]{0:T(128)} %bitcast.sel_ref, bf16[256,2048]{1,0:T(8,128)(2,1)} %shard_map.57.a_ref, bf16[2048,4096]{1,0:T(8,128)(2,1)} %w_ref.7), custom_call_target="tpu_custom_call" | custom-call | flops 2147483648 | bytes 10485760 | tf_op jit(solution)/shard_map/pallas_call | solution.py:139
  196.8 6.0 %collective-permute-done.5 = bf16[256,2048]{1,0:T(8,128)(2,1)S(1)} collective-permute-done((bf16[256,2048]{1,0:T(8,128)(2,1)}, bf16[256,2048]{1,0:T(8,128)(2,1)S(1)}, u32[]{:S(2)}, u32[]{:S(2)}) %collective-permute-start.5) | collective-permute-done | bytes 1048608 | tf_op jit(solution)/shard_map/ppermute | solution.py:287
  202.8 1.6 add_convert_fusion.1
  204.6 1.5 copy.10
  (34 shorter events, 8.2 us)
Async XLA Ops:
  3.3 2.6 %copy-start = (bf16[1,16,512,128]{3,2,1,0:T(8,128)(2,1)}, bf16[1,16,512,128]{3,2,1,0:T(8,128)(2,1)S(1)}, u32[]{:S(2)}) copy-start(bf16[1,16,512,128]{3,2,1,0:T(8,128)(2,1)S(1)} %get-tuple-element.50) | copy-start | bytes 6291460
  3.3 6.9 %copy-start.3 = (s32[128,5]{0,1:T(8,128)S(1)}, s32[128,5]{0,1:T(8,128)}, u32[]{:S(2)}) copy-start(s32[128,5]{0,1:T(8,128)} %param.8) | copy-start | bytes 7684
  5.9 61.5 %collective-permute-start = (bf16[2,16,512,128]{3,2,1,0:T(8,128)(2,1)}, bf16[2,16,512,128]{3,2,1,0:T(8,128)(2,1)}, u32[]{:S(2)}, u32[]{:S(2)}) collective-permute-start(bf16[2,16,512,128]{3,2,1,0:T(8,128)(2,1)} %pad_maximum_fusion.k_ref.v_ref), channel_id=1, source_target_pairs={{0,2},{2,4},{4,6},{6,8},{8,10},{10,12},{12,14},{14,16},{16,18},{18... | collective-permute-start | bytes 12582920 | tf_op jit(solution)/shard_map/ppermute | solution.py:20
  20.9 133.6 %collective-permute-start.1 = (bf16[2,16,256,128]{3,2,1,0:T(8,128)(2,1)}, bf16[2,16,256,128]{3,2,1,0:T(8,128)(2,1)}, u32[]{:S(2)}, u32[]{:S(2)}) collective-permute-start(bf16[2,16,256,128]{3,2,1,0:T(8,128)(2,1)} %pad_maximum_fusion.1), channel_id=1, source_target_pairs={{0,4},{4,8},{8,12},{12,16},{16,20},{20,24},{24,28},{1,5},{5,9},{9,... | collective-permute-start | bytes 6291464 | tf_op jit(solution)/shard_map/ppermute | solution.py:187
  71.1 83.4 %collective-permute-start.2 = (bf16[2,16,256,128]{3,2,1,0:T(8,128)(2,1)}, bf16[2,16,256,128]{3,2,1,0:T(8,128)(2,1)}, u32[]{:S(2)}, u32[]{:S(2)}) collective-permute-start(bf16[2,16,256,128]{3,2,1,0:T(8,128)(2,1)} %pad_maximum_fusion.2), channel_id=1, source_target_pairs={{0,2},{4,6},{8,10},{12,14},{16,18},{20,22},{24,26},{28,30},{1,3},{... | collective-permute-start | bytes 6291464 | tf_op jit(solution)/shard_map/ppermute | solution.py:234
  85.6 68.8 %collective-permute-start.4 = (bf16[2,16,64,128]{3,2,1,0:T(8,128)(2,1)}, bf16[2,16,64,128]{3,2,1,0:T(8,128)(2,1)S(1)}, u32[]{:S(2)}, u32[]{:S(2)}) collective-permute-start(bf16[2,16,64,128]{3,2,1,0:T(8,128)(2,1)} %get-tuple-element.23), channel_id=1, source_target_pairs={{0,16},{2,18},{4,20},{6,22},{8,24},{10,26},{12,28},{14,30},{1,17},... | collective-permute-start | bytes 1572872 | tf_op jit(solution)/shard_map/ppermute | solution.py:20
  93.9 60.5 %collective-permute-start.3 = (bf16[2,16,128,128]{3,2,1,0:T(8,128)(2,1)}, bf16[2,16,128,128]{3,2,1,0:T(8,128)(2,1)S(1)}, u32[]{:S(2)}, u32[]{:S(2)}) collective-permute-start(bf16[2,16,128,128]{3,2,1,0:T(8,128)(2,1)} %pad_maximum_fusion.4), channel_id=1, source_target_pairs={{0,8},{2,10},{4,12},{6,14},{8,16},{10,18},{12,20},{14,22},{16,24},... | collective-permute-start | bytes 3145736 | tf_op jit(solution)/shard_map/ppermute | solution.py:20
  152.9 35.6 %collective-permute-start.6 = (bf16[256,2048]{1,0:T(8,128)(2,1)}, bf16[256,2048]{1,0:T(8,128)(2,1)S(1)}, u32[]{:S(2)}, u32[]{:S(2)}) collective-permute-start(bf16[256,2048]{1,0:T(8,128)(2,1)} %shard_map.61), channel_id=1, source_target_pairs={{0,1},{1,0},{2,3},{3,2},{4,5},{5,4},{6,7},{7,6},{8,9},{9,8},{10,11... | collective-permute-start | bytes 3145736 | tf_op jit(solution)/shard_map/ppermute | solution.py:287
  154.4 0.8 copy-start.2
  154.5 1.1 copy-start.1
  181.4 21.4 %collective-permute-start.5 = (bf16[256,2048]{1,0:T(8,128)(2,1)}, bf16[256,2048]{1,0:T(8,128)(2,1)S(1)}, u32[]{:S(2)}, u32[]{:S(2)}) collective-permute-start(bf16[256,2048]{1,0:T(8,128)(2,1)} %shard_map.59), channel_id=1, source_target_pairs={{0,1},{1,0},{2,3},{3,2},{4,5},{5,4},{6,7},{7,6},{8,9},{9,8},{10,11... | collective-permute-start | bytes 3145736 | tf_op jit(solution)/shard_map/ppermute | solution.py:287

commit v5 on v4

--- a/solution.py
+++ b/solution.py
@@ -51,79 +51,104 @@
     return jnp.where(lane == 0, m, jnp.where(lane == 1, l, 0.0))
 
 
+TILE = 256
+
+
 def own_kernel(per_dev, width, scale, q_ref, k_ref, v_ref, acc_ref, st_ref):
     neg = jnp.float32(-jnp.inf)
-    for i in range(per_dev):
-        lo = i * BLOCK
-        q = q_ref[lo:lo + BLOCK, :]
-        n_own = lo + BLOCK
+    rows = per_dev * BLOCK
+    for lo in range(0, rows, TILE):
+        q = q_ref[lo:lo + TILE, :]
+        n_own = lo + TILE
         s_o = block_scores(q, k_ref[:n_own, :], scale)
-        r_ids = lax.broadcasted_iota(jnp.int32, (BLOCK, n_own), 0)
-        c_ids = lax.broadcasted_iota(jnp.int32, (BLOCK, n_own), 1)
+        r_ids = lax.broadcasted_iota(jnp.int32, (TILE, n_own), 0)
+        c_ids = lax.broadcasted_iota(jnp.int32, (TILE, n_own), 1)
         s_o = jnp.where(c_ids <= r_ids + lo, s_o, neg)
         m, l, acc = merge([(s_o, v_ref[:n_own, :])], None, None, None)
-        acc_ref[lo:lo + BLOCK, :] = acc
-        st_ref[lo:lo + BLOCK, :] = pack_stats(m, l, width)
+        acc_ref[lo:lo + TILE, :] = acc
+        st_ref[lo:lo + TILE, :] = pack_stats(m, l, width)
+
+
+def column_map(n_cols, values):
+    seg = lax.broadcasted_iota(jnp.int32, (1, n_cols), 1) // BLOCK
+    out = jnp.zeros((1, n_cols), jnp.int32)
+    for j, value in enumerate(values):
+        out = jnp.where(seg == j, value, out)
+    return out
 
 
 def prev_kernel(per_dev, width, scale, meta_ref, used_ref, q_ref, kp_ref, vp_ref, acc_ref, st_ref,
                 odd_ref, acc_out, st_out):
     prev_ok = meta_ref[0] > 0
     neg = jnp.float32(-jnp.inf)
-    for i in range(per_dev):
-        lo = i * BLOCK
-        q = q_ref[lo:lo + BLOCK, :]
-        n_prev = per_dev * BLOCK - lo
+    rows = per_dev * BLOCK
+    per_tile = TILE // BLOCK
+    for lo in range(0, rows, TILE):
+        q = q_ref[lo:lo + TILE, :]
+        n_prev = rows - lo
         s_p = block_scores(q, kp_ref[lo:, :], scale)
-        r_ids = lax.broadcasted_iota(jnp.int32, (BLOCK, n_prev), 0)
-        c_ids = lax.broadcasted_iota(jnp.int32, (BLOCK, n_prev), 1)
+        r_ids = lax.broadcasted_iota(jnp.int32, (TILE, n_prev), 0)
+        c_ids = lax.broadcasted_iota(jnp.int32, (TILE, n_prev), 1)
         s_p = jnp.where((c_ids > r_ids) & prev_ok, s_p, neg)
-        start = pl.multiple_of(meta_ref[1 + i] * BLOCK, BLOCK)
-        s_f = block_scores(q, kp_ref[pl.ds(start, BLOCK), :], scale)
-        s_f = jnp.where(used_ref[i * NOFF] > 0, s_f, neg)
-        st = st_ref[lo:lo + BLOCK, :]
+        blocks = range(lo // BLOCK, lo // BLOCK + per_tile)
+        starts = [pl.multiple_of(meta_ref[1 + i] * BLOCK, BLOCK) for i in blocks]
+        k0 = jnp.concatenate([kp_ref[pl.ds(st, BLOCK), :] for st in starts], axis=0)
+        v0 = jnp.concatenate([vp_ref[pl.ds(st, BLOCK), :] for st in starts], axis=0)
+        s_f = block_scores(q, k0, scale)
+        flags = column_map(TILE, [used_ref[i * NOFF] for i in blocks])
+        r_blk = lax.broadcasted_iota(jnp.int32, (TILE, TILE), 0) // BLOCK
+        c_blk = lax.broadcasted_iota(jnp.int32, (TILE, TILE), 1) // BLOCK
+        s_f = jnp.where((r_blk == c_blk) & (flags > 0), s_f, neg)
+        st = st_ref[lo:lo + TILE, :]
         m, l, acc = merge(
-            [(s_p, vp_ref[lo:, :]), (s_f, vp_ref[pl.ds(start, BLOCK), :])],
-            st[:, 0:1], st[:, 1:2], acc_ref[lo:lo + BLOCK, :],
+            [(s_p, vp_ref[lo:, :]), (s_f, v0)], st[:, 0:1], st[:, 1:2], acc_ref[lo:lo + TILE, :]
         )
-        half = (i // 2) * BLOCK
-        if i % 2:
-            odd_ref[half:half + BLOCK, :] = (acc / l).astype(odd_ref.dtype)
-        else:
-            acc_out[half:half + BLOCK, :] = acc
-            st_out[half:half + BLOCK, :] = pack_stats(m, l, width)
+        for b, i in enumerate(blocks):
+            sl = slice(b * BLOCK, (b + 1) * BLOCK)
+            half = (i // 2) * BLOCK
+            if i % 2:
+                odd_ref[half:half + BLOCK, :] = (acc[sl] / l[sl]).astype(odd_ref.dtype)
+            else:
+                acc_out[half:half + BLOCK, :] = acc[sl]
+                st_out[half:half + BLOCK, :] = pack_stats(m[sl], l[sl], width)
 
 
 def far_kernel(levels, per_dev, width, scale, meta_ref, used_ref, q_ref, acc_ref, st_ref, *rest):
     far_refs = rest[:-1]
     even_ref = rest[-1]
     neg = jnp.float32(-jnp.inf)
-    for i in range(0, per_dev, 2):
-        lo = i * BLOCK
-        half = (i // 2) * BLOCK
-        q = q_ref[lo:lo + BLOCK, :]
-        pieces = []
-        pos = 0
-        for level in levels:
-            offset = 2**level
-            n_src = 2 if level == 1 else 1
-            refs = far_refs[pos:pos + 2 * n_src]
-            pos += 2 * n_src
-            if i % offset:
-                continue
-            flo = (i // offset) * BLOCK
-            k_blk = refs[0][flo:flo + BLOCK, :]
-            v_blk = refs[1][flo:flo + BLOCK, :]
-            if n_src == 2:
-                odd = meta_ref[1 + per_dev] > 0
-                k_blk = jnp.where(odd, refs[2][flo:flo + BLOCK, :], k_blk)
-                v_blk = jnp.where(odd, refs[3][flo:flo + BLOCK, :], v_blk)
-            s_f = block_scores(q, k_blk, scale)
-            s_f = jnp.where(used_ref[i * NOFF + level] > 0, s_f, neg)
-            pieces.append((s_f, v_blk))
-        st = st_ref[half:half + BLOCK, :]
-        m, l, acc = merge(pieces, st[:, 0:1], st[:, 1:2], acc_ref[half:half + BLOCK, :])
-        even_ref[half:half + BLOCK, :] = (acc / l).astype(even_ref.dtype)
+    n_even = per_dev // 2
+    q = jnp.concatenate([q_ref[2 * e * BLOCK:(2 * e + 1) * BLOCK, :] for e in range(n_even)], axis=0)
+    keys, vals, targets, flags = [], [], [], []
+    pos = 0
+    for level in levels:
+        offset = 2**level
+        n_src = 2 if level == 1 else 1
+        refs = far_refs[pos:pos + 2 * n_src]
+        pos += 2 * n_src
+        k_lvl = refs[0][...]
+        v_lvl = refs[1][...]
+        if n_src == 2:
+            odd = meta_ref[1 + per_dev] > 0
+            k_lvl = jnp.where(odd, refs[2][...], k_lvl)
+            v_lvl = jnp.where(odd, refs[3][...], v_lvl)
+        keys.append(k_lvl)
+        vals.append(v_lvl)
+        for k in range(k_lvl.shape[0] // BLOCK):
+            qblock = k * offset
+            targets.append(qblock // 2)
+            flags.append(used_ref[qblock * NOFF + level])
+    k_far = jnp.concatenate(keys, axis=0)
+    v_far = jnp.concatenate(vals, axis=0)
+    n_keys = k_far.shape[0]
+    s_f = block_scores(q, k_far, scale)
+    col_target = column_map(n_keys, targets)
+    col_flag = column_map(n_keys, flags)
+    r_blk = lax.broadcasted_iota(jnp.int32, (n_even * BLOCK, n_keys), 0) // BLOCK
+    s_f = jnp.where((r_blk == col_target) & (col_flag > 0), s_f, neg)
+    st = st_ref[...]
+    m, l, acc = merge([(s_f, v_far)], st[:, 0:1], st[:, 1:2], acc_ref[...])
+    even_ref[...] = (acc / l).astype(even_ref.dtype)
 
 
 def matmul_kernel(sel_ref, a_ref, w_ref, o_ref):

time: 207 us -> 187 us (0.903)
  the two profiles are of different devices: /device:TPU:0 before, /device:TPU:16 now
where the time goes in v5:
time: 187 us; the launch traced here: 185 us
  Pallas kernels  82.8 us (44%)
  waiting for transfers between devices  50.4 us (27%)
  starting transfers between devices  15.7 us (8%)
  other arithmetic  14.9 us (8%)
  local copies, waits for them, and re-layouts  14.4 us (8%)
  between operations  7.27 us (4%)
    ppermute x3, waiting for transfers between devices, from_behind(): lax.ppermute(value, axis, [(source, source + steps) for source in range(i...  41.4 us
    pallas_call x4, Pallas kernels, project_half(): pl.pallas_call(matmul_kernel, out_shape=jax.ShapeDtypeStruct((rows, cw),...  26.4 us
    pallas_call x1, Pallas kernels, per_device(): pl.pallas_call(functools.partial(prev_kernel, per_dev, width, scale), out...  22.8 us
    pallas_call x1, Pallas kernels, per_device(): pl.pallas_call(functools.partial(own_kernel, per_dev, width, scale), out_...  17.1 us
    pallas_call x1, Pallas kernels, per_device(): pl.pallas_call(functools.partial(far_kernel, levels, per_dev, width, scal...  16.5 us
    ppermute x2, waiting for transfers between devices, per_device(): received = lax.ppermute(p_other, 'head', [(0, 1), (1, 0)])  8.99 us
    ppermute x3, starting transfers between devices, from_behind(): lax.ppermute(value, axis, [(source, source + steps) for source in range(i...  6.66 us
    another operation x3, other arithmetic, per_device(): jnp.stack([jnp.transpose(keys, (1, 0, 2)), jnp.transpose(values, (1, 0, 2...  6.63 us
  transfers between devices with their start and end apart: 7, of which 3 were waited for; matrix products, arithmetic and copies ran while one was open for 10% of the time, Pallas kernels for 45%

profile of v5, /device:TPU:16, one launch (start us, length us, event | category | flops | bytes accessed | tf_op | source)
XLA Modules:
  0.0 185.5 jit_solution(2031108441479708144)
XLA Ops:
  0.0 3.3 %copy_bitcast_fusion = (bf16[1,16,512,128]{3,2,1,0:T(8,128)(2,1)S(1)}, bf16[1,16,512,128]{3,2,1,0:T(8,128)(2,1)S(1)}) fusion(bf16[512,16,128]{2,1,0:T(8,128)(2,1)} %param.7, bf16[512,16,128]{2,1,0:T(8,128)(2,1)} %param.6), kind=kLoop, calls=%fused_computation.18 | loop fusion | bytes 8388608 | tf_op jit(solution)/shard_map/stack | solution.py:199
  3.3 2.6 %pad_maximum_fusion.k_ref.v_ref = bf16[2,16,512,128]{3,2,1,0:T(8,128)(2,1)} fusion(bf16[1,16,512,128]{3,2,1,0:T(8,128)(2,1)S(1)} %get-tuple-element.49, bf16[1,16,512,128]{3,2,1,0:T(8,128)(2,1)S(1)} %get-tuple-element.50), kind=kLoop, calls=%fused_computation.7 | loop fusion | flops 2097152 | bytes 8388608 | tf_op jit(solution)/shard_map/stack | solution.py:199
  5.9 1.9 %collective-permute-start = (bf16[2,16,512,128]{3,2,1,0:T(8,128)(2,1)}, bf16[2,16,512,128]{3,2,1,0:T(8,128)(2,1)}, u32[]{:S(2)}, u32[]{:S(2)}) collective-permute-start(bf16[2,16,512,128]{3,2,1,0:T(8,128)(2,1)} %pad_maximum_fusion.k_ref.v_ref), channel_id=1, source_target_pairs={{0,2},{2,4},{4,6},{6,8},{8,10},{10,12},{12,14},{14,16},{16,18},{18... | collective-permute-start | bytes 12582920 | tf_op jit(solution)/shard_map/ppermute | solution.py:20
  13.9 3.1 %fusion.6 = (bf16[2,16,64,128]{3,2,1,0:T(8,128)(2,1)}, bf16[2,16,64,128]{3,2,1,0:T(8,128)(2,1)S(1)}, bf16[2,16,64,128]{3,2,1,0:T(8,128)(2,1)S(1)}, bf16[2,16,64,...) fusion(s32[]{:T(128)S(6)} %select_n.71, ...), kind=kLoop, calls=%fused_computation.30 | loop fusion | flops 6291456 | bytes 7340056 | tf_op jit(solution)/shard_map/stack | solution.py:199
  16.9 1.5 pad_maximum_fusion.1
  18.4 3.4 %collective-permute-start.1 = (bf16[2,16,256,128]{3,2,1,0:T(8,128)(2,1)}, bf16[2,16,256,128]{3,2,1,0:T(8,128)(2,1)}, u32[]{:S(2)}, u32[]{:S(2)}) collective-permute-start(bf16[2,16,256,128]{3,2,1,0:T(8,128)(2,1)} %pad_maximum_fusion.1), channel_id=1, source_target_pairs={{0,4},{4,8},{8,12},{12,16},{16,20},{20,24},{24,28},{1,5},{5,9},{9,... | collective-permute-start | bytes 6291464 | tf_op jit(solution)/shard_map/ppermute | solution.py:212
  25.2 3.5 %copy.14 = bf16[512,16,128]{2,0,1:T(8,128)(2,1)} copy(bf16[512,16,128]{2,1,0:T(8,128)(2,1)} %param.5) | data formatting | bytes 4194304 | tf_op args[0]
  28.6 17.1 %shard_map.55 = (f32[16,512,128]{2,1,0:T(8,128)}, f32[16,512,128]{2,1,0:T(8,128)}) custom-call(bf16[16,512,128]{2,1,0:T(8,128)(2,1)} %bitcast.33, bf16[2,16,512,128]{3,2,1,0:T(8,128)(2,1)} %pad_maximum_fusion.k_ref.v_ref, bf16[2,16,512,128]{3,2,1,0:T(8,128)(2,1)} %pad_maximum_fusion.k_ref.v_ref), custom_call_target="tpu_custom_call" | custom-call | flops 1073741824 | bytes 29360128 | tf_op jit(solution)/shard_map/pallas_call | solution.py:247
  45.8 33.7 %collective-permute-done.kp_ref.vp_ref = bf16[2,16,512,128]{3,2,1,0:T(8,128)(2,1)} collective-permute-done((bf16[2,16,512,128]{3,2,1,0:T(8,128)(2,1)}, bf16[2,16,512,128]{3,2,1,0:T(8,128)(2,1)}, u32[]{:S(2)}, u32[]{:S(2)}) %collective-permute-start) | collective-permute-done | bytes 4194336 | tf_op jit(solution)/shard_map/ppermute | solution.py:20
  79.4 1.7 constant_dynamic-slice_fusion.5
  81.1 1.5 pad_maximum_fusion.2
  82.7 2.6 %collective-permute-start.2 = (bf16[2,16,256,128]{3,2,1,0:T(8,128)(2,1)}, bf16[2,16,256,128]{3,2,1,0:T(8,128)(2,1)}, u32[]{:S(2)}, u32[]{:S(2)}) collective-permute-start(bf16[2,16,256,128]{3,2,1,0:T(8,128)(2,1)} %pad_maximum_fusion.2), channel_id=1, source_target_pairs={{0,2},{4,6},{8,10},{12,14},{16,18},{20,22},{24,26},{28,30},{1,3},{... | collective-permute-start | bytes 6291464 | tf_op jit(solution)/shard_map/ppermute | solution.py:259
  89.2 3.5 %collective-permute-start.3 = (bf16[2,16,128,128]{3,2,1,0:T(8,128)(2,1)}, bf16[2,16,128,128]{3,2,1,0:T(8,128)(2,1)S(1)}, u32[]{:S(2)}, u32[]{:S(2)}) collective-permute-start(bf16[2,16,128,128]{3,2,1,0:T(8,128)(2,1)} %pad_maximum_fusion.4), channel_id=1, source_target_pairs={{0,8},{2,10},{4,12},{6,14},{8,16},{10,18},{12,20},{14,22},{16,24},... | collective-permute-start | bytes 3145736 | tf_op jit(solution)/shard_map/ppermute | solution.py:20
  94.2 22.8 %shard_map.56 = (bf16[256,2048]{1,0:T(8,128)(2,1)}, f32[16,256,128]{2,1,0:T(8,128)}, f32[16,256,128]{2,1,0:T(8,128)}) custom-call(s32[10]{0:T(128)} %pad_add_fusion.meta_ref, s32[40]{0:T(128)} %reshape.110.used_ref, bf16[16,512,128]{2,1,0:T(8,128)(2,1)} %bitcast.34, bf16[2,16,512,128]{3,2,1,0:T(8,128)(2,1)} %collective-permute-done.kp_ref.vp_ref, ...), custom_call_target="tpu_custom_call" | custom-call | flops 1342177280 | bytes 23068672 | tf_op jit(solution)/shard_map/pallas_call | solution.py:269
  116.9 6.6 %shard_map.61 = bf16[256,2048]{1,0:T(8,128)(2,1)} custom-call(s32[1]{0:T(128)} %bitcast.22.sel_ref, bf16[256,2048]{1,0:T(8,128)(2,1)} %get-tuple-element.20.a_ref, bf16[2048,4096]{1,0:T(8,128)(2,1)} %w_ref.7), custom_call_target="tpu_custom_call" | custom-call | flops 2147483648 | bytes 10485760 | tf_op jit(solution)/shard_map/pallas_call | solution.py:164
  123.5 1.5 collective-permute-start.6
  125.0 7.7 %collective-permute-done.3.rest_4_.rest_5_ = bf16[2,16,128,128]{3,2,1,0:T(8,128)(2,1)S(1)} collective-permute-done((bf16[2,16,128,128]{3,2,1,0:T(8,128)(2,1)}, bf16[2,16,128,128]{3,2,1,0:T(8,128)(2,1)S(1)}, u32[]{:S(2)}, u32[]{:S(2)}) %collective-permute-start.3) | collective-permute-done | bytes 1048608 | tf_op jit(solution)/shard_map/ppermute | solution.py:20
  133.8 16.5 %shard_map.57.a_ref = bf16[256,2048]{1,0:T(8,128)(2,1)} custom-call(s32[10]{0:T(128)} %pad_add_fusion.meta_ref, s32[40]{0:T(128)} %reshape.110.used_ref, bf16[16,512,128]{2,1,0:T(8,128)(2,1)} %bitcast.35, f32[16,256,128]{2,1,0:T(8,128)} %get-tuple-element.18.acc_ref, f32[16,256,128]{2,1,0:T(8,128)} %get-tuple-element.19.st_ref, ...), custom_call_target="tpu_custom_call" | custom-call | flops 268435456 | bytes 12058624 | tf_op jit(solution)/shard_map/pallas_call | solution.py:286
  150.3 6.6 %shard_map.59 = bf16[256,2048]{1,0:T(8,128)(2,1)} custom-call(s32[1]{0:T(128)} %bitcast.22.sel_ref, bf16[256,2048]{1,0:T(8,128)(2,1)} %shard_map.57.a_ref, bf16[2048,4096]{1,0:T(8,128)(2,1)} %w_ref.7), custom_call_target="tpu_custom_call" | custom-call | flops 2147483648 | bytes 10485760 | tf_op jit(solution)/shard_map/pallas_call | solution.py:164
  158.4 6.6 %shard_map.60 = bf16[256,2048]{1,0:T(8,128)(2,1)} custom-call(s32[1]{0:T(128)} %bitcast.sel_ref, bf16[256,2048]{1,0:T(8,128)(2,1)} %get-tuple-element.20.a_ref, bf16[2048,4096]{1,0:T(8,128)(2,1)} %w_ref.7), custom_call_target="tpu_custom_call" | custom-call | flops 2147483648 | bytes 10485760 | tf_op jit(solution)/shard_map/pallas_call | solution.py:164
  165.0 1.6 add_convert_fusion
  166.6 6.6 %shard_map.58 = bf16[256,2048]{1,0:T(8,128)(2,1)} custom-call(s32[1]{0:T(128)} %bitcast.sel_ref, bf16[256,2048]{1,0:T(8,128)(2,1)} %shard_map.57.a_ref, bf16[2048,4096]{1,0:T(8,128)(2,1)} %w_ref.7), custom_call_target="tpu_custom_call" | custom-call | flops 2147483648 | bytes 10485760 | tf_op jit(solution)/shard_map/pallas_call | solution.py:164
  173.2 9.0 %collective-permute-done.5 = bf16[256,2048]{1,0:T(8,128)(2,1)S(1)} collective-permute-done((bf16[256,2048]{1,0:T(8,128)(2,1)}, bf16[256,2048]{1,0:T(8,128)(2,1)S(1)}, u32[]{:S(2)}, u32[]{:S(2)}) %collective-permute-start.5) | collective-permute-done | bytes 1048608 | tf_op jit(solution)/shard_map/ppermute | solution.py:312
  182.2 1.6 add_convert_fusion.1
  (34 shorter events, 11.7 us)
Async XLA Ops:
  3.3 2.6 %copy-start = (bf16[1,16,512,128]{3,2,1,0:T(8,128)(2,1)}, bf16[1,16,512,128]{3,2,1,0:T(8,128)(2,1)S(1)}, u32[]{:S(2)}) copy-start(bf16[1,16,512,128]{3,2,1,0:T(8,128)(2,1)S(1)} %get-tuple-element.50) | copy-start | bytes 6291460
  3.3 4.5 %copy-start.3 = (s32[128,5]{0,1:T(8,128)S(1)}, s32[128,5]{0,1:T(8,128)}, u32[]{:S(2)}) copy-start(s32[128,5]{0,1:T(8,128)} %param.8) | copy-start | bytes 7684
  5.9 73.5 %collective-permute-start = (bf16[2,16,512,128]{3,2,1,0:T(8,128)(2,1)}, bf16[2,16,512,128]{3,2,1,0:T(8,128)(2,1)}, u32[]{:S(2)}, u32[]{:S(2)}) collective-permute-start(bf16[2,16,512,128]{3,2,1,0:T(8,128)(2,1)} %pad_maximum_fusion.k_ref.v_ref), channel_id=1, source_target_pairs={{0,2},{2,4},{4,6},{6,8},{8,10},{10,12},{12,14},{14,16},{16,18},{18... | collective-permute-start | bytes 12582920 | tf_op jit(solution)/shard_map/ppermute | solution.py:20
  18.4 114.4 %collective-permute-start.1 = (bf16[2,16,256,128]{3,2,1,0:T(8,128)(2,1)}, bf16[2,16,256,128]{3,2,1,0:T(8,128)(2,1)}, u32[]{:S(2)}, u32[]{:S(2)}) collective-permute-start(bf16[2,16,256,128]{3,2,1,0:T(8,128)(2,1)} %pad_maximum_fusion.1), channel_id=1, source_target_pairs={{0,4},{4,8},{8,12},{12,16},{16,20},{20,24},{24,28},{1,5},{5,9},{9,... | collective-permute-start | bytes 6291464 | tf_op jit(solution)/shard_map/ppermute | solution.py:212
  82.7 50.1 %collective-permute-start.2 = (bf16[2,16,256,128]{3,2,1,0:T(8,128)(2,1)}, bf16[2,16,256,128]{3,2,1,0:T(8,128)(2,1)}, u32[]{:S(2)}, u32[]{:S(2)}) collective-permute-start(bf16[2,16,256,128]{3,2,1,0:T(8,128)(2,1)} %pad_maximum_fusion.2), channel_id=1, source_target_pairs={{0,2},{4,6},{8,10},{12,14},{16,18},{20,22},{24,26},{28,30},{1,3},{... | collective-permute-start | bytes 6291464 | tf_op jit(solution)/shard_map/ppermute | solution.py:259
  85.3 39.7 %collective-permute-start.4 = (bf16[2,16,64,128]{3,2,1,0:T(8,128)(2,1)}, bf16[2,16,64,128]{3,2,1,0:T(8,128)(2,1)S(1)}, u32[]{:S(2)}, u32[]{:S(2)}) collective-permute-start(bf16[2,16,64,128]{3,2,1,0:T(8,128)(2,1)} %get-tuple-element.23), channel_id=1, source_target_pairs={{0,16},{2,18},{4,20},{6,22},{8,24},{10,26},{12,28},{14,30},{1,17},... | collective-permute-start | bytes 1572872 | tf_op jit(solution)/shard_map/ppermute | solution.py:20
  89.2 43.6 %collective-permute-start.3 = (bf16[2,16,128,128]{3,2,1,0:T(8,128)(2,1)}, bf16[2,16,128,128]{3,2,1,0:T(8,128)(2,1)S(1)}, u32[]{:S(2)}, u32[]{:S(2)}) collective-permute-start(bf16[2,16,128,128]{3,2,1,0:T(8,128)(2,1)} %pad_maximum_fusion.4), channel_id=1, source_target_pairs={{0,8},{2,10},{4,12},{6,14},{8,16},{10,18},{12,20},{14,22},{16,24},... | collective-permute-start | bytes 3145736 | tf_op jit(solution)/shard_map/ppermute | solution.py:20
  123.5 41.4 %collective-permute-start.6 = (bf16[256,2048]{1,0:T(8,128)(2,1)}, bf16[256,2048]{1,0:T(8,128)(2,1)S(1)}, u32[]{:S(2)}, u32[]{:S(2)}) collective-permute-start(bf16[256,2048]{1,0:T(8,128)(2,1)} %shard_map.61), channel_id=1, source_target_pairs={{0,1},{1,0},{2,3},{3,2},{4,5},{5,4},{6,7},{7,6},{8,9},{9,8},{10,11... | collective-permute-start | bytes 3145736 | tf_op jit(solution)/shard_map/ppermute | solution.py:312
  125.0 7.8 %copy-start.2 = (bf16[2,16,64,128]{3,2,1,0:T(8,128)(2,1)}, bf16[2,16,64,128]{3,2,1,0:T(8,128)(2,1)S(1)}, u32[]{:S(2)}) copy-start(bf16[2,16,64,128]{3,2,1,0:T(8,128)(2,1)S(1)} %collective-permute-done.4.rest_6_.rest_7_) | copy-start | bytes 1572868
  132.8 1.0 copy-start.1
  156.9 25.3 %collective-permute-start.5 = (bf16[256,2048]{1,0:T(8,128)(2,1)}, bf16[256,2048]{1,0:T(8,128)(2,1)S(1)}, u32[]{:S(2)}, u32[]{:S(2)}) collective-permute-start(bf16[256,2048]{1,0:T(8,128)(2,1)} %shard_map.59), channel_id=1, source_target_pairs={{0,1},{1,0},{2,3},{3,2},{4,5},{5,4},{6,7},{7,6},{8,9},{9,8},{10,11... | collective-permute-start | bytes 3145736 | tf_op jit(solution)/shard_map/ppermute | solution.py:312

commit v6 on v5

--- a/solution.py
+++ b/solution.py
@@ -199,7 +199,7 @@
     kv_t = jnp.stack([jnp.transpose(keys, (1, 0, 2)), jnp.transpose(values, (1, 0, 2))])
     prev_kv = from_behind(kv_t, "ctx", 1)
     levels = []
-    far_arrays = []
+    sends = []
     for level in range(1, NOFF):
         offset = 2**level
         if offset >= cycle_size:
@@ -209,16 +209,18 @@
         ]
         local = jnp.clip(target - device * per_dev, 0, per_dev - 1)
         if level == 1:
-            direct = lax.ppermute(
-                pick_blocks(kv_t, local), "ctx",
-                [(s, s + 2) for s in range(0, cycle_size - 2, 2)],
-            )
+            pairs = [(s, s + 2) for s in range(0, cycle_size - 2, 2)]
             nxt = lax.dynamic_slice_in_dim(far_blocks, (device + 1) * per_dev, per_dev, 0)[::2, 1]
             fwd_local = jnp.clip(nxt - (device - 1) * per_dev, 0, per_dev - 1)
-            far_arrays.append((direct, None))
         else:
-            far_arrays.append((from_behind(pick_blocks(kv_t, local), "ctx", offset),))
+            pairs = [(s, s + offset) for s in range(0, cycle_size - offset)]
+        sends.append((pick_blocks(kv_t, local), pairs))
         levels.append(level)
+    q_t, kv_t, *operands = lax.optimization_barrier((q_t, kv_t, *[op for op, _ in sends]))
+    far_arrays = []
+    for (_, pairs), op, level in zip(sends, operands, levels):
+        received = lax.ppermute(op, "ctx", pairs)
+        far_arrays.append((received, None) if level == 1 else (received,))
 
     own = lax.dynamic_slice_in_dim(far_blocks, device * per_dev, per_dev, 0)
     query_index = device * per_dev + jnp.arange(per_dev, dtype=jnp.int32)
@@ -283,21 +285,21 @@
         cost_estimate=cost(WINDOW // 2 + BLOCK, rows, heads * rows * width * (3 * 2 + 2 * 4 + 8)),
     )(meta, used, q_t, prev_kv, prev_kv, acc0, st0)
 
-    att_even = pl.pallas_call(
-        functools.partial(far_kernel, levels, per_dev, width, scale),
-        out_shape=jax.ShapeDtypeStruct((half_rows, heads * width), queries.dtype),
-        grid_spec=pltpu.PrefetchScalarGridSpec(
-            num_scalar_prefetch=2,
-            grid=(heads,),
-            in_specs=[row_spec(rows), row_spec(half_rows), row_spec(half_rows)] + far_specs,
-            out_specs=out_spec(half_rows),
-        ),
-        compiler_params=params,
-        cost_estimate=cost(2 * BLOCK, half_rows, heads * width * (2 * rows + 8 * half_rows + 2 * sum(a.shape[2] for a in far_operands))),
-    )(meta, used, q_t, acc1, st1, *far_operands)
-
     n_head = lax.axis_size("head")
     if n_head != 2:
+        att_even = pl.pallas_call(
+            functools.partial(far_kernel, levels, per_dev, width, scale),
+            out_shape=jax.ShapeDtypeStruct((half_rows, heads * width), queries.dtype),
+            grid_spec=pltpu.PrefetchScalarGridSpec(
+                num_scalar_prefetch=2,
+                grid=(heads,),
+                in_specs=[row_spec(rows), row_spec(half_rows), row_spec(half_rows)] + far_specs,
+                out_specs=out_spec(half_rows),
+            ),
+            compiler_params=params,
+            cost_estimate=cost(2 * BLOCK, half_rows, heads * width * (2 * rows + 8 * half_rows + 2 * sum(a.shape[2] for a in far_operands))),
+        )(meta, used, q_t, acc1, st1, *far_operands)
+
         parts = []
         for att in (att_even, att_odd):
             partial_value = jnp.dot(att, out_weight, preferred_element_type=jnp.float32)
@@ -306,15 +308,29 @@
             ))
     else:
         hidx = lax.axis_index("head")
-        parts = []
-        for att in (att_odd, att_even):
-            p_other = project_half(att, out_weight, 1 - hidx)
-            received = lax.ppermute(p_other, "head", [(0, 1), (1, 0)])
-            p_own = project_half(att, out_weight, hidx)
-            parts.append(
-                (p_own.astype(jnp.float32) + received.astype(jnp.float32)).astype(jnp.bfloat16)
-            )
-        parts = parts[::-1]
+        swap = [(0, 1), (1, 0)]
+        received_odd = lax.ppermute(project_half(att_odd, out_weight, 1 - hidx), "head", swap)
+        own_odd = project_half(att_odd, out_weight, hidx)
+        acc1, st1, own_odd = lax.optimization_barrier((acc1, st1, own_odd))
+        att_even = pl.pallas_call(
+            functools.partial(far_kernel, levels, per_dev, width, scale),
+            out_shape=jax.ShapeDtypeStruct((half_rows, heads * width), queries.dtype),
+            grid_spec=pltpu.PrefetchScalarGridSpec(
+                num_scalar_prefetch=2,
+                grid=(heads,),
+                in_specs=[row_spec(rows), row_spec(half_rows), row_spec(half_rows)] + far_specs,
+                out_specs=out_spec(half_rows),
+            ),
+            compiler_params=params,
+            cost_estimate=cost(2 * BLOCK, half_rows, heads * width * (2 * rows + 8 * half_rows + 2 * sum(a.shape[2] for a in far_operands))),
+        )(meta, used, q_t, acc1, st1, *far_operands)
+
+        received_even = lax.ppermute(project_half(att_even, out_weight, 1 - hidx), "head", swap)
+        own_even = project_half(att_even, out_weight, hidx)
+        parts = [
+            (own.astype(jnp.float32) + got.astype(jnp.float32)).astype(jnp.bfloat16)
+            for own, got in ((own_even, received_even), (own_odd, received_odd))
+        ]
     even, odd = (p.reshape(per_dev // 2, BLOCK, -1) for p in parts)
     return jnp.stack([even, odd], axis=1).reshape(rows, -1)
 

time: 187 us -> 186 us (level)
  the two profiles are of different devices: /device:TPU:16 before, /device:TPU:28 now
where the time goes in v6:
time: 186 us; the launch traced here: 182 us
  Pallas kernels  82.9 us (45%)
  waiting for transfers between devices  51.5 us (28%)
  local copies, waits for them, and re-layouts  15.6 us (8%)
  other arithmetic  13.6 us (7%)
  starting transfers between devices  11.4 us (6%)
  between operations  7.12 us (4%)
    ppermute x1, waiting for transfers between devices, from_behind(): lax.ppermute(value, axis, [(source, source + steps) for source in range(i...  33.2 us
    pallas_call x4, Pallas kernels, project_half(): pl.pallas_call(matmul_kernel, out_shape=jax.ShapeDtypeStruct((rows, cw),...  26.5 us
    pallas_call x1, Pallas kernels, per_device(): pl.pallas_call(functools.partial(prev_kernel, per_dev, width, scale), out...  22.7 us
    pallas_call x1, Pallas kernels, per_device(): pl.pallas_call(functools.partial(own_kernel, per_dev, width, scale), out_...  17.2 us
    pallas_call x1, Pallas kernels, per_device(): pl.pallas_call(functools.partial(far_kernel, levels, per_dev, width, scal...  16.5 us
    ppermute x1, waiting for transfers between devices, per_device(): lax.ppermute(project_half(att_even, out_weight, 1 - hidx), 'head', swap)  12.4 us
    ppermute x3, waiting for transfers between devices, per_device(): received = lax.ppermute(op, 'ctx', pairs)  5.9 us
    unnamed x13, local copies, waits for them, and re-layouts  5.65 us
  transfers between devices with their start and end apart: 7, of which 3 were waited for; matrix products, arithmetic and copies ran while one was open for 10% of the time, Pallas kernels for 46%

profile of v6, /device:TPU:28, one launch (start us, length us, event | category | flops | bytes accessed | tf_op | source)
XLA Modules:
  0.0 182.2 jit_solution(3217202320983064613)
XLA Ops:
  0.0 3.3 %copy_bitcast_fusion = (bf16[1,16,512,128]{3,2,1,0:T(8,128)(2,1)S(1)}, bf16[1,16,512,128]{3,2,1,0:T(8,128)(2,1)S(1)}) fusion(bf16[512,16,128]{2,1,0:T(8,128)(2,1)} %param.7, bf16[512,16,128]{2,1,0:T(8,128)(2,1)} %param.6), kind=kLoop, calls=%fused_computation.18 | loop fusion | bytes 8388608 | tf_op jit(solution)/shard_map/stack | solution.py:199
  3.3 2.6 %pad_maximum_fusion.k_ref.v_ref = bf16[2,16,512,128]{3,2,1,0:T(8,128)(2,1)} fusion(bf16[1,16,512,128]{3,2,1,0:T(8,128)(2,1)S(1)} %get-tuple-element.65, bf16[1,16,512,128]{3,2,1,0:T(8,128)(2,1)S(1)} %get-tuple-element.66), kind=kLoop, calls=%fused_computation.7 | loop fusion | flops 2097152 | bytes 8388608 | tf_op jit(solution)/shard_map/stack | solution.py:199
  6.0 1.9 %collective-permute-start = (bf16[2,16,512,128]{3,2,1,0:T(8,128)(2,1)}, bf16[2,16,512,128]{3,2,1,0:T(8,128)(2,1)}, u32[]{:S(2)}, u32[]{:S(2)}) collective-permute-start(bf16[2,16,512,128]{3,2,1,0:T(8,128)(2,1)} %pad_maximum_fusion.k_ref.v_ref), channel_id=1, source_target_pairs={{0,2},{2,4},{4,6},{6,8},{8,10},{10,12},{12,14},{14,16},{16,18},{18... | collective-permute-start | bytes 12582920 | tf_op jit(solution)/shard_map/ppermute | solution.py:20
  14.4 3.5 %copy.14 = bf16[512,16,128]{2,0,1:T(8,128)(2,1)} copy(bf16[512,16,128]{2,1,0:T(8,128)(2,1)} %param.5) | data formatting | bytes 4194304 | tf_op args[0]
  19.5 1.6 fusion.6
  22.2 1.5 pad_maximum_fusion.1
  28.2 17.2 %shard_map.55 = (f32[16,512,128]{2,1,0:T(8,128)}, f32[16,512,128]{2,1,0:T(8,128)}) custom-call(bf16[16,512,128]{2,1,0:T(8,128)(2,1)} %bitcast.33, bf16[2,16,512,128]{3,2,1,0:T(8,128)(2,1)} %pad_maximum_fusion.k_ref.v_ref, bf16[2,16,512,128]{3,2,1,0:T(8,128)(2,1)} %pad_maximum_fusion.k_ref.v_ref), custom_call_target="tpu_custom_call" | custom-call | flops 1073741824 | bytes 29360128 | tf_op jit(solution)/shard_map/pallas_call | solution.py:249
  45.4 33.2 %collective-permute-done.kp_ref.vp_ref = bf16[2,16,512,128]{3,2,1,0:T(8,128)(2,1)} collective-permute-done((bf16[2,16,512,128]{3,2,1,0:T(8,128)(2,1)}, bf16[2,16,512,128]{3,2,1,0:T(8,128)(2,1)}, u32[]{:S(2)}, u32[]{:S(2)}) %collective-permute-start) | collective-permute-done | bytes 4194336 | tf_op jit(solution)/shard_map/ppermute | solution.py:20
  78.6 1.7 constant_dynamic-slice_fusion.3
  80.3 1.6 pad_maximum_fusion.2
  81.8 2.6 %collective-permute-start.2 = (bf16[2,16,256,128]{3,2,1,0:T(8,128)(2,1)}, bf16[2,16,256,128]{3,2,1,0:T(8,128)(2,1)}, u32[]{:S(2)}, u32[]{:S(2)}) collective-permute-start(bf16[2,16,256,128]{3,2,1,0:T(8,128)(2,1)} %pad_maximum_fusion.2), channel_id=1, source_target_pairs={{0,2},{4,6},{8,10},{12,14},{16,18},{20,22},{24,26},{28,30},{1,3},{... | collective-permute-start | bytes 6291464 | tf_op jit(solution)/shard_map/ppermute | solution.py:261
  88.5 22.7 %shard_map.56 = (bf16[256,2048]{1,0:T(8,128)(2,1)}, f32[16,256,128]{2,1,0:T(8,128)}, f32[16,256,128]{2,1,0:T(8,128)}) custom-call(s32[10]{0:T(128)} %pad_add_fusion.meta_ref, s32[40]{0:T(128)} %reshape.110.used_ref, bf16[16,512,128]{2,1,0:T(8,128)(2,1)} %bitcast.34, bf16[2,16,512,128]{3,2,1,0:T(8,128)(2,1)} %collective-permute-done.kp_ref.vp_ref, ...), custom_call_target="tpu_custom_call" | custom-call | flops 1342177280 | bytes 23068672 | tf_op jit(solution)/shard_map/pallas_call | solution.py:271
  111.3 6.6 %shard_map.61 = bf16[256,2048]{1,0:T(8,128)(2,1)} custom-call(s32[1]{0:T(128)} %bitcast.22.sel_ref, bf16[256,2048]{1,0:T(8,128)(2,1)} %get-tuple-element.30.a_ref, bf16[2048,4096]{1,0:T(8,128)(2,1)} %w_ref.7), custom_call_target="tpu_custom_call" | custom-call | flops 2147483648 | bytes 10485760 | tf_op jit(solution)/shard_map/pallas_call | solution.py:164
  117.9 1.5 collective-permute-start.6
  119.4 6.6 %shard_map.57 = bf16[256,2048]{1,0:T(8,128)(2,1)} custom-call(s32[1]{0:T(128)} %bitcast.sel_ref, bf16[256,2048]{1,0:T(8,128)(2,1)} %get-tuple-element.30.a_ref, bf16[2048,4096]{1,0:T(8,128)(2,1)} %w_ref.7), custom_call_target="tpu_custom_call" | custom-call | flops 2147483648 | bytes 10485760 | tf_op jit(solution)/shard_map/pallas_call | solution.py:164
  126.0 5.9 %collective-permute-done.4.rest_6_.rest_7_ = bf16[2,16,64,128]{3,2,1,0:T(8,128)(2,1)} collective-permute-done((bf16[2,16,64,128]{3,2,1,0:T(8,128)(2,1)}, bf16[2,16,64,128]{3,2,1,0:T(8,128)(2,1)}, u32[]{:S(2)}, u32[]{:S(2)}) %collective-permute-start.4) | collective-permute-done | bytes 524320 | tf_op jit(solution)/shard_map/ppermute | solution.py:222
  133.5 16.5 %shard_map.58.a_ref = bf16[256,2048]{1,0:T(8,128)(2,1)} custom-call(s32[10]{0:T(128)} %pad_add_fusion.meta_ref, s32[40]{0:T(128)} %reshape.110.used_ref, bf16[16,512,128]{2,1,0:T(8,128)(2,1)} %bitcast.35, f32[16,256,128]{2,1,0:T(8,128)} %get-tuple-element.31.acc_ref, f32[16,256,128]{2,1,0:T(8,128)} %get-tuple-element.32.st_ref, ...), custom_call_target="tpu_custom_call" | custom-call | flops 268435456 | bytes 12058624 | tf_op jit(solution)/shard_map/pallas_call | solution.py:315
  150.1 6.7 %shard_map.60 = bf16[256,2048]{1,0:T(8,128)(2,1)} custom-call(s32[1]{0:T(128)} %bitcast.22.sel_ref, bf16[256,2048]{1,0:T(8,128)(2,1)} %shard_map.58.a_ref, bf16[2048,4096]{1,0:T(8,128)(2,1)} %w_ref.7), custom_call_target="tpu_custom_call" | custom-call | flops 2147483648 | bytes 10485760 | tf_op jit(solution)/shard_map/pallas_call | solution.py:164
  156.8 1.5 collective-permute-start.5
  158.3 1.6 add_convert_fusion
  159.9 6.6 %shard_map.59 = bf16[256,2048]{1,0:T(8,128)(2,1)} custom-call(s32[1]{0:T(128)} %bitcast.sel_ref, bf16[256,2048]{1,0:T(8,128)(2,1)} %shard_map.58.a_ref, bf16[2048,4096]{1,0:T(8,128)(2,1)} %w_ref.7), custom_call_target="tpu_custom_call" | custom-call | flops 2147483648 | bytes 10485760 | tf_op jit(solution)/shard_map/pallas_call | solution.py:164
  166.5 12.4 %collective-permute-done.5 = bf16[256,2048]{1,0:T(8,128)(2,1)S(1)} collective-permute-done((bf16[256,2048]{1,0:T(8,128)(2,1)}, bf16[256,2048]{1,0:T(8,128)(2,1)S(1)}, u32[]{:S(2)}, u32[]{:S(2)}) %collective-permute-start.5) | collective-permute-done | bytes 1048608 | tf_op jit(solution)/shard_map/ppermute | solution.py:328
  178.9 1.6 add_convert_fusion.1
  180.7 1.5 copy.10
  (38 shorter events, 12.7 us)
Async XLA Ops:
  3.3 2.7 %copy-start = (bf16[1,16,512,128]{3,2,1,0:T(8,128)(2,1)}, bf16[1,16,512,128]{3,2,1,0:T(8,128)(2,1)S(1)}, u32[]{:S(2)}) copy-start(bf16[1,16,512,128]{3,2,1,0:T(8,128)(2,1)S(1)} %get-tuple-element.66) | copy-start | bytes 6291460
  3.3 4.6 %copy-start.5 = (s32[128,5]{0,1:T(8,128)S(1)}, s32[128,5]{0,1:T(8,128)}, u32[]{:S(2)}) copy-start(s32[128,5]{0,1:T(8,128)} %param.8) | copy-start | bytes 7684
  6.0 72.6 %collective-permute-start = (bf16[2,16,512,128]{3,2,1,0:T(8,128)(2,1)}, bf16[2,16,512,128]{3,2,1,0:T(8,128)(2,1)}, u32[]{:S(2)}, u32[]{:S(2)}) collective-permute-start(bf16[2,16,512,128]{3,2,1,0:T(8,128)(2,1)} %pad_maximum_fusion.k_ref.v_ref), channel_id=1, source_target_pairs={{0,2},{2,4},{4,6},{6,8},{8,10},{10,12},{12,14},{14,16},{16,18},{18... | collective-permute-start | bytes 12582920 | tf_op jit(solution)/shard_map/ppermute | solution.py:20
  17.9 1.7 copy-start.1
  23.7 108.2 %collective-permute-start.1 = (bf16[2,16,256,128]{3,2,1,0:T(8,128)(2,1)}, bf16[2,16,256,128]{3,2,1,0:T(8,128)(2,1)S(1)}, u32[]{:S(2)}, u32[]{:S(2)}) collective-permute-start(bf16[2,16,256,128]{3,2,1,0:T(8,128)(2,1)} %pad_maximum_fusion.1), channel_id=1, source_target_pairs={{0,4},{4,8},{8,12},{12,16},{16,20},{20,24},{24,28},{1,5},{5,9},{9,... | collective-permute-start | bytes 6291464 | tf_op jit(solution)/shard_map/ppermute | solution.py:222
  81.8 50.1 %collective-permute-start.2 = (bf16[2,16,256,128]{3,2,1,0:T(8,128)(2,1)}, bf16[2,16,256,128]{3,2,1,0:T(8,128)(2,1)}, u32[]{:S(2)}, u32[]{:S(2)}) collective-permute-start(bf16[2,16,256,128]{3,2,1,0:T(8,128)(2,1)} %pad_maximum_fusion.2), channel_id=1, source_target_pairs={{0,2},{4,6},{8,10},{12,14},{16,18},{20,22},{24,26},{28,30},{1,3},{... | collective-permute-start | bytes 6291464 | tf_op jit(solution)/shard_map/ppermute | solution.py:261
  84.5 47.4 %collective-permute-start.3 = (bf16[2,16,128,128]{3,2,1,0:T(8,128)(2,1)}, bf16[2,16,128,128]{3,2,1,0:T(8,128)(2,1)S(1)}, u32[]{:S(2)}, u32[]{:S(2)}) collective-permute-start(bf16[2,16,128,128]{3,2,1,0:T(8,128)(2,1)} %pad_maximum_fusion.4), channel_id=1, source_target_pairs={{0,8},{2,10},{4,12},{6,14},{8,16},{10,18},{12,20},{14,22},{16,24},... | collective-permute-start | bytes 3145736 | tf_op jit(solution)/shard_map/ppermute | solution.py:222
  85.7 46.2 %collective-permute-start.4 = (bf16[2,16,64,128]{3,2,1,0:T(8,128)(2,1)}, bf16[2,16,64,128]{3,2,1,0:T(8,128)(2,1)}, u32[]{:S(2)}, u32[]{:S(2)}) collective-permute-start(bf16[2,16,64,128]{3,2,1,0:T(8,128)(2,1)} %get-tuple-element.35), channel_id=1, source_target_pairs={{0,16},{2,18},{4,20},{6,22},{8,24},{10,26},{12,28},{14,30},{1,17},... | collective-permute-start | bytes 1572872 | tf_op jit(solution)/shard_map/ppermute | solution.py:222
  117.9 40.4 %collective-permute-start.6 = (bf16[256,2048]{1,0:T(8,128)(2,1)}, bf16[256,2048]{1,0:T(8,128)(2,1)}, u32[]{:S(2)}, u32[]{:S(2)}) collective-permute-start(bf16[256,2048]{1,0:T(8,128)(2,1)} %shard_map.61), channel_id=1, source_target_pairs={{0,1},{1,0},{2,3},{3,2},{4,5},{5,4},{6,7},{7,6},{8,9},{9,8},{10,11... | collective-permute-start | bytes 3145736 | tf_op jit(solution)/shard_map/ppermute | solution.py:312
  131.9 1.0 copy-start.3
  131.9 1.6 copy-start.2
  150.1 8.2 %copy-start.4 = (bf16[256,2048]{1,0:T(8,128)(2,1)S(1)}, bf16[256,2048]{1,0:T(8,128)(2,1)}, u32[]{:S(2)}) copy-start(bf16[256,2048]{1,0:T(8,128)(2,1)} %shard_map.57) | copy-start | bytes 3145732
  156.8 22.2 %collective-permute-start.5 = (bf16[256,2048]{1,0:T(8,128)(2,1)}, bf16[256,2048]{1,0:T(8,128)(2,1)S(1)}, u32[]{:S(2)}, u32[]{:S(2)}) collective-permute-start(bf16[256,2048]{1,0:T(8,128)(2,1)} %shard_map.60), channel_id=1, source_target_pairs={{0,1},{1,0},{2,3},{3,2},{4,5},{5,4},{6,7},{7,6},{8,9},{9,8},{10,11... | collective-permute-start | bytes 3145736 | tf_op jit(solution)/shard_map/ppermute | solution.py:328

commit v7 on v6

--- a/solution.py
+++ b/solution.py
@@ -11,7 +11,7 @@
 BLOCK = 64
 WINDOW = 512
 NOFF = 5
-HEADS_PER_STEP = 1
+HEADS_PER_STEP = 4
 
 
 def from_behind(value, axis, steps):
@@ -54,6 +54,41 @@
 TILE = 256
 
 
+class HeadView:
+    def __init__(self, ref, head, width=None):
+        self.ref, self.head, self.width = ref, head, width
+
+    def _index(self, idx):
+        if idx is Ellipsis:
+            idx = (slice(None), slice(None))
+        if self.width is None:
+            return (self.head,) + tuple(idx)
+        return (idx[0], pl.ds(self.head * self.width, self.width))
+
+    @property
+    def dtype(self):
+        return self.ref.dtype
+
+    def __getitem__(self, idx):
+        return self.ref[self._index(idx)]
+
+    def __setitem__(self, idx, value):
+        self.ref[self._index(idx)] = value
+
+
+def per_head(body, n_prefetch, n_head_major, n_rows_out, width, heads_per_step):
+    def kernel(*refs):
+        pre = refs[:n_prefetch]
+        rest = refs[n_prefetch:]
+        n_major = len(rest) - n_rows_out
+        for hh in range(heads_per_step):
+            views = [HeadView(r, hh) for r in rest[:n_major]]
+            outs = [HeadView(r, hh, width) for r in rest[n_major:]]
+            body(*pre, *views, *outs)
+
+    return kernel
+
+
 def own_kernel(per_dev, width, scale, q_ref, k_ref, v_ref, acc_ref, st_ref):
     neg = jnp.float32(-jnp.inf)
     rows = per_dev * BLOCK
@@ -78,7 +113,7 @@
 
 
 def prev_kernel(per_dev, width, scale, meta_ref, used_ref, q_ref, kp_ref, vp_ref, acc_ref, st_ref,
-                odd_ref, acc_out, st_out):
+                acc_out, st_out, odd_ref):
     prev_ok = meta_ref[0] > 0
     neg = jnp.float32(-jnp.inf)
     rows = per_dev * BLOCK
@@ -230,10 +265,11 @@
         [(device > 0).astype(jnp.int32)[None], pick.astype(jnp.int32), (device % 2)[None]]
     )
 
-    row_spec = lambda n: pl.BlockSpec((None, n, width), lambda h, *_: (h, 0, 0))
-    out_spec = lambda n: pl.BlockSpec((n, width), lambda h, *_: (0, h))
-    k_spec = lambda n: pl.BlockSpec((None, None, n, width), lambda h, *_: (0, h, 0, 0))
-    v_spec = lambda n: pl.BlockSpec((None, None, n, width), lambda h, *_: (1, h, 0, 0))
+    hb = math.gcd(heads, HEADS_PER_STEP)
+    row_spec = lambda n: pl.BlockSpec((hb, n, width), lambda h, *_: (h, 0, 0))
+    out_spec = lambda n: pl.BlockSpec((n, hb * width), lambda h, *_: (0, h))
+    k_spec = lambda n: pl.BlockSpec((None, hb, n, width), lambda h, *_: (0, h, 0, 0))
+    v_spec = lambda n: pl.BlockSpec((None, hb, n, width), lambda h, *_: (1, h, 0, 0))
     half_rows = rows // 2
     f32 = jnp.float32
     params = pltpu.CompilerParams(dimension_semantics=("arbitrary",))
@@ -247,9 +283,9 @@
         )
 
     acc0, st0 = pl.pallas_call(
-        functools.partial(own_kernel, per_dev, width, scale),
+        per_head(functools.partial(own_kernel, per_dev, width, scale), 0, 5, 0, width, hb),
         out_shape=(state(rows), state(rows)),
-        grid=(heads,),
+        grid=(heads // hb,),
         in_specs=[row_spec(rows), k_spec(rows), v_spec(rows)],
         out_specs=(row_spec(rows), row_spec(rows)),
         compiler_params=params,
@@ -268,18 +304,18 @@
         for a in group:
             far_specs += [k_spec(a.shape[2]), v_spec(a.shape[2])]
             far_operands += [a, a]
-    att_odd, acc1, st1 = pl.pallas_call(
-        functools.partial(prev_kernel, per_dev, width, scale),
+    acc1, st1, att_odd = pl.pallas_call(
+        per_head(functools.partial(prev_kernel, per_dev, width, scale), 2, 7, 1, width, hb),
         out_shape=(
-            jax.ShapeDtypeStruct((half_rows, heads * width), queries.dtype),
             state(half_rows),
             state(half_rows),
+            jax.ShapeDtypeStruct((half_rows, heads * width), queries.dtype),
         ),
         grid_spec=pltpu.PrefetchScalarGridSpec(
             num_scalar_prefetch=2,
-            grid=(heads,),
+            grid=(heads // hb,),
             in_specs=[row_spec(rows), k_spec(rows), v_spec(rows), row_spec(rows), row_spec(rows)],
-            out_specs=(out_spec(half_rows), row_spec(half_rows), row_spec(half_rows)),
+            out_specs=(row_spec(half_rows), row_spec(half_rows), out_spec(half_rows)),
         ),
         compiler_params=params,
         cost_estimate=cost(WINDOW // 2 + BLOCK, rows, heads * rows * width * (3 * 2 + 2 * 4 + 8)),
@@ -288,11 +324,11 @@
     n_head = lax.axis_size("head")
     if n_head != 2:
         att_even = pl.pallas_call(
-            functools.partial(far_kernel, levels, per_dev, width, scale),
+            per_head(functools.partial(far_kernel, levels, per_dev, width, scale), 2, 0, 1, width, hb),
             out_shape=jax.ShapeDtypeStruct((half_rows, heads * width), queries.dtype),
             grid_spec=pltpu.PrefetchScalarGridSpec(
                 num_scalar_prefetch=2,
-                grid=(heads,),
+                grid=(heads // hb,),
                 in_specs=[row_spec(rows), row_spec(half_rows), row_spec(half_rows)] + far_specs,
                 out_specs=out_spec(half_rows),
             ),
@@ -313,11 +349,11 @@
         own_odd = project_half(att_odd, out_weight, hidx)
         acc1, st1, own_odd = lax.optimization_barrier((acc1, st1, own_odd))
         att_even = pl.pallas_call(
-            functools.partial(far_kernel, levels, per_dev, width, scale),
+            per_head(functools.partial(far_kernel, levels, per_dev, width, scale), 2, 0, 1, width, hb),
             out_shape=jax.ShapeDtypeStruct((half_rows, heads * width), queries.dtype),
             grid_spec=pltpu.PrefetchScalarGridSpec(
                 num_scalar_prefetch=2,
-                grid=(heads,),
+                grid=(heads // hb,),
                 in_specs=[row_spec(rows), row_spec(half_rows), row_spec(half_rows)] + far_specs,
                 out_specs=out_spec(half_rows),
             ),

time: 186 us -> 177 us (0.952); the launches traced: 182 us -> 176 us
  Pallas kernels: 82.9 us -> 70.3 us
  waiting for transfers between devices: 51.5 us -> 58.1 us
    pallas_call x3, Pallas kernels: 56.4 us -> 43.8 us  [the longest x1 20.1 us: per_device(): pl.pallas_call(per_head(functools.partial(prev_kernel, per_dev, width, sc...]
    ppermute x1, waiting for transfers between devices: 33.2 us -> 37.3 us  [from_behind(): lax.ppermute(value, axis, [(source, source + steps) for source in range(i...]
    ppermute x3, waiting for transfers between devices: 5.9 us -> 8.34 us  [per_device(): received = lax.ppermute(op, 'ctx', pairs)]
  transfers between devices with their start and end apart: 7 -> 7, of which waited for: 3 -> 3; matrix products, arithmetic and copies ran while one was open for 10% -> 10% of each run, Pallas kernels for 46% -> 40%
where the time goes in v7:
time: 177 us; the launch traced here: 176 us
  Pallas kernels  70.3 us (40%)
  waiting for transfers between devices  58.1 us (33%)
  local copies, waits for them, and re-layouts  15.6 us (9%)
  other arithmetic  13.6 us (8%)
  starting transfers between devices  11.6 us (7%)
  between operations  7.12 us (4%)
    ppermute x1, waiting for transfers between devices, from_behind(): lax.ppermute(value, axis, [(source, source + steps) for source in range(i...  37.3 us
    pallas_call x4, Pallas kernels, project_half(): pl.pallas_call(matmul_kernel, out_shape=jax.ShapeDtypeStruct((rows, cw),...  26.5 us
    pallas_call x1, Pallas kernels, per_device(): pl.pallas_call(per_head(functools.partial(prev_kernel, per_dev, width, sc...  20.1 us
    pallas_call x1, Pallas kernels, per_device(): pl.pallas_call(per_head(functools.partial(own_kernel, per_dev, width, sca...  13.1 us
    ppermute x1, waiting for transfers between devices, per_device(): lax.ppermute(project_half(att_even, out_weight, 1 - hidx), 'head', swap)  12.5 us
    pallas_call x1, Pallas kernels, per_device(): pl.pallas_call(per_head(functools.partial(far_kernel, levels, per_dev, wi...  10.6 us
    ppermute x3, waiting for transfers between devices, per_device(): received = lax.ppermute(op, 'ctx', pairs)  8.34 us
    unnamed x13, local copies, waits for them, and re-layouts  5.65 us
  transfers between devices with their start and end apart: 7, of which 3 were waited for; matrix products, arithmetic and copies ran while one was open for 10% of the time, Pallas kernels for 40%

profile of v7, /device:TPU:28, one launch (start us, length us, event | category | flops | bytes accessed | tf_op | source)
XLA Modules:
  0.0 176.4 jit_solution(16656576671688841352)
XLA Ops:
  0.0 3.3 %copy_bitcast_fusion = (bf16[1,16,512,128]{3,2,1,0:T(8,128)(2,1)S(1)}, bf16[1,16,512,128]{3,2,1,0:T(8,128)(2,1)S(1)}) fusion(bf16[512,16,128]{2,1,0:T(8,128)(2,1)} %param.7, bf16[512,16,128]{2,1,0:T(8,128)(2,1)} %param.6), kind=kLoop, calls=%fused_computation.18 | loop fusion | bytes 8388608 | tf_op jit(solution)/shard_map/stack | solution.py:234
  3.3 2.6 %pad_maximum_fusion.refs_1_.refs_2_ = bf16[2,16,512,128]{3,2,1,0:T(8,128)(2,1)} fusion(bf16[1,16,512,128]{3,2,1,0:T(8,128)(2,1)S(1)} %get-tuple-element.65, bf16[1,16,512,128]{3,2,1,0:T(8,128)(2,1)S(1)} %get-tuple-element.66), kind=kLoop, calls=%fused_computation.7 | loop fusion | flops 2097152 | bytes 8388608 | tf_op jit(solution)/shard_map/stack | solution.py:234
  6.0 1.9 %collective-permute-start = (bf16[2,16,512,128]{3,2,1,0:T(8,128)(2,1)}, bf16[2,16,512,128]{3,2,1,0:T(8,128)(2,1)}, u32[]{:S(2)}, u32[]{:S(2)}) collective-permute-start(bf16[2,16,512,128]{3,2,1,0:T(8,128)(2,1)} %pad_maximum_fusion.refs_1_.refs_2_), channel_id=1, source_target_pairs={{0,2},{2,4},{4,6},{6,8},{8,10},{10,12},{12,14},{14,16},{16,18},{18... | collective-permute-start | bytes 12582920 | tf_op jit(solution)/shard_map/ppermute | solution.py:20
  14.4 3.5 %copy.14 = bf16[512,16,128]{2,0,1:T(8,128)(2,1)} copy(bf16[512,16,128]{2,1,0:T(8,128)(2,1)} %param.5) | data formatting | bytes 4194304 | tf_op args[0]
  19.5 1.6 fusion.6
  22.2 1.5 pad_maximum_fusion.1
  28.2 13.1 %shard_map.55 = (f32[16,512,128]{2,1,0:T(8,128)}, f32[16,512,128]{2,1,0:T(8,128)}) custom-call(bf16[16,512,128]{2,1,0:T(8,128)(2,1)} %bitcast.33, bf16[2,16,512,128]{3,2,1,0:T(8,128)(2,1)} %pad_maximum_fusion.refs_1_.refs_2_, bf16[2,16,512,128]{3,2,1,0:T(8,128)(2,1)} %pad_maximum_fusion.refs_1_.refs_2_), custom_call_target="tpu_custom_call" | custom-call | flops 1073741824 | bytes 29360128 | tf_op jit(solution)/shard_map/pallas_call | solution.py:285
  41.3 37.3 %collective-permute-done.refs_3_.refs_4_ = bf16[2,16,512,128]{3,2,1,0:T(8,128)(2,1)} collective-permute-done((bf16[2,16,512,128]{3,2,1,0:T(8,128)(2,1)}, bf16[2,16,512,128]{3,2,1,0:T(8,128)(2,1)}, u32[]{:S(2)}, u32[]{:S(2)}) %collective-permute-start) | collective-permute-done | bytes 4194336 | tf_op jit(solution)/shard_map/ppermute | solution.py:20
  78.6 1.7 constant_dynamic-slice_fusion.3
  80.3 1.6 pad_maximum_fusion.2
  81.8 2.6 %collective-permute-start.2 = (bf16[2,16,256,128]{3,2,1,0:T(8,128)(2,1)}, bf16[2,16,256,128]{3,2,1,0:T(8,128)(2,1)}, u32[]{:S(2)}, u32[]{:S(2)}) collective-permute-start(bf16[2,16,256,128]{3,2,1,0:T(8,128)(2,1)} %pad_maximum_fusion.2), channel_id=1, source_target_pairs={{0,2},{4,6},{8,10},{12,14},{16,18},{20,22},{24,26},{28,30},{1,3},{... | collective-permute-start | bytes 6291464 | tf_op jit(solution)/shard_map/ppermute | solution.py:297
  85.8 1.5 collective-permute-start.4
  88.7 20.1 %shard_map.56 = (f32[16,256,128]{2,1,0:T(8,128)}, f32[16,256,128]{2,1,0:T(8,128)}, bf16[256,2048]{1,0:T(8,128)(2,1)}) custom-call(s32[10]{0:T(128)} %pad_add_fusion.refs_0_, s32[40]{0:T(128)} %reshape.110.refs_1_, bf16[16,512,128]{2,1,0:T(8,128)(2,1)} %bitcast.34, bf16[2,16,512,128]{3,2,1,0:T(8,128)(2,1)} %collective-permute-done.refs_3_.refs_4_, ...), custom_call_target="tpu_custom_call" | custom-call | flops 1342177280 | bytes 23068672 | tf_op jit(solution)/shard_map/pallas_call | solution.py:307
  108.9 6.6 %shard_map.61 = bf16[256,2048]{1,0:T(8,128)(2,1)} custom-call(s32[1]{0:T(128)} %bitcast.22.sel_ref, bf16[256,2048]{1,0:T(8,128)(2,1)} %get-tuple-element.30.a_ref, bf16[2048,4096]{1,0:T(8,128)(2,1)} %w_ref.7), custom_call_target="tpu_custom_call" | custom-call | flops 2147483648 | bytes 10485760 | tf_op jit(solution)/shard_map/pallas_call | solution.py:199
  115.5 1.5 collective-permute-start.6
  116.9 6.6 %shard_map.57 = bf16[256,2048]{1,0:T(8,128)(2,1)} custom-call(s32[1]{0:T(128)} %bitcast.sel_ref, bf16[256,2048]{1,0:T(8,128)(2,1)} %get-tuple-element.30.a_ref, bf16[2048,4096]{1,0:T(8,128)(2,1)} %w_ref.7), custom_call_target="tpu_custom_call" | custom-call | flops 2147483648 | bytes 10485760 | tf_op jit(solution)/shard_map/pallas_call | solution.py:199
  123.6 8.3 %collective-permute-done.4.refs_11_.refs_12_ = bf16[2,16,64,128]{3,2,1,0:T(8,128)(2,1)} collective-permute-done((bf16[2,16,64,128]{3,2,1,0:T(8,128)(2,1)}, bf16[2,16,64,128]{3,2,1,0:T(8,128)(2,1)}, u32[]{:S(2)}, u32[]{:S(2)}) %collective-permute-start.4) | collective-permute-done | bytes 524320 | tf_op jit(solution)/shard_map/ppermute | solution.py:257
  133.6 10.6 %shard_map.58.a_ref = bf16[256,2048]{1,0:T(8,128)(2,1)} custom-call(s32[10]{0:T(128)} %pad_add_fusion.refs_0_, s32[40]{0:T(128)} %reshape.110.refs_1_, bf16[16,512,128]{2,1,0:T(8,128)(2,1)} %bitcast.35, f32[16,256,128]{2,1,0:T(8,128)} %get-tuple-element.31.refs_3_, f32[16,256,128]{2,1,0:T(8,128)} %get-tuple-element.32.refs_4_, ...), custom_call_target="tpu_custom_call" | custom-call | flops 268435456 | bytes 12058624 | tf_op jit(solution)/shard_map/pallas_call | solution.py:351
  144.1 6.7 %shard_map.60 = bf16[256,2048]{1,0:T(8,128)(2,1)} custom-call(s32[1]{0:T(128)} %bitcast.22.sel_ref, bf16[256,2048]{1,0:T(8,128)(2,1)} %shard_map.58.a_ref, bf16[2048,4096]{1,0:T(8,128)(2,1)} %w_ref.7), custom_call_target="tpu_custom_call" | custom-call | flops 2147483648 | bytes 10485760 | tf_op jit(solution)/shard_map/pallas_call | solution.py:199
  150.8 1.5 collective-permute-start.5
  152.3 1.6 add_convert_fusion
  153.9 6.6 %shard_map.59 = bf16[256,2048]{1,0:T(8,128)(2,1)} custom-call(s32[1]{0:T(128)} %bitcast.sel_ref, bf16[256,2048]{1,0:T(8,128)(2,1)} %shard_map.58.a_ref, bf16[2048,4096]{1,0:T(8,128)(2,1)} %w_ref.7), custom_call_target="tpu_custom_call" | custom-call | flops 2147483648 | bytes 10485760 | tf_op jit(solution)/shard_map/pallas_call | solution.py:199
  160.6 12.5 %collective-permute-done.5 = bf16[256,2048]{1,0:T(8,128)(2,1)S(1)} collective-permute-done((bf16[256,2048]{1,0:T(8,128)(2,1)}, bf16[256,2048]{1,0:T(8,128)(2,1)S(1)}, u32[]{:S(2)}, u32[]{:S(2)}) %collective-permute-start.5) | collective-permute-done | bytes 1048608 | tf_op jit(solution)/shard_map/ppermute | solution.py:364
  173.1 1.6 add_convert_fusion.1
  (38 shorter events, 12.9 us)
Async XLA Ops:
  3.3 2.7 %copy-start = (bf16[1,16,512,128]{3,2,1,0:T(8,128)(2,1)}, bf16[1,16,512,128]{3,2,1,0:T(8,128)(2,1)S(1)}, u32[]{:S(2)}) copy-start(bf16[1,16,512,128]{3,2,1,0:T(8,128)(2,1)S(1)} %get-tuple-element.66) | copy-start | bytes 6291460
  3.3 4.6 %copy-start.5 = (s32[128,5]{0,1:T(8,128)S(1)}, s32[128,5]{0,1:T(8,128)}, u32[]{:S(2)}) copy-start(s32[128,5]{0,1:T(8,128)} %param.8) | copy-start | bytes 7684
  6.0 72.6 %collective-permute-start = (bf16[2,16,512,128]{3,2,1,0:T(8,128)(2,1)}, bf16[2,16,512,128]{3,2,1,0:T(8,128)(2,1)}, u32[]{:S(2)}, u32[]{:S(2)}) collective-permute-start(bf16[2,16,512,128]{3,2,1,0:T(8,128)(2,1)} %pad_maximum_fusion.refs_1_.refs_2_), channel_id=1, source_target_pairs={{0,2},{2,4},{4,6},{6,8},{8,10},{10,12},{12,14},{14,16},{16,18},{18... | collective-permute-start | bytes 12582920 | tf_op jit(solution)/shard_map/ppermute | solution.py:20
  17.9 1.7 copy-start.1
  23.7 108.2 %collective-permute-start.1 = (bf16[2,16,256,128]{3,2,1,0:T(8,128)(2,1)}, bf16[2,16,256,128]{3,2,1,0:T(8,128)(2,1)S(1)}, u32[]{:S(2)}, u32[]{:S(2)}) collective-permute-start(bf16[2,16,256,128]{3,2,1,0:T(8,128)(2,1)} %pad_maximum_fusion.1), channel_id=1, source_target_pairs={{0,4},{4,8},{8,12},{12,16},{16,20},{20,24},{24,28},{1,5},{5,9},{9,... | collective-permute-start | bytes 6291464 | tf_op jit(solution)/shard_map/ppermute | solution.py:257
  81.8 50.1 %collective-permute-start.2 = (bf16[2,16,256,128]{3,2,1,0:T(8,128)(2,1)}, bf16[2,16,256,128]{3,2,1,0:T(8,128)(2,1)}, u32[]{:S(2)}, u32[]{:S(2)}) collective-permute-start(bf16[2,16,256,128]{3,2,1,0:T(8,128)(2,1)} %pad_maximum_fusion.2), channel_id=1, source_target_pairs={{0,2},{4,6},{8,10},{12,14},{16,18},{20,22},{24,26},{28,30},{1,3},{... | collective-permute-start | bytes 6291464 | tf_op jit(solution)/shard_map/ppermute | solution.py:297
  84.5 47.4 %collective-permute-start.3 = (bf16[2,16,128,128]{3,2,1,0:T(8,128)(2,1)}, bf16[2,16,128,128]{3,2,1,0:T(8,128)(2,1)S(1)}, u32[]{:S(2)}, u32[]{:S(2)}) collective-permute-start(bf16[2,16,128,128]{3,2,1,0:T(8,128)(2,1)} %pad_maximum_fusion.4), channel_id=1, source_target_pairs={{0,8},{2,10},{4,12},{6,14},{8,16},{10,18},{12,20},{14,22},{16,24},... | collective-permute-start | bytes 3145736 | tf_op jit(solution)/shard_map/ppermute | solution.py:257
  85.8 46.2 %collective-permute-start.4 = (bf16[2,16,64,128]{3,2,1,0:T(8,128)(2,1)}, bf16[2,16,64,128]{3,2,1,0:T(8,128)(2,1)}, u32[]{:S(2)}, u32[]{:S(2)}) collective-permute-start(bf16[2,16,64,128]{3,2,1,0:T(8,128)(2,1)} %get-tuple-element.35), channel_id=1, source_target_pairs={{0,16},{2,18},{4,20},{6,22},{8,24},{10,26},{12,28},{14,30},{1,17},... | collective-permute-start | bytes 1572872 | tf_op jit(solution)/shard_map/ppermute | solution.py:257
  115.5 36.9 %collective-permute-start.6 = (bf16[256,2048]{1,0:T(8,128)(2,1)}, bf16[256,2048]{1,0:T(8,128)(2,1)}, u32[]{:S(2)}, u32[]{:S(2)}) collective-permute-start(bf16[256,2048]{1,0:T(8,128)(2,1)} %shard_map.61), channel_id=1, source_target_pairs={{0,1},{1,0},{2,3},{3,2},{4,5},{5,4},{6,7},{7,6},{8,9},{9,8},{10,11... | collective-permute-start | bytes 3145736 | tf_op jit(solution)/shard_map/ppermute | solution.py:348
  131.9 1.0 copy-start.3
  131.9 1.6 copy-start.2
  144.1 8.2 %copy-start.4 = (bf16[256,2048]{1,0:T(8,128)(2,1)S(1)}, bf16[256,2048]{1,0:T(8,128)(2,1)}, u32[]{:S(2)}) copy-start(bf16[256,2048]{1,0:T(8,128)(2,1)} %shard_map.57) | copy-start | bytes 3145732
  150.8 22.2 %collective-permute-start.5 = (bf16[256,2048]{1,0:T(8,128)(2,1)}, bf16[256,2048]{1,0:T(8,128)(2,1)S(1)}, u32[]{:S(2)}, u32[]{:S(2)}) collective-permute-start(bf16[256,2048]{1,0:T(8,128)(2,1)} %shard_map.60), channel_id=1, source_target_pairs={{0,1},{1,0},{2,3},{3,2},{4,5},{5,4},{6,7},{7,6},{8,9},{9,8},{10,11... | collective-permute-start | bytes 3145736 | tf_op jit(solution)/shard_map/ppermute | solution.py:364

commit v8 on v7

--- a/solution.py
+++ b/solution.py
@@ -254,8 +254,10 @@
     q_t, kv_t, *operands = lax.optimization_barrier((q_t, kv_t, *[op for op, _ in sends]))
     far_arrays = []
     for (_, pairs), op, level in zip(sends, operands, levels):
-        received = lax.ppermute(op, "ctx", pairs)
-        far_arrays.append((received, None) if level == 1 else (received,))
+        if level == 1:
+            far_arrays.append((op, pairs))
+        else:
+            far_arrays.append((lax.ppermute(op, "ctx", pairs),))
 
     own = lax.dynamic_slice_in_dim(far_blocks, device * per_dev, per_dev, 0)
     query_index = device * per_dev + jnp.arange(per_dev, dtype=jnp.int32)
@@ -292,13 +294,17 @@
         cost_estimate=cost(WINDOW // 2, rows, 2 * heads * rows * width * (3 * 2 + 2 * 4)),
     )(q_t, kv_t, kv_t)
 
-    prev_kv, acc0, st0 = lax.optimization_barrier((prev_kv, acc0, st0))
-    if far_arrays and far_arrays[0][1] is None:
+    if levels and levels[0] == 1:
+        direct_op, direct_pairs = far_arrays[0]
+        prev_kv, acc0, st0, direct_op = lax.optimization_barrier((prev_kv, acc0, st0, direct_op))
+        direct = lax.ppermute(direct_op, "ctx", direct_pairs)
         forwarded = lax.ppermute(
             pick_blocks(prev_kv, fwd_local), "ctx",
             [(s, s + 1) for s in range(0, cycle_size - 1, 2)],
         )
-        far_arrays[0] = (far_arrays[0][0], forwarded)
+        far_arrays[0] = (direct, forwarded)
+    else:
+        prev_kv, acc0, st0 = lax.optimization_barrier((prev_kv, acc0, st0))
     far_specs, far_operands = [], []
     for group in far_arrays:
         for a in group:

time: 177 us -> 168 us (0.949)
  waiting for transfers between devices: 58.1 us -> 49.2 us
    ppermute x1, waiting for transfers between devices: 37.3 us -> 16.3 us  [from_behind(): lax.ppermute(value, axis, [(source, source + steps) for source in range(i...]
    ppermute x3, waiting for transfers between devices: 8.34 us -> 27.6 us  [the longest x2 27.6 us: per_device(): far_arrays.append((lax.ppermute(op, 'ctx', pairs),))]
    ppermute x1, waiting for transfers between devices: 12.5 us -> 5.28 us  [per_device(): lax.ppermute(project_half(att_even, out_weight, 1 - hidx), 'head', swap)]
  transfers between devices with their start and end apart: 7 -> 7, of which waited for: 3 -> 3; matrix products, arithmetic and copies ran while one was open for 10% -> 11% of each run, Pallas kernels for 40% -> 42%
where the time goes in v8:
time: 168 us; the launch traced here: 167 us
  Pallas kernels  70.3 us (42%)
  waiting for transfers between devices  49.2 us (29%)
  local copies, waits for them, and re-layouts  15.6 us (9%)
  other arithmetic  13.7 us (8%)
  starting transfers between devices  11.6 us (7%)
  between operations  6.92 us (4%)
    ppermute x2, waiting for transfers between devices, per_device(): far_arrays.append((lax.ppermute(op, 'ctx', pairs),))  27.6 us
    pallas_call x4, Pallas kernels, project_half(): pl.pallas_call(matmul_kernel, out_shape=jax.ShapeDtypeStruct((rows, cw),...  26.5 us
    pallas_call x1, Pallas kernels, per_device(): pl.pallas_call(per_head(functools.partial(prev_kernel, per_dev, width, sc...  20.1 us
    ppermute x1, waiting for transfers between devices, from_behind(): lax.ppermute(value, axis, [(source, source + steps) for source in range(i...  16.3 us
    pallas_call x1, Pallas kernels, per_device(): pl.pallas_call(per_head(functools.partial(own_kernel, per_dev, width, sca...  13.1 us
    pallas_call x1, Pallas kernels, per_device(): pl.pallas_call(per_head(functools.partial(far_kernel, levels, per_dev, wi...  10.6 us
    unnamed x13, local copies, waits for them, and re-layouts  5.65 us
    another operation x3, other arithmetic, per_device(): jnp.stack([jnp.transpose(keys, (1, 0, 2)), jnp.transpose(values, (1, 0, 2...  5.37 us
  transfers between devices with their start and end apart: 7, of which 3 were waited for; matrix products, arithmetic and copies ran while one was open for 11% of the time, Pallas kernels for 42%

profile of v8, /device:TPU:28, one launch (start us, length us, event | category | flops | bytes accessed | tf_op | source)
XLA Modules:
  0.0 167.2 jit_solution(5940918189544383591)
XLA Ops:
  0.0 3.3 %copy_bitcast_fusion = (bf16[1,16,512,128]{3,2,1,0:T(8,128)(2,1)S(1)}, bf16[1,16,512,128]{3,2,1,0:T(8,128)(2,1)S(1)}) fusion(bf16[512,16,128]{2,1,0:T(8,128)(2,1)} %param.7, bf16[512,16,128]{2,1,0:T(8,128)(2,1)} %param.6), kind=kLoop, calls=%fused_computation.18 | loop fusion | bytes 8388608 | tf_op jit(solution)/shard_map/stack | solution.py:234
  3.3 2.6 %pad_maximum_fusion.refs_1_.refs_2_ = bf16[2,16,512,128]{3,2,1,0:T(8,128)(2,1)} fusion(bf16[1,16,512,128]{3,2,1,0:T(8,128)(2,1)S(1)} %get-tuple-element.67, bf16[1,16,512,128]{3,2,1,0:T(8,128)(2,1)S(1)} %get-tuple-element.68), kind=kLoop, calls=%fused_computation.7 | loop fusion | flops 2097152 | bytes 8388608 | tf_op jit(solution)/shard_map/stack | solution.py:234
  6.0 1.9 %collective-permute-start = (bf16[2,16,512,128]{3,2,1,0:T(8,128)(2,1)}, bf16[2,16,512,128]{3,2,1,0:T(8,128)(2,1)}, u32[]{:S(2)}, u32[]{:S(2)}) collective-permute-start(bf16[2,16,512,128]{3,2,1,0:T(8,128)(2,1)} %pad_maximum_fusion.refs_1_.refs_2_), channel_id=1, source_target_pairs={{0,2},{2,4},{4,6},{6,8},{8,10},{10,12},{12,14},{14,16},{16,18},{18... | collective-permute-start | bytes 12582920 | tf_op jit(solution)/shard_map/ppermute | solution.py:20
  17.4 3.5 %copy.14 = bf16[512,16,128]{2,0,1:T(8,128)(2,1)} copy(bf16[512,16,128]{2,1,0:T(8,128)(2,1)} %param.5) | data formatting | bytes 4194304 | tf_op args[0]
  22.5 1.6 fusion.6
  25.2 1.5 pad_maximum_fusion.1
  26.7 13.1 %shard_map.55 = (f32[16,512,128]{2,1,0:T(8,128)}, f32[16,512,128]{2,1,0:T(8,128)}) custom-call(bf16[16,512,128]{2,1,0:T(8,128)(2,1)} %bitcast.33, bf16[2,16,512,128]{3,2,1,0:T(8,128)(2,1)} %pad_maximum_fusion.refs_1_.refs_2_, bf16[2,16,512,128]{3,2,1,0:T(8,128)(2,1)} %pad_maximum_fusion.refs_1_.refs_2_), custom_call_target="tpu_custom_call" | custom-call | flops 1073741824 | bytes 29360128 | tf_op jit(solution)/shard_map/pallas_call | solution.py:287
  39.8 16.3 %collective-permute-done.refs_3_.refs_4_ = bf16[2,16,512,128]{3,2,1,0:T(8,128)(2,1)} collective-permute-done((bf16[2,16,512,128]{3,2,1,0:T(8,128)(2,1)}, bf16[2,16,512,128]{3,2,1,0:T(8,128)(2,1)}, u32[]{:S(2)}, u32[]{:S(2)}) %collective-permute-start) | collective-permute-done | bytes 4194336 | tf_op jit(solution)/shard_map/ppermute | solution.py:20
  57.4 1.7 %constant_dynamic-slice_fusion.3 = (bf16[2,16,64,128]{3,2,1,0:T(8,128)(2,1)S(1)}, bf16[2,16,64,128]{3,2,1,0:T(8,128)(2,1)S(1)}, bf16[2,16,64,128]{3,2,1,0:T(8,128)(2,1)S(1)}, bf16[2,16,64,128]{3,2,1,0:T(8,128)(2,1)S(1)}) fusion(bf16[2,16,512,128]{3,2,1,0:T(8,128)(2,1)} %collective-permute-done.refs_3_.refs_4_, s32[]{:T(128)S(6)} %select_n.68, ...), kind=kLoop, calls=%fused_computation.34 | loop fusion | bytes 4194320 | tf_op jit(solution)/shard_map/dynamic_slice | solution.py:222
  59.1 1.6 pad_maximum_fusion.2
  60.7 2.6 %collective-permute-start.2 = (bf16[2,16,256,128]{3,2,1,0:T(8,128)(2,1)}, bf16[2,16,256,128]{3,2,1,0:T(8,128)(2,1)}, u32[]{:S(2)}, u32[]{:S(2)}) collective-permute-start(bf16[2,16,256,128]{3,2,1,0:T(8,128)(2,1)} %pad_maximum_fusion.2), channel_id=1, source_target_pairs={{0,2},{4,6},{8,10},{12,14},{16,18},{20,22},{24,26},{28,30},{1,3},{... | collective-permute-start | bytes 6291464 | tf_op jit(solution)/shard_map/ppermute | solution.py:301
  64.6 1.5 collective-permute-start.4
  67.6 20.1 %shard_map.56 = (f32[16,256,128]{2,1,0:T(8,128)}, f32[16,256,128]{2,1,0:T(8,128)}, bf16[256,2048]{1,0:T(8,128)(2,1)}) custom-call(s32[10]{0:T(128)} %pad_add_fusion.refs_0_, s32[40]{0:T(128)} %reshape.110.refs_1_, bf16[16,512,128]{2,1,0:T(8,128)(2,1)} %bitcast.34, bf16[2,16,512,128]{3,2,1,0:T(8,128)(2,1)} %collective-permute-done.refs_3_.refs_4_, ...), custom_call_target="tpu_custom_call" | custom-call | flops 1342177280 | bytes 23068672 | tf_op jit(solution)/shard_map/pallas_call | solution.py:313
  87.7 6.6 %shard_map.61 = bf16[256,2048]{1,0:T(8,128)(2,1)} custom-call(s32[1]{0:T(128)} %bitcast.22.sel_ref, bf16[256,2048]{1,0:T(8,128)(2,1)} %get-tuple-element.32.a_ref, bf16[2048,4096]{1,0:T(8,128)(2,1)} %w_ref.7), custom_call_target="tpu_custom_call" | custom-call | flops 2147483648 | bytes 10485760 | tf_op jit(solution)/shard_map/pallas_call | solution.py:199
  94.3 1.5 collective-permute-start.6
  95.8 6.6 %shard_map.57 = bf16[256,2048]{1,0:T(8,128)(2,1)} custom-call(s32[1]{0:T(128)} %bitcast.sel_ref, bf16[256,2048]{1,0:T(8,128)(2,1)} %get-tuple-element.32.a_ref, bf16[2048,4096]{1,0:T(8,128)(2,1)} %w_ref.7), custom_call_target="tpu_custom_call" | custom-call | flops 2147483648 | bytes 10485760 | tf_op jit(solution)/shard_map/pallas_call | solution.py:199
  102.4 27.6 %collective-permute-done.4.refs_11_.refs_12_ = bf16[2,16,64,128]{3,2,1,0:T(8,128)(2,1)} collective-permute-done((bf16[2,16,64,128]{3,2,1,0:T(8,128)(2,1)}, bf16[2,16,64,128]{3,2,1,0:T(8,128)(2,1)}, u32[]{:S(2)}, u32[]{:S(2)}) %collective-permute-start.4) | collective-permute-done | bytes 524320 | tf_op jit(solution)/shard_map/ppermute | solution.py:260
  131.7 10.6 %shard_map.58.a_ref = bf16[256,2048]{1,0:T(8,128)(2,1)} custom-call(s32[10]{0:T(128)} %pad_add_fusion.refs_0_, s32[40]{0:T(128)} %reshape.110.refs_1_, bf16[16,512,128]{2,1,0:T(8,128)(2,1)} %bitcast.35, f32[16,256,128]{2,1,0:T(8,128)} %get-tuple-element.33.refs_3_, f32[16,256,128]{2,1,0:T(8,128)} %get-tuple-element.34.refs_4_, ...), custom_call_target="tpu_custom_call" | custom-call | flops 268435456 | bytes 12058624 | tf_op jit(solution)/shard_map/pallas_call | solution.py:357
  142.2 6.7 %shard_map.60 = bf16[256,2048]{1,0:T(8,128)(2,1)} custom-call(s32[1]{0:T(128)} %bitcast.22.sel_ref, bf16[256,2048]{1,0:T(8,128)(2,1)} %shard_map.58.a_ref, bf16[2048,4096]{1,0:T(8,128)(2,1)} %w_ref.7), custom_call_target="tpu_custom_call" | custom-call | flops 2147483648 | bytes 10485760 | tf_op jit(solution)/shard_map/pallas_call | solution.py:199
  148.9 1.5 collective-permute-start.5
  150.4 1.6 add_convert_fusion
  152.0 6.6 %shard_map.59 = bf16[256,2048]{1,0:T(8,128)(2,1)} custom-call(s32[1]{0:T(128)} %bitcast.sel_ref, bf16[256,2048]{1,0:T(8,128)(2,1)} %shard_map.58.a_ref, bf16[2048,4096]{1,0:T(8,128)(2,1)} %w_ref.7), custom_call_target="tpu_custom_call" | custom-call | flops 2147483648 | bytes 10485760 | tf_op jit(solution)/shard_map/pallas_call | solution.py:199
  158.7 5.3 %collective-permute-done.5 = bf16[256,2048]{1,0:T(8,128)(2,1)S(1)} collective-permute-done((bf16[256,2048]{1,0:T(8,128)(2,1)}, bf16[256,2048]{1,0:T(8,128)(2,1)S(1)}, u32[]{:S(2)}, u32[]{:S(2)}) %collective-permute-start.5) | collective-permute-done | bytes 1048608 | tf_op jit(solution)/shard_map/ppermute | solution.py:370
  163.9 1.6 add_convert_fusion.1
  (38 shorter events, 12.8 us)
Async XLA Ops:
  3.3 2.7 %copy-start = (bf16[1,16,512,128]{3,2,1,0:T(8,128)(2,1)}, bf16[1,16,512,128]{3,2,1,0:T(8,128)(2,1)S(1)}, u32[]{:S(2)}) copy-start(bf16[1,16,512,128]{3,2,1,0:T(8,128)(2,1)S(1)} %get-tuple-element.68) | copy-start | bytes 6291460
  3.3 4.6 %copy-start.5 = (s32[128,5]{0,1:T(8,128)S(1)}, s32[128,5]{0,1:T(8,128)}, u32[]{:S(2)}) copy-start(s32[128,5]{0,1:T(8,128)} %param.8) | copy-start | bytes 7684
  6.0 50.1 %collective-permute-start = (bf16[2,16,512,128]{3,2,1,0:T(8,128)(2,1)}, bf16[2,16,512,128]{3,2,1,0:T(8,128)(2,1)}, u32[]{:S(2)}, u32[]{:S(2)}) collective-permute-start(bf16[2,16,512,128]{3,2,1,0:T(8,128)(2,1)} %pad_maximum_fusion.refs_1_.refs_2_), channel_id=1, source_target_pairs={{0,2},{2,4},{4,6},{6,8},{8,10},{10,12},{12,14},{14,16},{16,18},{18... | collective-permute-start | bytes 12582920 | tf_op jit(solution)/shard_map/ppermute | solution.py:20
  20.9 1.7 copy-start.1
  56.1 73.9 %collective-permute-start.1 = (bf16[2,16,256,128]{3,2,1,0:T(8,128)(2,1)}, bf16[2,16,256,128]{3,2,1,0:T(8,128)(2,1)S(1)}, u32[]{:S(2)}, u32[]{:S(2)}) collective-permute-start(bf16[2,16,256,128]{3,2,1,0:T(8,128)(2,1)} %pad_maximum_fusion.1), channel_id=1, source_target_pairs={{0,4},{4,8},{8,12},{12,16},{16,20},{20,24},{24,28},{1,5},{5,9},{9,... | collective-permute-start | bytes 6291464 | tf_op jit(solution)/shard_map/ppermute | solution.py:300
  60.7 69.4 %collective-permute-start.2 = (bf16[2,16,256,128]{3,2,1,0:T(8,128)(2,1)}, bf16[2,16,256,128]{3,2,1,0:T(8,128)(2,1)}, u32[]{:S(2)}, u32[]{:S(2)}) collective-permute-start(bf16[2,16,256,128]{3,2,1,0:T(8,128)(2,1)} %pad_maximum_fusion.2), channel_id=1, source_target_pairs={{0,2},{4,6},{8,10},{12,14},{16,18},{20,22},{24,26},{28,30},{1,3},{... | collective-permute-start | bytes 6291464 | tf_op jit(solution)/shard_map/ppermute | solution.py:301
  63.3 66.7 %collective-permute-start.3 = (bf16[2,16,128,128]{3,2,1,0:T(8,128)(2,1)}, bf16[2,16,128,128]{3,2,1,0:T(8,128)(2,1)S(1)}, u32[]{:S(2)}, u32[]{:S(2)}) collective-permute-start(bf16[2,16,128,128]{3,2,1,0:T(8,128)(2,1)} %pad_maximum_fusion.4), channel_id=1, source_target_pairs={{0,8},{2,10},{4,12},{6,14},{8,16},{10,18},{12,20},{14,22},{16,24},... | collective-permute-start | bytes 3145736 | tf_op jit(solution)/shard_map/ppermute | solution.py:260
  64.6 65.4 %collective-permute-start.4 = (bf16[2,16,64,128]{3,2,1,0:T(8,128)(2,1)}, bf16[2,16,64,128]{3,2,1,0:T(8,128)(2,1)}, u32[]{:S(2)}, u32[]{:S(2)}) collective-permute-start(bf16[2,16,64,128]{3,2,1,0:T(8,128)(2,1)} %get-tuple-element.37), channel_id=1, source_target_pairs={{0,16},{2,18},{4,20},{6,22},{8,24},{10,26},{12,28},{14,30},{1,17},... | collective-permute-start | bytes 1572872 | tf_op jit(solution)/shard_map/ppermute | solution.py:260
  94.3 56.1 %collective-permute-start.6 = (bf16[256,2048]{1,0:T(8,128)(2,1)}, bf16[256,2048]{1,0:T(8,128)(2,1)}, u32[]{:S(2)}, u32[]{:S(2)}) collective-permute-start(bf16[256,2048]{1,0:T(8,128)(2,1)} %shard_map.61), channel_id=1, source_target_pairs={{0,1},{1,0},{2,3},{3,2},{4,5},{5,4},{6,7},{7,6},{8,9},{9,8},{10,11... | collective-permute-start | bytes 3145736 | tf_op jit(solution)/shard_map/ppermute | solution.py:354
  130.0 1.0 copy-start.3
  130.0 1.6 copy-start.2
  142.2 8.2 %copy-start.4 = (bf16[256,2048]{1,0:T(8,128)(2,1)S(1)}, bf16[256,2048]{1,0:T(8,128)(2,1)}, u32[]{:S(2)}) copy-start(bf16[256,2048]{1,0:T(8,128)(2,1)} %shard_map.57) | copy-start | bytes 3145732
  148.9 15.0 %collective-permute-start.5 = (bf16[256,2048]{1,0:T(8,128)(2,1)}, bf16[256,2048]{1,0:T(8,128)(2,1)S(1)}, u32[]{:S(2)}, u32[]{:S(2)}) collective-permute-start(bf16[256,2048]{1,0:T(8,128)(2,1)} %shard_map.60), channel_id=1, source_target_pairs={{0,1},{1,0},{2,3},{3,2},{4,5},{5,4},{6,7},{7,6},{8,9},{9,8},{10,11... | collective-permute-start | bytes 3145736 | tf_op jit(solution)/shard_map/ppermute | solution.py:370

commit v9 on v8

--- a/solution.py
+++ b/solution.py
@@ -158,15 +158,11 @@
     pos = 0
     for level in levels:
         offset = 2**level
-        n_src = 2 if level == 1 else 1
-        refs = far_refs[pos:pos + 2 * n_src]
-        pos += 2 * n_src
-        k_lvl = refs[0][...]
-        v_lvl = refs[1][...]
-        if n_src == 2:
-            odd = meta_ref[1 + per_dev] > 0
-            k_lvl = jnp.where(odd, refs[2][...], k_lvl)
-            v_lvl = jnp.where(odd, refs[3][...], v_lvl)
+        refs = far_refs[pos:pos + 4]
+        pos += 4
+        second = meta_ref[(1 if level == 1 else 2) + per_dev] > 0
+        k_lvl = jnp.where(second, refs[2][...], refs[0][...])
+        v_lvl = jnp.where(second, refs[3][...], refs[1][...])
         keys.append(k_lvl)
         vals.append(v_lvl)
         for k in range(k_lvl.shape[0] // BLOCK):
@@ -253,18 +249,25 @@
         levels.append(level)
     q_t, kv_t, *operands = lax.optimization_barrier((q_t, kv_t, *[op for op, _ in sends]))
     far_arrays = []
+    early_far = []
+    late_far = []
     for (_, pairs), op, level in zip(sends, operands, levels):
         if level == 1:
             far_arrays.append((op, pairs))
         else:
-            far_arrays.append((lax.ppermute(op, "ctx", pairs),))
+            soon = [(a, b) for a, b in pairs if (b // 2) % 2 == 1]
+            later = [(a, b) for a, b in pairs if (b // 2) % 2 == 0]
+            early_far.append(lax.ppermute(op, "ctx", soon))
+            late_far.append((op, later))
+            far_arrays.append(None)
 
     own = lax.dynamic_slice_in_dim(far_blocks, device * per_dev, per_dev, 0)
     query_index = device * per_dev + jnp.arange(per_dev, dtype=jnp.int32)
     used = (own <= (query_index - WINDOW // BLOCK - 1)[:, None]).astype(jnp.int32).reshape(-1)
     pick = jnp.clip(own[:, 0] - (device - 1) * per_dev, 0, per_dev - 1)
     meta = jnp.concatenate(
-        [(device > 0).astype(jnp.int32)[None], pick.astype(jnp.int32), (device % 2)[None]]
+        [(device > 0).astype(jnp.int32)[None], pick.astype(jnp.int32), (device % 2)[None],
+         ((device // 2) % 2)[None]]
     )
 
     hb = math.gcd(heads, HEADS_PER_STEP)
@@ -294,17 +297,23 @@
         cost_estimate=cost(WINDOW // 2, rows, 2 * heads * rows * width * (3 * 2 + 2 * 4)),
     )(q_t, kv_t, kv_t)
 
-    if levels and levels[0] == 1:
-        direct_op, direct_pairs = far_arrays[0]
-        prev_kv, acc0, st0, direct_op = lax.optimization_barrier((prev_kv, acc0, st0, direct_op))
-        direct = lax.ppermute(direct_op, "ctx", direct_pairs)
-        forwarded = lax.ppermute(
-            pick_blocks(prev_kv, fwd_local), "ctx",
-            [(s, s + 1) for s in range(0, cycle_size - 1, 2)],
-        )
-        far_arrays[0] = (direct, forwarded)
-    else:
-        prev_kv, acc0, st0 = lax.optimization_barrier((prev_kv, acc0, st0))
+    late_ops = [op for op, _ in late_far]
+    direct_op = [far_arrays[0][0]] if levels and levels[0] == 1 else []
+    prev_kv, acc0, st0, early_far, late_ops, direct_op = lax.optimization_barrier(
+        (prev_kv, acc0, st0, early_far, late_ops, direct_op)
+    )
+    late = iter(zip(early_far, late_ops, [p for _, p in late_far]))
+    for index, level in enumerate(levels):
+        if level == 1:
+            direct = lax.ppermute(direct_op[0], "ctx", far_arrays[0][1])
+            forwarded = lax.ppermute(
+                pick_blocks(prev_kv, fwd_local), "ctx",
+                [(s, s + 1) for s in range(0, cycle_size - 1, 2)],
+            )
+            far_arrays[index] = (direct, forwarded)
+        else:
+            got_early, op, pairs = next(late)
+            far_arrays[index] = (lax.ppermute(op, "ctx", pairs), got_early)
     far_specs, far_operands = [], []
     for group in far_arrays:
         for a in group:

time: 168 us -> 204 us (1.21)
  starting transfers between devices: 11.6 us -> 56.3 us
  waiting for transfers between devices: 49.2 us -> 40.2 us
    ppermute x1, starting transfers between devices: 2.63 us -> 46.4 us  [per_device(): lax.ppermute(pick_blocks(prev_kv, fwd_local), 'ctx', [(s, s + 1) for s in...]
    ppermute x1, waiting for transfers between devices: 16.3 us -> 0.01 us  [from_behind(): lax.ppermute(value, axis, [(source, source + steps) for source in range(i...]
    ppermute x1, waiting for transfers between devices: 5.28 us -> 14.3 us  [per_device(): lax.ppermute(project_half(att_even, out_weight, 1 - hidx), 'head', swap)]
    ppermute x3 -> x5, starting transfers between devices: 4.03 us -> 6.03 us  [the longest x2 2.57 us: per_device(): early_far.append(lax.ppermute(op, 'ctx', soon))]
    ppermute x3 -> x5, waiting for transfers between devices: 27.6 us -> 26 us  [the longest x2 25.9 us: per_device(): early_far.append(lax.ppermute(op, 'ctx', soon))]
    unnamed x13 -> x19, local copies, waits for them, and re-layouts: 5.65 us -> 6.47 us
  transfers between devices with their start and end apart: 7 -> 9, of which waited for: 3 -> 2; matrix products, arithmetic and copies ran while one was open for 11% -> 8% of each run, Pallas kernels for 42% -> 35%
where the time goes in v9:
time: 204 us; the launch traced here: 203 us
  Pallas kernels  70.5 us (35%)
  starting transfers between devices  56.3 us (28%)
  waiting for transfers between devices  40.2 us (20%)
  local copies, waits for them, and re-layouts  16.4 us (8%)
  other arithmetic  12.8 us (6%)
  between operations  7.08 us (3%)
    ppermute x1, starting transfers between devices, per_device(): lax.ppermute(pick_blocks(prev_kv, fwd_local), 'ctx', [(s, s + 1) for s in...  46.4 us
    pallas_call x4, Pallas kernels, project_half(): pl.pallas_call(matmul_kernel, out_shape=jax.ShapeDtypeStruct((rows, cw),...  26.5 us
    ppermute x2, waiting for transfers between devices, per_device(): early_far.append(lax.ppermute(op, 'ctx', soon))  25.9 us
    pallas_call x1, Pallas kernels, per_device(): pl.pallas_call(per_head(functools.partial(prev_kernel, per_dev, width, sc...  20.1 us
    ppermute x1, waiting for transfers between devices, per_device(): lax.ppermute(project_half(att_even, out_weight, 1 - hidx), 'head', swap)  14.3 us
    pallas_call x1, Pallas kernels, per_device(): pl.pallas_call(per_head(functools.partial(own_kernel, per_dev, width, sca...  13.1 us
    pallas_call x1, Pallas kernels, per_device(): pl.pallas_call(per_head(functools.partial(far_kernel, levels, per_dev, wi...  10.8 us
    unnamed x19, local copies, waits for them, and re-layouts  6.47 us
  transfers between devices with their start and end apart: 9, of which 2 were waited for; matrix products, arithmetic and copies ran while one was open for 8% of the time, Pallas kernels for 35%

profile of v9, /device:TPU:28, one launch (start us, length us, event | category | flops | bytes accessed | tf_op | source)
XLA Modules:
  0.0 203.3 jit_solution(7967171499114399026)
XLA Ops:
  0.0 3.3 %copy_bitcast_fusion = (bf16[1,16,512,128]{3,2,1,0:T(8,128)(2,1)S(1)}, bf16[1,16,512,128]{3,2,1,0:T(8,128)(2,1)S(1)}) fusion(bf16[512,16,128]{2,1,0:T(8,128)(2,1)} %param.7, bf16[512,16,128]{2,1,0:T(8,128)(2,1)} %param.6), kind=kLoop, calls=%fused_computation.18 | loop fusion | bytes 8388608 | tf_op jit(solution)/shard_map/stack | solution.py:230
  3.3 2.6 %pad_maximum_fusion.refs_1_.refs_2_ = bf16[2,16,512,128]{3,2,1,0:T(8,128)(2,1)} fusion(bf16[1,16,512,128]{3,2,1,0:T(8,128)(2,1)S(1)} %get-tuple-element.75, bf16[1,16,512,128]{3,2,1,0:T(8,128)(2,1)S(1)} %get-tuple-element.76), kind=kLoop, calls=%fused_computation.7 | loop fusion | flops 2097152 | bytes 8388608 | tf_op jit(solution)/shard_map/stack | solution.py:230
  6.0 1.9 collective-permute-start
  14.5 3.5 %copy.14 = bf16[512,16,128]{2,0,1:T(8,128)(2,1)} copy(bf16[512,16,128]{2,1,0:T(8,128)(2,1)} %param.5) | data formatting | bytes 4194304 | tf_op args[0]
  19.6 1.6 fusion.6
  21.3 1.6 pad_maximum_fusion.1
  24.2 1.3 collective-permute-start.2
  28.6 13.1 %shard_map.55 = (f32[16,512,128]{2,1,0:T(8,128)}, f32[16,512,128]{2,1,0:T(8,128)}) custom-call(bf16[16,512,128]{2,1,0:T(8,128)(2,1)} %bitcast.34, bf16[2,16,512,128]{3,2,1,0:T(8,128)(2,1)} %pad_maximum_fusion.refs_1_.refs_2_, bf16[2,16,512,128]{3,2,1,0:T(8,128)(2,1)} %pad_maximum_fusion.refs_1_.refs_2_), custom_call_target="tpu_custom_call" | custom-call | flops 1073741824 | bytes 29360128 | tf_op jit(solution)/shard_map/pallas_call | solution.py:290
  41.6 25.9 %collective-permute-done.2.refs_15_.refs_16_ = bf16[2,16,64,128]{3,2,1,0:T(8,128)(2,1)S(1)} collective-permute-done((bf16[2,16,64,128]{3,2,1,0:T(8,128)(2,1)}, bf16[2,16,64,128]{3,2,1,0:T(8,128)(2,1)S(1)}, u32[]{:S(2)}, u32[]{:S(2)}) %collective-permute-start.2) | collective-permute-done | bytes 524320 | tf_op jit(solution)/shard_map/ppermute | solution.py:260
  69.7 1.7 constant_dynamic-slice_fusion.3
  71.4 1.6 pad_maximum_fusion.2
  73.0 46.4 %collective-permute-start.4 = (bf16[2,16,256,128]{3,2,1,0:T(8,128)(2,1)}, bf16[2,16,256,128]{3,2,1,0:T(8,128)(2,1)}, u32[]{:S(2)}, u32[]{:S(2)}) collective-permute-start(bf16[2,16,256,128]{3,2,1,0:T(8,128)(2,1)} %pad_maximum_fusion.2), channel_id=1, source_target_pairs={{0,2},{4,6},{8,10},{12,14},{16,18},{20,22},{24,26},{28,30},{1,3},{... | collective-permute-start | bytes 6291464 | tf_op jit(solution)/shard_map/ppermute | solution.py:309
  121.6 1.5 collective-permute-start.6
  123.0 20.1 %shard_map.56 = (f32[16,256,128]{2,1,0:T(8,128)}, f32[16,256,128]{2,1,0:T(8,128)}, bf16[256,2048]{1,0:T(8,128)(2,1)}) custom-call(s32[11]{0:T(128)} %pad_add_fusion.refs_0_, s32[40]{0:T(128)} %reshape.110.refs_1_, bf16[16,512,128]{2,1,0:T(8,128)(2,1)} %bitcast.35, bf16[2,16,512,128]{3,2,1,0:T(8,128)(2,1)} %collective-permute-done.refs_3_.refs_4_, ...), custom_call_target="tpu_custom_call" | custom-call | flops 1342177280 | bytes 23068672 | tf_op jit(solution)/shard_map/pallas_call | solution.py:322
  143.1 6.6 %shard_map.61 = bf16[256,2048]{1,0:T(8,128)(2,1)} custom-call(s32[1]{0:T(128)} %bitcast.23.sel_ref, bf16[256,2048]{1,0:T(8,128)(2,1)} %get-tuple-element.38.a_ref, bf16[2048,4096]{1,0:T(8,128)(2,1)} %w_ref.7), custom_call_target="tpu_custom_call" | custom-call | flops 2147483648 | bytes 10485760 | tf_op jit(solution)/shard_map/pallas_call | solution.py:195
  149.7 1.5 collective-permute-start.8
  151.2 6.6 %shard_map.57 = bf16[256,2048]{1,0:T(8,128)(2,1)} custom-call(s32[1]{0:T(128)} %bitcast.sel_ref, bf16[256,2048]{1,0:T(8,128)(2,1)} %get-tuple-element.38.a_ref, bf16[2048,4096]{1,0:T(8,128)(2,1)} %w_ref.7), custom_call_target="tpu_custom_call" | custom-call | flops 2147483648 | bytes 10485760 | tf_op jit(solution)/shard_map/pallas_call | solution.py:195
  159.5 10.8 %shard_map.58.a_ref = bf16[256,2048]{1,0:T(8,128)(2,1)} custom-call(s32[11]{0:T(128)} %pad_add_fusion.refs_0_, s32[40]{0:T(128)} %reshape.110.refs_1_, bf16[16,512,128]{2,1,0:T(8,128)(2,1)} %bitcast.36, f32[16,256,128]{2,1,0:T(8,128)} %get-tuple-element.39.refs_3_, f32[16,256,128]{2,1,0:T(8,128)} %get-tuple-element.40.refs_4_, ...), custom_call_target="tpu_custom_call" | custom-call | flops 268435456 | bytes 13631488 | tf_op jit(solution)/shard_map/pallas_call | solution.py:366
  170.3 6.7 %shard_map.60 = bf16[256,2048]{1,0:T(8,128)(2,1)} custom-call(s32[1]{0:T(128)} %bitcast.23.sel_ref, bf16[256,2048]{1,0:T(8,128)(2,1)} %shard_map.58.a_ref, bf16[2048,4096]{1,0:T(8,128)(2,1)} %w_ref.7), custom_call_target="tpu_custom_call" | custom-call | flops 2147483648 | bytes 10485760 | tf_op jit(solution)/shard_map/pallas_call | solution.py:195
  177.5 1.6 add_convert_fusion
  179.1 6.6 %shard_map.59 = bf16[256,2048]{1,0:T(8,128)(2,1)} custom-call(s32[1]{0:T(128)} %bitcast.sel_ref, bf16[256,2048]{1,0:T(8,128)(2,1)} %shard_map.58.a_ref, bf16[2048,4096]{1,0:T(8,128)(2,1)} %w_ref.7), custom_call_target="tpu_custom_call" | custom-call | flops 2147483648 | bytes 10485760 | tf_op jit(solution)/shard_map/pallas_call | solution.py:195
  185.8 14.3 %collective-permute-done.7 = bf16[256,2048]{1,0:T(8,128)(2,1)S(1)} collective-permute-done((bf16[256,2048]{1,0:T(8,128)(2,1)}, bf16[256,2048]{1,0:T(8,128)(2,1)S(1)}, u32[]{:S(2)}, u32[]{:S(2)}) %collective-permute-start.7) | collective-permute-done | bytes 1048608 | tf_op jit(solution)/shard_map/ppermute | solution.py:379
  200.1 1.6 add_convert_fusion.1
  201.9 1.5 copy.10
  (48 shorter events, 12.5 us)
Async XLA Ops:
  3.3 2.7 %copy-start = (bf16[1,16,512,128]{3,2,1,0:T(8,128)(2,1)}, bf16[1,16,512,128]{3,2,1,0:T(8,128)(2,1)S(1)}, u32[]{:S(2)}) copy-start(bf16[1,16,512,128]{3,2,1,0:T(8,128)(2,1)S(1)} %get-tuple-element.76) | copy-start | bytes 6291460
  3.3 4.6 %copy-start.8 = (s32[128,5]{0,1:T(8,128)S(1)}, s32[128,5]{0,1:T(8,128)}, u32[]{:S(2)}) copy-start(s32[128,5]{0,1:T(8,128)} %param.8) | copy-start | bytes 7684
  6.0 61.6 %collective-permute-start = (bf16[2,16,512,128]{3,2,1,0:T(8,128)(2,1)}, bf16[2,16,512,128]{3,2,1,0:T(8,128)(2,1)}, u32[]{:S(2)}, u32[]{:S(2)}) collective-permute-start(bf16[2,16,512,128]{3,2,1,0:T(8,128)(2,1)} %pad_maximum_fusion.refs_1_.refs_2_), channel_id=1, source_target_pairs={{0,2},{2,4},{4,6},{6,8},{8,10},{10,12},{12,14},{14,16},{16,18},{18... | collective-permute-start | bytes 12582920 | tf_op jit(solution)/shard_map/ppermute | solution.py:20
  17.9 1.7 copy-start.1
  21.3 1.7 copy-start.7
  22.9 44.6 %collective-permute-start.1 = (bf16[2,16,128,128]{3,2,1,0:T(8,128)(2,1)S(1)}, bf16[2,16,128,128]{3,2,1,0:T(8,128)(2,1)S(1)}, u32[]{:S(2)}, u32[]{:S(2)}) collective-permute-start(bf16[2,16,128,128]{3,2,1,0:T(8,128)(2,1)S(1)} %pad_maximum_fusion.4), channel_id=1, source_target_pairs={{4,12},{6,14},{12,20},{14,22},{20,28},{22,30},{5,13},{7,15},{13,21... | collective-permute-start | bytes 3145736 | tf_op jit(solution)/shard_map/ppermute | solution.py:260
  24.2 43.3 %collective-permute-start.2 = (bf16[2,16,64,128]{3,2,1,0:T(8,128)(2,1)}, bf16[2,16,64,128]{3,2,1,0:T(8,128)(2,1)S(1)}, u32[]{:S(2)}, u32[]{:S(2)}) collective-permute-start(bf16[2,16,64,128]{3,2,1,0:T(8,128)(2,1)} %get-tuple-element.44), channel_id=1, source_target_pairs={{4,20},{6,22},{12,28},{14,30},{5,21},{7,23},{13,29},{15,31}} | collective-permute-start | bytes 1572872 | tf_op jit(solution)/shard_map/ppermute | solution.py:260
  67.6 0.8 copy-start.6
  67.6 3.8 %copy-start.3 = (bf16[2,16,128,128]{3,2,1,0:T(8,128)(2,1)}, bf16[2,16,128,128]{3,2,1,0:T(8,128)(2,1)S(1)}, u32[]{:S(2)}) copy-start(bf16[2,16,128,128]{3,2,1,0:T(8,128)(2,1)S(1)} %collective-permute-done.1.refs_11_.refs_12_) | copy-start | bytes 3145732
  68.4 89.5 %collective-permute-start.3 = (bf16[2,16,256,128]{3,2,1,0:T(8,128)(2,1)}, bf16[2,16,256,128]{3,2,1,0:T(8,128)(2,1)S(1)}, u32[]{:S(2)}, u32[]{:S(2)}) collective-permute-start(bf16[2,16,256,128]{3,2,1,0:T(8,128)(2,1)} %pad_maximum_fusion.1), channel_id=1, source_target_pairs={{0,4},{4,8},{8,12},{12,16},{16,20},{20,24},{24,28},{1,5},{5,9},{9,... | collective-permute-start | bytes 6291464 | tf_op jit(solution)/shard_map/ppermute | solution.py:308
  73.0 84.9 %collective-permute-start.4 = (bf16[2,16,256,128]{3,2,1,0:T(8,128)(2,1)}, bf16[2,16,256,128]{3,2,1,0:T(8,128)(2,1)}, u32[]{:S(2)}, u32[]{:S(2)}) collective-permute-start(bf16[2,16,256,128]{3,2,1,0:T(8,128)(2,1)} %pad_maximum_fusion.2), channel_id=1, source_target_pairs={{0,2},{4,6},{8,10},{12,14},{16,18},{20,22},{24,26},{28,30},{1,3},{... | collective-permute-start | bytes 6291464 | tf_op jit(solution)/shard_map/ppermute | solution.py:309
  119.4 38.4 %collective-permute-start.5 = (bf16[2,16,128,128]{3,2,1,0:T(8,128)(2,1)}, bf16[2,16,128,128]{3,2,1,0:T(8,128)(2,1)S(1)}, u32[]{:S(2)}, u32[]{:S(2)}) collective-permute-start(bf16[2,16,128,128]{3,2,1,0:T(8,128)(2,1)} %copy-done.7), channel_id=1, source_target_pairs={{0,8},{2,10},{8,16},{10,18},{16,24},{18,26},{1,9},{3,11},{9,17},{1... | collective-permute-start | bytes 3145736 | tf_op jit(solution)/shard_map/ppermute | solution.py:316
  121.6 36.3 %collective-permute-start.6 = (bf16[2,16,64,128]{3,2,1,0:T(8,128)(2,1)}, bf16[2,16,64,128]{3,2,1,0:T(8,128)(2,1)}, u32[]{:S(2)}, u32[]{:S(2)}) collective-permute-start(bf16[2,16,64,128]{3,2,1,0:T(8,128)(2,1)} %get-tuple-element.44), channel_id=1, source_target_pairs={{0,16},{2,18},{8,24},{10,26},{1,17},{3,19},{9,25},{11,27}} | collective-permute-start | bytes 1572872 | tf_op jit(solution)/shard_map/ppermute | solution.py:316
  149.7 27.8 %collective-permute-start.8 = (bf16[256,2048]{1,0:T(8,128)(2,1)}, bf16[256,2048]{1,0:T(8,128)(2,1)}, u32[]{:S(2)}, u32[]{:S(2)}) collective-permute-start(bf16[256,2048]{1,0:T(8,128)(2,1)} %shard_map.61), channel_id=1, source_target_pairs={{0,1},{1,0},{2,3},{3,2},{4,5},{5,4},{6,7},{7,6},{8,9},{9,8},{10,11... | collective-permute-start | bytes 3145736 | tf_op jit(solution)/shard_map/ppermute | solution.py:363
  157.8 1.0 copy-start.4
  157.9 1.6 copy-start.2
  170.3 7.2 %copy-start.5 = (bf16[256,2048]{1,0:T(8,128)(2,1)S(1)}, bf16[256,2048]{1,0:T(8,128)(2,1)}, u32[]{:S(2)}) copy-start(bf16[256,2048]{1,0:T(8,128)(2,1)} %shard_map.57) | copy-start | bytes 3145732
  177.0 23.1 %collective-permute-start.7 = (bf16[256,2048]{1,0:T(8,128)(2,1)}, bf16[256,2048]{1,0:T(8,128)(2,1)S(1)}, u32[]{:S(2)}, u32[]{:S(2)}) collective-permute-start(bf16[256,2048]{1,0:T(8,128)(2,1)} %shard_map.60), channel_id=1, source_target_pairs={{0,1},{1,0},{2,3},{3,2},{4,5},{5,4},{6,7},{7,6},{8,9},{9,8},{10,11... | collective-permute-start | bytes 3145736 | tf_op jit(solution)/shard_map/ppermute | solution.py:379

commit v10 on v7

--- a/solution.py
+++ b/solution.py
@@ -158,15 +158,10 @@
     pos = 0
     for level in levels:
         offset = 2**level
-        n_src = 2 if level == 1 else 1
-        refs = far_refs[pos:pos + 2 * n_src]
-        pos += 2 * n_src
+        refs = far_refs[pos:pos + 2]
+        pos += 2
         k_lvl = refs[0][...]
         v_lvl = refs[1][...]
-        if n_src == 2:
-            odd = meta_ref[1 + per_dev] > 0
-            k_lvl = jnp.where(odd, refs[2][...], k_lvl)
-            v_lvl = jnp.where(odd, refs[3][...], v_lvl)
         keys.append(k_lvl)
         vals.append(v_lvl)
         for k in range(k_lvl.shape[0] // BLOCK):
@@ -243,19 +238,15 @@
             ::offset, level
         ]
         local = jnp.clip(target - device * per_dev, 0, per_dev - 1)
+        levels.append(level)
         if level == 1:
-            pairs = [(s, s + 2) for s in range(0, cycle_size - 2, 2)]
             nxt = lax.dynamic_slice_in_dim(far_blocks, (device + 1) * per_dev, per_dev, 0)[::2, 1]
             fwd_local = jnp.clip(nxt - (device - 1) * per_dev, 0, per_dev - 1)
-        else:
-            pairs = [(s, s + offset) for s in range(0, cycle_size - offset)]
+            continue
+        pairs = [(s, s + offset) for s in range(0, cycle_size - offset)]
         sends.append((pick_blocks(kv_t, local), pairs))
-        levels.append(level)
     q_t, kv_t, *operands = lax.optimization_barrier((q_t, kv_t, *[op for op, _ in sends]))
-    far_arrays = []
-    for (_, pairs), op, level in zip(sends, operands, levels):
-        received = lax.ppermute(op, "ctx", pairs)
-        far_arrays.append((received, None) if level == 1 else (received,))
+    far_arrays = [(lax.ppermute(op, "ctx", pairs),) for (_, pairs), op in zip(sends, operands)]
 
     own = lax.dynamic_slice_in_dim(far_blocks, device * per_dev, per_dev, 0)
     query_index = device * per_dev + jnp.arange(per_dev, dtype=jnp.int32)
@@ -293,12 +284,8 @@
     )(q_t, kv_t, kv_t)
 
     prev_kv, acc0, st0 = lax.optimization_barrier((prev_kv, acc0, st0))
-    if far_arrays and far_arrays[0][1] is None:
-        forwarded = lax.ppermute(
-            pick_blocks(prev_kv, fwd_local), "ctx",
-            [(s, s + 1) for s in range(0, cycle_size - 1, 2)],
-        )
-        far_arrays[0] = (far_arrays[0][0], forwarded)
+    if levels and levels[0] == 1:
+        far_arrays.insert(0, (from_behind(pick_blocks(prev_kv, fwd_local), "ctx", 1),))
     far_specs, far_operands = [], []
     for group in far_arrays:
         for a in group:

time: 177 us -> 170 us (0.960)
  the two profiles are of different devices: /device:TPU:28 before, /device:TPU:23 now
where the time goes in v10:
time: 170 us; the launch traced here: 169 us
  Pallas kernels  70.1 us (41%)
  waiting for transfers between devices  55.2 us (32%)
  local copies, waits for them, and re-layouts  15 us (9%)
  starting transfers between devices  13 us (8%)
  other arithmetic  11.4 us (7%)
  between operations  4.61 us (3%)
    ppermute x2, waiting for transfers between devices, per_device(): lax.ppermute(op, 'ctx', pairs)  30.3 us
    pallas_call x4, Pallas kernels, project_half(): pl.pallas_call(matmul_kernel, out_shape=jax.ShapeDtypeStruct((rows, cw),...  26.5 us
    pallas_call x1, Pallas kernels, per_device(): pl.pallas_call(per_head(functools.partial(prev_kernel, per_dev, width, sc...  20.2 us
    ppermute x2, waiting for transfers between devices, from_behind(): lax.ppermute(value, axis, [(source, source + steps) for source in range(i...  19.6 us
    pallas_call x1, Pallas kernels, per_device(): pl.pallas_call(per_head(functools.partial(own_kernel, per_dev, width, sca...  13 us
    pallas_call x1, Pallas kernels, per_device(): pl.pallas_call(per_head(functools.partial(far_kernel, levels, per_dev, wi...  10.3 us
    ppermute x2, starting transfers between devices, from_behind(): lax.ppermute(value, axis, [(source, source + steps) for source in range(i...  9.06 us
    unnamed x11, local copies, waits for them, and re-layouts  5.82 us
  transfers between devices with their start and end apart: 6, of which 4 were waited for; matrix products, arithmetic and copies ran while one was open for 7% of the time, Pallas kernels for 41%

profile of v10, /device:TPU:23, one launch (start us, length us, event | category | flops | bytes accessed | tf_op | source)
XLA Modules:
  0.0 169.3 jit_solution(5447891153697167697)
XLA Ops:
  0.0 3.3 %copy_bitcast_fusion = (bf16[1,16,512,128]{3,2,1,0:T(8,128)(2,1)S(1)}, bf16[1,16,512,128]{3,2,1,0:T(8,128)(2,1)S(1)}) fusion(bf16[512,16,128]{2,1,0:T(8,128)(2,1)} %param.7, bf16[512,16,128]{2,1,0:T(8,128)(2,1)} %param.6), kind=kLoop, calls=%fused_computation.9 | loop fusion | bytes 8388608 | tf_op jit(solution)/shard_map/stack | solution.py:229
  3.3 2.6 %pad_maximum_fusion.refs_1_.refs_2_ = bf16[2,16,512,128]{3,2,1,0:T(8,128)(2,1)} fusion(bf16[1,16,512,128]{3,2,1,0:T(8,128)(2,1)S(1)} %get-tuple-element.53, bf16[1,16,512,128]{3,2,1,0:T(8,128)(2,1)S(1)} %get-tuple-element.54), kind=kLoop, calls=%fused_computation.3 | loop fusion | flops 2097152 | bytes 8388608 | tf_op jit(solution)/shard_map/stack | solution.py:229
  5.9 3.7 %collective-permute-start = (bf16[2,16,512,128]{3,2,1,0:T(8,128)(2,1)}, bf16[2,16,512,128]{3,2,1,0:T(8,128)(2,1)}, u32[]{:S(2)}, u32[]{:S(2)}) collective-permute-start(bf16[2,16,512,128]{3,2,1,0:T(8,128)(2,1)} %pad_maximum_fusion.refs_1_.refs_2_), channel_id=1, source_target_pairs={{0,2},{2,4},{4,6},{6,8},{8,10},{10,12},{12,14},{14,16},{16,18},{18... | collective-permute-start | bytes 12582920 | tf_op jit(solution)/shard_map/ppermute | solution.py:20
  16.3 3.5 %copy.14 = bf16[512,16,128]{2,0,1:T(8,128)(2,1)} copy(bf16[512,16,128]{2,1,0:T(8,128)(2,1)} %param.5) | data formatting | bytes 4194304 | tf_op args[0]
  19.7 2.0 %fusion.2 = (bf16[2,16,64,128]{3,2,1,0:T(8,128)(2,1)}, bf16[2,16,64,128]{3,2,1,0:T(8,128)(2,1)S(1)}, bf16[2,16,64,128]{3,2,1,0:T(8,128)(2,1)S(1)}) fusion(s32[]{:T(128)S(6)} %select_n.46, bf16[1,16,512,128]{3,2,1,0:T(8,128)(2,1)} %copy-done, bf16[1,16,512,128]{3,2,1,0:T(8,128)(2,1)S(1)} %get-tuple-element.53, s32[]{:T(128)S(6)} %select_n.43, s32[]{:T(128)S(6)} %select_n.44), kind=kLoop, calls=%fused_computation.17 | loop fusion | flops 3145728 | bytes 5767180 | tf_op jit(solution)/shard_map/stack | solution.py:229
  22.8 13.0 %shard_map.55 = (f32[16,512,128]{2,1,0:T(8,128)}, f32[16,512,128]{2,1,0:T(8,128)}) custom-call(bf16[16,512,128]{2,1,0:T(8,128)(2,1)} %bitcast.29, bf16[2,16,512,128]{3,2,1,0:T(8,128)(2,1)} %pad_maximum_fusion.refs_1_.refs_2_, bf16[2,16,512,128]{3,2,1,0:T(8,128)(2,1)} %pad_maximum_fusion.refs_1_.refs_2_), custom_call_target="tpu_custom_call" | custom-call | flops 1073741824 | bytes 29360128 | tf_op jit(solution)/shard_map/pallas_call | solution.py:276
  35.8 19.6 %collective-permute-done.refs_3_.refs_4_ = bf16[2,16,512,128]{3,2,1,0:T(8,128)(2,1)} collective-permute-done((bf16[2,16,512,128]{3,2,1,0:T(8,128)(2,1)}, bf16[2,16,512,128]{3,2,1,0:T(8,128)(2,1)}, u32[]{:S(2)}, u32[]{:S(2)}) %collective-permute-start) | collective-permute-done | bytes 4194336 | tf_op jit(solution)/shard_map/ppermute | solution.py:20
  55.4 1.7 %constant_dynamic-slice_fusion.3 = (bf16[2,16,64,128]{3,2,1,0:T(8,128)(2,1)S(1)}, bf16[2,16,64,128]{3,2,1,0:T(8,128)(2,1)S(1)}, bf16[2,16,64,128]{3,2,1,0:T(8,128)(2,1)S(1)}, bf16[2,16,64,128]{3,2,1,0:T(8,128)(2,1)S(1)}) fusion(bf16[2,16,512,128]{3,2,1,0:T(8,128)(2,1)} %collective-permute-done.refs_3_.refs_4_, s32[]{:T(128)S(6)} %select_n.48, ...), kind=kLoop, calls=%fused_computation.22 | loop fusion | bytes 4194320 | tf_op jit(solution)/shard_map/dynamic_slice | solution.py:217
  57.1 1.5 pad_maximum_fusion.1
  58.6 5.4 %collective-permute-start.1 = (bf16[2,16,256,128]{3,2,1,0:T(8,128)(2,1)}, bf16[2,16,256,128]{3,2,1,0:T(8,128)(2,1)S(1)}, u32[]{:S(2)}, u32[]{:S(2)}) collective-permute-start(bf16[2,16,256,128]{3,2,1,0:T(8,128)(2,1)} %pad_maximum_fusion.1), channel_id=1, source_target_pairs={{0,2},{2,4},{4,6},{6,8},{8,10},{10,12},{12,14},{14,16},{16,18},{18... | collective-permute-start | bytes 6291464 | tf_op jit(solution)/shard_map/ppermute | solution.py:20
  65.3 2.1 %collective-permute-start.2 = (bf16[2,16,128,128]{3,2,1,0:T(8,128)(2,1)}, bf16[2,16,128,128]{3,2,1,0:T(8,128)(2,1)S(1)}, u32[]{:S(2)}, u32[]{:S(2)}) collective-permute-start(bf16[2,16,128,128]{3,2,1,0:T(8,128)(2,1)} %pad_maximum_fusion.3), channel_id=1, source_target_pairs={{0,8},{2,10},{4,12},{6,14},{8,16},{10,18},{12,20},{14,22},{16,24},... | collective-permute-start | bytes 3145736 | tf_op jit(solution)/shard_map/ppermute | solution.py:249
  68.8 20.2 %shard_map.56 = (f32[16,256,128]{2,1,0:T(8,128)}, f32[16,256,128]{2,1,0:T(8,128)}, bf16[256,2048]{1,0:T(8,128)(2,1)}) custom-call(s32[10]{0:T(128)} %pad_add_fusion.refs_0_, s32[40]{0:T(128)} %reshape.81.refs_1_, bf16[16,512,128]{2,1,0:T(8,128)(2,1)} %bitcast.30, bf16[2,16,512,128]{3,2,1,0:T(8,128)(2,1)} %collective-permute-done.refs_3_.refs_4_, ...), custom_call_target="tpu_custom_call" | custom-call | flops 1342177280 | bytes 23068672 | tf_op jit(solution)/shard_map/pallas_call | solution.py:294
  89.0 6.6 %shard_map.61 = bf16[256,2048]{1,0:T(8,128)(2,1)} custom-call(s32[1]{0:T(128)} %bitcast.18.sel_ref, bf16[256,2048]{1,0:T(8,128)(2,1)} %get-tuple-element.29.a_ref, bf16[2048,4096]{1,0:T(8,128)(2,1)} %w_ref.7), custom_call_target="tpu_custom_call" | custom-call | flops 2147483648 | bytes 10485760 | tf_op jit(solution)/shard_map/pallas_call | solution.py:194
  95.9 6.6 %shard_map.57 = bf16[256,2048]{1,0:T(8,128)(2,1)} custom-call(s32[1]{0:T(128)} %bitcast.sel_ref, bf16[256,2048]{1,0:T(8,128)(2,1)} %get-tuple-element.29.a_ref, bf16[2048,4096]{1,0:T(8,128)(2,1)} %w_ref.7), custom_call_target="tpu_custom_call" | custom-call | flops 2147483648 | bytes 10485760 | tf_op jit(solution)/shard_map/pallas_call | solution.py:194
  102.5 7.8 %collective-permute-done.3.refs_9_.refs_10_ = bf16[2,16,64,128]{3,2,1,0:T(8,128)(2,1)} collective-permute-done((bf16[2,16,64,128]{3,2,1,0:T(8,128)(2,1)}, bf16[2,16,64,128]{3,2,1,0:T(8,128)(2,1)}, u32[]{:S(2)}, u32[]{:S(2)}) %collective-permute-start.3) | collective-permute-done | bytes 524320 | tf_op jit(solution)/shard_map/ppermute | solution.py:249
  110.3 22.5 %collective-permute-done.2.refs_7_.refs_8_ = bf16[2,16,128,128]{3,2,1,0:T(8,128)(2,1)S(1)} collective-permute-done((bf16[2,16,128,128]{3,2,1,0:T(8,128)(2,1)}, bf16[2,16,128,128]{3,2,1,0:T(8,128)(2,1)S(1)}, u32[]{:S(2)}, u32[]{:S(2)}) %collective-permute-start.2) | collective-permute-done | bytes 1048608 | tf_op jit(solution)/shard_map/ppermute | solution.py:249
  133.8 1.3 copy-done.1
  135.1 10.3 %shard_map.58.a_ref = bf16[256,2048]{1,0:T(8,128)(2,1)} custom-call(s32[10]{0:T(128)} %pad_add_fusion.refs_0_, s32[40]{0:T(128)} %reshape.81.refs_1_, bf16[16,512,128]{2,1,0:T(8,128)(2,1)} %bitcast.31, f32[16,256,128]{2,1,0:T(8,128)} %get-tuple-element.30.refs_3_, f32[16,256,128]{2,1,0:T(8,128)} %get-tuple-element.31.refs_4_, ...), custom_call_target="tpu_custom_call" | custom-call | flops 268435456 | bytes 9961472 | tf_op jit(solution)/shard_map/pallas_call | solution.py:338
  145.4 6.7 %shard_map.60 = bf16[256,2048]{1,0:T(8,128)(2,1)} custom-call(s32[1]{0:T(128)} %bitcast.18.sel_ref, bf16[256,2048]{1,0:T(8,128)(2,1)} %shard_map.58.a_ref, bf16[2048,4096]{1,0:T(8,128)(2,1)} %w_ref.7), custom_call_target="tpu_custom_call" | custom-call | flops 2147483648 | bytes 10485760 | tf_op jit(solution)/shard_map/pallas_call | solution.py:194
  152.4 1.6 add_convert_fusion
  154.0 6.6 %shard_map.59 = bf16[256,2048]{1,0:T(8,128)(2,1)} custom-call(s32[1]{0:T(128)} %bitcast.sel_ref, bf16[256,2048]{1,0:T(8,128)(2,1)} %shard_map.58.a_ref, bf16[2048,4096]{1,0:T(8,128)(2,1)} %w_ref.7), custom_call_target="tpu_custom_call" | custom-call | flops 2147483648 | bytes 10485760 | tf_op jit(solution)/shard_map/pallas_call | solution.py:194
  160.6 5.4 %collective-permute-done.4 = bf16[256,2048]{1,0:T(8,128)(2,1)S(1)} collective-permute-done((bf16[256,2048]{1,0:T(8,128)(2,1)}, bf16[256,2048]{1,0:T(8,128)(2,1)S(1)}, u32[]{:S(2)}, u32[]{:S(2)}) %collective-permute-start.4) | collective-permute-done | bytes 1048608 | tf_op jit(solution)/shard_map/ppermute | solution.py:351
  166.0 1.6 add_convert_fusion.1
  167.8 1.5 copy.10
  (30 shorter events, 7.6 us)
Async XLA Ops:
  3.3 2.6 %copy-start = (bf16[1,16,512,128]{3,2,1,0:T(8,128)(2,1)}, bf16[1,16,512,128]{3,2,1,0:T(8,128)(2,1)S(1)}, u32[]{:S(2)}) copy-start(bf16[1,16,512,128]{3,2,1,0:T(8,128)(2,1)S(1)} %get-tuple-element.54) | copy-start | bytes 6291460
  3.3 6.4 %copy-start.4 = (s32[128,5]{0,1:T(8,128)S(1)}, s32[128,5]{0,1:T(8,128)}, u32[]{:S(2)}) copy-start(s32[128,5]{0,1:T(8,128)} %param.8) | copy-start | bytes 7684
  5.9 49.4 %collective-permute-start = (bf16[2,16,512,128]{3,2,1,0:T(8,128)(2,1)}, bf16[2,16,512,128]{3,2,1,0:T(8,128)(2,1)}, u32[]{:S(2)}, u32[]{:S(2)}) collective-permute-start(bf16[2,16,512,128]{3,2,1,0:T(8,128)(2,1)} %pad_maximum_fusion.refs_1_.refs_2_), channel_id=1, source_target_pairs={{0,2},{2,4},{4,6},{6,8},{8,10},{10,12},{12,14},{14,16},{16,18},{18... | collective-permute-start | bytes 12582920 | tf_op jit(solution)/shard_map/ppermute | solution.py:20
  58.6 74.2 %collective-permute-start.1 = (bf16[2,16,256,128]{3,2,1,0:T(8,128)(2,1)}, bf16[2,16,256,128]{3,2,1,0:T(8,128)(2,1)S(1)}, u32[]{:S(2)}, u32[]{:S(2)}) collective-permute-start(bf16[2,16,256,128]{3,2,1,0:T(8,128)(2,1)} %pad_maximum_fusion.1), channel_id=1, source_target_pairs={{0,2},{2,4},{4,6},{6,8},{8,10},{10,12},{12,14},{14,16},{16,18},{18... | collective-permute-start | bytes 6291464 | tf_op jit(solution)/shard_map/ppermute | solution.py:20
  64.0 46.3 %collective-permute-start.3 = (bf16[2,16,64,128]{3,2,1,0:T(8,128)(2,1)}, bf16[2,16,64,128]{3,2,1,0:T(8,128)(2,1)}, u32[]{:S(2)}, u32[]{:S(2)}) collective-permute-start(bf16[2,16,64,128]{3,2,1,0:T(8,128)(2,1)} %get-tuple-element.33), channel_id=1, source_target_pairs={{0,16},{2,18},{4,20},{6,22},{8,24},{10,26},{12,28},{14,30},{1,17},... | collective-permute-start | bytes 1572872 | tf_op jit(solution)/shard_map/ppermute | solution.py:249
  65.3 67.5 %collective-permute-start.2 = (bf16[2,16,128,128]{3,2,1,0:T(8,128)(2,1)}, bf16[2,16,128,128]{3,2,1,0:T(8,128)(2,1)S(1)}, u32[]{:S(2)}, u32[]{:S(2)}) collective-permute-start(bf16[2,16,128,128]{3,2,1,0:T(8,128)(2,1)} %pad_maximum_fusion.3), channel_id=1, source_target_pairs={{0,8},{2,10},{4,12},{6,14},{8,16},{10,18},{12,20},{14,22},{16,24},... | collective-permute-start | bytes 3145736 | tf_op jit(solution)/shard_map/ppermute | solution.py:249
  95.6 56.8 %collective-permute-start.5 = (bf16[256,2048]{1,0:T(8,128)(2,1)}, bf16[256,2048]{1,0:T(8,128)(2,1)}, u32[]{:S(2)}, u32[]{:S(2)}) collective-permute-start(bf16[256,2048]{1,0:T(8,128)(2,1)} %shard_map.61), channel_id=1, source_target_pairs={{0,1},{1,0},{2,3},{3,2},{4,5},{5,4},{6,7},{7,6},{8,9},{9,8},{10,11... | collective-permute-start | bytes 3145736 | tf_op jit(solution)/shard_map/ppermute | solution.py:335
  132.8 1.0 copy-start.2
  133.8 1.3 copy-start.1
  145.4 6.9 %copy-start.3 = (bf16[256,2048]{1,0:T(8,128)(2,1)S(1)}, bf16[256,2048]{1,0:T(8,128)(2,1)}, u32[]{:S(2)}) copy-start(bf16[256,2048]{1,0:T(8,128)(2,1)} %shard_map.57) | copy-start | bytes 3145732
  152.1 13.9 %collective-permute-start.4 = (bf16[256,2048]{1,0:T(8,128)(2,1)}, bf16[256,2048]{1,0:T(8,128)(2,1)S(1)}, u32[]{:S(2)}, u32[]{:S(2)}) collective-permute-start(bf16[256,2048]{1,0:T(8,128)(2,1)} %shard_map.60), channel_id=1, source_target_pairs={{0,1},{1,0},{2,3},{3,2},{4,5},{5,4},{6,7},{7,6},{8,9},{9,8},{10,11... | collective-permute-start | bytes 3145736 | tf_op jit(solution)/shard_map/ppermute | solution.py:351

commit v11 on v8

--- a/solution.py
+++ b/solution.py
@@ -11,7 +11,7 @@
 BLOCK = 64
 WINDOW = 512
 NOFF = 5
-HEADS_PER_STEP = 4
+HEADS_PER_STEP = 8
 
 
 def from_behind(value, axis, steps):

time: 168 us -> 169 us (level)
  Pallas kernels: 70.3 us -> 72.9 us
  waiting for transfers between devices: 49.2 us -> 47.3 us
  transfers between devices with their start and end apart: 7 -> 7, of which waited for: 3 -> 3; matrix products, arithmetic and copies ran while one was open for 11% -> 11% of each run, Pallas kernels for 42% -> 43%
where the time goes in v11:
time: 169 us; the launch traced here: 168 us
  Pallas kernels  72.9 us (43%)
  waiting for transfers between devices  47.3 us (28%)
  local copies, waits for them, and re-layouts  15.6 us (9%)
  other arithmetic  13.7 us (8%)
  starting transfers between devices  11.6 us (7%)
  between operations  6.92 us (4%)
    pallas_call x4, Pallas kernels, project_half(): pl.pallas_call(matmul_kernel, out_shape=jax.ShapeDtypeStruct((rows, cw),...  26.5 us
    ppermute x2, waiting for transfers between devices, per_device(): far_arrays.append((lax.ppermute(op, 'ctx', pairs),))  26.5 us
    pallas_call x1, Pallas kernels, per_device(): pl.pallas_call(per_head(functools.partial(prev_kernel, per_dev, width, sc...  21.2 us
    ppermute x1, waiting for transfers between devices, from_behind(): lax.ppermute(value, axis, [(source, source + steps) for source in range(i...  15.6 us
    pallas_call x1, Pallas kernels, per_device(): pl.pallas_call(per_head(functools.partial(own_kernel, per_dev, width, sca...  13.8 us
    pallas_call x1, Pallas kernels, per_device(): pl.pallas_call(per_head(functools.partial(far_kernel, levels, per_dev, wi...  11.3 us
    unnamed x13, local copies, waits for them, and re-layouts  5.65 us
    another operation x3, other arithmetic, per_device(): jnp.stack([jnp.transpose(keys, (1, 0, 2)), jnp.transpose(values, (1, 0, 2...  5.37 us
  transfers between devices with their start and end apart: 7, of which 3 were waited for; matrix products, arithmetic and copies ran while one was open for 11% of the time, Pallas kernels for 43%

profile of v11, /device:TPU:28, one launch (start us, length us, event | category | flops | bytes accessed | tf_op | source)
XLA Modules:
  0.0 167.9 jit_solution(1770519242473786708)
XLA Ops:
  0.0 3.3 %copy_bitcast_fusion = (bf16[1,16,512,128]{3,2,1,0:T(8,128)(2,1)S(1)}, bf16[1,16,512,128]{3,2,1,0:T(8,128)(2,1)S(1)}) fusion(bf16[512,16,128]{2,1,0:T(8,128)(2,1)} %param.7, bf16[512,16,128]{2,1,0:T(8,128)(2,1)} %param.6), kind=kLoop, calls=%fused_computation.18 | loop fusion | bytes 8388608 | tf_op jit(solution)/shard_map/stack | solution.py:234
  3.3 2.6 %pad_maximum_fusion.refs_1_.refs_2_ = bf16[2,16,512,128]{3,2,1,0:T(8,128)(2,1)} fusion(bf16[1,16,512,128]{3,2,1,0:T(8,128)(2,1)S(1)} %get-tuple-element.67, bf16[1,16,512,128]{3,2,1,0:T(8,128)(2,1)S(1)} %get-tuple-element.68), kind=kLoop, calls=%fused_computation.7 | loop fusion | flops 2097152 | bytes 8388608 | tf_op jit(solution)/shard_map/stack | solution.py:234
  6.0 1.9 %collective-permute-start = (bf16[2,16,512,128]{3,2,1,0:T(8,128)(2,1)}, bf16[2,16,512,128]{3,2,1,0:T(8,128)(2,1)}, u32[]{:S(2)}, u32[]{:S(2)}) collective-permute-start(bf16[2,16,512,128]{3,2,1,0:T(8,128)(2,1)} %pad_maximum_fusion.refs_1_.refs_2_), channel_id=1, source_target_pairs={{0,2},{2,4},{4,6},{6,8},{8,10},{10,12},{12,14},{14,16},{16,18},{18... | collective-permute-start | bytes 12582920 | tf_op jit(solution)/shard_map/ppermute | solution.py:20
  17.4 3.5 %copy.14 = bf16[512,16,128]{2,0,1:T(8,128)(2,1)} copy(bf16[512,16,128]{2,1,0:T(8,128)(2,1)} %param.5) | data formatting | bytes 4194304 | tf_op args[0]
  22.5 1.6 fusion.6
  25.2 1.5 pad_maximum_fusion.1
  26.7 13.8 %shard_map.55 = (f32[16,512,128]{2,1,0:T(8,128)}, f32[16,512,128]{2,1,0:T(8,128)}) custom-call(bf16[16,512,128]{2,1,0:T(8,128)(2,1)} %bitcast.33, bf16[2,16,512,128]{3,2,1,0:T(8,128)(2,1)} %pad_maximum_fusion.refs_1_.refs_2_, bf16[2,16,512,128]{3,2,1,0:T(8,128)(2,1)} %pad_maximum_fusion.refs_1_.refs_2_), custom_call_target="tpu_custom_call" | custom-call | flops 1073741824 | bytes 29360128 | tf_op jit(solution)/shard_map/pallas_call | solution.py:287
  40.5 15.6 %collective-permute-done.refs_3_.refs_4_ = bf16[2,16,512,128]{3,2,1,0:T(8,128)(2,1)} collective-permute-done((bf16[2,16,512,128]{3,2,1,0:T(8,128)(2,1)}, bf16[2,16,512,128]{3,2,1,0:T(8,128)(2,1)}, u32[]{:S(2)}, u32[]{:S(2)}) %collective-permute-start) | collective-permute-done | bytes 4194336 | tf_op jit(solution)/shard_map/ppermute | solution.py:20
  57.4 1.7 %constant_dynamic-slice_fusion.3 = (bf16[2,16,64,128]{3,2,1,0:T(8,128)(2,1)S(1)}, bf16[2,16,64,128]{3,2,1,0:T(8,128)(2,1)S(1)}, bf16[2,16,64,128]{3,2,1,0:T(8,128)(2,1)S(1)}, bf16[2,16,64,128]{3,2,1,0:T(8,128)(2,1)S(1)}) fusion(bf16[2,16,512,128]{3,2,1,0:T(8,128)(2,1)} %collective-permute-done.refs_3_.refs_4_, s32[]{:T(128)S(6)} %select_n.68, ...), kind=kLoop, calls=%fused_computation.34 | loop fusion | bytes 4194320 | tf_op jit(solution)/shard_map/dynamic_slice | solution.py:222
  59.1 1.6 pad_maximum_fusion.2
  60.7 2.6 %collective-permute-start.2 = (bf16[2,16,256,128]{3,2,1,0:T(8,128)(2,1)}, bf16[2,16,256,128]{3,2,1,0:T(8,128)(2,1)}, u32[]{:S(2)}, u32[]{:S(2)}) collective-permute-start(bf16[2,16,256,128]{3,2,1,0:T(8,128)(2,1)} %pad_maximum_fusion.2), channel_id=1, source_target_pairs={{0,2},{4,6},{8,10},{12,14},{16,18},{20,22},{24,26},{28,30},{1,3},{... | collective-permute-start | bytes 6291464 | tf_op jit(solution)/shard_map/ppermute | solution.py:301
  64.6 1.5 collective-permute-start.4
  67.6 21.2 %shard_map.56 = (f32[16,256,128]{2,1,0:T(8,128)}, f32[16,256,128]{2,1,0:T(8,128)}, bf16[256,2048]{1,0:T(8,128)(2,1)}) custom-call(s32[10]{0:T(128)} %pad_add_fusion.refs_0_, s32[40]{0:T(128)} %reshape.110.refs_1_, bf16[16,512,128]{2,1,0:T(8,128)(2,1)} %bitcast.34, bf16[2,16,512,128]{3,2,1,0:T(8,128)(2,1)} %collective-permute-done.refs_3_.refs_4_, ...), custom_call_target="tpu_custom_call" | custom-call | flops 1342177280 | bytes 23068672 | tf_op jit(solution)/shard_map/pallas_call | solution.py:313
  88.8 6.6 %shard_map.61 = bf16[256,2048]{1,0:T(8,128)(2,1)} custom-call(s32[1]{0:T(128)} %bitcast.22.sel_ref, bf16[256,2048]{1,0:T(8,128)(2,1)} %get-tuple-element.32.a_ref, bf16[2048,4096]{1,0:T(8,128)(2,1)} %w_ref.7), custom_call_target="tpu_custom_call" | custom-call | flops 2147483648 | bytes 10485760 | tf_op jit(solution)/shard_map/pallas_call | solution.py:199
  95.4 1.5 collective-permute-start.6
  96.9 6.6 %shard_map.57 = bf16[256,2048]{1,0:T(8,128)(2,1)} custom-call(s32[1]{0:T(128)} %bitcast.sel_ref, bf16[256,2048]{1,0:T(8,128)(2,1)} %get-tuple-element.32.a_ref, bf16[2048,4096]{1,0:T(8,128)(2,1)} %w_ref.7), custom_call_target="tpu_custom_call" | custom-call | flops 2147483648 | bytes 10485760 | tf_op jit(solution)/shard_map/pallas_call | solution.py:199
  103.5 26.5 %collective-permute-done.4.refs_11_.refs_12_ = bf16[2,16,64,128]{3,2,1,0:T(8,128)(2,1)} collective-permute-done((bf16[2,16,64,128]{3,2,1,0:T(8,128)(2,1)}, bf16[2,16,64,128]{3,2,1,0:T(8,128)(2,1)}, u32[]{:S(2)}, u32[]{:S(2)}) %collective-permute-start.4) | collective-permute-done | bytes 524320 | tf_op jit(solution)/shard_map/ppermute | solution.py:260
  131.7 11.3 %shard_map.58.a_ref = bf16[256,2048]{1,0:T(8,128)(2,1)} custom-call(s32[10]{0:T(128)} %pad_add_fusion.refs_0_, s32[40]{0:T(128)} %reshape.110.refs_1_, bf16[16,512,128]{2,1,0:T(8,128)(2,1)} %bitcast.35, f32[16,256,128]{2,1,0:T(8,128)} %get-tuple-element.33.refs_3_, f32[16,256,128]{2,1,0:T(8,128)} %get-tuple-element.34.refs_4_, ...), custom_call_target="tpu_custom_call" | custom-call | flops 268435456 | bytes 12058624 | tf_op jit(solution)/shard_map/pallas_call | solution.py:357
  142.9 6.7 %shard_map.60 = bf16[256,2048]{1,0:T(8,128)(2,1)} custom-call(s32[1]{0:T(128)} %bitcast.22.sel_ref, bf16[256,2048]{1,0:T(8,128)(2,1)} %shard_map.58.a_ref, bf16[2048,4096]{1,0:T(8,128)(2,1)} %w_ref.7), custom_call_target="tpu_custom_call" | custom-call | flops 2147483648 | bytes 10485760 | tf_op jit(solution)/shard_map/pallas_call | solution.py:199
  149.6 1.5 collective-permute-start.5
  151.1 1.6 add_convert_fusion
  152.8 6.6 %shard_map.59 = bf16[256,2048]{1,0:T(8,128)(2,1)} custom-call(s32[1]{0:T(128)} %bitcast.sel_ref, bf16[256,2048]{1,0:T(8,128)(2,1)} %shard_map.58.a_ref, bf16[2048,4096]{1,0:T(8,128)(2,1)} %w_ref.7), custom_call_target="tpu_custom_call" | custom-call | flops 2147483648 | bytes 10485760 | tf_op jit(solution)/shard_map/pallas_call | solution.py:199
  159.4 5.3 %collective-permute-done.5 = bf16[256,2048]{1,0:T(8,128)(2,1)S(1)} collective-permute-done((bf16[256,2048]{1,0:T(8,128)(2,1)}, bf16[256,2048]{1,0:T(8,128)(2,1)S(1)}, u32[]{:S(2)}, u32[]{:S(2)}) %collective-permute-start.5) | collective-permute-done | bytes 1048608 | tf_op jit(solution)/shard_map/ppermute | solution.py:370
  164.7 1.6 add_convert_fusion.1
  (38 shorter events, 12.8 us)
Async XLA Ops:
  3.3 2.7 %copy-start = (bf16[1,16,512,128]{3,2,1,0:T(8,128)(2,1)}, bf16[1,16,512,128]{3,2,1,0:T(8,128)(2,1)S(1)}, u32[]{:S(2)}) copy-start(bf16[1,16,512,128]{3,2,1,0:T(8,128)(2,1)S(1)} %get-tuple-element.68) | copy-start | bytes 6291460
  3.3 4.6 %copy-start.5 = (s32[128,5]{0,1:T(8,128)S(1)}, s32[128,5]{0,1:T(8,128)}, u32[]{:S(2)}) copy-start(s32[128,5]{0,1:T(8,128)} %param.8) | copy-start | bytes 7684
  6.0 50.1 %collective-permute-start = (bf16[2,16,512,128]{3,2,1,0:T(8,128)(2,1)}, bf16[2,16,512,128]{3,2,1,0:T(8,128)(2,1)}, u32[]{:S(2)}, u32[]{:S(2)}) collective-permute-start(bf16[2,16,512,128]{3,2,1,0:T(8,128)(2,1)} %pad_maximum_fusion.refs_1_.refs_2_), channel_id=1, source_target_pairs={{0,2},{2,4},{4,6},{6,8},{8,10},{10,12},{12,14},{14,16},{16,18},{18... | collective-permute-start | bytes 12582920 | tf_op jit(solution)/shard_map/ppermute | solution.py:20
  20.9 1.7 copy-start.1
  56.1 73.9 %collective-permute-start.1 = (bf16[2,16,256,128]{3,2,1,0:T(8,128)(2,1)}, bf16[2,16,256,128]{3,2,1,0:T(8,128)(2,1)S(1)}, u32[]{:S(2)}, u32[]{:S(2)}) collective-permute-start(bf16[2,16,256,128]{3,2,1,0:T(8,128)(2,1)} %pad_maximum_fusion.1), channel_id=1, source_target_pairs={{0,4},{4,8},{8,12},{12,16},{16,20},{20,24},{24,28},{1,5},{5,9},{9,... | collective-permute-start | bytes 6291464 | tf_op jit(solution)/shard_map/ppermute | solution.py:300
  60.7 69.3 %collective-permute-start.2 = (bf16[2,16,256,128]{3,2,1,0:T(8,128)(2,1)}, bf16[2,16,256,128]{3,2,1,0:T(8,128)(2,1)}, u32[]{:S(2)}, u32[]{:S(2)}) collective-permute-start(bf16[2,16,256,128]{3,2,1,0:T(8,128)(2,1)} %pad_maximum_fusion.2), channel_id=1, source_target_pairs={{0,2},{4,6},{8,10},{12,14},{16,18},{20,22},{24,26},{28,30},{1,3},{... | collective-permute-start | bytes 6291464 | tf_op jit(solution)/shard_map/ppermute | solution.py:301
  63.3 66.7 %collective-permute-start.3 = (bf16[2,16,128,128]{3,2,1,0:T(8,128)(2,1)}, bf16[2,16,128,128]{3,2,1,0:T(8,128)(2,1)S(1)}, u32[]{:S(2)}, u32[]{:S(2)}) collective-permute-start(bf16[2,16,128,128]{3,2,1,0:T(8,128)(2,1)} %pad_maximum_fusion.4), channel_id=1, source_target_pairs={{0,8},{2,10},{4,12},{6,14},{8,16},{10,18},{12,20},{14,22},{16,24},... | collective-permute-start | bytes 3145736 | tf_op jit(solution)/shard_map/ppermute | solution.py:260
  64.6 65.4 %collective-permute-start.4 = (bf16[2,16,64,128]{3,2,1,0:T(8,128)(2,1)}, bf16[2,16,64,128]{3,2,1,0:T(8,128)(2,1)}, u32[]{:S(2)}, u32[]{:S(2)}) collective-permute-start(bf16[2,16,64,128]{3,2,1,0:T(8,128)(2,1)} %get-tuple-element.37), channel_id=1, source_target_pairs={{0,16},{2,18},{4,20},{6,22},{8,24},{10,26},{12,28},{14,30},{1,17},... | collective-permute-start | bytes 1572872 | tf_op jit(solution)/shard_map/ppermute | solution.py:260
  95.4 55.7 %collective-permute-start.6 = (bf16[256,2048]{1,0:T(8,128)(2,1)}, bf16[256,2048]{1,0:T(8,128)(2,1)}, u32[]{:S(2)}, u32[]{:S(2)}) collective-permute-start(bf16[256,2048]{1,0:T(8,128)(2,1)} %shard_map.61), channel_id=1, source_target_pairs={{0,1},{1,0},{2,3},{3,2},{4,5},{5,4},{6,7},{7,6},{8,9},{9,8},{10,11... | collective-permute-start | bytes 3145736 | tf_op jit(solution)/shard_map/ppermute | solution.py:354
  130.0 1.0 copy-start.3
  130.0 1.6 copy-start.2
  142.9 8.2 %copy-start.4 = (bf16[256,2048]{1,0:T(8,128)(2,1)S(1)}, bf16[256,2048]{1,0:T(8,128)(2,1)}, u32[]{:S(2)}) copy-start(bf16[256,2048]{1,0:T(8,128)(2,1)} %shard_map.57) | copy-start | bytes 3145732
  149.6 15.0 %collective-permute-start.5 = (bf16[256,2048]{1,0:T(8,128)(2,1)}, bf16[256,2048]{1,0:T(8,128)(2,1)S(1)}, u32[]{:S(2)}, u32[]{:S(2)}) collective-permute-start(bf16[256,2048]{1,0:T(8,128)(2,1)} %shard_map.60), channel_id=1, source_target_pairs={{0,1},{1,0},{2,3},{3,2},{4,5},{5,4},{6,7},{7,6},{8,9},{9,8},{10,11... | collective-permute-start | bytes 3145736 | tf_op jit(solution)/shard_map/ppermute | solution.py:370

commit v12 on v8

--- a/solution.py
+++ b/solution.py
@@ -120,23 +120,22 @@
     per_tile = TILE // BLOCK
     for lo in range(0, rows, TILE):
         q = q_ref[lo:lo + TILE, :]
-        n_prev = rows - lo
-        s_p = block_scores(q, kp_ref[lo:, :], scale)
-        r_ids = lax.broadcasted_iota(jnp.int32, (TILE, n_prev), 0)
-        c_ids = lax.broadcasted_iota(jnp.int32, (TILE, n_prev), 1)
-        s_p = jnp.where((c_ids > r_ids) & prev_ok, s_p, neg)
+        s_p = block_scores(q, kp_ref[...], scale)
+        r_ids = lax.broadcasted_iota(jnp.int32, (TILE, rows), 0)
+        c_ids = lax.broadcasted_iota(jnp.int32, (TILE, rows), 1)
         blocks = range(lo // BLOCK, lo // BLOCK + per_tile)
-        starts = [pl.multiple_of(meta_ref[1 + i] * BLOCK, BLOCK) for i in blocks]
-        k0 = jnp.concatenate([kp_ref[pl.ds(st, BLOCK), :] for st in starts], axis=0)
-        v0 = jnp.concatenate([vp_ref[pl.ds(st, BLOCK), :] for st in starts], axis=0)
-        s_f = block_scores(q, k0, scale)
-        flags = column_map(TILE, [used_ref[i * NOFF] for i in blocks])
-        r_blk = lax.broadcasted_iota(jnp.int32, (TILE, TILE), 0) // BLOCK
-        c_blk = lax.broadcasted_iota(jnp.int32, (TILE, TILE), 1) // BLOCK
-        s_f = jnp.where((r_blk == c_blk) & (flags > 0), s_f, neg)
+        r_blk = lax.broadcasted_iota(jnp.int32, (TILE, 1), 0) // BLOCK
+        row_pick = jnp.zeros((TILE, 1), jnp.int32)
+        row_used = jnp.zeros((TILE, 1), jnp.int32)
+        for b, i in enumerate(blocks):
+            row_pick = jnp.where(r_blk == b, meta_ref[1 + i], row_pick)
+            row_used = jnp.where(r_blk == b, used_ref[i * NOFF], row_used)
+        in_window = (c_ids > r_ids + lo) & prev_ok
+        far_zero = ((c_ids // BLOCK) == row_pick) & (row_used > 0)
+        s_p = jnp.where(in_window | far_zero, s_p, neg)
         st = st_ref[lo:lo + TILE, :]
         m, l, acc = merge(
-            [(s_p, vp_ref[lo:, :]), (s_f, v0)], st[:, 0:1], st[:, 1:2], acc_ref[lo:lo + TILE, :]
+            [(s_p, vp_ref[...])], st[:, 0:1], st[:, 1:2], acc_ref[lo:lo + TILE, :]
         )
         for b, i in enumerate(blocks):
             sl = slice(b * BLOCK, (b + 1) * BLOCK)

time: 168 us -> 168 us (level)
  Pallas kernels: 70.3 us -> 68.1 us
  waiting for transfers between devices: 49.2 us -> 51.4 us
    pallas_call x1, Pallas kernels: 20.1 us -> 17.9 us  [per_device(): pl.pallas_call(per_head(functools.partial(prev_kernel, per_dev, width, sc...]
    ppermute x2, waiting for transfers between devices: 27.6 us -> 29.8 us  [per_device(): far_arrays.append((lax.ppermute(op, 'ctx', pairs),))]
  transfers between devices with their start and end apart: 7 -> 7, of which waited for: 3 -> 3; matrix products, arithmetic and copies ran while one was open for 11% -> 11% of each run, Pallas kernels for 42% -> 41%
where the time goes in v12:
time: 168 us; the launch traced here: 167 us
  Pallas kernels  68.1 us (41%)
  waiting for transfers between devices  51.4 us (31%)
  local copies, waits for them, and re-layouts  15.6 us (9%)
  other arithmetic  13.7 us (8%)
  starting transfers between devices  11.5 us (7%)
  between operations  6.92 us (4%)
    ppermute x2, waiting for transfers between devices, per_device(): far_arrays.append((lax.ppermute(op, 'ctx', pairs),))  29.8 us
    pallas_call x4, Pallas kernels, project_half(): pl.pallas_call(matmul_kernel, out_shape=jax.ShapeDtypeStruct((rows, cw),...  26.5 us
    pallas_call x1, Pallas kernels, per_device(): pl.pallas_call(per_head(functools.partial(prev_kernel, per_dev, width, sc...  17.9 us
    ppermute x1, waiting for transfers between devices, from_behind(): lax.ppermute(value, axis, [(source, source + steps) for source in range(i...  16.3 us
    pallas_call x1, Pallas kernels, per_device(): pl.pallas_call(per_head(functools.partial(own_kernel, per_dev, width, sca...  13.1 us
    pallas_call x1, Pallas kernels, per_device(): pl.pallas_call(per_head(functools.partial(far_kernel, levels, per_dev, wi...  10.6 us
    unnamed x13, local copies, waits for them, and re-layouts  5.65 us
    another operation x3, other arithmetic, per_device(): jnp.stack([jnp.transpose(keys, (1, 0, 2)), jnp.transpose(values, (1, 0, 2...  5.37 us
  transfers between devices with their start and end apart: 7, of which 3 were waited for; matrix products, arithmetic and copies ran while one was open for 11% of the time, Pallas kernels for 41%

profile of v12, /device:TPU:28, one launch (start us, length us, event | category | flops | bytes accessed | tf_op | source)
XLA Modules:
  0.0 167.2 jit_solution(17063115944118747141)
XLA Ops:
  0.0 3.3 %copy_bitcast_fusion = (bf16[1,16,512,128]{3,2,1,0:T(8,128)(2,1)S(1)}, bf16[1,16,512,128]{3,2,1,0:T(8,128)(2,1)S(1)}) fusion(bf16[512,16,128]{2,1,0:T(8,128)(2,1)} %param.7, bf16[512,16,128]{2,1,0:T(8,128)(2,1)} %param.6), kind=kLoop, calls=%fused_computation.18 | loop fusion | bytes 8388608 | tf_op jit(solution)/shard_map/stack | solution.py:233
  3.3 2.6 %pad_maximum_fusion.refs_1_.refs_2_ = bf16[2,16,512,128]{3,2,1,0:T(8,128)(2,1)} fusion(bf16[1,16,512,128]{3,2,1,0:T(8,128)(2,1)S(1)} %get-tuple-element.67, bf16[1,16,512,128]{3,2,1,0:T(8,128)(2,1)S(1)} %get-tuple-element.68), kind=kLoop, calls=%fused_computation.7 | loop fusion | flops 2097152 | bytes 8388608 | tf_op jit(solution)/shard_map/stack | solution.py:233
  6.0 1.9 %collective-permute-start = (bf16[2,16,512,128]{3,2,1,0:T(8,128)(2,1)}, bf16[2,16,512,128]{3,2,1,0:T(8,128)(2,1)}, u32[]{:S(2)}, u32[]{:S(2)}) collective-permute-start(bf16[2,16,512,128]{3,2,1,0:T(8,128)(2,1)} %pad_maximum_fusion.refs_1_.refs_2_), channel_id=1, source_target_pairs={{0,2},{2,4},{4,6},{6,8},{8,10},{10,12},{12,14},{14,16},{16,18},{18... | collective-permute-start | bytes 12582920 | tf_op jit(solution)/shard_map/ppermute | solution.py:20
  17.4 3.5 %copy.14 = bf16[512,16,128]{2,0,1:T(8,128)(2,1)} copy(bf16[512,16,128]{2,1,0:T(8,128)(2,1)} %param.5) | data formatting | bytes 4194304 | tf_op args[0]
  22.5 1.6 fusion.6
  25.2 1.5 pad_maximum_fusion.1
  26.7 13.1 %shard_map.55 = (f32[16,512,128]{2,1,0:T(8,128)}, f32[16,512,128]{2,1,0:T(8,128)}) custom-call(bf16[16,512,128]{2,1,0:T(8,128)(2,1)} %bitcast.33, bf16[2,16,512,128]{3,2,1,0:T(8,128)(2,1)} %pad_maximum_fusion.refs_1_.refs_2_, bf16[2,16,512,128]{3,2,1,0:T(8,128)(2,1)} %pad_maximum_fusion.refs_1_.refs_2_), custom_call_target="tpu_custom_call" | custom-call | flops 1073741824 | bytes 29360128 | tf_op jit(solution)/shard_map/pallas_call | solution.py:286
  39.8 16.3 %collective-permute-done.refs_3_.refs_4_ = bf16[2,16,512,128]{3,2,1,0:T(8,128)(2,1)} collective-permute-done((bf16[2,16,512,128]{3,2,1,0:T(8,128)(2,1)}, bf16[2,16,512,128]{3,2,1,0:T(8,128)(2,1)}, u32[]{:S(2)}, u32[]{:S(2)}) %collective-permute-start) | collective-permute-done | bytes 4194336 | tf_op jit(solution)/shard_map/ppermute | solution.py:20
  57.4 1.7 %constant_dynamic-slice_fusion.3 = (bf16[2,16,64,128]{3,2,1,0:T(8,128)(2,1)S(1)}, bf16[2,16,64,128]{3,2,1,0:T(8,128)(2,1)S(1)}, bf16[2,16,64,128]{3,2,1,0:T(8,128)(2,1)S(1)}, bf16[2,16,64,128]{3,2,1,0:T(8,128)(2,1)S(1)}) fusion(bf16[2,16,512,128]{3,2,1,0:T(8,128)(2,1)} %collective-permute-done.refs_3_.refs_4_, s32[]{:T(128)S(6)} %select_n.68, ...), kind=kLoop, calls=%fused_computation.34 | loop fusion | bytes 4194320 | tf_op jit(solution)/shard_map/dynamic_slice | solution.py:221
  59.1 1.6 pad_maximum_fusion.2
  60.7 2.6 %collective-permute-start.2 = (bf16[2,16,256,128]{3,2,1,0:T(8,128)(2,1)}, bf16[2,16,256,128]{3,2,1,0:T(8,128)(2,1)}, u32[]{:S(2)}, u32[]{:S(2)}) collective-permute-start(bf16[2,16,256,128]{3,2,1,0:T(8,128)(2,1)} %pad_maximum_fusion.2), channel_id=1, source_target_pairs={{0,2},{4,6},{8,10},{12,14},{16,18},{20,22},{24,26},{28,30},{1,3},{... | collective-permute-start | bytes 6291464 | tf_op jit(solution)/shard_map/ppermute | solution.py:300
  64.6 1.5 collective-permute-start.4
  67.6 17.9 %shard_map.56 = (f32[16,256,128]{2,1,0:T(8,128)}, f32[16,256,128]{2,1,0:T(8,128)}, bf16[256,2048]{1,0:T(8,128)(2,1)}) custom-call(s32[10]{0:T(128)} %pad_add_fusion.refs_0_, s32[40]{0:T(128)} %reshape.110.refs_1_, bf16[16,512,128]{2,1,0:T(8,128)(2,1)} %bitcast.34, bf16[2,16,512,128]{3,2,1,0:T(8,128)(2,1)} %collective-permute-done.refs_3_.refs_4_, ...), custom_call_target="tpu_custom_call" | custom-call | flops 1342177280 | bytes 23068672 | tf_op jit(solution)/shard_map/pallas_call | solution.py:312
  85.5 6.6 %shard_map.61 = bf16[256,2048]{1,0:T(8,128)(2,1)} custom-call(s32[1]{0:T(128)} %bitcast.22.sel_ref, bf16[256,2048]{1,0:T(8,128)(2,1)} %get-tuple-element.32.a_ref, bf16[2048,4096]{1,0:T(8,128)(2,1)} %w_ref.7), custom_call_target="tpu_custom_call" | custom-call | flops 2147483648 | bytes 10485760 | tf_op jit(solution)/shard_map/pallas_call | solution.py:198
  92.1 1.5 collective-permute-start.6
  93.6 6.6 %shard_map.57 = bf16[256,2048]{1,0:T(8,128)(2,1)} custom-call(s32[1]{0:T(128)} %bitcast.sel_ref, bf16[256,2048]{1,0:T(8,128)(2,1)} %get-tuple-element.32.a_ref, bf16[2048,4096]{1,0:T(8,128)(2,1)} %w_ref.7), custom_call_target="tpu_custom_call" | custom-call | flops 2147483648 | bytes 10485760 | tf_op jit(solution)/shard_map/pallas_call | solution.py:198
  100.2 29.8 %collective-permute-done.4.refs_11_.refs_12_ = bf16[2,16,64,128]{3,2,1,0:T(8,128)(2,1)} collective-permute-done((bf16[2,16,64,128]{3,2,1,0:T(8,128)(2,1)}, bf16[2,16,64,128]{3,2,1,0:T(8,128)(2,1)}, u32[]{:S(2)}, u32[]{:S(2)}) %collective-permute-start.4) | collective-permute-done | bytes 524320 | tf_op jit(solution)/shard_map/ppermute | solution.py:259
  131.7 10.6 %shard_map.58.a_ref = bf16[256,2048]{1,0:T(8,128)(2,1)} custom-call(s32[10]{0:T(128)} %pad_add_fusion.refs_0_, s32[40]{0:T(128)} %reshape.110.refs_1_, bf16[16,512,128]{2,1,0:T(8,128)(2,1)} %bitcast.35, f32[16,256,128]{2,1,0:T(8,128)} %get-tuple-element.33.refs_3_, f32[16,256,128]{2,1,0:T(8,128)} %get-tuple-element.34.refs_4_, ...), custom_call_target="tpu_custom_call" | custom-call | flops 268435456 | bytes 12058624 | tf_op jit(solution)/shard_map/pallas_call | solution.py:356
  142.2 6.7 %shard_map.60 = bf16[256,2048]{1,0:T(8,128)(2,1)} custom-call(s32[1]{0:T(128)} %bitcast.22.sel_ref, bf16[256,2048]{1,0:T(8,128)(2,1)} %shard_map.58.a_ref, bf16[2048,4096]{1,0:T(8,128)(2,1)} %w_ref.7), custom_call_target="tpu_custom_call" | custom-call | flops 2147483648 | bytes 10485760 | tf_op jit(solution)/shard_map/pallas_call | solution.py:198
  148.9 1.5 collective-permute-start.5
  150.4 1.6 add_convert_fusion
  152.0 6.6 %shard_map.59 = bf16[256,2048]{1,0:T(8,128)(2,1)} custom-call(s32[1]{0:T(128)} %bitcast.sel_ref, bf16[256,2048]{1,0:T(8,128)(2,1)} %shard_map.58.a_ref, bf16[2048,4096]{1,0:T(8,128)(2,1)} %w_ref.7), custom_call_target="tpu_custom_call" | custom-call | flops 2147483648 | bytes 10485760 | tf_op jit(solution)/shard_map/pallas_call | solution.py:198
  158.7 5.3 %collective-permute-done.5 = bf16[256,2048]{1,0:T(8,128)(2,1)S(1)} collective-permute-done((bf16[256,2048]{1,0:T(8,128)(2,1)}, bf16[256,2048]{1,0:T(8,128)(2,1)S(1)}, u32[]{:S(2)}, u32[]{:S(2)}) %collective-permute-start.5) | collective-permute-done | bytes 1048608 | tf_op jit(solution)/shard_map/ppermute | solution.py:369
  163.9 1.6 add_convert_fusion.1
  (38 shorter events, 12.8 us)
Async XLA Ops:
  3.3 2.7 %copy-start = (bf16[1,16,512,128]{3,2,1,0:T(8,128)(2,1)}, bf16[1,16,512,128]{3,2,1,0:T(8,128)(2,1)S(1)}, u32[]{:S(2)}) copy-start(bf16[1,16,512,128]{3,2,1,0:T(8,128)(2,1)S(1)} %get-tuple-element.68) | copy-start | bytes 6291460
  3.3 4.6 %copy-start.5 = (s32[128,5]{0,1:T(8,128)S(1)}, s32[128,5]{0,1:T(8,128)}, u32[]{:S(2)}) copy-start(s32[128,5]{0,1:T(8,128)} %param.8) | copy-start | bytes 7684
  6.0 50.1 %collective-permute-start = (bf16[2,16,512,128]{3,2,1,0:T(8,128)(2,1)}, bf16[2,16,512,128]{3,2,1,0:T(8,128)(2,1)}, u32[]{:S(2)}, u32[]{:S(2)}) collective-permute-start(bf16[2,16,512,128]{3,2,1,0:T(8,128)(2,1)} %pad_maximum_fusion.refs_1_.refs_2_), channel_id=1, source_target_pairs={{0,2},{2,4},{4,6},{6,8},{8,10},{10,12},{12,14},{14,16},{16,18},{18... | collective-permute-start | bytes 12582920 | tf_op jit(solution)/shard_map/ppermute | solution.py:20
  20.9 1.7 copy-start.1
  56.1 73.9 %collective-permute-start.1 = (bf16[2,16,256,128]{3,2,1,0:T(8,128)(2,1)}, bf16[2,16,256,128]{3,2,1,0:T(8,128)(2,1)S(1)}, u32[]{:S(2)}, u32[]{:S(2)}) collective-permute-start(bf16[2,16,256,128]{3,2,1,0:T(8,128)(2,1)} %pad_maximum_fusion.1), channel_id=1, source_target_pairs={{0,4},{4,8},{8,12},{12,16},{16,20},{20,24},{24,28},{1,5},{5,9},{9,... | collective-permute-start | bytes 6291464 | tf_op jit(solution)/shard_map/ppermute | solution.py:299
  60.7 69.3 %collective-permute-start.2 = (bf16[2,16,256,128]{3,2,1,0:T(8,128)(2,1)}, bf16[2,16,256,128]{3,2,1,0:T(8,128)(2,1)}, u32[]{:S(2)}, u32[]{:S(2)}) collective-permute-start(bf16[2,16,256,128]{3,2,1,0:T(8,128)(2,1)} %pad_maximum_fusion.2), channel_id=1, source_target_pairs={{0,2},{4,6},{8,10},{12,14},{16,18},{20,22},{24,26},{28,30},{1,3},{... | collective-permute-start | bytes 6291464 | tf_op jit(solution)/shard_map/ppermute | solution.py:300
  63.3 66.7 %collective-permute-start.3 = (bf16[2,16,128,128]{3,2,1,0:T(8,128)(2,1)}, bf16[2,16,128,128]{3,2,1,0:T(8,128)(2,1)S(1)}, u32[]{:S(2)}, u32[]{:S(2)}) collective-permute-start(bf16[2,16,128,128]{3,2,1,0:T(8,128)(2,1)} %pad_maximum_fusion.4), channel_id=1, source_target_pairs={{0,8},{2,10},{4,12},{6,14},{8,16},{10,18},{12,20},{14,22},{16,24},... | collective-permute-start | bytes 3145736 | tf_op jit(solution)/shard_map/ppermute | solution.py:259
  64.6 65.4 %collective-permute-start.4 = (bf16[2,16,64,128]{3,2,1,0:T(8,128)(2,1)}, bf16[2,16,64,128]{3,2,1,0:T(8,128)(2,1)}, u32[]{:S(2)}, u32[]{:S(2)}) collective-permute-start(bf16[2,16,64,128]{3,2,1,0:T(8,128)(2,1)} %get-tuple-element.37), channel_id=1, source_target_pairs={{0,16},{2,18},{4,20},{6,22},{8,24},{10,26},{12,28},{14,30},{1,17},... | collective-permute-start | bytes 1572872 | tf_op jit(solution)/shard_map/ppermute | solution.py:259
  92.1 58.3 %collective-permute-start.6 = (bf16[256,2048]{1,0:T(8,128)(2,1)}, bf16[256,2048]{1,0:T(8,128)(2,1)}, u32[]{:S(2)}, u32[]{:S(2)}) collective-permute-start(bf16[256,2048]{1,0:T(8,128)(2,1)} %shard_map.61), channel_id=1, source_target_pairs={{0,1},{1,0},{2,3},{3,2},{4,5},{5,4},{6,7},{7,6},{8,9},{9,8},{10,11... | collective-permute-start | bytes 3145736 | tf_op jit(solution)/shard_map/ppermute | solution.py:353
  130.0 1.0 copy-start.3
  130.0 1.6 copy-start.2
  142.2 8.2 %copy-start.4 = (bf16[256,2048]{1,0:T(8,128)(2,1)S(1)}, bf16[256,2048]{1,0:T(8,128)(2,1)}, u32[]{:S(2)}) copy-start(bf16[256,2048]{1,0:T(8,128)(2,1)} %shard_map.57) | copy-start | bytes 3145732
  148.9 15.0 %collective-permute-start.5 = (bf16[256,2048]{1,0:T(8,128)(2,1)}, bf16[256,2048]{1,0:T(8,128)(2,1)S(1)}, u32[]{:S(2)}, u32[]{:S(2)}) collective-permute-start(bf16[256,2048]{1,0:T(8,128)(2,1)} %shard_map.60), channel_id=1, source_target_pairs={{0,1},{1,0},{2,3},{3,2},{4,5},{5,4},{6,7},{7,6},{8,9},{9,8},{10,11... | collective-permute-start | bytes 3145736 | tf_op jit(solution)/shard_map/ppermute | solution.py:369

commit v13 on v8

--- a/solution.py
+++ b/solution.py
@@ -296,7 +296,11 @@
 
     if levels and levels[0] == 1:
         direct_op, direct_pairs = far_arrays[0]
-        prev_kv, acc0, st0, direct_op = lax.optimization_barrier((prev_kv, acc0, st0, direct_op))
+        tied = [g[0] for g in far_arrays[1:]]
+        prev_kv, acc0, st0, direct_op, tied = lax.optimization_barrier(
+            (prev_kv, acc0, st0, direct_op, tied)
+        )
+        far_arrays[1:] = [(t,) for t in tied]
         direct = lax.ppermute(direct_op, "ctx", direct_pairs)
         forwarded = lax.ppermute(
             pick_blocks(prev_kv, fwd_local), "ctx",

time: 168 us -> 202 us (1.20)
  starting transfers between devices: 11.6 us -> 54.6 us
  waiting for transfers between devices: 49.2 us -> 41.7 us
    ppermute x1, starting transfers between devices: 2.63 us -> 46.8 us  [per_device(): lax.ppermute(pick_blocks(prev_kv, fwd_local), 'ctx', [(s, s + 1) for s in...]
    ppermute x1, waiting for transfers between devices: 16.3 us -> 0.01 us  [from_behind(): lax.ppermute(value, axis, [(source, source + steps) for source in range(i...]
    ppermute x1, waiting for transfers between devices: 5.28 us -> 15.7 us  [per_device(): lax.ppermute(project_half(att_even, out_weight, 1 - hidx), 'head', swap)]
    unnamed x13 -> x15, local copies, waits for them, and re-layouts: 5.65 us -> 6.22 us
  transfers between devices with their start and end apart: 7 -> 7, of which waited for: 3 -> 2; matrix products, arithmetic and copies ran while one was open for 11% -> 8% of each run, Pallas kernels for 42% -> 35%
where the time goes in v13:
time: 202 us; the launch traced here: 201 us
  Pallas kernels  70.3 us (35%)
  starting transfers between devices  54.6 us (27%)
  waiting for transfers between devices  41.7 us (21%)
  local copies, waits for them, and re-layouts  16 us (8%)
  other arithmetic  11.7 us (6%)
  between operations  6.89 us (3%)
    ppermute x1, starting transfers between devices, per_device(): lax.ppermute(pick_blocks(prev_kv, fwd_local), 'ctx', [(s, s + 1) for s in...  46.8 us
    pallas_call x4, Pallas kernels, project_half(): pl.pallas_call(matmul_kernel, out_shape=jax.ShapeDtypeStruct((rows, cw),...  26.6 us
    ppermute x2, waiting for transfers between devices, per_device(): far_arrays.append((lax.ppermute(op, 'ctx', pairs),))  25.9 us
    pallas_call x1, Pallas kernels, per_device(): pl.pallas_call(per_head(functools.partial(prev_kernel, per_dev, width, sc...  20.1 us
    ppermute x1, waiting for transfers between devices, per_device(): lax.ppermute(project_half(att_even, out_weight, 1 - hidx), 'head', swap)  15.7 us
    pallas_call x1, Pallas kernels, per_device(): pl.pallas_call(per_head(functools.partial(own_kernel, per_dev, width, sca...  13.1 us
    pallas_call x1, Pallas kernels, per_device(): pl.pallas_call(per_head(functools.partial(far_kernel, levels, per_dev, wi...  10.6 us
    unnamed x15, local copies, waits for them, and re-layouts  6.22 us
  transfers between devices with their start and end apart: 7, of which 2 were waited for; matrix products, arithmetic and copies ran while one was open for 8% of the time, Pallas kernels for 35%

profile of v13, /device:TPU:28, one launch (start us, length us, event | category | flops | bytes accessed | tf_op | source)
XLA Modules:
  0.0 201.2 jit_solution(1808091365806973545)
XLA Ops:
  0.0 3.3 %copy_bitcast_fusion = (bf16[1,16,512,128]{3,2,1,0:T(8,128)(2,1)S(1)}, bf16[1,16,512,128]{3,2,1,0:T(8,128)(2,1)S(1)}) fusion(bf16[512,16,128]{2,1,0:T(8,128)(2,1)} %param.7, bf16[512,16,128]{2,1,0:T(8,128)(2,1)} %param.6), kind=kLoop, calls=%fused_computation.18 | loop fusion | bytes 8388608 | tf_op jit(solution)/shard_map/stack | solution.py:234
  3.3 2.6 %pad_maximum_fusion.refs_1_.refs_2_ = bf16[2,16,512,128]{3,2,1,0:T(8,128)(2,1)} fusion(bf16[1,16,512,128]{3,2,1,0:T(8,128)(2,1)S(1)} %get-tuple-element.71, bf16[1,16,512,128]{3,2,1,0:T(8,128)(2,1)S(1)} %get-tuple-element.72), kind=kLoop, calls=%fused_computation.7 | loop fusion | flops 2097152 | bytes 8388608 | tf_op jit(solution)/shard_map/stack | solution.py:234
  6.0 1.9 collective-permute-start
  14.3 3.5 %copy.14 = bf16[512,16,128]{2,0,1:T(8,128)(2,1)} copy(bf16[512,16,128]{2,1,0:T(8,128)(2,1)} %param.5) | data formatting | bytes 4194304 | tf_op args[0]
  19.4 1.6 fusion.6
  21.0 1.5 pad_maximum_fusion.1
  22.5 1.3 collective-permute-start.1
  23.8 1.3 collective-permute-start.2
  28.2 13.1 %shard_map.55 = (f32[16,512,128]{2,1,0:T(8,128)}, f32[16,512,128]{2,1,0:T(8,128)}) custom-call(bf16[16,512,128]{2,1,0:T(8,128)(2,1)} %bitcast.33, bf16[2,16,512,128]{3,2,1,0:T(8,128)(2,1)} %pad_maximum_fusion.refs_1_.refs_2_, bf16[2,16,512,128]{3,2,1,0:T(8,128)(2,1)} %pad_maximum_fusion.refs_1_.refs_2_), custom_call_target="tpu_custom_call" | custom-call | flops 1073741824 | bytes 29360128 | tf_op jit(solution)/shard_map/pallas_call | solution.py:287
  41.2 25.9 %collective-permute-done.2.refs_11_.refs_12_ = bf16[2,16,64,128]{3,2,1,0:T(8,128)(2,1)S(1)} collective-permute-done((bf16[2,16,64,128]{3,2,1,0:T(8,128)(2,1)}, bf16[2,16,64,128]{3,2,1,0:T(8,128)(2,1)S(1)}, u32[]{:S(2)}, u32[]{:S(2)}) %collective-permute-start.2) | collective-permute-done | bytes 524320 | tf_op jit(solution)/shard_map/ppermute | solution.py:260
  69.3 1.7 constant_dynamic-slice_fusion.3
  71.1 1.5 pad_maximum_fusion.2
  72.6 46.8 %collective-permute-start.4 = (bf16[2,16,256,128]{3,2,1,0:T(8,128)(2,1)}, bf16[2,16,256,128]{3,2,1,0:T(8,128)(2,1)}, u32[]{:S(2)}, u32[]{:S(2)}) collective-permute-start(bf16[2,16,256,128]{3,2,1,0:T(8,128)(2,1)} %pad_maximum_fusion.2), channel_id=1, source_target_pairs={{0,2},{4,6},{8,10},{12,14},{16,18},{20,22},{24,26},{28,30},{1,3},{... | collective-permute-start | bytes 6291464 | tf_op jit(solution)/shard_map/ppermute | solution.py:305
  120.8 20.1 %shard_map.56 = (f32[16,256,128]{2,1,0:T(8,128)}, f32[16,256,128]{2,1,0:T(8,128)}, bf16[256,2048]{1,0:T(8,128)(2,1)}) custom-call(s32[10]{0:T(128)} %pad_add_fusion.refs_0_, s32[40]{0:T(128)} %reshape.110.refs_1_, bf16[16,512,128]{2,1,0:T(8,128)(2,1)} %bitcast.34, bf16[2,16,512,128]{3,2,1,0:T(8,128)(2,1)} %collective-permute-done.refs_3_.refs_4_, ...), custom_call_target="tpu_custom_call" | custom-call | flops 1342177280 | bytes 23068672 | tf_op jit(solution)/shard_map/pallas_call | solution.py:317
  141.0 6.6 %shard_map.61 = bf16[256,2048]{1,0:T(8,128)(2,1)} custom-call(s32[1]{0:T(128)} %bitcast.22.sel_ref, bf16[256,2048]{1,0:T(8,128)(2,1)} %get-tuple-element.36.a_ref, bf16[2048,4096]{1,0:T(8,128)(2,1)} %w_ref.7), custom_call_target="tpu_custom_call" | custom-call | flops 2147483648 | bytes 10485760 | tf_op jit(solution)/shard_map/pallas_call | solution.py:199
  147.6 1.5 collective-permute-start.6
  149.1 6.6 %shard_map.57 = bf16[256,2048]{1,0:T(8,128)(2,1)} custom-call(s32[1]{0:T(128)} %bitcast.sel_ref, bf16[256,2048]{1,0:T(8,128)(2,1)} %get-tuple-element.36.a_ref, bf16[2048,4096]{1,0:T(8,128)(2,1)} %w_ref.7), custom_call_target="tpu_custom_call" | custom-call | flops 2147483648 | bytes 10485760 | tf_op jit(solution)/shard_map/pallas_call | solution.py:199
  155.7 1.3 copy-done.2
  157.0 10.6 %shard_map.58.a_ref = bf16[256,2048]{1,0:T(8,128)(2,1)} custom-call(s32[10]{0:T(128)} %pad_add_fusion.refs_0_, s32[40]{0:T(128)} %reshape.110.refs_1_, bf16[16,512,128]{2,1,0:T(8,128)(2,1)} %bitcast.35, f32[16,256,128]{2,1,0:T(8,128)} %get-tuple-element.37.refs_3_, f32[16,256,128]{2,1,0:T(8,128)} %get-tuple-element.38.refs_4_, ...), custom_call_target="tpu_custom_call" | custom-call | flops 268435456 | bytes 12058624 | tf_op jit(solution)/shard_map/pallas_call | solution.py:361
  167.6 6.7 %shard_map.60 = bf16[256,2048]{1,0:T(8,128)(2,1)} custom-call(s32[1]{0:T(128)} %bitcast.22.sel_ref, bf16[256,2048]{1,0:T(8,128)(2,1)} %shard_map.58.a_ref, bf16[2048,4096]{1,0:T(8,128)(2,1)} %w_ref.7), custom_call_target="tpu_custom_call" | custom-call | flops 2147483648 | bytes 10485760 | tf_op jit(solution)/shard_map/pallas_call | solution.py:199
  175.2 6.7 %shard_map.59 = bf16[256,2048]{1,0:T(8,128)(2,1)} custom-call(s32[1]{0:T(128)} %bitcast.sel_ref, bf16[256,2048]{1,0:T(8,128)(2,1)} %shard_map.58.a_ref, bf16[2048,4096]{1,0:T(8,128)(2,1)} %w_ref.7), custom_call_target="tpu_custom_call" | custom-call | flops 2147483648 | bytes 10485760 | tf_op jit(solution)/shard_map/pallas_call | solution.py:199
  181.9 15.7 %collective-permute-done.5 = bf16[256,2048]{1,0:T(8,128)(2,1)} collective-permute-done((bf16[256,2048]{1,0:T(8,128)(2,1)}, bf16[256,2048]{1,0:T(8,128)(2,1)}, u32[]{:S(2)}, u32[]{:S(2)}) %collective-permute-start.5) | collective-permute-done | bytes 1048608 | tf_op jit(solution)/shard_map/ppermute | solution.py:374
  197.6 1.9 add_convert_fusion.1
  199.8 1.5 copy.10
  (40 shorter events, 9.1 us)
Async XLA Ops:
  3.3 2.6 %copy-start = (bf16[1,16,512,128]{3,2,1,0:T(8,128)(2,1)}, bf16[1,16,512,128]{3,2,1,0:T(8,128)(2,1)S(1)}, u32[]{:S(2)}) copy-start(bf16[1,16,512,128]{3,2,1,0:T(8,128)(2,1)S(1)} %get-tuple-element.72) | copy-start | bytes 6291460
  3.3 4.6 %copy-start.6 = (s32[128,5]{0,1:T(8,128)S(1)}, s32[128,5]{0,1:T(8,128)}, u32[]{:S(2)}) copy-start(s32[128,5]{0,1:T(8,128)} %param.8) | copy-start | bytes 7684
  6.0 61.2 %collective-permute-start = (bf16[2,16,512,128]{3,2,1,0:T(8,128)(2,1)}, bf16[2,16,512,128]{3,2,1,0:T(8,128)(2,1)}, u32[]{:S(2)}, u32[]{:S(2)}) collective-permute-start(bf16[2,16,512,128]{3,2,1,0:T(8,128)(2,1)} %pad_maximum_fusion.refs_1_.refs_2_), channel_id=1, source_target_pairs={{0,2},{2,4},{4,6},{6,8},{8,10},{10,12},{12,14},{14,16},{16,18},{18... | collective-permute-start | bytes 12582920 | tf_op jit(solution)/shard_map/ppermute | solution.py:20
  17.7 1.7 copy-start.1
  22.5 44.6 %collective-permute-start.1 = (bf16[2,16,128,128]{3,2,1,0:T(8,128)(2,1)S(1)}, bf16[2,16,128,128]{3,2,1,0:T(8,128)(2,1)S(1)}, u32[]{:S(2)}, u32[]{:S(2)}) collective-permute-start(bf16[2,16,128,128]{3,2,1,0:T(8,128)(2,1)S(1)} %pad_maximum_fusion.4), channel_id=1, source_target_pairs={{0,8},{2,10},{4,12},{6,14},{8,16},{10,18},{12,20},{14,22},{16,24},... | collective-permute-start | bytes 3145736 | tf_op jit(solution)/shard_map/ppermute | solution.py:260
  23.8 43.3 %collective-permute-start.2 = (bf16[2,16,64,128]{3,2,1,0:T(8,128)(2,1)}, bf16[2,16,64,128]{3,2,1,0:T(8,128)(2,1)S(1)}, u32[]{:S(2)}, u32[]{:S(2)}) collective-permute-start(bf16[2,16,64,128]{3,2,1,0:T(8,128)(2,1)} %get-tuple-element.30), channel_id=1, source_target_pairs={{0,16},{2,18},{4,20},{6,22},{8,24},{10,26},{12,28},{14,30},{1,17},... | collective-permute-start | bytes 1572872 | tf_op jit(solution)/shard_map/ppermute | solution.py:260
  67.2 0.9 copy-start.5
  67.2 3.9 %copy-start.3 = (bf16[2,16,128,128]{3,2,1,0:T(8,128)(2,1)}, bf16[2,16,128,128]{3,2,1,0:T(8,128)(2,1)S(1)}, u32[]{:S(2)}) copy-start(bf16[2,16,128,128]{3,2,1,0:T(8,128)(2,1)S(1)} %collective-permute-done.1.refs_9_.refs_10_) | copy-start | bytes 3145732
  68.0 87.6 %collective-permute-start.3 = (bf16[2,16,256,128]{3,2,1,0:T(8,128)(2,1)}, bf16[2,16,256,128]{3,2,1,0:T(8,128)(2,1)S(1)}, u32[]{:S(2)}, u32[]{:S(2)}) collective-permute-start(bf16[2,16,256,128]{3,2,1,0:T(8,128)(2,1)} %pad_maximum_fusion.1), channel_id=1, source_target_pairs={{0,4},{4,8},{8,12},{12,16},{16,20},{20,24},{24,28},{1,5},{5,9},{9,... | collective-permute-start | bytes 6291464 | tf_op jit(solution)/shard_map/ppermute | solution.py:304
  72.6 83.1 %collective-permute-start.4 = (bf16[2,16,256,128]{3,2,1,0:T(8,128)(2,1)}, bf16[2,16,256,128]{3,2,1,0:T(8,128)(2,1)}, u32[]{:S(2)}, u32[]{:S(2)}) collective-permute-start(bf16[2,16,256,128]{3,2,1,0:T(8,128)(2,1)} %pad_maximum_fusion.2), channel_id=1, source_target_pairs={{0,2},{4,6},{8,10},{12,14},{16,18},{20,22},{24,26},{28,30},{1,3},{... | collective-permute-start | bytes 6291464 | tf_op jit(solution)/shard_map/ppermute | solution.py:305
  147.6 27.3 %collective-permute-start.6 = (bf16[256,2048]{1,0:T(8,128)(2,1)}, bf16[256,2048]{1,0:T(8,128)(2,1)S(1)}, u32[]{:S(2)}, u32[]{:S(2)}) collective-permute-start(bf16[256,2048]{1,0:T(8,128)(2,1)} %shard_map.61), channel_id=1, source_target_pairs={{0,1},{1,0},{2,3},{3,2},{4,5},{5,4},{6,7},{7,6},{8,9},{9,8},{10,11... | collective-permute-start | bytes 3145736 | tf_op jit(solution)/shard_map/ppermute | solution.py:358
  155.7 1.3 copy-start.2
  167.6 7.2 %copy-start.4 = (bf16[256,2048]{1,0:T(8,128)(2,1)S(1)}, bf16[256,2048]{1,0:T(8,128)(2,1)}, u32[]{:S(2)}) copy-start(bf16[256,2048]{1,0:T(8,128)(2,1)} %shard_map.57) | copy-start | bytes 3145732
  174.3 23.3 %collective-permute-start.5 = (bf16[256,2048]{1,0:T(8,128)(2,1)}, bf16[256,2048]{1,0:T(8,128)(2,1)}, u32[]{:S(2)}, u32[]{:S(2)}) collective-permute-start(bf16[256,2048]{1,0:T(8,128)(2,1)} %shard_map.60), channel_id=1, source_target_pairs={{0,1},{1,0},{2,3},{3,2},{4,5},{5,4},{6,7},{7,6},{8,9},{9,8},{10,11... | collective-permute-start | bytes 3145736 | tf_op jit(solution)/shard_map/ppermute | solution.py:374

commit v14 on v8

--- a/solution.py
+++ b/solution.py
@@ -192,10 +192,13 @@
     )
 
 
-def project_half(attended, weight, half, tn=512):
+def project_half(attended, weight, half, tn=512, part=0, parts=1):
     rows, depth = attended.shape
     cw = weight.shape[1] // 2
-    steps = cw // tn
+    total_steps = cw // tn
+    steps = total_steps // parts
+    first = part * steps
+    cw = steps * tn
     return pl.pallas_call(
         matmul_kernel,
         out_shape=jax.ShapeDtypeStruct((rows, cw), jnp.bfloat16),
@@ -204,7 +207,7 @@
             grid=(steps,),
             in_specs=[
                 pl.BlockSpec((rows, depth), lambda j, sel: (0, 0)),
-                pl.BlockSpec((depth, tn), lambda j, sel: (0, sel[0] * steps + j)),
+                pl.BlockSpec((depth, tn), lambda j, sel: (0, sel[0] * total_steps + first + j)),
             ],
             out_specs=pl.BlockSpec((rows, tn), lambda j, sel: (0, j)),
         ),
@@ -367,7 +370,13 @@
             cost_estimate=cost(2 * BLOCK, half_rows, heads * width * (2 * rows + 8 * half_rows + 2 * sum(a.shape[2] for a in far_operands))),
         )(meta, used, q_t, acc1, st1, *far_operands)
 
-        received_even = lax.ppermute(project_half(att_even, out_weight, 1 - hidx), "head", swap)
+        received_even = jnp.concatenate(
+            [
+                lax.ppermute(project_half(att_even, out_weight, 1 - hidx, part=p, parts=2), "head", swap)
+                for p in range(2)
+            ],
+            axis=1,
+        )
         own_even = project_half(att_even, out_weight, hidx)
         parts = [
             (own.astype(jnp.float32) + got.astype(jnp.float32)).astype(jnp.bfloat16)

time: 168 us -> 165 us (0.982)
  waiting for transfers between devices: 49.2 us -> 44.6 us
    ppermute x1 -> x2, waiting for transfers between devices: 5.28 us -> 0.69 us  [per_device(): lax.ppermute(project_half(att_even, out_weight, 1 - hidx, part=p, parts=2...]
    pallas_call x4 -> x5, Pallas kernels: 26.5 us -> 28 us  [project_half(): pl.pallas_call(matmul_kernel, out_shape=jax.ShapeDtypeStruct((rows, cw),...]
  transfers between devices with their start and end apart: 7 -> 8, of which waited for: 3 -> 3; matrix products, arithmetic and copies ran while one was open for 11% -> 11% of each run, Pallas kernels for 42% -> 44%
where the time goes in v14:
time: 165 us
  Pallas kernels  71.7 us (43%)
  waiting for transfers between devices  44.6 us (27%)
  local copies, waits for them, and re-layouts  15.5 us (9%)
  other arithmetic  13.7 us (8%)
  starting transfers between devices  12.1 us (7%)
  between operations  6.99 us (4%)
    pallas_call x5, Pallas kernels, project_half(): pl.pallas_call(matmul_kernel, out_shape=jax.ShapeDtypeStruct((rows, cw),...  28 us
    ppermute x2, waiting for transfers between devices, per_device(): far_arrays.append((lax.ppermute(op, 'ctx', pairs),))  27.7 us
    pallas_call x1, Pallas kernels, per_device(): pl.pallas_call(per_head(functools.partial(prev_kernel, per_dev, width, sc...  20.1 us
    ppermute x1, waiting for transfers between devices, from_behind(): lax.ppermute(value, axis, [(source, source + steps) for source in range(i...  16.3 us
    pallas_call x1, Pallas kernels, per_device(): pl.pallas_call(per_head(functools.partial(own_kernel, per_dev, width, sca...  13 us
    pallas_call x1, Pallas kernels, per_device(): pl.pallas_call(per_head(functools.partial(far_kernel, levels, per_dev, wi...  10.5 us
    unnamed x13, local copies, waits for them, and re-layouts  5.64 us
    another operation x3, other arithmetic, per_device(): jnp.stack([jnp.transpose(keys, (1, 0, 2)), jnp.transpose(values, (1, 0, 2...  5.38 us
  transfers between devices with their start and end apart: 8, of which 3 were waited for; matrix products, arithmetic and copies ran while one was open for 11% of the time, Pallas kernels for 44%

profile of v14, /device:TPU:28, one launch (start us, length us, event | category | flops | bytes accessed | tf_op | source)
XLA Modules:
  0.0 164.5 jit_solution(1426070383129652305)
XLA Ops:
  0.0 3.3 %copy_bitcast_fusion = (bf16[1,16,512,128]{3,2,1,0:T(8,128)(2,1)S(1)}, bf16[1,16,512,128]{3,2,1,0:T(8,128)(2,1)S(1)}) fusion(bf16[512,16,128]{2,1,0:T(8,128)(2,1)} %param.7, bf16[512,16,128]{2,1,0:T(8,128)(2,1)} %param.6), kind=kLoop, calls=%fused_computation.18 | loop fusion | bytes 8388608 | tf_op jit(solution)/shard_map/stack | solution.py:237
  3.3 2.6 %pad_maximum_fusion.refs_1_.refs_2_ = bf16[2,16,512,128]{3,2,1,0:T(8,128)(2,1)} fusion(bf16[1,16,512,128]{3,2,1,0:T(8,128)(2,1)S(1)} %get-tuple-element.67, bf16[1,16,512,128]{3,2,1,0:T(8,128)(2,1)S(1)} %get-tuple-element.68), kind=kLoop, calls=%fused_computation.7 | loop fusion | flops 2097152 | bytes 8388608 | tf_op jit(solution)/shard_map/stack | solution.py:237
  6.0 1.9 %collective-permute-start = (bf16[2,16,512,128]{3,2,1,0:T(8,128)(2,1)}, bf16[2,16,512,128]{3,2,1,0:T(8,128)(2,1)}, u32[]{:S(2)}, u32[]{:S(2)}) collective-permute-start(bf16[2,16,512,128]{3,2,1,0:T(8,128)(2,1)} %pad_maximum_fusion.refs_1_.refs_2_), channel_id=1, source_target_pairs={{0,2},{2,4},{4,6},{6,8},{8,10},{10,12},{12,14},{14,16},{16,18},{18... | collective-permute-start | bytes 12582920 | tf_op jit(solution)/shard_map/ppermute | solution.py:20
  17.4 3.5 %copy.14 = bf16[512,16,128]{2,0,1:T(8,128)(2,1)} copy(bf16[512,16,128]{2,1,0:T(8,128)(2,1)} %param.5) | data formatting | bytes 4194304 | tf_op args[0]
  22.5 1.6 fusion.6
  25.2 1.5 pad_maximum_fusion.1
  26.8 13.0 %shard_map.55 = (f32[16,512,128]{2,1,0:T(8,128)}, f32[16,512,128]{2,1,0:T(8,128)}) custom-call(bf16[16,512,128]{2,1,0:T(8,128)(2,1)} %bitcast.33, bf16[2,16,512,128]{3,2,1,0:T(8,128)(2,1)} %pad_maximum_fusion.refs_1_.refs_2_, bf16[2,16,512,128]{3,2,1,0:T(8,128)(2,1)} %pad_maximum_fusion.refs_1_.refs_2_), custom_call_target="tpu_custom_call" | custom-call | flops 1073741824 | bytes 29360128 | tf_op jit(solution)/shard_map/pallas_call | solution.py:290
  39.8 16.3 %collective-permute-done.refs_3_.refs_4_ = bf16[2,16,512,128]{3,2,1,0:T(8,128)(2,1)} collective-permute-done((bf16[2,16,512,128]{3,2,1,0:T(8,128)(2,1)}, bf16[2,16,512,128]{3,2,1,0:T(8,128)(2,1)}, u32[]{:S(2)}, u32[]{:S(2)}) %collective-permute-start) | collective-permute-done | bytes 4194336 | tf_op jit(solution)/shard_map/ppermute | solution.py:20
  57.4 1.7 %constant_dynamic-slice_fusion.3 = (bf16[2,16,64,128]{3,2,1,0:T(8,128)(2,1)S(1)}, bf16[2,16,64,128]{3,2,1,0:T(8,128)(2,1)S(1)}, bf16[2,16,64,128]{3,2,1,0:T(8,128)(2,1)S(1)}, bf16[2,16,64,128]{3,2,1,0:T(8,128)(2,1)S(1)}) fusion(bf16[2,16,512,128]{3,2,1,0:T(8,128)(2,1)} %collective-permute-done.refs_3_.refs_4_, s32[]{:T(128)S(6)} %select_n.68, ...), kind=kLoop, calls=%fused_computation.34 | loop fusion | bytes 4194320 | tf_op jit(solution)/shard_map/dynamic_slice | solution.py:225
  59.1 1.5 pad_maximum_fusion.2
  60.6 2.6 %collective-permute-start.2 = (bf16[2,16,256,128]{3,2,1,0:T(8,128)(2,1)}, bf16[2,16,256,128]{3,2,1,0:T(8,128)(2,1)}, u32[]{:S(2)}, u32[]{:S(2)}) collective-permute-start(bf16[2,16,256,128]{3,2,1,0:T(8,128)(2,1)} %pad_maximum_fusion.2), channel_id=1, source_target_pairs={{0,2},{4,6},{8,10},{12,14},{16,18},{20,22},{24,26},{28,30},{1,3},{... | collective-permute-start | bytes 6291464 | tf_op jit(solution)/shard_map/ppermute | solution.py:304
  66.0 20.1 %shard_map.56 = (f32[16,256,128]{2,1,0:T(8,128)}, f32[16,256,128]{2,1,0:T(8,128)}, bf16[256,2048]{1,0:T(8,128)(2,1)}) custom-call(s32[10]{0:T(128)} %pad_add_fusion.refs_0_, s32[40]{0:T(128)} %reshape.111.refs_1_, bf16[16,512,128]{2,1,0:T(8,128)(2,1)} %bitcast.34, bf16[2,16,512,128]{3,2,1,0:T(8,128)(2,1)} %collective-permute-done.refs_3_.refs_4_, ...), custom_call_target="tpu_custom_call" | custom-call | flops 1342177280 | bytes 23068672 | tf_op jit(solution)/shard_map/pallas_call | solution.py:316
  86.1 6.6 %shard_map.62 = bf16[256,2048]{1,0:T(8,128)(2,1)} custom-call(s32[1]{0:T(128)} %bitcast.22.sel_ref, bf16[256,2048]{1,0:T(8,128)(2,1)} %get-tuple-element.32.a_ref, bf16[2048,4096]{1,0:T(8,128)(2,1)} %w_ref.9), custom_call_target="tpu_custom_call" | custom-call | flops 2147483648 | bytes 10485760 | tf_op jit(solution)/shard_map/pallas_call | solution.py:202
  92.7 1.5 collective-permute-start.7
  94.2 1.5 collective-permute-start.4
  95.7 6.6 %shard_map.57 = bf16[256,2048]{1,0:T(8,128)(2,1)} custom-call(s32[1]{0:T(128)} %bitcast.sel_ref, bf16[256,2048]{1,0:T(8,128)(2,1)} %get-tuple-element.32.a_ref, bf16[2048,4096]{1,0:T(8,128)(2,1)} %w_ref.9), custom_call_target="tpu_custom_call" | custom-call | flops 2147483648 | bytes 10485760 | tf_op jit(solution)/shard_map/pallas_call | solution.py:202
  102.3 27.6 %collective-permute-done.4.refs_11_.refs_12_ = bf16[2,16,64,128]{3,2,1,0:T(8,128)(2,1)} collective-permute-done((bf16[2,16,64,128]{3,2,1,0:T(8,128)(2,1)}, bf16[2,16,64,128]{3,2,1,0:T(8,128)(2,1)}, u32[]{:S(2)}, u32[]{:S(2)}) %collective-permute-start.4) | collective-permute-done | bytes 524320 | tf_op jit(solution)/shard_map/ppermute | solution.py:263
  131.6 10.5 %shard_map.58.a_ref = bf16[256,2048]{1,0:T(8,128)(2,1)} custom-call(s32[10]{0:T(128)} %pad_add_fusion.refs_0_, s32[40]{0:T(128)} %reshape.111.refs_1_, bf16[16,512,128]{2,1,0:T(8,128)(2,1)} %bitcast.35, f32[16,256,128]{2,1,0:T(8,128)} %get-tuple-element.33.refs_3_, f32[16,256,128]{2,1,0:T(8,128)} %get-tuple-element.34.refs_4_, ...), custom_call_target="tpu_custom_call" | custom-call | flops 268435456 | bytes 12058624 | tf_op jit(solution)/shard_map/pallas_call | solution.py:360
  142.2 4.1 %shard_map.61 = bf16[256,1024]{1,0:T(8,128)(2,1)} custom-call(s32[1]{0:T(128)} %bitcast.22.sel_ref, bf16[256,2048]{1,0:T(8,128)(2,1)} %shard_map.58.a_ref, bf16[2048,4096]{1,0:T(8,128)(2,1)} %w_ref.9), custom_call_target="tpu_custom_call" | custom-call | flops 1073741824 | bytes 5767168 | tf_op jit(solution)/shard_map/pallas_call | solution.py:202
  146.2 1.5 collective-permute-start.6
  147.7 4.1 %shard_map.60 = bf16[256,1024]{1,0:T(8,128)(2,1)} custom-call(s32[1]{0:T(128)} %bitcast.22.sel_ref, bf16[256,2048]{1,0:T(8,128)(2,1)} %shard_map.58.a_ref, bf16[2048,4096]{1,0:T(8,128)(2,1)} %w_ref.9), custom_call_target="tpu_custom_call" | custom-call | flops 1073741824 | bytes 5767168 | tf_op jit(solution)/shard_map/pallas_call | solution.py:202
  152.3 1.6 add_convert_fusion
  154.0 6.6 %shard_map.59 = bf16[256,2048]{1,0:T(8,128)(2,1)} custom-call(s32[1]{0:T(128)} %bitcast.sel_ref, bf16[256,2048]{1,0:T(8,128)(2,1)} %shard_map.58.a_ref, bf16[2048,4096]{1,0:T(8,128)(2,1)} %w_ref.9), custom_call_target="tpu_custom_call" | custom-call | flops 2147483648 | bytes 10485760 | tf_op jit(solution)/shard_map/pallas_call | solution.py:202
  161.3 1.6 add_convert_fusion.1
  (41 shorter events, 13.9 us)
Async XLA Ops:
  3.3 2.6 %copy-start = (bf16[1,16,512,128]{3,2,1,0:T(8,128)(2,1)}, bf16[1,16,512,128]{3,2,1,0:T(8,128)(2,1)S(1)}, u32[]{:S(2)}) copy-start(bf16[1,16,512,128]{3,2,1,0:T(8,128)(2,1)S(1)} %get-tuple-element.68) | copy-start | bytes 6291460
  3.3 4.6 %copy-start.5 = (s32[128,5]{0,1:T(8,128)S(1)}, s32[128,5]{0,1:T(8,128)}, u32[]{:S(2)}) copy-start(s32[128,5]{0,1:T(8,128)} %param.8) | copy-start | bytes 7684
  6.0 50.1 %collective-permute-start = (bf16[2,16,512,128]{3,2,1,0:T(8,128)(2,1)}, bf16[2,16,512,128]{3,2,1,0:T(8,128)(2,1)}, u32[]{:S(2)}, u32[]{:S(2)}) collective-permute-start(bf16[2,16,512,128]{3,2,1,0:T(8,128)(2,1)} %pad_maximum_fusion.refs_1_.refs_2_), channel_id=1, source_target_pairs={{0,2},{2,4},{4,6},{6,8},{8,10},{10,12},{12,14},{14,16},{16,18},{18... | collective-permute-start | bytes 12582920 | tf_op jit(solution)/shard_map/ppermute | solution.py:20
  20.9 1.7 %copy-start.1 = (bf16[1,16,512,128]{3,2,1,0:T(8,128)(2,1)S(1)}, bf16[1,16,512,128]{3,2,1,0:T(8,128)(2,1)}, u32[]{:S(2)}) copy-start(bf16[1,16,512,128]{3,2,1,0:T(8,128)(2,1)} %copy-done) | copy-start | bytes 6291460
  56.1 73.9 %collective-permute-start.1 = (bf16[2,16,256,128]{3,2,1,0:T(8,128)(2,1)}, bf16[2,16,256,128]{3,2,1,0:T(8,128)(2,1)S(1)}, u32[]{:S(2)}, u32[]{:S(2)}) collective-permute-start(bf16[2,16,256,128]{3,2,1,0:T(8,128)(2,1)} %pad_maximum_fusion.1), channel_id=1, source_target_pairs={{0,4},{4,8},{8,12},{12,16},{16,20},{20,24},{24,28},{1,5},{5,9},{9,... | collective-permute-start | bytes 6291464 | tf_op jit(solution)/shard_map/ppermute | solution.py:303
  60.6 69.4 %collective-permute-start.2 = (bf16[2,16,256,128]{3,2,1,0:T(8,128)(2,1)}, bf16[2,16,256,128]{3,2,1,0:T(8,128)(2,1)}, u32[]{:S(2)}, u32[]{:S(2)}) collective-permute-start(bf16[2,16,256,128]{3,2,1,0:T(8,128)(2,1)} %pad_maximum_fusion.2), channel_id=1, source_target_pairs={{0,2},{4,6},{8,10},{12,14},{16,18},{20,22},{24,26},{28,30},{1,3},{... | collective-permute-start | bytes 6291464 | tf_op jit(solution)/shard_map/ppermute | solution.py:304
  63.3 66.7 %collective-permute-start.3 = (bf16[2,16,128,128]{3,2,1,0:T(8,128)(2,1)}, bf16[2,16,128,128]{3,2,1,0:T(8,128)(2,1)S(1)}, u32[]{:S(2)}, u32[]{:S(2)}) collective-permute-start(bf16[2,16,128,128]{3,2,1,0:T(8,128)(2,1)} %pad_maximum_fusion.4), channel_id=1, source_target_pairs={{0,8},{2,10},{4,12},{6,14},{8,16},{10,18},{12,20},{14,22},{16,24},... | collective-permute-start | bytes 3145736 | tf_op jit(solution)/shard_map/ppermute | solution.py:263
  92.7 59.6 %collective-permute-start.7 = (bf16[256,2048]{1,0:T(8,128)(2,1)}, bf16[256,2048]{1,0:T(8,128)(2,1)}, u32[]{:S(2)}, u32[]{:S(2)}) collective-permute-start(bf16[256,2048]{1,0:T(8,128)(2,1)} %shard_map.62), channel_id=1, source_target_pairs={{0,1},{1,0},{2,3},{3,2},{4,5},{5,4},{6,7},{7,6},{8,9},{9,8},{10,11... | collective-permute-start | bytes 3145736 | tf_op jit(solution)/shard_map/ppermute | solution.py:357
  94.2 35.8 %collective-permute-start.4 = (bf16[2,16,64,128]{3,2,1,0:T(8,128)(2,1)}, bf16[2,16,64,128]{3,2,1,0:T(8,128)(2,1)}, u32[]{:S(2)}, u32[]{:S(2)}) collective-permute-start(bf16[2,16,64,128]{3,2,1,0:T(8,128)(2,1)} %get-tuple-element.37), channel_id=1, source_target_pairs={{0,16},{2,18},{4,20},{6,22},{8,24},{10,26},{12,28},{14,30},{1,17},... | collective-permute-start | bytes 1572872 | tf_op jit(solution)/shard_map/ppermute | solution.py:263
  130.0 1.0 copy-start.3
  130.0 1.6 copy-start.2
  146.2 6.1 %copy-start.4 = (bf16[256,2048]{1,0:T(8,128)(2,1)S(1)}, bf16[256,2048]{1,0:T(8,128)(2,1)}, u32[]{:S(2)}) copy-start(bf16[256,2048]{1,0:T(8,128)(2,1)} %shard_map.57) | copy-start | bytes 3145732
  146.2 14.3 %collective-permute-start.6 = (bf16[256,1024]{1,0:T(8,128)(2,1)}, bf16[256,1024]{1,0:T(8,128)(2,1)S(1)}, u32[]{:S(2)}, u32[]{:S(2)}) collective-permute-start(bf16[256,1024]{1,0:T(8,128)(2,1)} %shard_map.61), channel_id=1, source_target_pairs={{0,1},{1,0},{2,3},{3,2},{4,5},{5,4},{6,7},{7,6},{8,9},{9,8},{10,11... | collective-permute-start | bytes 1572872 | tf_op jit(solution)/shard_map/ppermute | solution.py:375
  151.8 9.5 %collective-permute-start.5 = (bf16[256,1024]{1,0:T(8,128)(2,1)}, bf16[256,1024]{1,0:T(8,128)(2,1)S(1)}, u32[]{:S(2)}, u32[]{:S(2)}) collective-permute-start(bf16[256,1024]{1,0:T(8,128)(2,1)} %shard_map.60), channel_id=1, source_target_pairs={{0,1},{1,0},{2,3},{3,2},{4,5},{5,4},{6,7},{7,6},{8,9},{9,8},{10,11... | collective-permute-start | bytes 1572872 | tf_op jit(solution)/shard_map/ppermute | solution.py:375

commit v15 on v14

--- a/solution.py
+++ b/solution.py
@@ -372,8 +372,10 @@
 
         received_even = jnp.concatenate(
             [
-                lax.ppermute(project_half(att_even, out_weight, 1 - hidx, part=p, parts=2), "head", swap)
-                for p in range(2)
+                lax.ppermute(
+                    project_half(att_even, out_weight, 1 - hidx, tn=256, part=p, parts=4), "head", swap
+                )
+                for p in range(4)
             ],
             axis=1,
         )

time: 165 us -> 171 us (1.036)
  Pallas kernels: 71.7 us -> 76.1 us
  starting transfers between devices: 12.1 us -> 14.1 us
    pallas_call x5 -> x7, Pallas kernels: 28 us -> 32.4 us  [project_half(): pl.pallas_call(matmul_kernel, out_shape=jax.ShapeDtypeStruct((rows, cw),...]
    ppermute x2 -> x4, starting transfers between devices: 2.03 us -> 4.05 us  [per_device(): lax.ppermute(project_half(att_even, out_weight, 1 - hidx, tn=256, part=p,...]
  transfers between devices with their start and end apart: 8 -> 10, of which waited for: 3 -> 2; matrix products, arithmetic and copies ran while one was open for 11% -> 11% of each run, Pallas kernels for 44% -> 45%
where the time goes in v15:
time: 171 us; the launch traced here: 170 us
  Pallas kernels  76.1 us (45%)
  waiting for transfers between devices  43.6 us (25%)
  local copies, waits for them, and re-layouts  15.7 us (9%)
  starting transfers between devices  14.1 us (8%)
  other arithmetic  13.6 us (8%)
  between operations  7.16 us (4%)
    pallas_call x7, Pallas kernels, project_half(): pl.pallas_call(matmul_kernel, out_shape=jax.ShapeDtypeStruct((rows, cw),...  32.4 us
    ppermute x2, waiting for transfers between devices, per_device(): far_arrays.append((lax.ppermute(op, 'ctx', pairs),))  27.5 us
    pallas_call x1, Pallas kernels, per_device(): pl.pallas_call(per_head(functools.partial(prev_kernel, per_dev, width, sc...  20.1 us
    ppermute x1, waiting for transfers between devices, from_behind(): lax.ppermute(value, axis, [(source, source + steps) for source in range(i...  16.1 us
    pallas_call x1, Pallas kernels, per_device(): pl.pallas_call(per_head(functools.partial(own_kernel, per_dev, width, sca...  13.1 us
    pallas_call x1, Pallas kernels, per_device(): pl.pallas_call(per_head(functools.partial(far_kernel, levels, per_dev, wi...  10.6 us
    unnamed x13, local copies, waits for them, and re-layouts  5.65 us
    another operation x3, other arithmetic, per_device(): jnp.stack([jnp.transpose(keys, (1, 0, 2)), jnp.transpose(values, (1, 0, 2...  5.37 us
  transfers between devices with their start and end apart: 10, of which 2 were waited for; matrix products, arithmetic and copies ran while one was open for 11% of the time, Pallas kernels for 45%

profile of v15, /device:TPU:28, one launch (start us, length us, event | category | flops | bytes accessed | tf_op | source)
XLA Modules:
  0.0 170.3 jit_solution(16590410843015179785)
XLA Ops:
  0.0 3.3 %copy_bitcast_fusion = (bf16[1,16,512,128]{3,2,1,0:T(8,128)(2,1)S(1)}, bf16[1,16,512,128]{3,2,1,0:T(8,128)(2,1)S(1)}) fusion(bf16[512,16,128]{2,1,0:T(8,128)(2,1)} %param.7, bf16[512,16,128]{2,1,0:T(8,128)(2,1)} %param.6), kind=kLoop, calls=%fused_computation.18 | loop fusion | bytes 8388608 | tf_op jit(solution)/shard_map/stack | solution.py:237
  3.3 2.6 %pad_maximum_fusion.refs_1_.refs_2_ = bf16[2,16,512,128]{3,2,1,0:T(8,128)(2,1)} fusion(bf16[1,16,512,128]{3,2,1,0:T(8,128)(2,1)S(1)} %get-tuple-element.67, bf16[1,16,512,128]{3,2,1,0:T(8,128)(2,1)S(1)} %get-tuple-element.68), kind=kLoop, calls=%fused_computation.7 | loop fusion | flops 2097152 | bytes 8388608 | tf_op jit(solution)/shard_map/stack | solution.py:237
  6.0 1.9 %collective-permute-start = (bf16[2,16,512,128]{3,2,1,0:T(8,128)(2,1)}, bf16[2,16,512,128]{3,2,1,0:T(8,128)(2,1)}, u32[]{:S(2)}, u32[]{:S(2)}) collective-permute-start(bf16[2,16,512,128]{3,2,1,0:T(8,128)(2,1)} %pad_maximum_fusion.refs_1_.refs_2_), channel_id=1, source_target_pairs={{0,2},{2,4},{4,6},{6,8},{8,10},{10,12},{12,14},{14,16},{16,18},{18... | collective-permute-start | bytes 12582920 | tf_op jit(solution)/shard_map/ppermute | solution.py:20
  17.7 3.5 %copy.14 = bf16[512,16,128]{2,0,1:T(8,128)(2,1)} copy(bf16[512,16,128]{2,1,0:T(8,128)(2,1)} %param.5) | data formatting | bytes 4194304 | tf_op args[0]
  22.8 1.6 fusion.6
  25.5 1.5 pad_maximum_fusion.1
  27.0 13.1 %shard_map.55 = (f32[16,512,128]{2,1,0:T(8,128)}, f32[16,512,128]{2,1,0:T(8,128)}) custom-call(bf16[16,512,128]{2,1,0:T(8,128)(2,1)} %bitcast.33, bf16[2,16,512,128]{3,2,1,0:T(8,128)(2,1)} %pad_maximum_fusion.refs_1_.refs_2_, bf16[2,16,512,128]{3,2,1,0:T(8,128)(2,1)} %pad_maximum_fusion.refs_1_.refs_2_), custom_call_target="tpu_custom_call" | custom-call | flops 1073741824 | bytes 29360128 | tf_op jit(solution)/shard_map/pallas_call | solution.py:290
  40.0 16.1 %collective-permute-done.refs_3_.refs_4_ = bf16[2,16,512,128]{3,2,1,0:T(8,128)(2,1)} collective-permute-done((bf16[2,16,512,128]{3,2,1,0:T(8,128)(2,1)}, bf16[2,16,512,128]{3,2,1,0:T(8,128)(2,1)}, u32[]{:S(2)}, u32[]{:S(2)}) %collective-permute-start) | collective-permute-done | bytes 4194336 | tf_op jit(solution)/shard_map/ppermute | solution.py:20
  57.4 1.8 %constant_dynamic-slice_fusion.3 = (bf16[2,16,64,128]{3,2,1,0:T(8,128)(2,1)S(1)}, bf16[2,16,64,128]{3,2,1,0:T(8,128)(2,1)S(1)}, bf16[2,16,64,128]{3,2,1,0:T(8,128)(2,1)S(1)}, bf16[2,16,64,128]{3,2,1,0:T(8,128)(2,1)S(1)}) fusion(bf16[2,16,512,128]{3,2,1,0:T(8,128)(2,1)} %collective-permute-done.refs_3_.refs_4_, s32[]{:T(128)S(6)} %select_n.68, ...), kind=kLoop, calls=%fused_computation.34 | loop fusion | bytes 4194320 | tf_op jit(solution)/shard_map/dynamic_slice | solution.py:225
  59.2 1.6 pad_maximum_fusion.2
  60.8 2.6 %collective-permute-start.2 = (bf16[2,16,256,128]{3,2,1,0:T(8,128)(2,1)}, bf16[2,16,256,128]{3,2,1,0:T(8,128)(2,1)}, u32[]{:S(2)}, u32[]{:S(2)}) collective-permute-start(bf16[2,16,256,128]{3,2,1,0:T(8,128)(2,1)} %pad_maximum_fusion.2), channel_id=1, source_target_pairs={{0,2},{4,6},{8,10},{12,14},{16,18},{20,22},{24,26},{28,30},{1,3},{... | collective-permute-start | bytes 6291464 | tf_op jit(solution)/shard_map/ppermute | solution.py:304
  66.2 20.1 %shard_map.56 = (f32[16,256,128]{2,1,0:T(8,128)}, f32[16,256,128]{2,1,0:T(8,128)}, bf16[256,2048]{1,0:T(8,128)(2,1)}) custom-call(s32[10]{0:T(128)} %pad_add_fusion.refs_0_, s32[40]{0:T(128)} %reshape.113.refs_1_, bf16[16,512,128]{2,1,0:T(8,128)(2,1)} %bitcast.34, bf16[2,16,512,128]{3,2,1,0:T(8,128)(2,1)} %collective-permute-done.refs_3_.refs_4_, ...), custom_call_target="tpu_custom_call" | custom-call | flops 1342177280 | bytes 23068672 | tf_op jit(solution)/shard_map/pallas_call | solution.py:316
  86.3 6.6 %shard_map.64 = bf16[256,2048]{1,0:T(8,128)(2,1)} custom-call(s32[1]{0:T(128)} %bitcast.22.sel_ref, bf16[256,2048]{1,0:T(8,128)(2,1)} %get-tuple-element.32.a_ref, bf16[2048,4096]{1,0:T(8,128)(2,1)} %w_ref.13), custom_call_target="tpu_custom_call" | custom-call | flops 2147483648 | bytes 10485760 | tf_op jit(solution)/shard_map/pallas_call | solution.py:202
  92.9 1.5 collective-permute-start.9
  95.9 6.6 %shard_map.57 = bf16[256,2048]{1,0:T(8,128)(2,1)} custom-call(s32[1]{0:T(128)} %bitcast.sel_ref, bf16[256,2048]{1,0:T(8,128)(2,1)} %get-tuple-element.32.a_ref, bf16[2048,4096]{1,0:T(8,128)(2,1)} %w_ref.13), custom_call_target="tpu_custom_call" | custom-call | flops 2147483648 | bytes 10485760 | tf_op jit(solution)/shard_map/pallas_call | solution.py:202
  102.5 27.5 %collective-permute-done.4.refs_11_.refs_12_ = bf16[2,16,64,128]{3,2,1,0:T(8,128)(2,1)} collective-permute-done((bf16[2,16,64,128]{3,2,1,0:T(8,128)(2,1)}, bf16[2,16,64,128]{3,2,1,0:T(8,128)(2,1)}, u32[]{:S(2)}, u32[]{:S(2)}) %collective-permute-start.4) | collective-permute-done | bytes 524320 | tf_op jit(solution)/shard_map/ppermute | solution.py:263
  131.7 10.6 %shard_map.58.a_ref = bf16[256,2048]{1,0:T(8,128)(2,1)} custom-call(s32[10]{0:T(128)} %pad_add_fusion.refs_0_, s32[40]{0:T(128)} %reshape.113.refs_1_, bf16[16,512,128]{2,1,0:T(8,128)(2,1)} %bitcast.35, f32[16,256,128]{2,1,0:T(8,128)} %get-tuple-element.33.refs_3_, f32[16,256,128]{2,1,0:T(8,128)} %get-tuple-element.34.refs_4_, ...), custom_call_target="tpu_custom_call" | custom-call | flops 268435456 | bytes 12058624 | tf_op jit(solution)/shard_map/pallas_call | solution.py:360
  142.2 3.2 %shard_map.63 = bf16[256,512]{1,0:T(8,128)(2,1)} custom-call(s32[1]{0:T(128)} %bitcast.22.sel_ref, bf16[256,2048]{1,0:T(8,128)(2,1)} %shard_map.58.a_ref, bf16[2048,4096]{1,0:T(8,128)(2,1)} %w_ref.13), custom_call_target="tpu_custom_call" | custom-call | flops 536870912 | bytes 3407872 | tf_op jit(solution)/shard_map/pallas_call | solution.py:202
  146.9 3.1 %shard_map.62 = bf16[256,512]{1,0:T(8,128)(2,1)} custom-call(s32[1]{0:T(128)} %bitcast.22.sel_ref, bf16[256,2048]{1,0:T(8,128)(2,1)} %shard_map.58.a_ref, bf16[2048,4096]{1,0:T(8,128)(2,1)} %w_ref.13), custom_call_target="tpu_custom_call" | custom-call | flops 536870912 | bytes 3407872 | tf_op jit(solution)/shard_map/pallas_call | solution.py:202
  150.5 3.2 %shard_map.61 = bf16[256,512]{1,0:T(8,128)(2,1)} custom-call(s32[1]{0:T(128)} %bitcast.22.sel_ref, bf16[256,2048]{1,0:T(8,128)(2,1)} %shard_map.58.a_ref, bf16[2048,4096]{1,0:T(8,128)(2,1)} %w_ref.13), custom_call_target="tpu_custom_call" | custom-call | flops 536870912 | bytes 3407872 | tf_op jit(solution)/shard_map/pallas_call | solution.py:202
  155.2 3.1 %shard_map.60 = bf16[256,512]{1,0:T(8,128)(2,1)} custom-call(s32[1]{0:T(128)} %bitcast.22.sel_ref, bf16[256,2048]{1,0:T(8,128)(2,1)} %shard_map.58.a_ref, bf16[2048,4096]{1,0:T(8,128)(2,1)} %w_ref.13), custom_call_target="tpu_custom_call" | custom-call | flops 536870912 | bytes 3407872 | tf_op jit(solution)/shard_map/pallas_call | solution.py:202
  158.9 1.6 add_convert_fusion
  160.5 6.6 %shard_map.59 = bf16[256,2048]{1,0:T(8,128)(2,1)} custom-call(s32[1]{0:T(128)} %bitcast.sel_ref, bf16[256,2048]{1,0:T(8,128)(2,1)} %shard_map.58.a_ref, bf16[2048,4096]{1,0:T(8,128)(2,1)} %w_ref.13), custom_call_target="tpu_custom_call" | custom-call | flops 2147483648 | bytes 10485760 | tf_op jit(solution)/shard_map/pallas_call | solution.py:202
  167.1 1.5 add_convert_fusion.1
  (47 shorter events, 18.4 us)
Async XLA Ops:
  3.3 2.7 %copy-start = (bf16[1,16,512,128]{3,2,1,0:T(8,128)(2,1)}, bf16[1,16,512,128]{3,2,1,0:T(8,128)(2,1)S(1)}, u32[]{:S(2)}) copy-start(bf16[1,16,512,128]{3,2,1,0:T(8,128)(2,1)S(1)} %get-tuple-element.68) | copy-start | bytes 6291460
  3.3 4.6 %copy-start.5 = (s32[128,5]{0,1:T(8,128)S(1)}, s32[128,5]{0,1:T(8,128)}, u32[]{:S(2)}) copy-start(s32[128,5]{0,1:T(8,128)} %param.8) | copy-start | bytes 7684
  6.0 50.1 %collective-permute-start = (bf16[2,16,512,128]{3,2,1,0:T(8,128)(2,1)}, bf16[2,16,512,128]{3,2,1,0:T(8,128)(2,1)}, u32[]{:S(2)}, u32[]{:S(2)}) collective-permute-start(bf16[2,16,512,128]{3,2,1,0:T(8,128)(2,1)} %pad_maximum_fusion.refs_1_.refs_2_), channel_id=1, source_target_pairs={{0,2},{2,4},{4,6},{6,8},{8,10},{10,12},{12,14},{14,16},{16,18},{18... | collective-permute-start | bytes 12582920 | tf_op jit(solution)/shard_map/ppermute | solution.py:20
  21.1 1.7 copy-start.1
  56.1 73.9 %collective-permute-start.1 = (bf16[2,16,256,128]{3,2,1,0:T(8,128)(2,1)}, bf16[2,16,256,128]{3,2,1,0:T(8,128)(2,1)S(1)}, u32[]{:S(2)}, u32[]{:S(2)}) collective-permute-start(bf16[2,16,256,128]{3,2,1,0:T(8,128)(2,1)} %pad_maximum_fusion.1), channel_id=1, source_target_pairs={{0,4},{4,8},{8,12},{12,16},{16,20},{20,24},{24,28},{1,5},{5,9},{9,... | collective-permute-start | bytes 6291464 | tf_op jit(solution)/shard_map/ppermute | solution.py:303
  60.8 69.3 %collective-permute-start.2 = (bf16[2,16,256,128]{3,2,1,0:T(8,128)(2,1)}, bf16[2,16,256,128]{3,2,1,0:T(8,128)(2,1)}, u32[]{:S(2)}, u32[]{:S(2)}) collective-permute-start(bf16[2,16,256,128]{3,2,1,0:T(8,128)(2,1)} %pad_maximum_fusion.2), channel_id=1, source_target_pairs={{0,2},{4,6},{8,10},{12,14},{16,18},{20,22},{24,26},{28,30},{1,3},{... | collective-permute-start | bytes 6291464 | tf_op jit(solution)/shard_map/ppermute | solution.py:304
  63.4 66.6 %collective-permute-start.3 = (bf16[2,16,128,128]{3,2,1,0:T(8,128)(2,1)}, bf16[2,16,128,128]{3,2,1,0:T(8,128)(2,1)S(1)}, u32[]{:S(2)}, u32[]{:S(2)}) collective-permute-start(bf16[2,16,128,128]{3,2,1,0:T(8,128)(2,1)} %pad_maximum_fusion.4), channel_id=1, source_target_pairs={{0,8},{2,10},{4,12},{6,14},{8,16},{10,18},{12,20},{14,22},{16,24},... | collective-permute-start | bytes 3145736 | tf_op jit(solution)/shard_map/ppermute | solution.py:263
  92.9 65.9 %collective-permute-start.9 = (bf16[256,2048]{1,0:T(8,128)(2,1)}, bf16[256,2048]{1,0:T(8,128)(2,1)}, u32[]{:S(2)}, u32[]{:S(2)}) collective-permute-start(bf16[256,2048]{1,0:T(8,128)(2,1)} %shard_map.64), channel_id=1, source_target_pairs={{0,1},{1,0},{2,3},{3,2},{4,5},{5,4},{6,7},{7,6},{8,9},{9,8},{10,11... | collective-permute-start | bytes 3145736 | tf_op jit(solution)/shard_map/ppermute | solution.py:357
  94.4 35.6 %collective-permute-start.4 = (bf16[2,16,64,128]{3,2,1,0:T(8,128)(2,1)}, bf16[2,16,64,128]{3,2,1,0:T(8,128)(2,1)}, u32[]{:S(2)}, u32[]{:S(2)}) collective-permute-start(bf16[2,16,64,128]{3,2,1,0:T(8,128)(2,1)} %get-tuple-element.37), channel_id=1, source_target_pairs={{0,16},{2,18},{4,20},{6,22},{8,24},{10,26},{12,28},{14,30},{1,17},... | collective-permute-start | bytes 1572872 | tf_op jit(solution)/shard_map/ppermute | solution.py:263
  130.0 1.0 copy-start.3
  130.0 1.6 copy-start.2
  145.4 21.7 %collective-permute-start.8 = (bf16[256,512]{1,0:T(8,128)(2,1)}, bf16[256,512]{1,0:T(8,128)(2,1)S(1)}, u32[]{:S(2)}, u32[]{:S(2)}) collective-permute-start(bf16[256,512]{1,0:T(8,128)(2,1)} %shard_map.63), channel_id=1, source_target_pairs={{0,1},{1,0},{2,3},{3,2},{4,5},{5,4},{6,7},{7,6},{8,9},{9,8},{10,11... | collective-permute-start | bytes 786440 | tf_op jit(solution)/shard_map/ppermute | solution.py:375
  150.0 17.1 %collective-permute-start.7 = (bf16[256,512]{1,0:T(8,128)(2,1)}, bf16[256,512]{1,0:T(8,128)(2,1)S(1)}, u32[]{:S(2)}, u32[]{:S(2)}) collective-permute-start(bf16[256,512]{1,0:T(8,128)(2,1)} %shard_map.62), channel_id=1, source_target_pairs={{0,1},{1,0},{2,3},{3,2},{4,5},{5,4},{6,7},{7,6},{8,9},{9,8},{10,11... | collective-permute-start | bytes 786440 | tf_op jit(solution)/shard_map/ppermute | solution.py:375
  153.7 5.2 %copy-start.4 = (bf16[256,2048]{1,0:T(8,128)(2,1)S(1)}, bf16[256,2048]{1,0:T(8,128)(2,1)}, u32[]{:S(2)}) copy-start(bf16[256,2048]{1,0:T(8,128)(2,1)} %shard_map.57) | copy-start | bytes 3145732
  153.7 13.4 %collective-permute-start.6 = (bf16[256,512]{1,0:T(8,128)(2,1)}, bf16[256,512]{1,0:T(8,128)(2,1)S(1)}, u32[]{:S(2)}, u32[]{:S(2)}) collective-permute-start(bf16[256,512]{1,0:T(8,128)(2,1)} %shard_map.61), channel_id=1, source_target_pairs={{0,1},{1,0},{2,3},{3,2},{4,5},{5,4},{6,7},{7,6},{8,9},{9,8},{10,11... | collective-permute-start | bytes 786440 | tf_op jit(solution)/shard_map/ppermute | solution.py:375
  158.3 8.8 %collective-permute-start.5 = (bf16[256,512]{1,0:T(8,128)(2,1)}, bf16[256,512]{1,0:T(8,128)(2,1)S(1)}, u32[]{:S(2)}, u32[]{:S(2)}) collective-permute-start(bf16[256,512]{1,0:T(8,128)(2,1)} %shard_map.60), channel_id=1, source_target_pairs={{0,1},{1,0},{2,3},{3,2},{4,5},{5,4},{6,7},{7,6},{8,9},{9,8},{10,11... | collective-permute-start | bytes 786440 | tf_op jit(solution)/shard_map/ppermute | solution.py:375

commit v16 on v14

--- a/solution.py
+++ b/solution.py
@@ -378,10 +378,14 @@
             axis=1,
         )
         own_even = project_half(att_even, out_weight, hidx)
-        parts = [
-            (own.astype(jnp.float32) + got.astype(jnp.float32)).astype(jnp.bfloat16)
-            for own, got in ((own_even, received_even), (own_odd, received_odd))
-        ]
+        out_blocks = []
+        for e in range(per_dev // 2):
+            for own, got in ((own_even, received_even), (own_odd, received_odd)):
+                rows_e = slice(e * BLOCK, (e + 1) * BLOCK)
+                out_blocks.append(
+                    (own[rows_e].astype(jnp.float32) + got[rows_e].astype(jnp.float32)).astype(jnp.bfloat16)
+                )
+        return jnp.concatenate(out_blocks, axis=0)
     even, odd = (p.reshape(per_dev // 2, BLOCK, -1) for p in parts)
     return jnp.stack([even, odd], axis=1).reshape(rows, -1)
 

time: 165 us -> 180 us (1.091)
  waiting for transfers between devices: 44.6 us -> 60.1 us
  other arithmetic: 13.7 us -> 11.5 us
    ppermute x1, waiting for transfers between devices: 0.01 us -> 8.24 us  [per_device(): lax.ppermute(project_half(att_odd, out_weight, 1 - hidx), 'head', swap)]
    ppermute x2, waiting for transfers between devices: 27.7 us -> 35.7 us  [per_device(): far_arrays.append((lax.ppermute(op, 'ctx', pairs),))]
    convert_element_type x2 -> x0, other arithmetic: 3.22 us -> none  [per_device(): (own.astype(jnp.float32) + got.astype(jnp.float32)).astype(jnp.bfloat16)]
    unnamed x13 -> x18, local copies, waits for them, and re-layouts: 5.64 us -> 8.14 us
  transfers between devices with their start and end apart: 8 -> 8, of which waited for: 3 -> 3; matrix products, arithmetic and copies ran while one was open for 11% -> 9% of each run, Pallas kernels for 44% -> 30%
where the time goes in v16:
time: 180 us; the launch traced here: 179 us
  Pallas kernels  71.6 us (40%)
  waiting for transfers between devices  60.1 us (33%)
  local copies, waits for them, and re-layouts  16.7 us (9%)
  starting transfers between devices  12.1 us (7%)
  other arithmetic  11.5 us (6%)
  between operations  7.18 us (4%)
    ppermute x2, waiting for transfers between devices, per_device(): far_arrays.append((lax.ppermute(op, 'ctx', pairs),))  35.7 us
    pallas_call x5, Pallas kernels, project_half(): pl.pallas_call(matmul_kernel, out_shape=jax.ShapeDtypeStruct((rows, cw),...  27.9 us
    pallas_call x1, Pallas kernels, per_device(): pl.pallas_call(per_head(functools.partial(prev_kernel, per_dev, width, sc...  20.1 us
    ppermute x1, waiting for transfers between devices, from_behind(): lax.ppermute(value, axis, [(source, source + steps) for source in range(i...  16.1 us
    pallas_call x1, Pallas kernels, per_device(): pl.pallas_call(per_head(functools.partial(own_kernel, per_dev, width, sca...  13.1 us
    pallas_call x1, Pallas kernels, per_device(): pl.pallas_call(per_head(functools.partial(far_kernel, levels, per_dev, wi...  10.6 us
    ppermute x1, waiting for transfers between devices, per_device(): lax.ppermute(project_half(att_odd, out_weight, 1 - hidx), 'head', swap)  8.24 us
    unnamed x18, local copies, waits for them, and re-layouts  8.14 us
  transfers between devices with their start and end apart: 8, of which 3 were waited for; matrix products, arithmetic and copies ran while one was open for 9% of the time, Pallas kernels for 30%

profile of v16, /device:TPU:28, one launch (start us, length us, event | category | flops | bytes accessed | tf_op | source)
XLA Modules:
  0.0 179.1 jit_solution(3842171549936599989)
XLA Ops:
  0.0 3.3 %copy_bitcast_fusion = (bf16[1,16,512,128]{3,2,1,0:T(8,128)(2,1)S(1)}, bf16[1,16,512,128]{3,2,1,0:T(8,128)(2,1)S(1)}) fusion(bf16[512,16,128]{2,1,0:T(8,128)(2,1)} %param.7, bf16[512,16,128]{2,1,0:T(8,128)(2,1)} %param.6), kind=kLoop, calls=%fused_computation.17 | loop fusion | bytes 8388608 | tf_op jit(solution)/shard_map/stack | solution.py:237
  3.3 2.6 %pad_maximum_fusion.refs_1_.refs_2_ = bf16[2,16,512,128]{3,2,1,0:T(8,128)(2,1)} fusion(bf16[1,16,512,128]{3,2,1,0:T(8,128)(2,1)S(1)} %get-tuple-element.67, bf16[1,16,512,128]{3,2,1,0:T(8,128)(2,1)S(1)} %get-tuple-element.68), kind=kLoop, calls=%fused_computation.7 | loop fusion | flops 2097152 | bytes 8388608 | tf_op jit(solution)/shard_map/stack | solution.py:237
  6.0 1.9 %collective-permute-start = (bf16[2,16,512,128]{3,2,1,0:T(8,128)(2,1)}, bf16[2,16,512,128]{3,2,1,0:T(8,128)(2,1)}, u32[]{:S(2)}, u32[]{:S(2)}) collective-permute-start(bf16[2,16,512,128]{3,2,1,0:T(8,128)(2,1)} %pad_maximum_fusion.refs_1_.refs_2_), channel_id=1, source_target_pairs={{0,2},{2,4},{4,6},{6,8},{8,10},{10,12},{12,14},{14,16},{16,18},{18... | collective-permute-start | bytes 12582920 | tf_op jit(solution)/shard_map/ppermute | solution.py:20
  17.7 3.5 %copy.13 = bf16[512,16,128]{2,0,1:T(8,128)(2,1)} copy(bf16[512,16,128]{2,1,0:T(8,128)(2,1)} %param.5) | data formatting | bytes 4194304 | tf_op args[0]
  22.8 1.6 fusion.6
  25.5 1.5 pad_maximum_fusion.1
  27.0 13.1 %shard_map.55 = (f32[16,512,128]{2,1,0:T(8,128)}, f32[16,512,128]{2,1,0:T(8,128)}) custom-call(bf16[16,512,128]{2,1,0:T(8,128)(2,1)} %bitcast.30, bf16[2,16,512,128]{3,2,1,0:T(8,128)(2,1)} %pad_maximum_fusion.refs_1_.refs_2_, bf16[2,16,512,128]{3,2,1,0:T(8,128)(2,1)} %pad_maximum_fusion.refs_1_.refs_2_), custom_call_target="tpu_custom_call" | custom-call | flops 1073741824 | bytes 29360128 | tf_op jit(solution)/shard_map/pallas_call | solution.py:290
  40.0 16.1 %collective-permute-done.refs_3_.refs_4_ = bf16[2,16,512,128]{3,2,1,0:T(8,128)(2,1)} collective-permute-done((bf16[2,16,512,128]{3,2,1,0:T(8,128)(2,1)}, bf16[2,16,512,128]{3,2,1,0:T(8,128)(2,1)}, u32[]{:S(2)}, u32[]{:S(2)}) %collective-permute-start) | collective-permute-done | bytes 4194336 | tf_op jit(solution)/shard_map/ppermute | solution.py:20
  57.4 1.7 constant_dynamic-slice_fusion.3
  59.1 1.6 pad_maximum_fusion.2
  60.7 2.6 %collective-permute-start.2 = (bf16[2,16,256,128]{3,2,1,0:T(8,128)(2,1)}, bf16[2,16,256,128]{3,2,1,0:T(8,128)(2,1)}, u32[]{:S(2)}, u32[]{:S(2)}) collective-permute-start(bf16[2,16,256,128]{3,2,1,0:T(8,128)(2,1)} %pad_maximum_fusion.2), channel_id=1, source_target_pairs={{0,2},{4,6},{8,10},{12,14},{16,18},{20,22},{24,26},{28,30},{1,3},{... | collective-permute-start | bytes 6291464 | tf_op jit(solution)/shard_map/ppermute | solution.py:304
  64.7 1.5 collective-permute-start.4
  67.5 20.1 %shard_map.56 = (f32[16,256,128]{2,1,0:T(8,128)}, f32[16,256,128]{2,1,0:T(8,128)}, bf16[256,2048]{1,0:T(8,128)(2,1)}) custom-call(s32[10]{0:T(128)} %pad_add_fusion.refs_0_, s32[40]{0:T(128)} %reshape.107.refs_1_, bf16[16,512,128]{2,1,0:T(8,128)(2,1)} %bitcast.31, bf16[2,16,512,128]{3,2,1,0:T(8,128)(2,1)} %collective-permute-done.refs_3_.refs_4_, ...), custom_call_target="tpu_custom_call" | custom-call | flops 1342177280 | bytes 23068672 | tf_op jit(solution)/shard_map/pallas_call | solution.py:316
  87.7 6.6 %shard_map.57 = bf16[256,2048]{1,0:T(8,128)(2,1)} custom-call(s32[1]{0:T(128)} %bitcast.sel_ref, bf16[256,2048]{1,0:T(8,128)(2,1)} %get-tuple-element.32.a_ref, bf16[2048,4096]{1,0:T(8,128)(2,1)} %w_ref.9), custom_call_target="tpu_custom_call" | custom-call | flops 2147483648 | bytes 10485760 | tf_op jit(solution)/shard_map/pallas_call | solution.py:202
  94.3 35.7 %collective-permute-done.4.refs_11_.refs_12_ = bf16[2,16,64,128]{3,2,1,0:T(8,128)(2,1)} collective-permute-done((bf16[2,16,64,128]{3,2,1,0:T(8,128)(2,1)}, bf16[2,16,64,128]{3,2,1,0:T(8,128)(2,1)}, u32[]{:S(2)}, u32[]{:S(2)}) %collective-permute-start.4) | collective-permute-done | bytes 524320 | tf_op jit(solution)/shard_map/ppermute | solution.py:263
  131.7 10.6 %shard_map.58.a_ref = bf16[256,2048]{1,0:T(8,128)(2,1)} custom-call(s32[10]{0:T(128)} %pad_add_fusion.refs_0_, s32[40]{0:T(128)} %reshape.107.refs_1_, bf16[16,512,128]{2,1,0:T(8,128)(2,1)} %bitcast.32, f32[16,256,128]{2,1,0:T(8,128)} %get-tuple-element.33.refs_3_, f32[16,256,128]{2,1,0:T(8,128)} %get-tuple-element.34.refs_4_, ...), custom_call_target="tpu_custom_call" | custom-call | flops 268435456 | bytes 12058624 | tf_op jit(solution)/shard_map/pallas_call | solution.py:360
  142.2 4.0 %shard_map.60 = bf16[256,1024]{1,0:T(8,128)(2,1)} custom-call(s32[1]{0:T(128)} %bitcast.22.sel_ref, bf16[256,2048]{1,0:T(8,128)(2,1)} %shard_map.58.a_ref, bf16[2048,4096]{1,0:T(8,128)(2,1)} %w_ref.9), custom_call_target="tpu_custom_call" | custom-call | flops 1073741824 | bytes 5767168 | tf_op jit(solution)/shard_map/pallas_call | solution.py:202
  146.3 4.0 %shard_map.61 = bf16[256,1024]{1,0:T(8,128)(2,1)} custom-call(s32[1]{0:T(128)} %bitcast.22.sel_ref, bf16[256,2048]{1,0:T(8,128)(2,1)} %shard_map.58.a_ref, bf16[2048,4096]{1,0:T(8,128)(2,1)} %w_ref.9), custom_call_target="tpu_custom_call" | custom-call | flops 1073741824 | bytes 5767168 | tf_op jit(solution)/shard_map/pallas_call | solution.py:202
  150.3 1.5 collective-permute-start.5
  152.4 6.6 %shard_map.62 = bf16[256,2048]{1,0:T(8,128)(2,1)} custom-call(s32[1]{0:T(128)} %bitcast.22.sel_ref, bf16[256,2048]{1,0:T(8,128)(2,1)} %get-tuple-element.32.a_ref, bf16[2048,4096]{1,0:T(8,128)(2,1)} %w_ref.9), custom_call_target="tpu_custom_call" | custom-call | flops 2147483648 | bytes 10485760 | tf_op jit(solution)/shard_map/pallas_call | solution.py:202
  159.0 1.5 collective-permute-start.7
  160.5 6.6 %shard_map.59 = bf16[256,2048]{1,0:T(8,128)(2,1)} custom-call(s32[1]{0:T(128)} %bitcast.sel_ref, bf16[256,2048]{1,0:T(8,128)(2,1)} %shard_map.58.a_ref, bf16[2048,4096]{1,0:T(8,128)(2,1)} %w_ref.9), custom_call_target="tpu_custom_call" | custom-call | flops 2147483648 | bytes 10485760 | tf_op jit(solution)/shard_map/pallas_call | solution.py:202
  168.3 8.2 %collective-permute-done.7 = bf16[256,2048]{1,0:T(8,128)(2,1)S(1)} collective-permute-done((bf16[256,2048]{1,0:T(8,128)(2,1)}, bf16[256,2048]{1,0:T(8,128)(2,1)S(1)}, u32[]{:S(2)}, u32[]{:S(2)}) %collective-permute-start.7) | collective-permute-done | bytes 1048608 | tf_op jit(solution)/shard_map/ppermute | solution.py:357
  177.0 1.3 copy-done.7
  (51 shorter events, 14.1 us)
Async XLA Ops:
  3.3 2.7 %copy-start = (bf16[1,16,512,128]{3,2,1,0:T(8,128)(2,1)}, bf16[1,16,512,128]{3,2,1,0:T(8,128)(2,1)S(1)}, u32[]{:S(2)}) copy-start(bf16[1,16,512,128]{3,2,1,0:T(8,128)(2,1)S(1)} %get-tuple-element.68) | copy-start | bytes 6291460
  3.3 4.6 %copy-start.6 = (s32[128,5]{0,1:T(8,128)S(1)}, s32[128,5]{0,1:T(8,128)}, u32[]{:S(2)}) copy-start(s32[128,5]{0,1:T(8,128)} %param.8) | copy-start | bytes 7684
  6.0 50.1 %collective-permute-start = (bf16[2,16,512,128]{3,2,1,0:T(8,128)(2,1)}, bf16[2,16,512,128]{3,2,1,0:T(8,128)(2,1)}, u32[]{:S(2)}, u32[]{:S(2)}) collective-permute-start(bf16[2,16,512,128]{3,2,1,0:T(8,128)(2,1)} %pad_maximum_fusion.refs_1_.refs_2_), channel_id=1, source_target_pairs={{0,2},{2,4},{4,6},{6,8},{8,10},{10,12},{12,14},{14,16},{16,18},{18... | collective-permute-start | bytes 12582920 | tf_op jit(solution)/shard_map/ppermute | solution.py:20
  21.1 1.7 copy-start.1
  56.1 73.9 %collective-permute-start.1 = (bf16[2,16,256,128]{3,2,1,0:T(8,128)(2,1)}, bf16[2,16,256,128]{3,2,1,0:T(8,128)(2,1)S(1)}, u32[]{:S(2)}, u32[]{:S(2)}) collective-permute-start(bf16[2,16,256,128]{3,2,1,0:T(8,128)(2,1)} %pad_maximum_fusion.1), channel_id=1, source_target_pairs={{0,4},{4,8},{8,12},{12,16},{16,20},{20,24},{24,28},{1,5},{5,9},{9,... | collective-permute-start | bytes 6291464 | tf_op jit(solution)/shard_map/ppermute | solution.py:303
  60.7 69.3 %collective-permute-start.2 = (bf16[2,16,256,128]{3,2,1,0:T(8,128)(2,1)}, bf16[2,16,256,128]{3,2,1,0:T(8,128)(2,1)}, u32[]{:S(2)}, u32[]{:S(2)}) collective-permute-start(bf16[2,16,256,128]{3,2,1,0:T(8,128)(2,1)} %pad_maximum_fusion.2), channel_id=1, source_target_pairs={{0,2},{4,6},{8,10},{12,14},{16,18},{20,22},{24,26},{28,30},{1,3},{... | collective-permute-start | bytes 6291464 | tf_op jit(solution)/shard_map/ppermute | solution.py:304
  63.4 66.7 %collective-permute-start.3 = (bf16[2,16,128,128]{3,2,1,0:T(8,128)(2,1)}, bf16[2,16,128,128]{3,2,1,0:T(8,128)(2,1)S(1)}, u32[]{:S(2)}, u32[]{:S(2)}) collective-permute-start(bf16[2,16,128,128]{3,2,1,0:T(8,128)(2,1)} %pad_maximum_fusion.3), channel_id=1, source_target_pairs={{0,8},{2,10},{4,12},{6,14},{8,16},{10,18},{12,20},{14,22},{16,24},... | collective-permute-start | bytes 3145736 | tf_op jit(solution)/shard_map/ppermute | solution.py:263
  64.7 65.4 %collective-permute-start.4 = (bf16[2,16,64,128]{3,2,1,0:T(8,128)(2,1)}, bf16[2,16,64,128]{3,2,1,0:T(8,128)(2,1)}, u32[]{:S(2)}, u32[]{:S(2)}) collective-permute-start(bf16[2,16,64,128]{3,2,1,0:T(8,128)(2,1)} %get-tuple-element.37), channel_id=1, source_target_pairs={{0,16},{2,18},{4,20},{6,22},{8,24},{10,26},{12,28},{14,30},{1,17},... | collective-permute-start | bytes 1572872 | tf_op jit(solution)/shard_map/ppermute | solution.py:263
  130.0 1.0 copy-start.3
  130.0 1.7 copy-start.2
  150.3 16.7 %collective-permute-start.5 = (bf16[256,1024]{1,0:T(8,128)(2,1)}, bf16[256,1024]{1,0:T(8,128)(2,1)S(1)}, u32[]{:S(2)}, u32[]{:S(2)}) collective-permute-start(bf16[256,1024]{1,0:T(8,128)(2,1)} %shard_map.60), channel_id=1, source_target_pairs={{0,1},{1,0},{2,3},{3,2},{4,5},{5,4},{6,7},{7,6},{8,9},{9,8},{10,11... | collective-permute-start | bytes 1572872 | tf_op jit(solution)/shard_map/ppermute | solution.py:375
  151.8 15.3 %collective-permute-start.6 = (bf16[256,1024]{1,0:T(8,128)(2,1)}, bf16[256,1024]{1,0:T(8,128)(2,1)S(1)}, u32[]{:S(2)}, u32[]{:S(2)}) collective-permute-start(bf16[256,1024]{1,0:T(8,128)(2,1)} %shard_map.61), channel_id=1, source_target_pairs={{0,1},{1,0},{2,3},{3,2},{4,5},{5,4},{6,7},{7,6},{8,9},{9,8},{10,11... | collective-permute-start | bytes 1572872 | tf_op jit(solution)/shard_map/ppermute | solution.py:375
  159.0 17.6 %collective-permute-start.7 = (bf16[256,2048]{1,0:T(8,128)(2,1)}, bf16[256,2048]{1,0:T(8,128)(2,1)S(1)}, u32[]{:S(2)}, u32[]{:S(2)}) collective-permute-start(bf16[256,2048]{1,0:T(8,128)(2,1)} %shard_map.62), channel_id=1, source_target_pairs={{0,1},{1,0},{2,3},{3,2},{4,5},{5,4},{6,7},{7,6},{8,9},{9,8},{10,11... | collective-permute-start | bytes 3145736 | tf_op jit(solution)/shard_map/ppermute | solution.py:357
  167.1 1.2 copy-start.5
  167.1 9.5 %copy-start.4 = (bf16[256,2048]{1,0:T(8,128)(2,1)S(1)}, bf16[256,2048]{1,0:T(8,128)(2,1)}, u32[]{:S(2)}) copy-start(bf16[256,2048]{1,0:T(8,128)(2,1)} %shard_map.57) | copy-start | bytes 3145732
  177.0 1.3 copy-start.7

commit v17 on v14

--- a/solution.py
+++ b/solution.py
@@ -153,7 +153,7 @@
     even_ref = rest[-1]
     neg = jnp.float32(-jnp.inf)
     n_even = per_dev // 2
-    q = jnp.concatenate([q_ref[2 * e * BLOCK:(2 * e + 1) * BLOCK, :] for e in range(n_even)], axis=0)
+    q = q_ref[...].reshape(n_even * BLOCK, -1)
     keys, vals, targets, flags = [], [], [], []
     pos = 0
     for level in levels:
@@ -276,6 +276,8 @@
     k_spec = lambda n: pl.BlockSpec((None, hb, n, width), lambda h, *_: (0, h, 0, 0))
     v_spec = lambda n: pl.BlockSpec((None, hb, n, width), lambda h, *_: (1, h, 0, 0))
     half_rows = rows // 2
+    q_pairs = q_t.reshape(heads, per_dev // 2, 2, BLOCK, width)
+    even_q_spec = pl.BlockSpec((hb, per_dev // 2, None, BLOCK, width), lambda h, *_: (h, 0, 0, 0, 0))
     f32 = jnp.float32
     params = pltpu.CompilerParams(dimension_semantics=("arbitrary",))
     state = lambda n: jax.ShapeDtypeStruct((heads, n, width), f32)
@@ -338,12 +340,12 @@
             grid_spec=pltpu.PrefetchScalarGridSpec(
                 num_scalar_prefetch=2,
                 grid=(heads // hb,),
-                in_specs=[row_spec(rows), row_spec(half_rows), row_spec(half_rows)] + far_specs,
+                in_specs=[even_q_spec, row_spec(half_rows), row_spec(half_rows)] + far_specs,
                 out_specs=out_spec(half_rows),
             ),
             compiler_params=params,
             cost_estimate=cost(2 * BLOCK, half_rows, heads * width * (2 * rows + 8 * half_rows + 2 * sum(a.shape[2] for a in far_operands))),
-        )(meta, used, q_t, acc1, st1, *far_operands)
+        )(meta, used, q_pairs, acc1, st1, *far_operands)
 
         parts = []
         for att in (att_even, att_odd):
@@ -363,12 +365,12 @@
             grid_spec=pltpu.PrefetchScalarGridSpec(
                 num_scalar_prefetch=2,
                 grid=(heads // hb,),
-                in_specs=[row_spec(rows), row_spec(half_rows), row_spec(half_rows)] + far_specs,
+                in_specs=[even_q_spec, row_spec(half_rows), row_spec(half_rows)] + far_specs,
                 out_specs=out_spec(half_rows),
             ),
             compiler_params=params,
             cost_estimate=cost(2 * BLOCK, half_rows, heads * width * (2 * rows + 8 * half_rows + 2 * sum(a.shape[2] for a in far_operands))),
-        )(meta, used, q_t, acc1, st1, *far_operands)
+        )(meta, used, q_pairs, acc1, st1, *far_operands)
 
         received_even = jnp.concatenate(
             [

time: 165 us -> 165 us (level)
  no operation moved by 1% of the time
where the time goes in v17:
time: 165 us; the launch traced here: 164 us
  Pallas kernels  71.6 us (43%)
  waiting for transfers between devices  44.6 us (27%)
  local copies, waits for them, and re-layouts  15.5 us (9%)
  other arithmetic  13.7 us (8%)
  starting transfers between devices  12.1 us (7%)
  between operations  6.99 us (4%)
    pallas_call x5, Pallas kernels, project_half(): pl.pallas_call(matmul_kernel, out_shape=jax.ShapeDtypeStruct((rows, cw),...  28 us
    ppermute x2, waiting for transfers between devices, per_device(): far_arrays.append((lax.ppermute(op, 'ctx', pairs),))  27.7 us
    pallas_call x1, Pallas kernels, per_device(): pl.pallas_call(per_head(functools.partial(prev_kernel, per_dev, width, sc...  20.1 us
    ppermute x1, waiting for transfers between devices, from_behind(): lax.ppermute(value, axis, [(source, source + steps) for source in range(i...  16.3 us
    pallas_call x1, Pallas kernels, per_device(): pl.pallas_call(per_head(functools.partial(own_kernel, per_dev, width, sca...  13 us
    pallas_call x1, Pallas kernels, per_device(): pl.pallas_call(per_head(functools.partial(far_kernel, levels, per_dev, wi...  10.5 us
    unnamed x13, local copies, waits for them, and re-layouts  5.64 us
    another operation x3, other arithmetic, per_device(): jnp.stack([jnp.transpose(keys, (1, 0, 2)), jnp.transpose(values, (1, 0, 2...  5.38 us
  transfers between devices with their start and end apart: 8, of which 3 were waited for; matrix products, arithmetic and copies ran while one was open for 11% of the time, Pallas kernels for 44%

profile of v17, /device:TPU:28, one launch (start us, length us, event | category | flops | bytes accessed | tf_op | source)
XLA Modules:
  0.0 164.4 jit_solution(6861713049894107995)
XLA Ops:
  0.0 3.3 %copy_bitcast_fusion = (bf16[1,16,512,128]{3,2,1,0:T(8,128)(2,1)S(1)}, bf16[1,16,512,128]{3,2,1,0:T(8,128)(2,1)S(1)}) fusion(bf16[512,16,128]{2,1,0:T(8,128)(2,1)} %param.7, bf16[512,16,128]{2,1,0:T(8,128)(2,1)} %param.6), kind=kLoop, calls=%fused_computation.18 | loop fusion | bytes 8388608 | tf_op jit(solution)/shard_map/stack | solution.py:237
  3.3 2.6 %pad_maximum_fusion.refs_1_.refs_2_ = bf16[2,16,512,128]{3,2,1,0:T(8,128)(2,1)} fusion(bf16[1,16,512,128]{3,2,1,0:T(8,128)(2,1)S(1)} %get-tuple-element.67, bf16[1,16,512,128]{3,2,1,0:T(8,128)(2,1)S(1)} %get-tuple-element.68), kind=kLoop, calls=%fused_computation.7 | loop fusion | flops 2097152 | bytes 8388608 | tf_op jit(solution)/shard_map/stack | solution.py:237
  6.0 1.9 %collective-permute-start = (bf16[2,16,512,128]{3,2,1,0:T(8,128)(2,1)}, bf16[2,16,512,128]{3,2,1,0:T(8,128)(2,1)}, u32[]{:S(2)}, u32[]{:S(2)}) collective-permute-start(bf16[2,16,512,128]{3,2,1,0:T(8,128)(2,1)} %pad_maximum_fusion.refs_1_.refs_2_), channel_id=1, source_target_pairs={{0,2},{2,4},{4,6},{6,8},{8,10},{10,12},{12,14},{14,16},{16,18},{18... | collective-permute-start | bytes 12582920 | tf_op jit(solution)/shard_map/ppermute | solution.py:20
  17.4 3.5 %copy.14 = bf16[512,16,128]{2,0,1:T(8,128)(2,1)} copy(bf16[512,16,128]{2,1,0:T(8,128)(2,1)} %param.5) | data formatting | bytes 4194304 | tf_op args[0]
  22.5 1.6 %fusion.6 = (bf16[2,16,64,128]{3,2,1,0:T(8,128)(2,1)}, bf16[2,16,64,128]{3,2,1,0:T(8,128)(2,1)S(1)}, bf16[2,16,64,128]{3,2,1,0:T(8,128)(2,1)S(1)}, bf16[2,16,64,...) fusion(s32[]{:T(128)S(6)} %select_n.66, ...), kind=kLoop, calls=%fused_computation.30 | loop fusion | flops 6291456 | bytes 7340056 | tf_op jit(solution)/shard_map/stack | solution.py:237
  25.2 1.5 pad_maximum_fusion.1
  26.8 13.0 %shard_map.55 = (f32[16,512,128]{2,1,0:T(8,128)}, f32[16,512,128]{2,1,0:T(8,128)}) custom-call(bf16[16,512,128]{2,1,0:T(8,128)(2,1)} %bitcast.34, bf16[2,16,512,128]{3,2,1,0:T(8,128)(2,1)} %pad_maximum_fusion.refs_1_.refs_2_, bf16[2,16,512,128]{3,2,1,0:T(8,128)(2,1)} %pad_maximum_fusion.refs_1_.refs_2_), custom_call_target="tpu_custom_call" | custom-call | flops 1073741824 | bytes 29360128 | tf_op jit(solution)/shard_map/pallas_call | solution.py:292
  39.8 16.3 %collective-permute-done.refs_3_.refs_4_ = bf16[2,16,512,128]{3,2,1,0:T(8,128)(2,1)} collective-permute-done((bf16[2,16,512,128]{3,2,1,0:T(8,128)(2,1)}, bf16[2,16,512,128]{3,2,1,0:T(8,128)(2,1)}, u32[]{:S(2)}, u32[]{:S(2)}) %collective-permute-start) | collective-permute-done | bytes 4194336 | tf_op jit(solution)/shard_map/ppermute | solution.py:20
  57.4 1.7 %constant_dynamic-slice_fusion.3 = (bf16[2,16,64,128]{3,2,1,0:T(8,128)(2,1)S(1)}, bf16[2,16,64,128]{3,2,1,0:T(8,128)(2,1)S(1)}, bf16[2,16,64,128]{3,2,1,0:T(8,128)(2,1)S(1)}, bf16[2,16,64,128]{3,2,1,0:T(8,128)(2,1)S(1)}) fusion(bf16[2,16,512,128]{3,2,1,0:T(8,128)(2,1)} %collective-permute-done.refs_3_.refs_4_, s32[]{:T(128)S(6)} %select_n.68, ...), kind=kLoop, calls=%fused_computation.34 | loop fusion | bytes 4194320 | tf_op jit(solution)/shard_map/dynamic_slice | solution.py:225
  59.1 1.5 pad_maximum_fusion.2
  60.6 2.6 %collective-permute-start.2 = (bf16[2,16,256,128]{3,2,1,0:T(8,128)(2,1)}, bf16[2,16,256,128]{3,2,1,0:T(8,128)(2,1)}, u32[]{:S(2)}, u32[]{:S(2)}) collective-permute-start(bf16[2,16,256,128]{3,2,1,0:T(8,128)(2,1)} %pad_maximum_fusion.2), channel_id=1, source_target_pairs={{0,2},{4,6},{8,10},{12,14},{16,18},{20,22},{24,26},{28,30},{1,3},{... | collective-permute-start | bytes 6291464 | tf_op jit(solution)/shard_map/ppermute | solution.py:306
  66.0 20.1 %shard_map.56 = (f32[16,256,128]{2,1,0:T(8,128)}, f32[16,256,128]{2,1,0:T(8,128)}, bf16[256,2048]{1,0:T(8,128)(2,1)}) custom-call(s32[10]{0:T(128)} %pad_add_fusion.refs_0_, s32[40]{0:T(128)} %reshape.115.refs_1_, bf16[16,512,128]{2,1,0:T(8,128)(2,1)} %bitcast.35, bf16[2,16,512,128]{3,2,1,0:T(8,128)(2,1)} %collective-permute-done.refs_3_.refs_4_, ...), custom_call_target="tpu_custom_call" | custom-call | flops 1342177280 | bytes 23068672 | tf_op jit(solution)/shard_map/pallas_call | solution.py:318
  86.1 6.6 %shard_map.62 = bf16[256,2048]{1,0:T(8,128)(2,1)} custom-call(s32[1]{0:T(128)} %bitcast.23.sel_ref, bf16[256,2048]{1,0:T(8,128)(2,1)} %get-tuple-element.32.a_ref, bf16[2048,4096]{1,0:T(8,128)(2,1)} %w_ref.9), custom_call_target="tpu_custom_call" | custom-call | flops 2147483648 | bytes 10485760 | tf_op jit(solution)/shard_map/pallas_call | solution.py:202
  92.7 1.5 collective-permute-start.7
  94.2 1.5 collective-permute-start.4
  95.7 6.6 %shard_map.57 = bf16[256,2048]{1,0:T(8,128)(2,1)} custom-call(s32[1]{0:T(128)} %bitcast.sel_ref, bf16[256,2048]{1,0:T(8,128)(2,1)} %get-tuple-element.32.a_ref, bf16[2048,4096]{1,0:T(8,128)(2,1)} %w_ref.9), custom_call_target="tpu_custom_call" | custom-call | flops 2147483648 | bytes 10485760 | tf_op jit(solution)/shard_map/pallas_call | solution.py:202
  102.3 27.6 %collective-permute-done.4.refs_11_.refs_12_ = bf16[2,16,64,128]{3,2,1,0:T(8,128)(2,1)} collective-permute-done((bf16[2,16,64,128]{3,2,1,0:T(8,128)(2,1)}, bf16[2,16,64,128]{3,2,1,0:T(8,128)(2,1)}, u32[]{:S(2)}, u32[]{:S(2)}) %collective-permute-start.4) | collective-permute-done | bytes 524320 | tf_op jit(solution)/shard_map/ppermute | solution.py:263
  131.6 10.5 %shard_map.58.a_ref = bf16[256,2048]{1,0:T(8,128)(2,1)} custom-call(s32[10]{0:T(128)} %pad_add_fusion.refs_0_, s32[40]{0:T(128)} %reshape.115.refs_1_, bf16[16,4,2,64,128]{4,3,2,1,0:T(8,128)(2,1)} %bitcast.36, f32[16,256,128]{2,1,0:T(8,128)} %get-tuple-element.33.refs_3_, f32[16,256,128]{2,1,0:T(8,128)} %get-tuple-element.34.refs_4_, ...), custom_call_target="tpu_custom_call" | custom-call | flops 268435456 | bytes 12058624 | tf_op jit(solution)/shard_map/pallas_call | solution.py:362
  142.1 4.1 %shard_map.61 = bf16[256,1024]{1,0:T(8,128)(2,1)} custom-call(s32[1]{0:T(128)} %bitcast.23.sel_ref, bf16[256,2048]{1,0:T(8,128)(2,1)} %shard_map.58.a_ref, bf16[2048,4096]{1,0:T(8,128)(2,1)} %w_ref.9), custom_call_target="tpu_custom_call" | custom-call | flops 1073741824 | bytes 5767168 | tf_op jit(solution)/shard_map/pallas_call | solution.py:202
  146.2 1.5 collective-permute-start.6
  147.6 4.1 %shard_map.60 = bf16[256,1024]{1,0:T(8,128)(2,1)} custom-call(s32[1]{0:T(128)} %bitcast.23.sel_ref, bf16[256,2048]{1,0:T(8,128)(2,1)} %shard_map.58.a_ref, bf16[2048,4096]{1,0:T(8,128)(2,1)} %w_ref.9), custom_call_target="tpu_custom_call" | custom-call | flops 1073741824 | bytes 5767168 | tf_op jit(solution)/shard_map/pallas_call | solution.py:202
  152.3 1.6 add_convert_fusion
  153.9 6.6 %shard_map.59 = bf16[256,2048]{1,0:T(8,128)(2,1)} custom-call(s32[1]{0:T(128)} %bitcast.sel_ref, bf16[256,2048]{1,0:T(8,128)(2,1)} %shard_map.58.a_ref, bf16[2048,4096]{1,0:T(8,128)(2,1)} %w_ref.9), custom_call_target="tpu_custom_call" | custom-call | flops 2147483648 | bytes 10485760 | tf_op jit(solution)/shard_map/pallas_call | solution.py:202
  161.2 1.6 add_convert_fusion.1
  (41 shorter events, 14.0 us)
Async XLA Ops:
  3.3 2.6 %copy-start = (bf16[1,16,512,128]{3,2,1,0:T(8,128)(2,1)}, bf16[1,16,512,128]{3,2,1,0:T(8,128)(2,1)S(1)}, u32[]{:S(2)}) copy-start(bf16[1,16,512,128]{3,2,1,0:T(8,128)(2,1)S(1)} %get-tuple-element.68) | copy-start | bytes 6291460
  3.3 4.6 %copy-start.5 = (s32[128,5]{0,1:T(8,128)S(1)}, s32[128,5]{0,1:T(8,128)}, u32[]{:S(2)}) copy-start(s32[128,5]{0,1:T(8,128)} %param.8) | copy-start | bytes 7684
  6.0 50.1 %collective-permute-start = (bf16[2,16,512,128]{3,2,1,0:T(8,128)(2,1)}, bf16[2,16,512,128]{3,2,1,0:T(8,128)(2,1)}, u32[]{:S(2)}, u32[]{:S(2)}) collective-permute-start(bf16[2,16,512,128]{3,2,1,0:T(8,128)(2,1)} %pad_maximum_fusion.refs_1_.refs_2_), channel_id=1, source_target_pairs={{0,2},{2,4},{4,6},{6,8},{8,10},{10,12},{12,14},{14,16},{16,18},{18... | collective-permute-start | bytes 12582920 | tf_op jit(solution)/shard_map/ppermute | solution.py:20
  20.9 1.7 %copy-start.1 = (bf16[1,16,512,128]{3,2,1,0:T(8,128)(2,1)S(1)}, bf16[1,16,512,128]{3,2,1,0:T(8,128)(2,1)}, u32[]{:S(2)}) copy-start(bf16[1,16,512,128]{3,2,1,0:T(8,128)(2,1)} %copy-done) | copy-start | bytes 6291460
  56.1 73.9 %collective-permute-start.1 = (bf16[2,16,256,128]{3,2,1,0:T(8,128)(2,1)}, bf16[2,16,256,128]{3,2,1,0:T(8,128)(2,1)S(1)}, u32[]{:S(2)}, u32[]{:S(2)}) collective-permute-start(bf16[2,16,256,128]{3,2,1,0:T(8,128)(2,1)} %pad_maximum_fusion.1), channel_id=1, source_target_pairs={{0,4},{4,8},{8,12},{12,16},{16,20},{20,24},{24,28},{1,5},{5,9},{9,... | collective-permute-start | bytes 6291464 | tf_op jit(solution)/shard_map/ppermute | solution.py:305
  60.6 69.4 %collective-permute-start.2 = (bf16[2,16,256,128]{3,2,1,0:T(8,128)(2,1)}, bf16[2,16,256,128]{3,2,1,0:T(8,128)(2,1)}, u32[]{:S(2)}, u32[]{:S(2)}) collective-permute-start(bf16[2,16,256,128]{3,2,1,0:T(8,128)(2,1)} %pad_maximum_fusion.2), channel_id=1, source_target_pairs={{0,2},{4,6},{8,10},{12,14},{16,18},{20,22},{24,26},{28,30},{1,3},{... | collective-permute-start | bytes 6291464 | tf_op jit(solution)/shard_map/ppermute | solution.py:306
  63.3 66.7 %collective-permute-start.3 = (bf16[2,16,128,128]{3,2,1,0:T(8,128)(2,1)}, bf16[2,16,128,128]{3,2,1,0:T(8,128)(2,1)S(1)}, u32[]{:S(2)}, u32[]{:S(2)}) collective-permute-start(bf16[2,16,128,128]{3,2,1,0:T(8,128)(2,1)} %pad_maximum_fusion.4), channel_id=1, source_target_pairs={{0,8},{2,10},{4,12},{6,14},{8,16},{10,18},{12,20},{14,22},{16,24},... | collective-permute-start | bytes 3145736 | tf_op jit(solution)/shard_map/ppermute | solution.py:263
  92.7 59.5 %collective-permute-start.7 = (bf16[256,2048]{1,0:T(8,128)(2,1)}, bf16[256,2048]{1,0:T(8,128)(2,1)}, u32[]{:S(2)}, u32[]{:S(2)}) collective-permute-start(bf16[256,2048]{1,0:T(8,128)(2,1)} %shard_map.62), channel_id=1, source_target_pairs={{0,1},{1,0},{2,3},{3,2},{4,5},{5,4},{6,7},{7,6},{8,9},{9,8},{10,11... | collective-permute-start | bytes 3145736 | tf_op jit(solution)/shard_map/ppermute | solution.py:359
  94.2 35.8 %collective-permute-start.4 = (bf16[2,16,64,128]{3,2,1,0:T(8,128)(2,1)}, bf16[2,16,64,128]{3,2,1,0:T(8,128)(2,1)}, u32[]{:S(2)}, u32[]{:S(2)}) collective-permute-start(bf16[2,16,64,128]{3,2,1,0:T(8,128)(2,1)} %get-tuple-element.37), channel_id=1, source_target_pairs={{0,16},{2,18},{4,20},{6,22},{8,24},{10,26},{12,28},{14,30},{1,17},... | collective-permute-start | bytes 1572872 | tf_op jit(solution)/shard_map/ppermute | solution.py:263
  130.0 1.0 copy-start.3
  130.0 1.6 %copy-start.2 = (bf16[2,16,256,128]{3,2,1,0:T(8,128)(2,1)}, bf16[2,16,256,128]{3,2,1,0:T(8,128)(2,1)S(1)}, u32[]{:S(2)}) copy-start(bf16[2,16,256,128]{3,2,1,0:T(8,128)(2,1)S(1)} %collective-permute-done.1.refs_5_.refs_6_) | copy-start | bytes 6291460
  146.2 6.1 %copy-start.4 = (bf16[256,2048]{1,0:T(8,128)(2,1)S(1)}, bf16[256,2048]{1,0:T(8,128)(2,1)}, u32[]{:S(2)}) copy-start(bf16[256,2048]{1,0:T(8,128)(2,1)} %shard_map.57) | copy-start | bytes 3145732
  146.2 14.3 %collective-permute-start.6 = (bf16[256,1024]{1,0:T(8,128)(2,1)}, bf16[256,1024]{1,0:T(8,128)(2,1)S(1)}, u32[]{:S(2)}, u32[]{:S(2)}) collective-permute-start(bf16[256,1024]{1,0:T(8,128)(2,1)} %shard_map.61), channel_id=1, source_target_pairs={{0,1},{1,0},{2,3},{3,2},{4,5},{5,4},{6,7},{7,6},{8,9},{9,8},{10,11... | collective-permute-start | bytes 1572872 | tf_op jit(solution)/shard_map/ppermute | solution.py:377
  151.7 9.5 %collective-permute-start.5 = (bf16[256,1024]{1,0:T(8,128)(2,1)}, bf16[256,1024]{1,0:T(8,128)(2,1)S(1)}, u32[]{:S(2)}, u32[]{:S(2)}) collective-permute-start(bf16[256,1024]{1,0:T(8,128)(2,1)} %shard_map.60), channel_id=1, source_target_pairs={{0,1},{1,0},{2,3},{3,2},{4,5},{5,4},{6,7},{7,6},{8,9},{9,8},{10,11... | collective-permute-start | bytes 1572872 | tf_op jit(solution)/shard_map/ppermute | solution.py:377

commit v18 on v17

--- a/solution.py
+++ b/solution.py
@@ -277,7 +277,12 @@
     v_spec = lambda n: pl.BlockSpec((None, hb, n, width), lambda h, *_: (1, h, 0, 0))
     half_rows = rows // 2
     q_pairs = q_t.reshape(heads, per_dev // 2, 2, BLOCK, width)
-    even_q_spec = pl.BlockSpec((hb, per_dev // 2, None, BLOCK, width), lambda h, *_: (h, 0, 0, 0, 0))
+    hc = math.gcd(heads, 2)
+    even_q_spec = pl.BlockSpec((hc, per_dev // 2, None, BLOCK, width), lambda h, *_: (h, 0, 0, 0, 0))
+    c_row = lambda n: pl.BlockSpec((hc, n, width), lambda h, *_: (h, 0, 0))
+    c_out = lambda n: pl.BlockSpec((n, hc * width), lambda h, *_: (0, h))
+    c_k = lambda n: pl.BlockSpec((None, hc, n, width), lambda h, *_: (0, h, 0, 0))
+    c_v = lambda n: pl.BlockSpec((None, hc, n, width), lambda h, *_: (1, h, 0, 0))
     f32 = jnp.float32
     params = pltpu.CompilerParams(dimension_semantics=("arbitrary",))
     state = lambda n: jax.ShapeDtypeStruct((heads, n, width), f32)
@@ -313,7 +318,7 @@
     far_specs, far_operands = [], []
     for group in far_arrays:
         for a in group:
-            far_specs += [k_spec(a.shape[2]), v_spec(a.shape[2])]
+            far_specs += [c_k(a.shape[2]), c_v(a.shape[2])]
             far_operands += [a, a]
     acc1, st1, att_odd = pl.pallas_call(
         per_head(functools.partial(prev_kernel, per_dev, width, scale), 2, 7, 1, width, hb),
@@ -335,13 +340,13 @@
     n_head = lax.axis_size("head")
     if n_head != 2:
         att_even = pl.pallas_call(
-            per_head(functools.partial(far_kernel, levels, per_dev, width, scale), 2, 0, 1, width, hb),
+            per_head(functools.partial(far_kernel, levels, per_dev, width, scale), 2, 0, 1, width, hc),
             out_shape=jax.ShapeDtypeStruct((half_rows, heads * width), queries.dtype),
             grid_spec=pltpu.PrefetchScalarGridSpec(
                 num_scalar_prefetch=2,
-                grid=(heads // hb,),
-                in_specs=[even_q_spec, row_spec(half_rows), row_spec(half_rows)] + far_specs,
-                out_specs=out_spec(half_rows),
+                grid=(heads // hc,),
+                in_specs=[even_q_spec, c_row(half_rows), c_row(half_rows)] + far_specs,
+                out_specs=c_out(half_rows),
             ),
             compiler_params=params,
             cost_estimate=cost(2 * BLOCK, half_rows, heads * width * (2 * rows + 8 * half_rows + 2 * sum(a.shape[2] for a in far_operands))),
@@ -360,13 +365,13 @@
         own_odd = project_half(att_odd, out_weight, hidx)
         acc1, st1, own_odd = lax.optimization_barrier((acc1, st1, own_odd))
         att_even = pl.pallas_call(
-            per_head(functools.partial(far_kernel, levels, per_dev, width, scale), 2, 0, 1, width, hb),
+            per_head(functools.partial(far_kernel, levels, per_dev, width, scale), 2, 0, 1, width, hc),
             out_shape=jax.ShapeDtypeStruct((half_rows, heads * width), queries.dtype),
             grid_spec=pltpu.PrefetchScalarGridSpec(
                 num_scalar_prefetch=2,
-                grid=(heads // hb,),
-                in_specs=[even_q_spec, row_spec(half_rows), row_spec(half_rows)] + far_specs,
-                out_specs=out_spec(half_rows),
+                grid=(heads // hc,),
+                in_specs=[even_q_spec, c_row(half_rows), c_row(half_rows)] + far_specs,
+                out_specs=c_out(half_rows),
             ),
             compiler_params=params,
             cost_estimate=cost(2 * BLOCK, half_rows, heads * width * (2 * rows + 8 * half_rows + 2 * sum(a.shape[2] for a in far_operands))),

time: 165 us -> 167 us (1.012)
  no operation moved by 1% of the time
where the time goes in v18:
time: 167 us; the launch traced here: 166 us
  Pallas kernels  73.2 us (44%)
  waiting for transfers between devices  44.6 us (27%)
  local copies, waits for them, and re-layouts  15.5 us (9%)
  other arithmetic  13.7 us (8%)
  starting transfers between devices  12.1 us (7%)
  between operations  6.99 us (4%)
    pallas_call x5, Pallas kernels, project_half(): pl.pallas_call(matmul_kernel, out_shape=jax.ShapeDtypeStruct((rows, cw),...  28 us
    ppermute x2, waiting for transfers between devices, per_device(): far_arrays.append((lax.ppermute(op, 'ctx', pairs),))  27.7 us
    pallas_call x1, Pallas kernels, per_device(): pl.pallas_call(per_head(functools.partial(prev_kernel, per_dev, width, sc...  20.1 us
    ppermute x1, waiting for transfers between devices, from_behind(): lax.ppermute(value, axis, [(source, source + steps) for source in range(i...  16.3 us
    pallas_call x1, Pallas kernels, per_device(): pl.pallas_call(per_head(functools.partial(own_kernel, per_dev, width, sca...  13 us
    pallas_call x1, Pallas kernels, per_device(): pl.pallas_call(per_head(functools.partial(far_kernel, levels, per_dev, wi...  12.1 us
    unnamed x13, local copies, waits for them, and re-layouts  5.64 us
    another operation x3, other arithmetic, per_device(): jnp.stack([jnp.transpose(keys, (1, 0, 2)), jnp.transpose(values, (1, 0, 2...  5.38 us
  transfers between devices with their start and end apart: 8, of which 3 were waited for; matrix products, arithmetic and copies ran while one was open for 11% of the time, Pallas kernels for 44%

profile of v18, /device:TPU:28, one launch (start us, length us, event | category | flops | bytes accessed | tf_op | source)
XLA Modules:
  0.0 166.1 jit_solution(12562170770872659606)
XLA Ops:
  0.0 3.3 %copy_bitcast_fusion = (bf16[1,16,512,128]{3,2,1,0:T(8,128)(2,1)S(1)}, bf16[1,16,512,128]{3,2,1,0:T(8,128)(2,1)S(1)}) fusion(bf16[512,16,128]{2,1,0:T(8,128)(2,1)} %param.7, bf16[512,16,128]{2,1,0:T(8,128)(2,1)} %param.6), kind=kLoop, calls=%fused_computation.18 | loop fusion | bytes 8388608 | tf_op jit(solution)/shard_map/stack | solution.py:237
  3.3 2.6 %pad_maximum_fusion.refs_1_.refs_2_ = bf16[2,16,512,128]{3,2,1,0:T(8,128)(2,1)} fusion(bf16[1,16,512,128]{3,2,1,0:T(8,128)(2,1)S(1)} %get-tuple-element.67, bf16[1,16,512,128]{3,2,1,0:T(8,128)(2,1)S(1)} %get-tuple-element.68), kind=kLoop, calls=%fused_computation.7 | loop fusion | flops 2097152 | bytes 8388608 | tf_op jit(solution)/shard_map/stack | solution.py:237
  6.0 1.9 %collective-permute-start = (bf16[2,16,512,128]{3,2,1,0:T(8,128)(2,1)}, bf16[2,16,512,128]{3,2,1,0:T(8,128)(2,1)}, u32[]{:S(2)}, u32[]{:S(2)}) collective-permute-start(bf16[2,16,512,128]{3,2,1,0:T(8,128)(2,1)} %pad_maximum_fusion.refs_1_.refs_2_), channel_id=1, source_target_pairs={{0,2},{2,4},{4,6},{6,8},{8,10},{10,12},{12,14},{14,16},{16,18},{18... | collective-permute-start | bytes 12582920 | tf_op jit(solution)/shard_map/ppermute | solution.py:20
  17.4 3.5 %copy.14 = bf16[512,16,128]{2,0,1:T(8,128)(2,1)} copy(bf16[512,16,128]{2,1,0:T(8,128)(2,1)} %param.5) | data formatting | bytes 4194304 | tf_op args[0]
  22.5 1.6 fusion.6
  25.2 1.5 pad_maximum_fusion.1
  26.8 13.0 %shard_map.55 = (f32[16,512,128]{2,1,0:T(8,128)}, f32[16,512,128]{2,1,0:T(8,128)}) custom-call(bf16[16,512,128]{2,1,0:T(8,128)(2,1)} %bitcast.34, bf16[2,16,512,128]{3,2,1,0:T(8,128)(2,1)} %pad_maximum_fusion.refs_1_.refs_2_, bf16[2,16,512,128]{3,2,1,0:T(8,128)(2,1)} %pad_maximum_fusion.refs_1_.refs_2_), custom_call_target="tpu_custom_call" | custom-call | flops 1073741824 | bytes 29360128 | tf_op jit(solution)/shard_map/pallas_call | solution.py:297
  39.8 16.3 %collective-permute-done.refs_3_.refs_4_ = bf16[2,16,512,128]{3,2,1,0:T(8,128)(2,1)} collective-permute-done((bf16[2,16,512,128]{3,2,1,0:T(8,128)(2,1)}, bf16[2,16,512,128]{3,2,1,0:T(8,128)(2,1)}, u32[]{:S(2)}, u32[]{:S(2)}) %collective-permute-start) | collective-permute-done | bytes 4194336 | tf_op jit(solution)/shard_map/ppermute | solution.py:20
  57.4 1.7 %constant_dynamic-slice_fusion.3 = (bf16[2,16,64,128]{3,2,1,0:T(8,128)(2,1)S(1)}, bf16[2,16,64,128]{3,2,1,0:T(8,128)(2,1)S(1)}, bf16[2,16,64,128]{3,2,1,0:T(8,128)(2,1)S(1)}, bf16[2,16,64,128]{3,2,1,0:T(8,128)(2,1)S(1)}) fusion(bf16[2,16,512,128]{3,2,1,0:T(8,128)(2,1)} %collective-permute-done.refs_3_.refs_4_, s32[]{:T(128)S(6)} %select_n.68, ...), kind=kLoop, calls=%fused_computation.34 | loop fusion | bytes 4194320 | tf_op jit(solution)/shard_map/dynamic_slice | solution.py:225
  59.1 1.5 pad_maximum_fusion.2
  60.6 2.6 %collective-permute-start.2 = (bf16[2,16,256,128]{3,2,1,0:T(8,128)(2,1)}, bf16[2,16,256,128]{3,2,1,0:T(8,128)(2,1)}, u32[]{:S(2)}, u32[]{:S(2)}) collective-permute-start(bf16[2,16,256,128]{3,2,1,0:T(8,128)(2,1)} %pad_maximum_fusion.2), channel_id=1, source_target_pairs={{0,2},{4,6},{8,10},{12,14},{16,18},{20,22},{24,26},{28,30},{1,3},{... | collective-permute-start | bytes 6291464 | tf_op jit(solution)/shard_map/ppermute | solution.py:311
  66.0 20.1 %shard_map.56 = (f32[16,256,128]{2,1,0:T(8,128)}, f32[16,256,128]{2,1,0:T(8,128)}, bf16[256,2048]{1,0:T(8,128)(2,1)}) custom-call(s32[10]{0:T(128)} %pad_add_fusion.refs_0_, s32[40]{0:T(128)} %reshape.115.refs_1_, bf16[16,512,128]{2,1,0:T(8,128)(2,1)} %bitcast.35, bf16[2,16,512,128]{3,2,1,0:T(8,128)(2,1)} %collective-permute-done.refs_3_.refs_4_, ...), custom_call_target="tpu_custom_call" | custom-call | flops 1342177280 | bytes 23068672 | tf_op jit(solution)/shard_map/pallas_call | solution.py:323
  86.1 6.6 %shard_map.62 = bf16[256,2048]{1,0:T(8,128)(2,1)} custom-call(s32[1]{0:T(128)} %bitcast.23.sel_ref, bf16[256,2048]{1,0:T(8,128)(2,1)} %get-tuple-element.32.a_ref, bf16[2048,4096]{1,0:T(8,128)(2,1)} %w_ref.9), custom_call_target="tpu_custom_call" | custom-call | flops 2147483648 | bytes 10485760 | tf_op jit(solution)/shard_map/pallas_call | solution.py:202
  92.7 1.5 collective-permute-start.7
  94.2 1.5 collective-permute-start.4
  95.7 6.6 %shard_map.57 = bf16[256,2048]{1,0:T(8,128)(2,1)} custom-call(s32[1]{0:T(128)} %bitcast.sel_ref, bf16[256,2048]{1,0:T(8,128)(2,1)} %get-tuple-element.32.a_ref, bf16[2048,4096]{1,0:T(8,128)(2,1)} %w_ref.9), custom_call_target="tpu_custom_call" | custom-call | flops 2147483648 | bytes 10485760 | tf_op jit(solution)/shard_map/pallas_call | solution.py:202
  102.3 27.6 %collective-permute-done.4.refs_11_.refs_12_ = bf16[2,16,64,128]{3,2,1,0:T(8,128)(2,1)} collective-permute-done((bf16[2,16,64,128]{3,2,1,0:T(8,128)(2,1)}, bf16[2,16,64,128]{3,2,1,0:T(8,128)(2,1)}, u32[]{:S(2)}, u32[]{:S(2)}) %collective-permute-start.4) | collective-permute-done | bytes 524320 | tf_op jit(solution)/shard_map/ppermute | solution.py:263
  131.6 12.1 %shard_map.58.a_ref = bf16[256,2048]{1,0:T(8,128)(2,1)} custom-call(s32[10]{0:T(128)} %pad_add_fusion.refs_0_, s32[40]{0:T(128)} %reshape.115.refs_1_, bf16[16,4,2,64,128]{4,3,2,1,0:T(8,128)(2,1)} %bitcast.36, f32[16,256,128]{2,1,0:T(8,128)} %get-tuple-element.33.refs_3_, f32[16,256,128]{2,1,0:T(8,128)} %get-tuple-element.34.refs_4_, ...), custom_call_target="tpu_custom_call" | custom-call | flops 268435456 | bytes 12058624 | tf_op jit(solution)/shard_map/pallas_call | solution.py:367
  143.7 4.1 %shard_map.61 = bf16[256,1024]{1,0:T(8,128)(2,1)} custom-call(s32[1]{0:T(128)} %bitcast.23.sel_ref, bf16[256,2048]{1,0:T(8,128)(2,1)} %shard_map.58.a_ref, bf16[2048,4096]{1,0:T(8,128)(2,1)} %w_ref.9), custom_call_target="tpu_custom_call" | custom-call | flops 1073741824 | bytes 5767168 | tf_op jit(solution)/shard_map/pallas_call | solution.py:202
  147.8 1.5 collective-permute-start.6
  149.3 4.1 %shard_map.60 = bf16[256,1024]{1,0:T(8,128)(2,1)} custom-call(s32[1]{0:T(128)} %bitcast.23.sel_ref, bf16[256,2048]{1,0:T(8,128)(2,1)} %shard_map.58.a_ref, bf16[2048,4096]{1,0:T(8,128)(2,1)} %w_ref.9), custom_call_target="tpu_custom_call" | custom-call | flops 1073741824 | bytes 5767168 | tf_op jit(solution)/shard_map/pallas_call | solution.py:202
  153.9 1.6 add_convert_fusion
  155.5 6.6 %shard_map.59 = bf16[256,2048]{1,0:T(8,128)(2,1)} custom-call(s32[1]{0:T(128)} %bitcast.sel_ref, bf16[256,2048]{1,0:T(8,128)(2,1)} %shard_map.58.a_ref, bf16[2048,4096]{1,0:T(8,128)(2,1)} %w_ref.9), custom_call_target="tpu_custom_call" | custom-call | flops 2147483648 | bytes 10485760 | tf_op jit(solution)/shard_map/pallas_call | solution.py:202
  162.8 1.6 add_convert_fusion.1
  (41 shorter events, 13.9 us)
Async XLA Ops:
  3.3 2.6 %copy-start = (bf16[1,16,512,128]{3,2,1,0:T(8,128)(2,1)}, bf16[1,16,512,128]{3,2,1,0:T(8,128)(2,1)S(1)}, u32[]{:S(2)}) copy-start(bf16[1,16,512,128]{3,2,1,0:T(8,128)(2,1)S(1)} %get-tuple-element.68) | copy-start | bytes 6291460
  3.3 4.6 %copy-start.5 = (s32[128,5]{0,1:T(8,128)S(1)}, s32[128,5]{0,1:T(8,128)}, u32[]{:S(2)}) copy-start(s32[128,5]{0,1:T(8,128)} %param.8) | copy-start | bytes 7684
  6.0 50.1 %collective-permute-start = (bf16[2,16,512,128]{3,2,1,0:T(8,128)(2,1)}, bf16[2,16,512,128]{3,2,1,0:T(8,128)(2,1)}, u32[]{:S(2)}, u32[]{:S(2)}) collective-permute-start(bf16[2,16,512,128]{3,2,1,0:T(8,128)(2,1)} %pad_maximum_fusion.refs_1_.refs_2_), channel_id=1, source_target_pairs={{0,2},{2,4},{4,6},{6,8},{8,10},{10,12},{12,14},{14,16},{16,18},{18... | collective-permute-start | bytes 12582920 | tf_op jit(solution)/shard_map/ppermute | solution.py:20
  20.9 1.7 %copy-start.1 = (bf16[1,16,512,128]{3,2,1,0:T(8,128)(2,1)S(1)}, bf16[1,16,512,128]{3,2,1,0:T(8,128)(2,1)}, u32[]{:S(2)}) copy-start(bf16[1,16,512,128]{3,2,1,0:T(8,128)(2,1)} %copy-done) | copy-start | bytes 6291460
  56.1 73.9 %collective-permute-start.1 = (bf16[2,16,256,128]{3,2,1,0:T(8,128)(2,1)}, bf16[2,16,256,128]{3,2,1,0:T(8,128)(2,1)S(1)}, u32[]{:S(2)}, u32[]{:S(2)}) collective-permute-start(bf16[2,16,256,128]{3,2,1,0:T(8,128)(2,1)} %pad_maximum_fusion.1), channel_id=1, source_target_pairs={{0,4},{4,8},{8,12},{12,16},{16,20},{20,24},{24,28},{1,5},{5,9},{9,... | collective-permute-start | bytes 6291464 | tf_op jit(solution)/shard_map/ppermute | solution.py:310
  60.6 69.4 %collective-permute-start.2 = (bf16[2,16,256,128]{3,2,1,0:T(8,128)(2,1)}, bf16[2,16,256,128]{3,2,1,0:T(8,128)(2,1)}, u32[]{:S(2)}, u32[]{:S(2)}) collective-permute-start(bf16[2,16,256,128]{3,2,1,0:T(8,128)(2,1)} %pad_maximum_fusion.2), channel_id=1, source_target_pairs={{0,2},{4,6},{8,10},{12,14},{16,18},{20,22},{24,26},{28,30},{1,3},{... | collective-permute-start | bytes 6291464 | tf_op jit(solution)/shard_map/ppermute | solution.py:311
  63.3 66.7 %collective-permute-start.3 = (bf16[2,16,128,128]{3,2,1,0:T(8,128)(2,1)}, bf16[2,16,128,128]{3,2,1,0:T(8,128)(2,1)S(1)}, u32[]{:S(2)}, u32[]{:S(2)}) collective-permute-start(bf16[2,16,128,128]{3,2,1,0:T(8,128)(2,1)} %pad_maximum_fusion.4), channel_id=1, source_target_pairs={{0,8},{2,10},{4,12},{6,14},{8,16},{10,18},{12,20},{14,22},{16,24},... | collective-permute-start | bytes 3145736 | tf_op jit(solution)/shard_map/ppermute | solution.py:263
  92.7 61.1 %collective-permute-start.7 = (bf16[256,2048]{1,0:T(8,128)(2,1)}, bf16[256,2048]{1,0:T(8,128)(2,1)}, u32[]{:S(2)}, u32[]{:S(2)}) collective-permute-start(bf16[256,2048]{1,0:T(8,128)(2,1)} %shard_map.62), channel_id=1, source_target_pairs={{0,1},{1,0},{2,3},{3,2},{4,5},{5,4},{6,7},{7,6},{8,9},{9,8},{10,11... | collective-permute-start | bytes 3145736 | tf_op jit(solution)/shard_map/ppermute | solution.py:364
  94.2 35.8 %collective-permute-start.4 = (bf16[2,16,64,128]{3,2,1,0:T(8,128)(2,1)}, bf16[2,16,64,128]{3,2,1,0:T(8,128)(2,1)}, u32[]{:S(2)}, u32[]{:S(2)}) collective-permute-start(bf16[2,16,64,128]{3,2,1,0:T(8,128)(2,1)} %get-tuple-element.37), channel_id=1, source_target_pairs={{0,16},{2,18},{4,20},{6,22},{8,24},{10,26},{12,28},{14,30},{1,17},... | collective-permute-start | bytes 1572872 | tf_op jit(solution)/shard_map/ppermute | solution.py:263
  130.0 1.0 copy-start.3
  130.0 1.6 copy-start.2
  147.8 6.1 %copy-start.4 = (bf16[256,2048]{1,0:T(8,128)(2,1)S(1)}, bf16[256,2048]{1,0:T(8,128)(2,1)}, u32[]{:S(2)}) copy-start(bf16[256,2048]{1,0:T(8,128)(2,1)} %shard_map.57) | copy-start | bytes 3145732
  147.8 14.3 %collective-permute-start.6 = (bf16[256,1024]{1,0:T(8,128)(2,1)}, bf16[256,1024]{1,0:T(8,128)(2,1)S(1)}, u32[]{:S(2)}, u32[]{:S(2)}) collective-permute-start(bf16[256,1024]{1,0:T(8,128)(2,1)} %shard_map.61), channel_id=1, source_target_pairs={{0,1},{1,0},{2,3},{3,2},{4,5},{5,4},{6,7},{7,6},{8,9},{9,8},{10,11... | collective-permute-start | bytes 1572872 | tf_op jit(solution)/shard_map/ppermute | solution.py:382
  153.3 9.5 %collective-permute-start.5 = (bf16[256,1024]{1,0:T(8,128)(2,1)}, bf16[256,1024]{1,0:T(8,128)(2,1)S(1)}, u32[]{:S(2)}, u32[]{:S(2)}) collective-permute-start(bf16[256,1024]{1,0:T(8,128)(2,1)} %shard_map.60), channel_id=1, source_target_pairs={{0,1},{1,0},{2,3},{3,2},{4,5},{5,4},{6,7},{7,6},{8,9},{9,8},{10,11... | collective-permute-start | bytes 1572872 | tf_op jit(solution)/shard_map/ppermute | solution.py:382

commit v19 on v14

--- a/solution.py
+++ b/solution.py
@@ -192,12 +192,14 @@
     )
 
 
-def project_half(attended, weight, half, tn=512, part=0, parts=1):
+def project_half(attended, weight, half, tn=512, part=0, parts=1, span=None):
     rows, depth = attended.shape
     cw = weight.shape[1] // 2
     total_steps = cw // tn
     steps = total_steps // parts
     first = part * steps
+    if span is not None:
+        first, steps = span
     cw = steps * tn
     return pl.pallas_call(
         matmul_kernel,
@@ -372,8 +374,8 @@
 
         received_even = jnp.concatenate(
             [
-                lax.ppermute(project_half(att_even, out_weight, 1 - hidx, part=p, parts=2), "head", swap)
-                for p in range(2)
+                lax.ppermute(project_half(att_even, out_weight, 1 - hidx, span=span), "head", swap)
+                for span in ((0, 1), (1, out_weight.shape[1] // 2 // 512 - 1))
             ],
             axis=1,
         )

time: 165 us -> 167 us (1.012)
  no operation moved by 1% of the time
where the time goes in v19:
time: 167 us; the launch traced here: 166 us
  Pallas kernels  72.7 us (44%)
  waiting for transfers between devices  45.2 us (27%)
  local copies, waits for them, and re-layouts  15.6 us (9%)
  other arithmetic  13.6 us (8%)
  starting transfers between devices  12.1 us (7%)
  between operations  6.99 us (4%)
    pallas_call x5, Pallas kernels, project_half(): pl.pallas_call(matmul_kernel, out_shape=jax.ShapeDtypeStruct((rows, cw),...  29 us
    ppermute x2, waiting for transfers between devices, per_device(): far_arrays.append((lax.ppermute(op, 'ctx', pairs),))  27.5 us
    pallas_call x1, Pallas kernels, per_device(): pl.pallas_call(per_head(functools.partial(prev_kernel, per_dev, width, sc...  20.1 us
    ppermute x1, waiting for transfers between devices, from_behind(): lax.ppermute(value, axis, [(source, source + steps) for source in range(i...  16.3 us
    pallas_call x1, Pallas kernels, per_device(): pl.pallas_call(per_head(functools.partial(own_kernel, per_dev, width, sca...  13 us
    pallas_call x1, Pallas kernels, per_device(): pl.pallas_call(per_head(functools.partial(far_kernel, levels, per_dev, wi...  10.5 us
    unnamed x13, local copies, waits for them, and re-layouts  5.64 us
    another operation x3, other arithmetic, per_device(): jnp.stack([jnp.transpose(keys, (1, 0, 2)), jnp.transpose(values, (1, 0, 2...  5.38 us
  transfers between devices with their start and end apart: 8, of which 3 were waited for; matrix products, arithmetic and copies ran while one was open for 11% of the time, Pallas kernels for 44%

profile of v19, /device:TPU:28, one launch (start us, length us, event | category | flops | bytes accessed | tf_op | source)
XLA Modules:
  0.0 166.2 jit_solution(17010075968095725768)
XLA Ops:
  0.0 3.3 %copy_bitcast_fusion = (bf16[1,16,512,128]{3,2,1,0:T(8,128)(2,1)S(1)}, bf16[1,16,512,128]{3,2,1,0:T(8,128)(2,1)S(1)}) fusion(bf16[512,16,128]{2,1,0:T(8,128)(2,1)} %param.7, bf16[512,16,128]{2,1,0:T(8,128)(2,1)} %param.6), kind=kLoop, calls=%fused_computation.18 | loop fusion | bytes 8388608 | tf_op jit(solution)/shard_map/stack | solution.py:239
  3.3 2.6 %pad_maximum_fusion.refs_1_.refs_2_ = bf16[2,16,512,128]{3,2,1,0:T(8,128)(2,1)} fusion(bf16[1,16,512,128]{3,2,1,0:T(8,128)(2,1)S(1)} %get-tuple-element.67, bf16[1,16,512,128]{3,2,1,0:T(8,128)(2,1)S(1)} %get-tuple-element.68), kind=kLoop, calls=%fused_computation.7 | loop fusion | flops 2097152 | bytes 8388608 | tf_op jit(solution)/shard_map/stack | solution.py:239
  6.0 1.9 %collective-permute-start = (bf16[2,16,512,128]{3,2,1,0:T(8,128)(2,1)}, bf16[2,16,512,128]{3,2,1,0:T(8,128)(2,1)}, u32[]{:S(2)}, u32[]{:S(2)}) collective-permute-start(bf16[2,16,512,128]{3,2,1,0:T(8,128)(2,1)} %pad_maximum_fusion.refs_1_.refs_2_), channel_id=1, source_target_pairs={{0,2},{2,4},{4,6},{6,8},{8,10},{10,12},{12,14},{14,16},{16,18},{18... | collective-permute-start | bytes 12582920 | tf_op jit(solution)/shard_map/ppermute | solution.py:20
  17.4 3.5 %copy.14 = bf16[512,16,128]{2,0,1:T(8,128)(2,1)} copy(bf16[512,16,128]{2,1,0:T(8,128)(2,1)} %param.5) | data formatting | bytes 4194304 | tf_op args[0]
  22.5 1.6 fusion.6
  25.2 1.5 pad_maximum_fusion.1
  26.8 13.0 %shard_map.55 = (f32[16,512,128]{2,1,0:T(8,128)}, f32[16,512,128]{2,1,0:T(8,128)}) custom-call(bf16[16,512,128]{2,1,0:T(8,128)(2,1)} %bitcast.33, bf16[2,16,512,128]{3,2,1,0:T(8,128)(2,1)} %pad_maximum_fusion.refs_1_.refs_2_, bf16[2,16,512,128]{3,2,1,0:T(8,128)(2,1)} %pad_maximum_fusion.refs_1_.refs_2_), custom_call_target="tpu_custom_call" | custom-call | flops 1073741824 | bytes 29360128 | tf_op jit(solution)/shard_map/pallas_call | solution.py:292
  39.8 16.3 %collective-permute-done.refs_3_.refs_4_ = bf16[2,16,512,128]{3,2,1,0:T(8,128)(2,1)} collective-permute-done((bf16[2,16,512,128]{3,2,1,0:T(8,128)(2,1)}, bf16[2,16,512,128]{3,2,1,0:T(8,128)(2,1)}, u32[]{:S(2)}, u32[]{:S(2)}) %collective-permute-start) | collective-permute-done | bytes 4194336 | tf_op jit(solution)/shard_map/ppermute | solution.py:20
  57.4 1.8 %constant_dynamic-slice_fusion.3 = (bf16[2,16,64,128]{3,2,1,0:T(8,128)(2,1)S(1)}, bf16[2,16,64,128]{3,2,1,0:T(8,128)(2,1)S(1)}, bf16[2,16,64,128]{3,2,1,0:T(8,128)(2,1)S(1)}, bf16[2,16,64,128]{3,2,1,0:T(8,128)(2,1)S(1)}) fusion(bf16[2,16,512,128]{3,2,1,0:T(8,128)(2,1)} %collective-permute-done.refs_3_.refs_4_, s32[]{:T(128)S(6)} %select_n.68, ...), kind=kLoop, calls=%fused_computation.34 | loop fusion | bytes 4194320 | tf_op jit(solution)/shard_map/dynamic_slice | solution.py:227
  59.2 1.5 pad_maximum_fusion.2
  60.8 2.6 %collective-permute-start.2 = (bf16[2,16,256,128]{3,2,1,0:T(8,128)(2,1)}, bf16[2,16,256,128]{3,2,1,0:T(8,128)(2,1)}, u32[]{:S(2)}, u32[]{:S(2)}) collective-permute-start(bf16[2,16,256,128]{3,2,1,0:T(8,128)(2,1)} %pad_maximum_fusion.2), channel_id=1, source_target_pairs={{0,2},{4,6},{8,10},{12,14},{16,18},{20,22},{24,26},{28,30},{1,3},{... | collective-permute-start | bytes 6291464 | tf_op jit(solution)/shard_map/ppermute | solution.py:306
  66.1 20.1 %shard_map.56 = (f32[16,256,128]{2,1,0:T(8,128)}, f32[16,256,128]{2,1,0:T(8,128)}, bf16[256,2048]{1,0:T(8,128)(2,1)}) custom-call(s32[10]{0:T(128)} %pad_add_fusion.refs_0_, s32[40]{0:T(128)} %reshape.111.refs_1_, bf16[16,512,128]{2,1,0:T(8,128)(2,1)} %bitcast.34, bf16[2,16,512,128]{3,2,1,0:T(8,128)(2,1)} %collective-permute-done.refs_3_.refs_4_, ...), custom_call_target="tpu_custom_call" | custom-call | flops 1342177280 | bytes 23068672 | tf_op jit(solution)/shard_map/pallas_call | solution.py:318
  86.3 6.6 %shard_map.62 = bf16[256,2048]{1,0:T(8,128)(2,1)} custom-call(s32[1]{0:T(128)} %bitcast.22.sel_ref, bf16[256,2048]{1,0:T(8,128)(2,1)} %get-tuple-element.32.a_ref, bf16[2048,4096]{1,0:T(8,128)(2,1)} %w_ref.9), custom_call_target="tpu_custom_call" | custom-call | flops 2147483648 | bytes 10485760 | tf_op jit(solution)/shard_map/pallas_call | solution.py:204
  92.9 1.5 collective-permute-start.7
  94.4 1.5 collective-permute-start.4
  95.8 6.6 %shard_map.57 = bf16[256,2048]{1,0:T(8,128)(2,1)} custom-call(s32[1]{0:T(128)} %bitcast.sel_ref, bf16[256,2048]{1,0:T(8,128)(2,1)} %get-tuple-element.32.a_ref, bf16[2048,4096]{1,0:T(8,128)(2,1)} %w_ref.9), custom_call_target="tpu_custom_call" | custom-call | flops 2147483648 | bytes 10485760 | tf_op jit(solution)/shard_map/pallas_call | solution.py:204
  102.5 27.5 %collective-permute-done.4.refs_11_.refs_12_ = bf16[2,16,64,128]{3,2,1,0:T(8,128)(2,1)} collective-permute-done((bf16[2,16,64,128]{3,2,1,0:T(8,128)(2,1)}, bf16[2,16,64,128]{3,2,1,0:T(8,128)(2,1)}, u32[]{:S(2)}, u32[]{:S(2)}) %collective-permute-start.4) | collective-permute-done | bytes 524320 | tf_op jit(solution)/shard_map/ppermute | solution.py:265
  131.6 10.5 %shard_map.58.a_ref = bf16[256,2048]{1,0:T(8,128)(2,1)} custom-call(s32[10]{0:T(128)} %pad_add_fusion.refs_0_, s32[40]{0:T(128)} %reshape.111.refs_1_, bf16[16,512,128]{2,1,0:T(8,128)(2,1)} %bitcast.35, f32[16,256,128]{2,1,0:T(8,128)} %get-tuple-element.33.refs_3_, f32[16,256,128]{2,1,0:T(8,128)} %get-tuple-element.34.refs_4_, ...), custom_call_target="tpu_custom_call" | custom-call | flops 268435456 | bytes 12058624 | tf_op jit(solution)/shard_map/pallas_call | solution.py:362
  142.2 5.8 %shard_map.61 = bf16[256,1536]{1,0:T(8,128)(2,1)} custom-call(s32[1]{0:T(128)} %bitcast.22.sel_ref, bf16[256,2048]{1,0:T(8,128)(2,1)} %shard_map.58.a_ref, bf16[2048,4096]{1,0:T(8,128)(2,1)} %w_ref.9), custom_call_target="tpu_custom_call" | custom-call | flops 1610612736 | bytes 8126464 | tf_op jit(solution)/shard_map/pallas_call | solution.py:204
  148.0 1.5 collective-permute-start.6
  149.5 3.3 %shard_map.60 = bf16[256,512]{1,0:T(8,128)(2,1)} custom-call(s32[1]{0:T(128)} %bitcast.22.sel_ref, bf16[256,2048]{1,0:T(8,128)(2,1)} %shard_map.58.a_ref, bf16[2048,4096]{1,0:T(8,128)(2,1)} %w_ref.9), custom_call_target="tpu_custom_call" | custom-call | flops 536870912 | bytes 3407872 | tf_op jit(solution)/shard_map/pallas_call | solution.py:204
  153.4 1.6 add_convert_fusion
  155.0 6.6 %shard_map.59 = bf16[256,2048]{1,0:T(8,128)(2,1)} custom-call(s32[1]{0:T(128)} %bitcast.sel_ref, bf16[256,2048]{1,0:T(8,128)(2,1)} %shard_map.58.a_ref, bf16[2048,4096]{1,0:T(8,128)(2,1)} %w_ref.9), custom_call_target="tpu_custom_call" | custom-call | flops 2147483648 | bytes 10485760 | tf_op jit(solution)/shard_map/pallas_call | solution.py:204
  163.0 1.5 add_convert_fusion.1
  (41 shorter events, 14.7 us)
Async XLA Ops:
  3.3 2.6 %copy-start = (bf16[1,16,512,128]{3,2,1,0:T(8,128)(2,1)}, bf16[1,16,512,128]{3,2,1,0:T(8,128)(2,1)S(1)}, u32[]{:S(2)}) copy-start(bf16[1,16,512,128]{3,2,1,0:T(8,128)(2,1)S(1)} %get-tuple-element.68) | copy-start | bytes 6291460
  3.3 4.6 %copy-start.5 = (s32[128,5]{0,1:T(8,128)S(1)}, s32[128,5]{0,1:T(8,128)}, u32[]{:S(2)}) copy-start(s32[128,5]{0,1:T(8,128)} %param.8) | copy-start | bytes 7684
  6.0 50.1 %collective-permute-start = (bf16[2,16,512,128]{3,2,1,0:T(8,128)(2,1)}, bf16[2,16,512,128]{3,2,1,0:T(8,128)(2,1)}, u32[]{:S(2)}, u32[]{:S(2)}) collective-permute-start(bf16[2,16,512,128]{3,2,1,0:T(8,128)(2,1)} %pad_maximum_fusion.refs_1_.refs_2_), channel_id=1, source_target_pairs={{0,2},{2,4},{4,6},{6,8},{8,10},{10,12},{12,14},{14,16},{16,18},{18... | collective-permute-start | bytes 12582920 | tf_op jit(solution)/shard_map/ppermute | solution.py:20
  20.9 1.7 %copy-start.1 = (bf16[1,16,512,128]{3,2,1,0:T(8,128)(2,1)S(1)}, bf16[1,16,512,128]{3,2,1,0:T(8,128)(2,1)}, u32[]{:S(2)}) copy-start(bf16[1,16,512,128]{3,2,1,0:T(8,128)(2,1)} %copy-done) | copy-start | bytes 6291460
  56.1 73.9 %collective-permute-start.1 = (bf16[2,16,256,128]{3,2,1,0:T(8,128)(2,1)}, bf16[2,16,256,128]{3,2,1,0:T(8,128)(2,1)S(1)}, u32[]{:S(2)}, u32[]{:S(2)}) collective-permute-start(bf16[2,16,256,128]{3,2,1,0:T(8,128)(2,1)} %pad_maximum_fusion.1), channel_id=1, source_target_pairs={{0,4},{4,8},{8,12},{12,16},{16,20},{20,24},{24,28},{1,5},{5,9},{9,... | collective-permute-start | bytes 6291464 | tf_op jit(solution)/shard_map/ppermute | solution.py:305
  60.8 69.2 %collective-permute-start.2 = (bf16[2,16,256,128]{3,2,1,0:T(8,128)(2,1)}, bf16[2,16,256,128]{3,2,1,0:T(8,128)(2,1)}, u32[]{:S(2)}, u32[]{:S(2)}) collective-permute-start(bf16[2,16,256,128]{3,2,1,0:T(8,128)(2,1)} %pad_maximum_fusion.2), channel_id=1, source_target_pairs={{0,2},{4,6},{8,10},{12,14},{16,18},{20,22},{24,26},{28,30},{1,3},{... | collective-permute-start | bytes 6291464 | tf_op jit(solution)/shard_map/ppermute | solution.py:306
  63.4 66.6 %collective-permute-start.3 = (bf16[2,16,128,128]{3,2,1,0:T(8,128)(2,1)}, bf16[2,16,128,128]{3,2,1,0:T(8,128)(2,1)S(1)}, u32[]{:S(2)}, u32[]{:S(2)}) collective-permute-start(bf16[2,16,128,128]{3,2,1,0:T(8,128)(2,1)} %pad_maximum_fusion.4), channel_id=1, source_target_pairs={{0,8},{2,10},{4,12},{6,14},{8,16},{10,18},{12,20},{14,22},{16,24},... | collective-permute-start | bytes 3145736 | tf_op jit(solution)/shard_map/ppermute | solution.py:265
  92.9 60.5 %collective-permute-start.7 = (bf16[256,2048]{1,0:T(8,128)(2,1)}, bf16[256,2048]{1,0:T(8,128)(2,1)}, u32[]{:S(2)}, u32[]{:S(2)}) collective-permute-start(bf16[256,2048]{1,0:T(8,128)(2,1)} %shard_map.62), channel_id=1, source_target_pairs={{0,1},{1,0},{2,3},{3,2},{4,5},{5,4},{6,7},{7,6},{8,9},{9,8},{10,11... | collective-permute-start | bytes 3145736 | tf_op jit(solution)/shard_map/ppermute | solution.py:359
  94.4 35.6 %collective-permute-start.4 = (bf16[2,16,64,128]{3,2,1,0:T(8,128)(2,1)}, bf16[2,16,64,128]{3,2,1,0:T(8,128)(2,1)}, u32[]{:S(2)}, u32[]{:S(2)}) collective-permute-start(bf16[2,16,64,128]{3,2,1,0:T(8,128)(2,1)} %get-tuple-element.37), channel_id=1, source_target_pairs={{0,16},{2,18},{4,20},{6,22},{8,24},{10,26},{12,28},{14,30},{1,17},... | collective-permute-start | bytes 1572872 | tf_op jit(solution)/shard_map/ppermute | solution.py:265
  130.0 1.0 copy-start.3
  130.0 1.6 copy-start.2
  148.0 5.4 %copy-start.4 = (bf16[256,2048]{1,0:T(8,128)(2,1)S(1)}, bf16[256,2048]{1,0:T(8,128)(2,1)}, u32[]{:S(2)}) copy-start(bf16[256,2048]{1,0:T(8,128)(2,1)} %shard_map.57) | copy-start | bytes 3145732
  148.0 15.0 %collective-permute-start.6 = (bf16[256,1536]{1,0:T(8,128)(2,1)}, bf16[256,1536]{1,0:T(8,128)(2,1)S(1)}, u32[]{:S(2)}, u32[]{:S(2)}) collective-permute-start(bf16[256,1536]{1,0:T(8,128)(2,1)} %shard_map.61), channel_id=1, source_target_pairs={{0,1},{1,0},{2,3},{3,2},{4,5},{5,4},{6,7},{7,6},{8,9},{9,8},{10,11... | collective-permute-start | bytes 2359304 | tf_op jit(solution)/shard_map/ppermute | solution.py:377
  152.8 10.2 %collective-permute-start.5 = (bf16[256,512]{1,0:T(8,128)(2,1)}, bf16[256,512]{1,0:T(8,128)(2,1)S(1)}, u32[]{:S(2)}, u32[]{:S(2)}) collective-permute-start(bf16[256,512]{1,0:T(8,128)(2,1)} %shard_map.60), channel_id=1, source_target_pairs={{0,1},{1,0},{2,3},{3,2},{4,5},{5,4},{6,7},{7,6},{8,9},{9,8},{10,11... | collective-permute-start | bytes 786440 | tf_op jit(solution)/shard_map/ppermute | solution.py:377
